TPU v7x, 32 devices: a whole 2x2x4 slice. The times are simulated.
32 devices in a mesh: cp: 2 (over y), tp: 4 (over x, core), ep: 4 (over z).
Axes of the slice: x: 2, y: 2, z: 4, core: 2. Of those that a mesh axis runs over, the one named last changes fastest.
Arguments:
- query: bfloat16 [8, 512, 4096], P('ep', 'cp', 'tp'), may hold values from -6 to 6
- keys: bfloat16 [8, 512, 512], P('ep', 'cp', 'tp'), may hold values from -6 to 6
- values: bfloat16 [8, 512, 512], P('ep', 'cp', 'tp'), may hold values from -24 to 24
- segment_ids: int32 [8, 512], P('ep', 'cp'), may hold values from 0 to 3, never falling along the last dimension, each value on 1 to 256 neighbouring positions
- query_norm_gain: float32 [128], replicated, may hold values from 0.25 to 1.75
- key_norm_gain: float32 [128], replicated, may hold values from 0.25 to 1.75
- out_weight: bfloat16 [4096, 2048], P('tp', 'cp'), may hold values from -0.09375 to 0.09375
- residual: bfloat16 [8, 512, 2048], P('ep', 'cp'), may hold values from -3 to 3
- norm_gain: float32 [2048], replicated, may hold values from 0.25 to 1.75
- router_weight: bfloat16 [2048, 16], replicated, may hold values from -0.125 to 0.125
- expert_ids: int32 [8, 512, 8], P('ep', 'cp'), may hold values from 0 to 15, all different within a row; in each aligned block of 64 rows (0 to 63, 64 to 127, ..., all dimensions but the last counted through in order) at most 36 rows name the same one
- expert_gate: bfloat16 [16, 2048, 768], P(('tp', 'ep'), None, 'cp'), may hold values from -0.125 to 0.125
- expert_up: bfloat16 [16, 2048, 768], P(('tp', 'ep'), None, 'cp'), may hold values from -0.125 to 0.125
- expert_down: bfloat16 [16, 2048, 768], P(('tp', 'ep'), None, 'cp'), may hold values from -0.21875 to 0.21875
Outputs:
- layer_out: bfloat16 [8, 512, 2048], P('ep', ('cp', 'tp'))
Inputs may be any that keep to these rules, and one draw needn't show every extreme that they name: `segment_ids`: document numbers never fall along a sequence. `expert_ids`: each token names 8 different experts; in every aligned block of 64 positions of a sequence no expert is named by more than 36 tokens, a bound that some block reaches.
All inputs are finite; a program needn't handle non-finite values.
Results may differ from a plain program's by a relative error of at most 0.007.
Values may be sent and summed in bfloat16 or wider, within the bound.
No kernel may reach another device: no remote copies, remote signals or barrier semaphores. Data moves between devices by JAX's collectives and lax.ppermute only.
A program may use at most 128 MiB of HBM per device.

v0:
```python
import jax
import jax.numpy as jnp
from jax import lax
from jax.sharding import PartitionSpec as P

HEAD_WIDTH = 128


def root_mean_scale(entries, gain):
    mean_sq = jnp.mean(entries * entries, axis=-1, keepdims=True)
    return entries * lax.rsqrt(mean_sq + 1e-06) * gain


def capacity(share, top_count, experts):
    return min(
        share, max(2, share * top_count // experts + max(1, share * top_count // (8 * experts)))
    )


def slot_numbers(ids, experts):
    flat_ids = ids.reshape(-1)
    table = (flat_ids[:, None] == jnp.arange(experts, dtype=jnp.int32)[None, :]).astype(jnp.int32)
    before = jnp.cumsum(table, axis=0) - table
    return jnp.sum(before * table, axis=1).reshape(ids.shape)


def route(state, ids, norm_gain, router_weight):
    normed = root_mean_scale(state, norm_gain).astype(jnp.bfloat16)
    logits = jnp.dot(normed, router_weight, preferred_element_type=jnp.float32)
    experts = router_weight.shape[1]
    picks = ids[:, :, None] == jnp.arange(experts, dtype=jnp.int32)[None, None, :]
    chosen = jnp.sum(jnp.where(picks, logits[:, None, :], jnp.float32(0.0)), axis=-1)
    raised = jnp.exp(chosen)
    return (normed, raised / jnp.sum(raised, axis=-1, keepdims=True))


def expert_rows(received, full_gate, full_up, full_down):
    width = received.shape[-1]
    flat_rows = received.reshape(-1, width)
    gate_act = jnp.dot(flat_rows, full_gate[0], preferred_element_type=jnp.float32)
    up_act = jnp.dot(flat_rows, full_up[0], preferred_element_type=jnp.float32)
    hidden_act = (jax.nn.silu(gate_act) * up_act).astype(jnp.bfloat16)
    served = jnp.einsum(
        "rf,df->rd", hidden_act, full_down[0], preferred_element_type=jnp.float32
    ).astype(jnp.bfloat16)
    return served.reshape(received.shape)


def shards(
    query,
    keys,
    values,
    segment_ids,
    query_norm_gain,
    key_norm_gain,
    out_weight,
    residual,
    norm_gain,
    router_weight,
    expert_ids,
    expert_gate,
    expert_up,
    expert_down,
):
    packs = query.shape[0]
    row_count = query.shape[1]
    head_count = query.shape[2] // HEAD_WIDTH
    width = residual.shape[2]
    experts = router_weight.shape[1]
    top_count = expert_ids.shape[2]
    score_scale = HEAD_WIDTH ** (-0.5)
    query_rows_normed = root_mean_scale(
        query.astype(jnp.float32).reshape(packs, row_count, head_count, HEAD_WIDTH), query_norm_gain
    ).astype(jnp.bfloat16)
    key_rows_normed = root_mean_scale(keys.astype(jnp.float32), key_norm_gain).astype(jnp.bfloat16)
    own_docs = segment_ids.astype(jnp.bfloat16)
    key_piece = lax.all_gather(key_rows_normed, "cp", axis=1, tiled=True)
    value_piece = lax.all_gather(values, "cp", axis=1, tiled=True)
    doc_piece = lax.all_gather(own_docs, "cp", axis=1, tiled=True)
    scores = (
        jnp.einsum(
            "pshd,pnd->phsn", query_rows_normed, key_piece, preferred_element_type=jnp.float32
        )
        * score_scale
    )
    same_doc = own_docs[:, :, None] == doc_piece[:, None, :]
    probs = jnp.where(same_doc[:, None], jnp.exp(scores), jnp.float32(0.0))
    denom = jnp.sum(probs, axis=-1)
    probs_b = probs.astype(jnp.bfloat16)
    summed = jnp.einsum("phsn,pnd->pshd", probs_b, value_piece, preferred_element_type=jnp.float32)
    denom, summed = (denom, summed)
    attn = (
        (summed / jnp.transpose(denom, (0, 2, 1))[:, :, :, None])
        .astype(jnp.bfloat16)
        .reshape(packs * row_count, head_count * HEAD_WIDTH)
    )
    partial_proj = jnp.dot(
        attn,
        lax.all_gather(out_weight, "cp", axis=1, tiled=True),
        preferred_element_type=jnp.float32,
    ).reshape(packs, row_count, width)
    full_gate, full_up, full_down = (
        lax.all_gather(expert_gate, "cp", axis=2, tiled=True),
        lax.all_gather(expert_up, "cp", axis=2, tiled=True),
        lax.all_gather(expert_down, "cp", axis=2, tiled=True),
    )
    share = row_count // lax.axis_size("tp")
    tp_index = lax.axis_index("tp")
    cap = capacity(share, top_count, experts)
    projected = lax.psum_scatter(partial_proj, "tp", scatter_dimension=1, tiled=True)
    first_row = tp_index * share
    state = lax.dynamic_slice_in_dim(residual, first_row, share, 1).astype(jnp.float32) + projected
    local_ids = lax.dynamic_slice_in_dim(expert_ids, first_row, share, 1).reshape(
        packs * share, top_count
    )
    normed, gates = route(state.reshape(packs * share, width), local_ids, norm_gain, router_weight)
    dev_cap = packs * cap
    slots = slot_numbers(local_ids, experts)
    target = (local_ids * dev_cap + slots).reshape(-1)
    sent_rows = jnp.broadcast_to(normed[:, None, :], (packs * share, top_count, width)).reshape(
        -1, width
    )
    buffer = (
        jnp.zeros((experts * dev_cap, width), jnp.bfloat16)
        .at[target]
        .set(sent_rows)
        .reshape(experts, dev_cap, width)
    )
    served = expert_rows(
        lax.all_to_all(buffer, ("tp", "ep"), split_axis=0, concat_axis=0, tiled=True),
        full_gate,
        full_up,
        full_down,
    )
    back = lax.all_to_all(served, ("tp", "ep"), split_axis=0, concat_axis=0, tiled=True)
    picked = back.reshape(experts * dev_cap, width)[target].reshape(packs * share, top_count, width)
    mixture = jnp.sum(gates[:, :, None] * picked.astype(jnp.float32), axis=1)
    layer_out = (state + mixture.reshape(packs, share, width)).astype(jnp.bfloat16)
    return layer_out


def solution(mesh):
    return jax.shard_map(
        shards,
        mesh=mesh,
        in_specs=(
            P("ep", "cp", "tp"),
            P("ep", "cp", "tp"),
            P("ep", "cp", "tp"),
            P("ep", "cp"),
            P(),
            P(),
            P("tp", "cp"),
            P("ep", "cp", None),
            P(),
            P(),
            P("ep", "cp", None),
            P(("tp", "ep"), None, "cp"),
            P(("tp", "ep"), None, "cp"),
            P(("tp", "ep"), None, "cp"),
        ),
        out_specs=P("ep", ("cp", "tp"), None),
        check_vma=False,
    )
```

profile of v0, /device:TPU:0, one launch (start us, length us, event | category | flops | bytes accessed | tf_op | source)
XLA Modules:
  0.0 424.7 jit_solution(739500518917911366)
XLA Ops:
  6.6 0.7 all-gather.5.cloned.1.call-update
  7.3 0.7 convert_element_type.52
  8.0 1.5 copy.74
  9.5 0.6 fusion.18
  10.5 5.2 %all_gather.21 = bf16[2,512]{1,0:T(2,128)(2,1)S(1)} all-gather(bf16[2,256]{1,0:T(2,128)(2,1)S(1)} %convert_element_type.52), channel_id=1, replica_groups=mesh['cp'=2,'tp'=4,'ep'=4] {'cp'}, dimensions={1}, use_global_device_ids=true | all-gather | bytes 3072 | tf_op jit(solution)/shard_map/all_gather | solution.py:79
  16.0 5.7 %all_gather.22 = bf16[2,512,128]{2,1,0:T(8,128)(2,1)S(1)} all-gather(bf16[2,256,128]{2,1,0:T(8,128)(2,1)S(1)} %fusion.31), channel_id=1, replica_groups=mesh['cp'=2,'tp'=4,'ep'=4] {'cp'}, dimensions={1}, use_global_device_ids=true | all-gather | bytes 393216 | tf_op jit(solution)/shard_map/all_gather | solution.py:77
  21.6 8.7 %all_gather.23 = bf16[2,512,128]{1,2,0:T(8,128)(2,1)S(1)} all-gather(bf16[2,256,128]{1,2,0:T(8,128)(2,1)S(1)} %copy.60), channel_id=1, replica_groups=mesh['cp'=2,'tp'=4,'ep'=4] {'cp'}, dimensions={1}, use_global_device_ids=true | all-gather | bytes 393216 | tf_op jit(solution)/shard_map/all_gather | solution.py:78
  30.6 0.7 fusion.20
  31.3 2.2 fusion.1
  33.5 1.7 fusion.21
  35.2 35.5 %all-gather.5.cloned.1.call-done = bf16[1024,2048]{1,0:T(8,128)(2,1)} async-done(((bf16[1024,1024]{1,0:T(8,128)(2,1)}), bf16[1024,2048]{1,0:T(8,128)(2,1)}) %all-gather.5.cloned.1.call-update) | async-done | bytes 4194320 | tf_op jit(solution)/shard_map/all_gather | solution.py:99
  70.7 6.5 %fusion.7 = f32[2,256,2048]{2,1,0:T(8,128)} fusion(bf16[2,256,1024]{1,2,0:T(8,128)(2,1)S(1)} %bitcast.104, bf16[1024,2048]{1,0:T(8,128)(2,1)} %all-gather.5.cloned.1.call-done), kind=kOutput, calls=%fused_computation.11 | convolution fusion | flops 2147483648 | bytes 9437184 | tf_op jit(solution)/shard_map/dot_general | solution.py:97
  77.2 0.7 copy-done.4
  78.3 4.5 %reduce-window.6 = s32[16,8,128]{2,1,0:T(8,128)S(1)} reduce-window(s32[16,8,128]{2,1,0:T(8,128)S(1)} %fusion.37, s32[]{:T(128)} %constant.14.clone.1), window={size=1x1x128 pad=0_0x0_0x127_0}, to_apply=%region_7.8 | reduce-window | flops 2080768 | bytes 131076 | tf_op jit(solution)/shard_map/reduce-window
  83.5 39.1 %reduce-scatter.2.cloned.1.call-done = f32[2,64,2048]{2,1,0:T(8,128)} async-done(((f32[2,256,2048]{2,1,0:T(8,128)}), f32[2,64,2048]{2,1,0:T(8,128)}) %reduce-scatter.2.cloned.1.call-update) | async-done | bytes 1048592 | tf_op jit(solution)/shard_map/reduce_scatter | solution.py:110
  122.6 1.6 multiply_reduce_fusion
  124.5 9.4 %scatter_custom_fusion = bf16[1152,2048]{1,0:T(8,128)(2,1)} fusion(s32[1024]{0:T(1024)S(1)} %bitcast.109, bf16[]{:T(256)} %constant.37.clone.1, bf16[128,2048]{1,0:T(8,128)(2,1)S(1)} %fusion.26), kind=kCustom, calls=%fused_computation.9 | custom fusion | bytes 5242882 | tf_op jit(solution)/shard_map/scatter | solution.py:126
  133.8 4.8 %all-to-all-start = ((bf16[16,72,2048]{2,1,0:T(8,128)(2,1)}), bf16[16,72,2048]{2,1,0:T(8,128)(2,1)}, u32[]{:S(2)}, u32[]{:S(2)}) async-start(bf16[16,72,2048]{2,1,0:T(8,128)(2,1)} %bitcast.101), calls=%async_computation.1 | async-start | bytes 9437184 | tf_op jit(solution)/shard_map/all_to_all | solution.py:130
  138.7 0.7 all-gather.7.cloned.1.call-update
  139.4 0.5 all-gather.9.cloned.1.call-update
  140.0 0.5 all-gather.11.cloned.1.call-update
  140.5 46.8 %all-gather.7.cloned.1.call-done = bf16[1,2048,768]{2,1,0:T(8,128)(2,1)} async-done(((bf16[1,2048,384]{2,1,0:T(8,128)(2,1)}), bf16[1,2048,768]{2,1,0:T(8,128)(2,1)}) %all-gather.7.cloned.1.call-update) | async-done | bytes 3145744 | tf_op jit(solution)/shard_map/all_gather | solution.py:103
  187.3 57.0 %all-to-all-done = bf16[16,72,2048]{2,1,0:T(8,128)(2,1)} async-done(((bf16[16,72,2048]{2,1,0:T(8,128)(2,1)}), bf16[16,72,2048]{2,1,0:T(8,128)(2,1)}, u32[]{:S(2)}, u32[]{:S(2)}) %all-to-all-start) | async-done | bytes 4718624 | tf_op jit(solution)/shard_map/all_to_all | solution.py:130
  244.3 9.4 %fusion.15 = f32[1152,768]{1,0:T(8,128)} fusion(bf16[1152,2048]{1,0:T(8,128)(2,1)} %bitcast.16, bf16[1,2048,768]{2,1,0:T(8,128)(2,1)} %all-gather.7.cloned.1.call-done), kind=kOutput, calls=%fused_computation.20 | convolution fusion | flops 3623878656 | bytes 11403264 | tf_op jit(solution)/shard_map/dot_general | solution.py:40
  253.7 8.5 %fusion.12 = bf16[1152,768]{1,0:T(8,128)(2,1)S(1)} fusion(bf16[1152,2048]{1,0:T(8,128)(2,1)} %bitcast.16, f32[1152,768]{1,0:T(8,128)} %fusion.15, bf16[1,2048,768]{2,1,0:T(8,128)(2,1)} %all-gather.9.cloned.1.call-done), kind=kOutput, calls=%fused_computation.17 | convolution fusion | flops 3629187072 | bytes 13172736 | tf_op jit(solution)/shard_map/dot_general | solution.py:41
  262.2 18.0 %all-gather.11.cloned.1.call-done = bf16[1,2048,768]{2,1,0:T(8,128)(2,1)} async-done(((bf16[1,2048,384]{2,1,0:T(8,128)(2,1)}), bf16[1,2048,768]{2,1,0:T(8,128)(2,1)}) %all-gather.11.cloned.1.call-update) | async-done | bytes 3145744 | tf_op jit(solution)/shard_map/all_gather | solution.py:105
  280.1 7.4 %convolution_convert_fusion = bf16[1152,2048]{1,0:T(8,128)(2,1)} fusion(bf16[1152,768]{1,0:T(8,128)(2,1)S(1)} %fusion.12, bf16[1,2048,768]{2,1,0:T(8,128)(2,1)} %all-gather.11.cloned.1.call-done), kind=kOutput, calls=%fused_computation.5 | convolution fusion | flops 3626237952 | bytes 9633792 | tf_op jit(solution)/shard_map/rf,df->rd/dot_general | solution.py:43
  287.6 5.7 %all-to-all-start.1 = ((bf16[16,72,2048]{2,1,0:T(8,128)(2,1)}), bf16[16,72,2048]{2,1,0:T(8,128)(2,1)}, u32[]{:S(2)}, u32[]{:S(2)}) async-start(bf16[16,72,2048]{2,1,0:T(8,128)(2,1)} %bitcast.102), calls=%async_computation.2 | async-start | bytes 9437184 | tf_op jit(solution)/shard_map/all_to_all | solution.py:135
  293.8 105.2 %all-to-all-done.1 = bf16[16,72,2048]{2,1,0:T(8,128)(2,1)} async-done(((bf16[16,72,2048]{2,1,0:T(8,128)(2,1)}), bf16[16,72,2048]{2,1,0:T(8,128)(2,1)}, u32[]{:S(2)}, u32[]{:S(2)}) %all-to-all-start.1) | async-done | bytes 4718624 | tf_op jit(solution)/shard_map/all_to_all | solution.py:135
  398.9 11.8 %gather_fusion = bf16[1024,2048]{1,0:T(8,128)(2,1)} fusion(bf16[1152,2048]{1,0:T(8,128)(2,1)} %bitcast.21, s32[1024]{0:T(1024)S(1)} %broadcast_clamp_fusion), kind=kCustom, calls=%fused_computation | custom fusion | bytes 8392704 | tf_op jit(solution)/shard_map/gather | solution.py:136
  410.7 6.5 %fusion = f32[128,2048]{1,0:T(8,128)S(1)} fusion(bf16[1024,2048]{1,0:T(8,128)(2,1)} %gather_fusion, f32[128,8]{1,0:T(8,128)S(1)} %copy.64), kind=kLoop, calls=%fused_computation.3 | loop fusion | flops 6029312 | bytes 5246976 | tf_op jit(solution)/shard_map/reduce_sum | solution.py:137
  417.3 0.9 add_convert_fusion
  (54 shorter events, 2.8 us)
Async XLA Ops:
  6.5 286.8 %copy-start = (bf16[2048,16]{0,1:T(8,128)(2,1)S(1)}, bf16[2048,16]{0,1:T(8,128)(2,1)}, u32[]{:S(2)}) copy-start(bf16[2048,16]{0,1:T(8,128)(2,1)} %param.23) | copy-start | bytes 196612
  6.5 3.8 copy-start.2
  6.5 9.1 %copy-start.1 = (bf16[2,256,128]{2,1,0:T(8,128)(2,1)S(1)}, bf16[2,256,128]{2,1,0:T(8,128)(2,1)}, u32[]{:S(2)}) copy-start(bf16[2,256,128]{2,1,0:T(8,128)(2,1)} %param.15) | copy-start | bytes 393220
  6.5 9.3 %copy-start.5 = (f32[128]{0:T(128)S(1)}, f32[128]{0:T(128)}, u32[]{:S(2)}) copy-start(f32[128]{0:T(128)} %param.19) | copy-start | bytes 1540
  6.5 64.2 %all-gather.5.cloned.1.call-start = ((), (), s32[]{:S(2)}) async-start(), calls=%async_computation.3 | async-start | bytes 6291456 | tf_op jit(solution)/shard_map/all_gather | solution.py:99
  7.3 23.3 %copy-start.6 = (f32[128]{0:T(128)S(1)}, f32[128]{0:T(128)}, u32[]{:S(2)}) copy-start(f32[128]{0:T(128)} %param.18) | copy-start | bytes 1540
  7.3 115.3 %reduce-scatter.2.cloned.1.call-start = ((), (), s32[]{:S(2)}) async-start(), calls=%async_computation.4 | async-start | bytes 5242880 | tf_op jit(solution)/shard_map/reduce_scatter | solution.py:110
  77.2 0.7 copy-start.4
  77.2 47.1 %copy-start.3 = (f32[2048]{0:T(1024)S(1)}, f32[2048]{0:T(1024)}, u32[]{:S(2)}) copy-start(f32[2048]{0:T(1024)} %param.22) | copy-start | bytes 24580
  133.8 110.5 %all-to-all-start = ((bf16[16,72,2048]{2,1,0:T(8,128)(2,1)}), bf16[16,72,2048]{2,1,0:T(8,128)(2,1)}, u32[]{:S(2)}, u32[]{:S(2)}) async-start(bf16[16,72,2048]{2,1,0:T(8,128)(2,1)} %bitcast.101), calls=%async_computation.1 | async-start | bytes 9437184 | tf_op jit(solution)/shard_map/all_to_all | solution.py:130
  138.6 48.7 %all-gather.7.cloned.1.call-start = ((), (), s32[]{:S(2)}) async-start(), calls=%async_computation.5 | async-start | bytes 4718592 | tf_op jit(solution)/shard_map/all_gather | solution.py:103
  139.3 114.3 %all-gather.9.cloned.1.call-start = ((), (), s32[]{:S(2)}) async-start(), calls=%async_computation.6 | async-start | bytes 4718592 | tf_op jit(solution)/shard_map/all_gather | solution.py:104
  139.9 140.2 %all-gather.11.cloned.1.call-start = ((), (), s32[]{:S(2)}) async-start(), calls=%async_computation.7 | async-start | bytes 4718592 | tf_op jit(solution)/shard_map/all_gather | solution.py:105
  287.6 111.3 %all-to-all-start.1 = ((bf16[16,72,2048]{2,1,0:T(8,128)(2,1)}), bf16[16,72,2048]{2,1,0:T(8,128)(2,1)}, u32[]{:S(2)}, u32[]{:S(2)}) async-start(bf16[16,72,2048]{2,1,0:T(8,128)(2,1)} %bitcast.102), calls=%async_computation.2 | async-start | bytes 9437184 | tf_op jit(solution)/shard_map/all_to_all | solution.py:135
Sparse Core Ops, SparseCore 0:
  8.9 61.7 all-gather.4
  77.4 45.2 reduce-scatter.1
  141.1 46.1 all-gather.6
  188.7 44.9 all-gather.8
  235.2 44.9 all-gather.10
where the time goes:
time: 425 us
  waiting for transfers between devices  304 us (72%)
  matrix products  35.9 us (8%)
  local copies, waits for them, and re-layouts  24.7 us (6%)
  blocking collectives  19.5 us (5%)
  other arithmetic  16.6 us (4%)
  between operations  13.4 us (3%)
  starting transfers between devices  10.6 us (2%)
    all_to_all x1, waiting for transfers between devices, shards(): lax.all_to_all(served, ('tp', 'ep'), split_axis=0, concat_axis=0, tiled=T...  105 us
    all_to_all x1, waiting for transfers between devices, shards(): lax.all_to_all(buffer, ('tp', 'ep'), split_axis=0, concat_axis=0, tiled=T...  57 us
    all_gather x1, waiting for transfers between devices, shards(): lax.all_gather(expert_gate, 'cp', axis=2, tiled=True)  46.8 us
    reduce_scatter x1, waiting for transfers between devices, shards(): lax.psum_scatter(partial_proj, 'tp', scatter_dimension=1, tiled=True)  39.1 us
    all_gather x1, waiting for transfers between devices, shards(): lax.all_gather(out_weight, 'cp', axis=1, tiled=True)  35.5 us
    all_gather x1, waiting for transfers between devices, shards(): lax.all_gather(expert_down, 'cp', axis=2, tiled=True)  18 us
    gather x1, local copies, waits for them, and re-layouts, shards(): back.reshape(experts * dev_cap, width)[target]  11.8 us
    dot_general x1, matrix products, expert_rows(): jnp.dot(flat_rows, full_gate[0], preferred_element_type=jnp.float32)  9.4 us
  transfers between devices with their start and end apart: 7, of which 6 were waited for; matrix products, arithmetic and copies ran while one was open for 8% of the time, Pallas kernels for 0%

commit v1 on v0

--- a/solution.py
+++ b/solution.py
@@ -1,3 +1,5 @@
+import functools
+
 import jax
 import jax.numpy as jnp
 from jax import lax
@@ -32,6 +34,14 @@
     chosen = jnp.sum(jnp.where(picks, logits[:, None, :], jnp.float32(0.0)), axis=-1)
     raised = jnp.exp(chosen)
     return (normed, raised / jnp.sum(raised, axis=-1, keepdims=True))
+
+
+def cp_pieces(x, n_cp):
+    pieces = [x]
+    for shift in range(1, n_cp):
+        perm = [(i, (i + shift) % n_cp) for i in range(n_cp)]
+        pieces.append(lax.ppermute(x, "cp", perm))
+    return pieces
 
 
 def expert_rows(received, full_gate, full_up, full_down):
@@ -61,6 +71,10 @@
     expert_gate,
     expert_up,
     expert_down,
+    *,
+    n_cp,
+    n_tp,
+    n_ep,
 ):
     packs = query.shape[0]
     row_count = query.shape[1]
@@ -69,43 +83,47 @@
     experts = router_weight.shape[1]
     top_count = expert_ids.shape[2]
     score_scale = HEAD_WIDTH ** (-0.5)
+
     query_rows_normed = root_mean_scale(
         query.astype(jnp.float32).reshape(packs, row_count, head_count, HEAD_WIDTH), query_norm_gain
     ).astype(jnp.bfloat16)
     key_rows_normed = root_mean_scale(keys.astype(jnp.float32), key_norm_gain).astype(jnp.bfloat16)
-    own_docs = segment_ids.astype(jnp.bfloat16)
-    key_piece = lax.all_gather(key_rows_normed, "cp", axis=1, tiled=True)
-    value_piece = lax.all_gather(values, "cp", axis=1, tiled=True)
-    doc_piece = lax.all_gather(own_docs, "cp", axis=1, tiled=True)
+    key_value = jnp.concatenate([key_rows_normed, values], axis=-1)
+    kv_all = jnp.concatenate(cp_pieces(key_value, n_cp), axis=1)
+    doc_all = jnp.concatenate(cp_pieces(segment_ids, n_cp), axis=1)
+    key_piece = kv_all[..., :HEAD_WIDTH]
+    value_piece = kv_all[..., HEAD_WIDTH:]
     scores = (
         jnp.einsum(
             "pshd,pnd->phsn", query_rows_normed, key_piece, preferred_element_type=jnp.float32
         )
         * score_scale
     )
-    same_doc = own_docs[:, :, None] == doc_piece[:, None, :]
+    same_doc = segment_ids[:, :, None] == doc_all[:, None, :]
     probs = jnp.where(same_doc[:, None], jnp.exp(scores), jnp.float32(0.0))
     denom = jnp.sum(probs, axis=-1)
     probs_b = probs.astype(jnp.bfloat16)
     summed = jnp.einsum("phsn,pnd->pshd", probs_b, value_piece, preferred_element_type=jnp.float32)
-    denom, summed = (denom, summed)
     attn = (
         (summed / jnp.transpose(denom, (0, 2, 1))[:, :, :, None])
         .astype(jnp.bfloat16)
         .reshape(packs * row_count, head_count * HEAD_WIDTH)
     )
+    full_out_weight = lax.all_gather(out_weight, "cp", axis=1, tiled=True)
     partial_proj = jnp.dot(
-        attn,
-        lax.all_gather(out_weight, "cp", axis=1, tiled=True),
-        preferred_element_type=jnp.float32,
+        attn, full_out_weight, preferred_element_type=jnp.float32
     ).reshape(packs, row_count, width)
-    full_gate, full_up, full_down = (
-        lax.all_gather(expert_gate, "cp", axis=2, tiled=True),
-        lax.all_gather(expert_up, "cp", axis=2, tiled=True),
-        lax.all_gather(expert_down, "cp", axis=2, tiled=True),
-    )
-    share = row_count // lax.axis_size("tp")
+
+    full_out_weight, expert_gate, expert_up, expert_down = lax.optimization_barrier(
+        (full_out_weight, expert_gate, expert_up, expert_down)
+    )
+    full_gate = jnp.concatenate(cp_pieces(expert_gate, n_cp), axis=2)
+    full_up = jnp.concatenate(cp_pieces(expert_up, n_cp), axis=2)
+    full_down = jnp.concatenate(cp_pieces(expert_down, n_cp), axis=2)
+
+    share = row_count // n_tp
     tp_index = lax.axis_index("tp")
+    ep_index = lax.axis_index("ep")
     cap = capacity(share, top_count, experts)
     projected = lax.psum_scatter(partial_proj, "tp", scatter_dimension=1, tiled=True)
     first_row = tp_index * share
@@ -116,32 +134,56 @@
     normed, gates = route(state.reshape(packs * share, width), local_ids, norm_gain, router_weight)
     dev_cap = packs * cap
     slots = slot_numbers(local_ids, experts)
-    target = (local_ids * dev_cap + slots).reshape(-1)
-    sent_rows = jnp.broadcast_to(normed[:, None, :], (packs * share, top_count, width)).reshape(
-        -1, width
-    )
-    buffer = (
-        jnp.zeros((experts * dev_cap, width), jnp.bfloat16)
-        .at[target]
-        .set(sent_rows)
-        .reshape(experts, dev_cap, width)
-    )
-    served = expert_rows(
-        lax.all_to_all(buffer, ("tp", "ep"), split_axis=0, concat_axis=0, tiled=True),
-        full_gate,
-        full_up,
-        full_down,
-    )
-    back = lax.all_to_all(served, ("tp", "ep"), split_axis=0, concat_axis=0, tiled=True)
-    picked = back.reshape(experts * dev_cap, width)[target].reshape(packs * share, top_count, width)
-    mixture = jnp.sum(gates[:, :, None] * picked.astype(jnp.float32), axis=1)
+
+    home_rows = packs * share
+    meta = jnp.concatenate(
+        [local_ids.astype(jnp.float32), slots.astype(jnp.float32), gates], axis=-1
+    )
+    normed_all = lax.all_gather(normed, "ep", axis=0, tiled=True)
+    meta_all = lax.all_gather(meta, "ep", axis=0, tiled=True)
+    ids_all = meta_all[:, :top_count].astype(jnp.int32)
+    slots_all = meta_all[:, top_count : 2 * top_count].astype(jnp.int32)
+    gates_all = meta_all[:, 2 * top_count :]
+    gathered = n_ep * home_rows
+    home_of = (jnp.arange(gathered, dtype=jnp.int32) // home_rows)[:, None]
+    cap2 = n_ep * dev_cap
+    n_slots = n_tp * cap2
+    mine = (ids_all % n_ep) == ep_index
+    target = jnp.where(
+        mine, (ids_all // n_ep) * cap2 + home_of * dev_cap + slots_all, jnp.int32(-1)
+    )
+    hit = target[None, :, :] == jnp.arange(n_slots, dtype=jnp.int32)[:, None, None]
+    select = jnp.any(hit, axis=-1).astype(jnp.bfloat16)
+    weight = jnp.sum(jnp.where(hit, gates_all[None, :, :], jnp.float32(0.0)), axis=-1)
+
+    buffer = jnp.dot(select, normed_all, preferred_element_type=jnp.float32).astype(jnp.bfloat16)
+    received = lax.all_to_all(
+        buffer.reshape(n_tp, cap2, width), "tp", split_axis=0, concat_axis=0, tiled=True
+    )
+    served = expert_rows(received, full_gate, full_up, full_down)
+    back = lax.all_to_all(served, "tp", split_axis=0, concat_axis=0, tiled=True).reshape(
+        n_slots, width
+    )
+
+    weight_hi = weight.astype(jnp.bfloat16)
+    weight_lo = (weight - weight_hi.astype(jnp.float32)).astype(jnp.bfloat16)
+    contract = (((0,), (0,)), ((), ()))
+    partial = lax.dot_general(
+        weight_hi, back, contract, preferred_element_type=jnp.float32
+    ) + lax.dot_general(weight_lo, back, contract, preferred_element_type=jnp.float32)
+    mixture = lax.psum_scatter(
+        partial.reshape(n_ep, home_rows, width), "ep", scatter_dimension=0, tiled=True
+    )
     layer_out = (state + mixture.reshape(packs, share, width)).astype(jnp.bfloat16)
     return layer_out
 
 
 def solution(mesh):
+    body = functools.partial(
+        shards, n_cp=mesh.shape["cp"], n_tp=mesh.shape["tp"], n_ep=mesh.shape["ep"]
+    )
     return jax.shard_map(
-        shards,
+        body,
         mesh=mesh,
         in_specs=(
             P("ep", "cp", "tp"),

time: 425 us -> 453 us (1.066)
  local copies, waits for them, and re-layouts: 24.7 us -> 2.69 us
  other arithmetic: 16.6 us -> 38.4 us
  matrix products: 35.9 us -> 51.9 us
  waiting for transfers between devices: 304 us -> 316 us
  starting transfers between devices: 10.6 us -> 17 us
  blocking collectives: 19.5 us -> 13.7 us
    all_to_all x2, waiting for transfers between devices: 162 us -> 58.2 us  [the longest x1 41.8 us: shards(): lax.all_to_all(served, 'tp', split_axis=0, concat_axis=0, tiled=True)]
    ppermute x0 -> x5, waiting for transfers between devices: none -> 80.2 us  [cp_pieces(): pieces.append(lax.ppermute(x, 'cp', perm))]
    reduce_scatter x0 -> x1, waiting for transfers between devices: none -> 74.7 us  [shards(): lax.psum_scatter(partial.reshape(n_ep, home_rows, width), 'ep', scatter_d...]
    all_gather x4 -> x2, waiting for transfers between devices: 100 us -> 57.1 us  [the longest x1 43.3 us: shards(): full_out_weight = lax.all_gather(out_weight, 'cp', axis=1, tiled=True)]
    reduce_or x0 -> x1, other arithmetic: none -> 12.3 us  [shards(): select = jnp.any(hit, axis=-1).astype(jnp.bfloat16)]
    gather x1 -> x0, local copies, waits for them, and re-layouts: 11.8 us -> none  [shards(): back.reshape(experts * dev_cap, width)[target]]
    scatter x1 -> x0, local copies, waits for them, and re-layouts: 9.36 us -> none  [shards(): buffer = jnp.zeros((experts * dev_cap, width), jnp.bfloat16).at[target].s...]
    dot_general x2 -> x4, matrix products: 15 us -> 24 us  [the longest x1 6.88 us: shards(): lax.dot_general(weight_lo, back, contract, preferred_element_type=jnp.flo...]
  transfers between devices with their start and end apart: 7 -> 11, of which waited for: 6 -> 10; matrix products, arithmetic and copies ran while one was open for 8% -> 11% of each run, Pallas kernels for 0% -> 0%
where the time goes in v1:
time: 453 us
  waiting for transfers between devices  316 us (70%)
  matrix products  51.9 us (11%)
  other arithmetic  38.4 us (8%)
  starting transfers between devices  17 us (4%)
  blocking collectives  13.7 us (3%)
  between operations  13.4 us (3%)
    ppermute x5, waiting for transfers between devices, cp_pieces(): pieces.append(lax.ppermute(x, 'cp', perm))  80.2 us
    reduce_scatter x1, waiting for transfers between devices, shards(): lax.psum_scatter(partial.reshape(n_ep, home_rows, width), 'ep', scatter_d...  74.7 us
    reduce_scatter x1, waiting for transfers between devices, shards(): lax.psum_scatter(partial_proj, 'tp', scatter_dimension=1, tiled=True)  44.6 us
    all_gather x1, waiting for transfers between devices, shards(): full_out_weight = lax.all_gather(out_weight, 'cp', axis=1, tiled=True)  43.3 us
    all_to_all x1, waiting for transfers between devices, shards(): lax.all_to_all(served, 'tp', split_axis=0, concat_axis=0, tiled=True)  41.8 us
    all_to_all x1, waiting for transfers between devices, shards(): lax.all_to_all(buffer.reshape(n_tp, cap2, width), 'tp', split_axis=0, con...  16.4 us
    dot_general x1, matrix products, expert_rows(): jnp.einsum('rf,df->rd', hidden_act, full_down[0], preferred_element_type=...  14.3 us
    all_gather x1, waiting for transfers between devices, shards(): normed_all = lax.all_gather(normed, 'ep', axis=0, tiled=True)  13.8 us
  transfers between devices with their start and end apart: 11, of which 10 were waited for; matrix products, arithmetic and copies ran while one was open for 11% of the time, Pallas kernels for 0%

profile of v1, /device:TPU:0, one launch (start us, length us, event | category | flops | bytes accessed | tf_op | source)
XLA Modules:
  0.0 452.7 jit_solution(11138849658086565979)
XLA Ops:
  7.3 3.0 collective-permute-start.1
  10.3 1.0 fusion.31
  13.5 1.5 copy.78
  16.9 4.4 collective-permute-done
  21.3 2.2 fusion.1
  23.5 1.6 fusion.21
  25.1 43.3 %all-gather.3.cloned.1.call-done = bf16[1024,2048]{1,0:T(8,128)(2,1)} async-done(((bf16[1024,1024]{1,0:T(8,128)(2,1)}), bf16[1024,2048]{1,0:T(8,128)(2,1)}) %all-gather.3.cloned.1.call-update) | async-done | bytes 4194320 | tf_op jit(solution)/shard_map/all_gather | solution.py:112
  68.4 6.5 %fusion.5 = f32[2,256,2048]{2,1,0:T(8,128)} fusion(bf16[2,256,1024]{1,2,0:T(8,128)(2,1)S(1)} %bitcast.104, bf16[1024,2048]{1,0:T(8,128)(2,1)} %all-gather.3.cloned.1.call-done), kind=kOutput, calls=%fused_computation.9 | convolution fusion | flops 2147483648 | bytes 9437184 | tf_op jit(solution)/shard_map/dot_general | solution.py:113
  75.0 44.6 %reduce-scatter.3.cloned.1.call-done = f32[2,64,2048]{2,1,0:T(8,128)} async-done(((f32[2,256,2048]{2,1,0:T(8,128)}), f32[2,64,2048]{2,1,0:T(8,128)}) %reduce-scatter.3.cloned.1.call-update) | async-done | bytes 1048592 | tf_op jit(solution)/shard_map/reduce_scatter | solution.py:128
  119.6 1.6 multiply_reduce_fusion
  122.7 4.5 reduce-window.6
  127.8 1.3 fusion.55
  129.2 13.7 %all_gather.10 = f32[512,24]{0,1:T(8,128)S(1)} all-gather(f32[128,24]{0,1:T(8,128)S(1)} %pad_maximum_fusion.2), channel_id=1, replica_groups=mesh['cp'=2,'tp'=4,'ep'=4] {'ep'}, dimensions={0}, use_global_device_ids=true | all-gather | bytes 61440 | tf_op jit(solution)/shard_map/all_gather | solution.py:143
  142.9 12.3 %fusion = pred[1152,512]{1,0:T(8,128)(4,1)S(1)} fusion(s32[512,8]{0,1:T(8,128)S(1)} %fusion.42), kind=kLoop, calls=%fused_computation.2 | loop fusion | flops 8847360 | bytes 606208 | tf_op jit(solution)/shard_map/reduce_or | solution.py:156
  155.3 13.8 %all-gather.5.cloned.1.call-done = bf16[512,2048]{1,0:T(8,128)(2,1)} async-done(((bf16[128,2048]{1,0:T(8,128)(2,1)}), bf16[512,2048]{1,0:T(8,128)(2,1)}) %all-gather.5.cloned.1.call-update) | async-done | bytes 2097168 | tf_op jit(solution)/shard_map/all_gather | solution.py:142
  169.1 5.8 %convolution_convert_fusion.1 = bf16[1152,2048]{1,0:T(8,128)(2,1)} fusion(pred[1152,512]{1,0:T(8,128)(4,1)S(1)} %fusion, bf16[512,2048]{1,0:T(8,128)(2,1)} %all-gather.5.cloned.1.call-done), kind=kOutput, calls=%fused_computation.5 | convolution fusion | flops 2418278400 | bytes 7405568 | tf_op jit(solution)/shard_map/dot_general | solution.py:159
  174.9 5.1 %all-to-all-start = ((bf16[4,288,2048]{2,1,0:T(8,128)(2,1)}), bf16[4,288,2048]{2,1,0:T(8,128)(2,1)}, u32[]{:S(2)}, u32[]{:S(2)}) async-start(bf16[4,288,2048]{2,1,0:T(8,128)(2,1)} %bitcast.102), calls=%async_computation.1 | async-start | bytes 9437184 | tf_op jit(solution)/shard_map/all_to_all | solution.py:160
  180.0 1.6 collective-permute-start.2
  182.1 1.5 collective-permute-start.3
  183.6 33.8 %collective-permute-done.2 = bf16[1,2048,384]{2,1,0:T(8,128)(2,1)} collective-permute-done((bf16[1,2048,384]{2,1,0:T(8,128)(2,1)S(1)}, bf16[1,2048,384]{2,1,0:T(8,128)(2,1)}, u32[]{:S(2)}, u32[]{:S(2)}) %collective-permute-start.2) | collective-permute-done | bytes 1572896 | tf_op jit(solution)/shard_map/ppermute | solution.py:43
  217.4 16.4 %all-to-all-done = bf16[4,288,2048]{2,1,0:T(8,128)(2,1)} async-done(((bf16[4,288,2048]{2,1,0:T(8,128)(2,1)}), bf16[4,288,2048]{2,1,0:T(8,128)(2,1)}, u32[]{:S(2)}, u32[]{:S(2)}) %all-to-all-start) | async-done | bytes 4718624 | tf_op jit(solution)/shard_map/all_to_all | solution.py:160
  233.8 8.5 %fusion.10 = f32[1152,768]{1,0:T(8,128)} fusion(bf16[1152,2048]{1,0:T(8,128)(2,1)} %bitcast.12, bf16[1,2048,384]{2,1,0:T(8,128)(2,1)} %collective-permute-done.2, bf16[1,2048,384]{2,1,0:T(8,128)(2,1)S(1)} %copy-done.7), kind=kOutput, calls=%fused_computation.16 | convolution fusion | flops 3630170112 | bytes 11403264 | tf_op jit(solution)/shard_map/dot_general | solution.py:50
  242.3 8.8 %collective-permute-done.4 = bf16[1,2048,384]{2,1,0:T(8,128)(2,1)} collective-permute-done((bf16[1,2048,384]{2,1,0:T(8,128)(2,1)}, bf16[1,2048,384]{2,1,0:T(8,128)(2,1)}, u32[]{:S(2)}, u32[]{:S(2)}) %collective-permute-start.4) | collective-permute-done | bytes 1572896 | tf_op jit(solution)/shard_map/ppermute | solution.py:43
  251.1 33.2 %collective-permute-done.3 = bf16[1,2048,384]{2,1,0:T(8,128)(2,1)} collective-permute-done((bf16[1,2048,384]{2,1,0:T(8,128)(2,1)}, bf16[1,2048,384]{2,1,0:T(8,128)(2,1)}, u32[]{:S(2)}, u32[]{:S(2)}) %collective-permute-start.3) | collective-permute-done | bytes 1572896 | tf_op jit(solution)/shard_map/ppermute | solution.py:43
  284.3 14.3 %convolution_convert_fusion = bf16[1152,2048]{1,0:T(8,128)(2,1)} fusion(bf16[1,2048,384]{2,1,0:T(8,128)(2,1)} %collective-permute-done.4, bf16[1,2048,384]{2,1,0:T(8,128)(2,1)} %param.27, f32[1152,768]{1,0:T(8,128)} %fusion.10, bf16[1152,2048]{1,0:T(8,128)(2,1)} %bitcast.12, bf16[1,2048,384]{2,1,0:T(8,128)(2,1)} %collective-permute-done.3, ...), kind=kOutput, calls=%fused_computation.4 | convolution fusion | flops 7268007936 | bytes 19267584 | tf_op jit(solution)/shard_map/rf,df->rd/dot_general | solution.py:53
  298.6 5.2 %all-to-all-start.1 = ((bf16[4,288,2048]{2,1,0:T(8,128)(2,1)}), bf16[4,288,2048]{2,1,0:T(8,128)(2,1)}, u32[]{:S(2)}, u32[]{:S(2)}) async-start(bf16[4,288,2048]{2,1,0:T(8,128)(2,1)} %bitcast.103), calls=%async_computation.2 | async-start | bytes 9437184 | tf_op jit(solution)/shard_map/all_to_all | solution.py:164
  303.8 12.0 %select_reduce_fusion = f32[1152,512]{1,0:T(8,128)S(1)} fusion(f32[512,8]{0,1:T(8,128)S(1)} %slice.34, s32[512,8]{0,1:T(8,128)S(1)} %fusion.42), kind=kLoop, calls=%fused_computation | loop fusion | flops 13565952 | bytes 2392064 | tf_op jit(solution)/shard_map/reduce_sum | solution.py:157
  315.8 41.8 %all-to-all-done.1 = bf16[4,288,2048]{2,1,0:T(8,128)(2,1)} async-done(((bf16[4,288,2048]{2,1,0:T(8,128)(2,1)}), bf16[4,288,2048]{2,1,0:T(8,128)(2,1)}, u32[]{:S(2)}, u32[]{:S(2)}) %all-to-all-start.1) | async-done | bytes 4718624 | tf_op jit(solution)/shard_map/all_to_all | solution.py:164
  357.6 4.8 %fusion.29 = f32[512,2048]{1,0:T(8,128)S(1)} fusion(bf16[1152,2048]{1,0:T(8,128)(2,1)} %bitcast.17, f32[1152,512]{1,0:T(8,128)S(1)} %select_reduce_fusion), kind=kOutput, calls=%fused_computation.44 | convolution fusion | flops 2416508928 | bytes 11272192 | tf_op jit(solution)/shard_map/dot_general | solution.py:171
  362.4 6.9 %convolution_add_fusion = f32[512,2048]{1,0:T(8,128)} fusion(f32[512,2048]{1,0:T(8,128)S(1)} %fusion.29, bf16[1152,2048]{1,0:T(8,128)(2,1)} %bitcast.17, f32[1152,512]{1,0:T(8,128)S(1)} %select_reduce_fusion), kind=kOutput, calls=%fused_computation.26 | convolution fusion | flops 2419326976 | bytes 15466496 | tf_op jit(solution)/shard_map/dot_general | solution.py:173
  369.3 74.7 %reduce-scatter.5.cloned.1.call-done = f32[1,128,2048]{2,1,0:T(8,128)} async-done(((f32[4,128,2048]{2,1,0:T(8,128)}), f32[1,128,2048]{2,1,0:T(8,128)}) %reduce-scatter.5.cloned.1.call-update) | async-done | bytes 1048592 | tf_op jit(solution)/shard_map/reduce_scatter | solution.py:174
  444.0 2.1 add_convert_fusion
  (66 shorter events, 7.6 us)
Async XLA Ops:
  6.5 121.3 %copy-start = (bf16[2048,16]{0,1:T(8,128)(2,1)S(1)}, bf16[2048,16]{0,1:T(8,128)(2,1)}, u32[]{:S(2)}) copy-start(bf16[2048,16]{0,1:T(8,128)(2,1)} %param.23) | copy-start | bytes 196612
  6.5 61.8 %all-gather.3.cloned.1.call-start = ((), (), s32[]{:S(2)}) async-start(), calls=%async_computation.4 | async-start | bytes 6291456 | tf_op jit(solution)/shard_map/all_gather | solution.py:112
  7.3 8.6 %copy-start.6 = (f32[128]{0:T(128)S(1)}, f32[128]{0:T(128)}, u32[]{:S(2)}) copy-start(f32[128]{0:T(128)} %param.18) | copy-start | bytes 1540
  7.3 112.3 %reduce-scatter.3.cloned.1.call-start = ((), (), s32[]{:S(2)}) async-start(), calls=%async_computation.5 | async-start | bytes 5242880 | tf_op jit(solution)/shard_map/reduce_scatter | solution.py:128
  7.3 9.3 %collective-permute-start.1 = (s32[2,256]{1,0:T(2,128)}, s32[2,256]{1,0:T(2,128)S(1)}, u32[]{:S(2)}, u32[]{:S(2)}) collective-permute-start(s32[2,256]{1,0:T(2,128)} %param.17), channel_id=1, source_target_pairs={{0,16},{16,0},{1,17},{17,1},{2,18},{18,2},{3,19},{19,3},{4,20},{20... | collective-permute-start | bytes 6152 | tf_op jit(solution)/shard_map/ppermute | solution.py:43
  13.4 7.8 %collective-permute-start = (bf16[2,256,256]{2,1,0:T(8,128)(2,1)S(1)}, bf16[2,256,256]{2,1,0:T(8,128)(2,1)S(1)}, u32[]{:S(2)}, u32[]{:S(2)}) collective-permute-start(bf16[2,256,256]{2,1,0:T(8,128)(2,1)S(1)} %pad_maximum_fusion.1), channel_id=1, source_target_pairs={{0,16},{16,0},{1,17},{17,1},{2,18},{18,2},{3,19},{19,3},{4,20},{20... | collective-permute-start | bytes 786440 | tf_op jit(solution)/shard_map/ppermute | solution.py:43
  15.0 1.6 copy-start.4
  15.0 6.2 %copy-start.2 = (bf16[2,256,128]{2,1,0:T(8,128)(2,1)S(1)}, bf16[2,256,128]{2,1,0:T(8,128)(2,1)}, u32[]{:S(2)}) copy-start(bf16[2,256,128]{2,1,0:T(8,128)(2,1)} %param.16) | copy-start | bytes 393220
  74.9 46.4 %copy-start.3 = (f32[2048]{0:T(1024)S(1)}, f32[2048]{0:T(1024)}, u32[]{:S(2)}) copy-start(f32[2048]{0:T(1024)} %param.22) | copy-start | bytes 24580
  74.9 47.3 %copy-start.5 = (s32[2,256,8]{1,2,0:T(8,128)S(1)}, s32[2,256,8]{1,2,0:T(8,128)}, u32[]{:S(2)}) copy-start(s32[2,256,8]{1,2,0:T(8,128)} %param.24) | copy-start | bytes 49156
  74.9 94.2 %all-gather.5.cloned.1.call-start = ((), (), s32[]{:S(2)}) async-start(), calls=%async_computation.6 | async-start | bytes 2621440 | tf_op jit(solution)/shard_map/all_gather | solution.py:142
  174.9 5.1 %copy-start.7 = (bf16[1,2048,384]{2,1,0:T(8,128)(2,1)S(1)}, bf16[1,2048,384]{2,1,0:T(8,128)(2,1)}, u32[]{:S(2)}) copy-start(bf16[1,2048,384]{2,1,0:T(8,128)(2,1)} %param.25) | copy-start | bytes 4718596
  174.9 58.9 %all-to-all-start = ((bf16[4,288,2048]{2,1,0:T(8,128)(2,1)}), bf16[4,288,2048]{2,1,0:T(8,128)(2,1)}, u32[]{:S(2)}, u32[]{:S(2)}) async-start(bf16[4,288,2048]{2,1,0:T(8,128)(2,1)} %bitcast.102), calls=%async_computation.1 | async-start | bytes 9437184 | tf_op jit(solution)/shard_map/all_to_all | solution.py:160
  180.0 37.4 %collective-permute-start.2 = (bf16[1,2048,384]{2,1,0:T(8,128)(2,1)S(1)}, bf16[1,2048,384]{2,1,0:T(8,128)(2,1)}, u32[]{:S(2)}, u32[]{:S(2)}) collective-permute-start(bf16[1,2048,384]{2,1,0:T(8,128)(2,1)S(1)} %copy-done.7), channel_id=1, source_target_pairs={{0,16},{16,0},{1,17},{17,1},{2,18},{18,2},{3,19},{19,3},{4,20},{20... | collective-permute-start | bytes 4718600 | tf_op jit(solution)/shard_map/ppermute | solution.py:43
  181.5 69.6 %collective-permute-start.4 = (bf16[1,2048,384]{2,1,0:T(8,128)(2,1)}, bf16[1,2048,384]{2,1,0:T(8,128)(2,1)}, u32[]{:S(2)}, u32[]{:S(2)}) collective-permute-start(bf16[1,2048,384]{2,1,0:T(8,128)(2,1)} %param.27), channel_id=1, source_target_pairs={{0,16},{16,0},{1,17},{17,1},{2,18},{18,2},{3,19},{19,3},{4,20},{20... | collective-permute-start | bytes 4718600 | tf_op jit(solution)/shard_map/ppermute | solution.py:43
  182.1 102.2 %collective-permute-start.3 = (bf16[1,2048,384]{2,1,0:T(8,128)(2,1)}, bf16[1,2048,384]{2,1,0:T(8,128)(2,1)}, u32[]{:S(2)}, u32[]{:S(2)}) collective-permute-start(bf16[1,2048,384]{2,1,0:T(8,128)(2,1)} %param.26), channel_id=1, source_target_pairs={{0,16},{16,0},{1,17},{17,1},{2,18},{18,2},{3,19},{19,3},{4,20},{20... | collective-permute-start | bytes 4718600 | tf_op jit(solution)/shard_map/ppermute | solution.py:43
  298.6 59.0 %all-to-all-start.1 = ((bf16[4,288,2048]{2,1,0:T(8,128)(2,1)}), bf16[4,288,2048]{2,1,0:T(8,128)(2,1)}, u32[]{:S(2)}, u32[]{:S(2)}) async-start(bf16[4,288,2048]{2,1,0:T(8,128)(2,1)} %bitcast.103), calls=%async_computation.2 | async-start | bytes 9437184 | tf_op jit(solution)/shard_map/all_to_all | solution.py:164
  303.7 140.3 %reduce-scatter.5.cloned.1.call-start = ((), (), s32[]{:S(2)}) async-start(), calls=%async_computation.7 | async-start | bytes 5242880 | tf_op jit(solution)/shard_map/reduce_scatter | solution.py:174
  362.4 83.8 %copy-start.1 = (bf16[2048,16]{0,1:T(8,128)(2,1)S(1)}, bf16[2048,16]{0,1:T(8,128)(2,1)}, u32[]{:S(2)}) copy-start(bf16[2048,16]{0,1:T(8,128)(2,1)} %param.23) | copy-start | bytes 196612
Sparse Core Ops, SparseCore 0:
  8.9 59.4 all-gather.2
  75.0 44.4 reduce-scatter.2
  122.3 46.6 all-gather.4
  369.4 74.5 reduce-scatter.4

commit v2 on v1

--- a/solution.py
+++ b/solution.py
@@ -114,13 +114,6 @@
         attn, full_out_weight, preferred_element_type=jnp.float32
     ).reshape(packs, row_count, width)
 
-    full_out_weight, expert_gate, expert_up, expert_down = lax.optimization_barrier(
-        (full_out_weight, expert_gate, expert_up, expert_down)
-    )
-    full_gate = jnp.concatenate(cp_pieces(expert_gate, n_cp), axis=2)
-    full_up = jnp.concatenate(cp_pieces(expert_up, n_cp), axis=2)
-    full_down = jnp.concatenate(cp_pieces(expert_down, n_cp), axis=2)
-
     share = row_count // n_tp
     tp_index = lax.axis_index("tp")
     ep_index = lax.axis_index("ep")
@@ -131,32 +124,56 @@
     local_ids = lax.dynamic_slice_in_dim(expert_ids, first_row, share, 1).reshape(
         packs * share, top_count
     )
-    normed, gates = route(state.reshape(packs * share, width), local_ids, norm_gain, router_weight)
+    home_rows = packs * share
+    normed = root_mean_scale(state.reshape(home_rows, width), norm_gain).astype(jnp.bfloat16)
+
+    full_out_weight, expert_gate, expert_up, expert_down = lax.optimization_barrier(
+        (full_out_weight, expert_gate, expert_up, expert_down)
+    )
+    gate_pieces = cp_pieces(expert_gate, n_cp)
+    up_pieces = cp_pieces(expert_up, n_cp)
+    down_pieces = cp_pieces(expert_down, n_cp)
+    normed, gate_pieces, up_pieces = lax.optimization_barrier((normed, gate_pieces, up_pieces))
+
+    lanes = 128
+    id_lanes = jnp.pad(local_ids.astype(jnp.bfloat16), ((0, 0), (0, lanes - top_count)))
+    rows_all = lax.all_gather(
+        jnp.concatenate([normed, id_lanes], axis=1), "ep", axis=0, tiled=True
+    )
+    normed_all = rows_all[:, :width]
+    ids_all = rows_all[:, width : width + top_count].astype(jnp.int32)
+    logits = jnp.dot(normed_all, router_weight, preferred_element_type=jnp.float32)
+    picks = ids_all[:, :, None] == jnp.arange(experts, dtype=jnp.int32)[None, None, :]
+    raised = jnp.exp(jnp.sum(jnp.where(picks, logits[:, None, :], jnp.float32(0.0)), axis=-1))
+    gates_all = raised / jnp.sum(raised, axis=-1, keepdims=True)
+
+    gathered = n_ep * home_rows
     dev_cap = packs * cap
-    slots = slot_numbers(local_ids, experts)
-
-    home_rows = packs * share
-    meta = jnp.concatenate(
-        [local_ids.astype(jnp.float32), slots.astype(jnp.float32), gates], axis=-1
-    )
-    normed_all = lax.all_gather(normed, "ep", axis=0, tiled=True)
-    meta_all = lax.all_gather(meta, "ep", axis=0, tiled=True)
-    ids_all = meta_all[:, :top_count].astype(jnp.int32)
-    slots_all = meta_all[:, top_count : 2 * top_count].astype(jnp.int32)
-    gates_all = meta_all[:, 2 * top_count :]
-    gathered = n_ep * home_rows
-    home_of = (jnp.arange(gathered, dtype=jnp.int32) // home_rows)[:, None]
     cap2 = n_ep * dev_cap
     n_slots = n_tp * cap2
     mine = (ids_all % n_ep) == ep_index
-    target = jnp.where(
-        mine, (ids_all // n_ep) * cap2 + home_of * dev_cap + slots_all, jnp.int32(-1)
-    )
-    hit = target[None, :, :] == jnp.arange(n_slots, dtype=jnp.int32)[:, None, None]
-    select = jnp.any(hit, axis=-1).astype(jnp.bfloat16)
-    weight = jnp.sum(jnp.where(hit, gates_all[None, :, :], jnp.float32(0.0)), axis=-1)
+    dest = ids_all // n_ep
+    named = jnp.stack(
+        [jnp.any(mine & (dest == j), axis=1) for j in range(n_tp)], axis=1
+    ).astype(jnp.bfloat16)
+    row_iota = jnp.arange(gathered, dtype=jnp.int32)
+    earlier = (row_iota[:, None] > row_iota[None, :]).astype(jnp.bfloat16)
+    rank = jnp.dot(earlier, named, preferred_element_type=jnp.float32).astype(jnp.int32)
+    rank_of = jnp.sum(
+        jnp.where(dest[:, :, None] == jnp.arange(n_tp, dtype=jnp.int32)[None, None, :],
+                  rank[:, None, :], 0),
+        axis=-1,
+    )
+    target = jnp.where(mine, dest * cap2 + rank_of, jnp.int32(-1)).T
+    hit = target[:, None, :] == jnp.arange(n_slots, dtype=jnp.int32)[None, :, None]
+    select = jnp.any(hit, axis=0).astype(jnp.bfloat16)
+    weight = jnp.sum(jnp.where(hit, gates_all.T[:, None, :], jnp.float32(0.0)), axis=0)
 
     buffer = jnp.dot(select, normed_all, preferred_element_type=jnp.float32).astype(jnp.bfloat16)
+    buffer, down_pieces = lax.optimization_barrier((buffer, down_pieces))
+    full_gate = jnp.concatenate(gate_pieces, axis=2)
+    full_up = jnp.concatenate(up_pieces, axis=2)
+    full_down = jnp.concatenate(down_pieces, axis=2)
     received = lax.all_to_all(
         buffer.reshape(n_tp, cap2, width), "tp", split_axis=0, concat_axis=0, tiled=True
     )
@@ -172,9 +189,14 @@
         weight_hi, back, contract, preferred_element_type=jnp.float32
     ) + lax.dot_general(weight_lo, back, contract, preferred_element_type=jnp.float32)
     mixture = lax.psum_scatter(
-        partial.reshape(n_ep, home_rows, width), "ep", scatter_dimension=0, tiled=True
-    )
-    layer_out = (state + mixture.reshape(packs, share, width)).astype(jnp.bfloat16)
+        partial.astype(jnp.bfloat16).reshape(n_ep, home_rows, width),
+        "ep",
+        scatter_dimension=0,
+        tiled=True,
+    )
+    layer_out = (state + mixture.astype(jnp.float32).reshape(packs, share, width)).astype(
+        jnp.bfloat16
+    )
     return layer_out
 
 

time: 453 us -> 405 us (0.89)
  waiting for transfers between devices: 316 us -> 254 us
  blocking collectives: 13.7 us -> 56.4 us
  other arithmetic: 38.4 us -> 18 us
  starting transfers between devices: 17 us -> 11.2 us
    all_to_all x0 -> x1, blocking collectives: none -> 56.4 us  [shards(): lax.all_to_all(buffer.reshape(n_tp, cap2, width), 'tp', split_axis=0, con...]
    ppermute x5, waiting for transfers between devices: 80.2 us -> 29.3 us  [cp_pieces(): pieces.append(lax.ppermute(x, 'cp', perm))]
    all_gather x1, waiting for transfers between devices: 13.8 us -> 48 us  [shards(): lax.all_gather(jnp.concatenate([normed, id_lanes], axis=1), 'ep', axis=0,...]
    reduce_scatter x1, waiting for transfers between devices: 74.7 us -> 41.3 us  [shards(): lax.psum_scatter(partial.astype(jnp.bfloat16).reshape(n_ep, home_rows, wi...]
    all_to_all x1 -> x0, waiting for transfers between devices: 16.4 us -> none  [shards(): lax.all_to_all(buffer.reshape(n_tp, cap2, width), 'tp', split_axis=0, con...]
    all_gather x1 -> x0, blocking collectives: 13.7 us -> none  [shards(): meta_all = lax.all_gather(meta, 'ep', axis=0, tiled=True)]
    reduce_sum x4, other arithmetic: 12.1 us -> 2.62 us  [the longest x1 2.49 us: shards(): jnp.sum(jnp.where(hit, gates_all.T[:, None, :], jnp.float32(0.0)), axis=0)]
    all_to_all x1, waiting for transfers between devices: 41.8 us -> 50.8 us  [shards(): lax.all_to_all(served, 'tp', split_axis=0, concat_axis=0, tiled=True)]
  transfers between devices with their start and end apart: 11 -> 10, of which waited for: 10 -> 7; matrix products, arithmetic and copies ran while one was open for 11% -> 6% of each run, Pallas kernels for 0% -> 0%
where the time goes in v2:
time: 405 us; the launch traced here: 404 us
  waiting for transfers between devices  254 us (63%)
  blocking collectives  56.4 us (14%)
  matrix products  48.2 us (12%)
  other arithmetic  18 us (4%)
  between operations  13.4 us (3%)
  starting transfers between devices  11.2 us (3%)
    all_to_all x1, blocking collectives, shards(): lax.all_to_all(buffer.reshape(n_tp, cap2, width), 'tp', split_axis=0, con...  56.4 us
    all_to_all x1, waiting for transfers between devices, shards(): lax.all_to_all(served, 'tp', split_axis=0, concat_axis=0, tiled=True)  50.8 us
    all_gather x1, waiting for transfers between devices, shards(): lax.all_gather(jnp.concatenate([normed, id_lanes], axis=1), 'ep', axis=0,...  48 us
    reduce_scatter x1, waiting for transfers between devices, shards(): lax.psum_scatter(partial_proj, 'tp', scatter_dimension=1, tiled=True)  42.2 us
    all_gather x1, waiting for transfers between devices, shards(): full_out_weight = lax.all_gather(out_weight, 'cp', axis=1, tiled=True)  41.4 us
    reduce_scatter x1, waiting for transfers between devices, shards(): lax.psum_scatter(partial.astype(jnp.bfloat16).reshape(n_ep, home_rows, wi...  41.3 us
    ppermute x5, waiting for transfers between devices, cp_pieces(): pieces.append(lax.ppermute(x, 'cp', perm))  29.3 us
    dot_general x1, matrix products, expert_rows(): jnp.einsum('rf,df->rd', hidden_act, full_down[0], preferred_element_type=...  13.9 us
  transfers between devices with their start and end apart: 10, of which 7 were waited for; matrix products, arithmetic and copies ran while one was open for 6% of the time, Pallas kernels for 0%

profile of v2, /device:TPU:0, one launch (start us, length us, event | category | flops | bytes accessed | tf_op | source)
XLA Modules:
  0.0 404.1 jit_solution(2239054506291978910)
XLA Ops:
  6.5 0.7 all-gather.3.cloned.1.call-update
  7.3 3.0 collective-permute-start.1
  10.3 1.0 fusion.35
  11.4 1.0 fusion.37
  12.5 1.6 pad_maximum_fusion.1
  15.3 0.7 fusion.20
  16.3 5.9 %collective-permute-done = bf16[2,256,256]{2,1,0:T(8,128)(2,1)} collective-permute-done((bf16[2,256,256]{2,1,0:T(8,128)(2,1)}, bf16[2,256,256]{2,1,0:T(8,128)(2,1)}, u32[]{:S(2)}, u32[]{:S(2)}) %collective-permute-start) | collective-permute-done | bytes 262176 | tf_op jit(solution)/shard_map/ppermute | solution.py:43
  22.2 1.0 pad_maximum_fusion
  23.2 2.2 fusion.1
  25.4 1.6 fusion.21
  27.0 41.4 %all-gather.3.cloned.1.call-done = bf16[1024,2048]{1,0:T(8,128)(2,1)} async-done(((bf16[1024,1024]{1,0:T(8,128)(2,1)}), bf16[1024,2048]{1,0:T(8,128)(2,1)}) %all-gather.3.cloned.1.call-update) | async-done | bytes 4194320 | tf_op jit(solution)/shard_map/all_gather | solution.py:112
  68.4 6.6 %fusion.5 = f32[2,256,2048]{2,1,0:T(8,128)} fusion(bf16[2,256,1024]{1,2,0:T(8,128)(2,1)S(1)} %bitcast.85, bf16[1024,2048]{1,0:T(8,128)(2,1)} %all-gather.3.cloned.1.call-done), kind=kOutput, calls=%fused_computation.9 | convolution fusion | flops 2147483648 | bytes 9437184 | tf_op jit(solution)/shard_map/dot_general | solution.py:113
  75.6 1.7 collective-permute-start.3
  77.5 42.2 %reduce-scatter.3.cloned.1.call-done = f32[2,64,2048]{2,1,0:T(8,128)} async-done(((f32[2,256,2048]{2,1,0:T(8,128)}), f32[2,64,2048]{2,1,0:T(8,128)}) %reduce-scatter.3.cloned.1.call-update) | async-done | bytes 1048592 | tf_op jit(solution)/shard_map/reduce_scatter | solution.py:121
  119.7 1.6 multiply_reduce_fusion
  122.0 23.4 %collective-permute-done.3 = bf16[1,2048,384]{2,1,0:T(8,128)(2,1)} collective-permute-done((bf16[1,2048,384]{2,1,0:T(8,128)(2,1)}, bf16[1,2048,384]{2,1,0:T(8,128)(2,1)}, u32[]{:S(2)}, u32[]{:S(2)}) %collective-permute-start.3) | collective-permute-done | bytes 1572896 | tf_op jit(solution)/shard_map/ppermute | solution.py:43
  145.5 0.9 fusion.34
  146.9 48.0 %all-gather.5.cloned.1.call-done = bf16[512,2176]{0,1:T(8,128)(2,1)} async-done(((bf16[128,2176]{0,1:T(8,128)(2,1)}), bf16[512,2176]{0,1:T(8,128)(2,1)}) %all-gather.5.cloned.1.call-update) | async-done | bytes 2228240 | tf_op jit(solution)/shard_map/all_gather | solution.py:140
  194.9 0.8 and_reduce_fusion.3
  196.0 3.5 fusion
  199.5 4.5 %convolution_convert_fusion.1 = bf16[1152,2048]{1,0:T(8,128)(2,1)S(1)} fusion(pred[1152,512]{1,0:T(8,128)(4,1)S(1)} %fusion, bf16[512,2176]{0,1:T(8,128)(2,1)} %all-gather.5.cloned.1.call-done), kind=kOutput, calls=%fused_computation.5 | convolution fusion | flops 2418278400 | bytes 7405568 | tf_op jit(solution)/shard_map/dot_general | solution.py:172
  204.0 56.4 %all_to_all.10 = bf16[4,288,2048]{2,1,0:T(8,128)(2,1)S(1)} all-to-all(bf16[4,288,2048]{2,1,0:T(8,128)(2,1)S(1)} %bitcast.84), channel_id=1, replica_groups=mesh['cp'=2,'tp'=4,'ep'=4] {'tp'}, dimensions={0} | all-to-all | bytes 9437184 | tf_op jit(solution)/shard_map/all_to_all | solution.py:177
  260.4 2.2 copy-done.1
  262.5 7.6 %fusion.11 = f32[1152,768]{1,0:T(8,128)} fusion(bf16[1152,2048]{1,0:T(8,128)(2,1)S(1)} %bitcast.82, bf16[1,2048,384]{2,1,0:T(8,128)(2,1)} %collective-permute-done.2, bf16[1,2048,384]{2,1,0:T(8,128)(2,1)} %param.25), kind=kOutput, calls=%fused_computation.18 | convolution fusion | flops 3630170112 | bytes 11403264 | tf_op jit(solution)/shard_map/dot_general | solution.py:50
  270.1 13.9 %convolution_convert_fusion = bf16[1152,2048]{1,0:T(8,128)(2,1)} fusion(bf16[1,2048,384]{2,1,0:T(8,128)(2,1)} %copy-done.10, bf16[1,2048,384]{2,1,0:T(8,128)(2,1)S(1)} %copy-done.9, bf16[1152,2048]{1,0:T(8,128)(2,1)} %bitcast.83, f32[1152,768]{1,0:T(8,128)} %fusion.11, bf16[1,2048,384]{2,1,0:T(8,128)(2,1)} %collective-permute-done.3, ...), kind=kOutput, calls=%fused_computation.4 | convolution fusion | flops 7268007936 | bytes 19267584 | tf_op jit(solution)/shard_map/rf,df->rd/dot_general | solution.py:53
  284.0 5.2 %all-to-all-start.1 = ((bf16[4,288,2048]{2,1,0:T(8,128)(2,1)}), bf16[4,288,2048]{2,1,0:T(8,128)(2,1)}, u32[]{:S(2)}, u32[]{:S(2)}) async-start(bf16[4,288,2048]{2,1,0:T(8,128)(2,1)} %bitcast.81), calls=%async_computation.2 | async-start | bytes 9437184 | tf_op jit(solution)/shard_map/all_to_all | solution.py:181
  289.7 2.5 select_reduce_fusion
  292.2 50.8 %all-to-all-done.1 = bf16[4,288,2048]{2,1,0:T(8,128)(2,1)} async-done(((bf16[4,288,2048]{2,1,0:T(8,128)(2,1)}), bf16[4,288,2048]{2,1,0:T(8,128)(2,1)}, u32[]{:S(2)}, u32[]{:S(2)}) %all-to-all-start.1) | async-done | bytes 4718624 | tf_op jit(solution)/shard_map/all_to_all | solution.py:181
  343.0 4.8 %fusion.32 = f32[512,2048]{1,0:T(8,128)S(1)} fusion(bf16[1152,2048]{1,0:T(8,128)(2,1)} %bitcast.17, f32[1152,512]{1,0:T(8,128)S(1)} %select_reduce_fusion), kind=kOutput, calls=%fused_computation.50 | convolution fusion | flops 2416508928 | bytes 11272192 | tf_op jit(solution)/shard_map/dot_general | solution.py:188
  347.8 6.5 %add_convert_fusion = bf16[512,2048]{1,0:T(8,128)(2,1)} fusion(f32[512,2048]{1,0:T(8,128)S(1)} %fusion.32, bf16[1152,2048]{1,0:T(8,128)(2,1)} %bitcast.17, f32[1152,512]{1,0:T(8,128)S(1)} %select_reduce_fusion), kind=kOutput, calls=%fused_computation.11 | convolution fusion | flops 2420375552 | bytes 13369344 | tf_op jit(solution)/shard_map/dot_general | solution.py:190
  354.3 41.3 %reduce-scatter.5.cloned.1.call-done = bf16[1,128,2048]{2,1,0:T(8,128)(2,1)} async-done(((bf16[4,128,2048]{2,1,0:T(8,128)(2,1)}), bf16[1,128,2048]{2,1,0:T(8,128)(2,1)}) %reduce-scatter.5.cloned.1.call-update) | async-done | bytes 524304 | tf_op jit(solution)/shard_map/reduce_scatter | solution.py:191
  395.7 1.9 fusion.28
  (61 shorter events, 4.4 us)
Async XLA Ops:
  6.5 282.7 %copy-start = (bf16[2048,16]{0,1:T(8,128)(2,1)S(1)}, bf16[2048,16]{0,1:T(8,128)(2,1)}, u32[]{:S(2)}) copy-start(bf16[2048,16]{0,1:T(8,128)(2,1)} %param.23) | copy-start | bytes 196612
  6.5 7.6 %copy-start.3 = (bf16[2,256,1024]{2,1,0:T(8,128)(2,1)S(1)}, bf16[2,256,1024]{2,1,0:T(8,128)(2,1)}, u32[]{:S(2)}) copy-start(bf16[2,256,1024]{2,1,0:T(8,128)(2,1)} %param.14) | copy-start | bytes 3145732
  6.5 61.8 %all-gather.3.cloned.1.call-start = ((), (), s32[]{:S(2)}) async-start(), calls=%async_computation.4 | async-start | bytes 6291456 | tf_op jit(solution)/shard_map/all_gather | solution.py:112
  7.3 112.4 %reduce-scatter.3.cloned.1.call-start = ((), (), s32[]{:S(2)}) async-start(), calls=%async_computation.5 | async-start | bytes 5242880 | tf_op jit(solution)/shard_map/reduce_scatter | solution.py:121
  7.3 8.7 %collective-permute-start.1 = (s32[2,256]{1,0:T(2,128)}, s32[2,256]{1,0:T(2,128)S(1)}, u32[]{:S(2)}, u32[]{:S(2)}) collective-permute-start(s32[2,256]{1,0:T(2,128)} %param.17), channel_id=1, source_target_pairs={{0,16},{16,0},{1,17},{17,1},{2,18},{18,2},{3,19},{19,3},{4,20},{20... | collective-permute-start | bytes 6152 | tf_op jit(solution)/shard_map/ppermute | solution.py:43
  14.1 1.2 copy-start.8
  14.1 8.1 %collective-permute-start = (bf16[2,256,256]{2,1,0:T(8,128)(2,1)}, bf16[2,256,256]{2,1,0:T(8,128)(2,1)}, u32[]{:S(2)}, u32[]{:S(2)}) collective-permute-start(bf16[2,256,256]{2,1,0:T(8,128)(2,1)} %pad_maximum_fusion.1), channel_id=1, source_target_pairs={{0,16},{16,0},{1,17},{17,1},{2,18},{18,2},{3,19},{19,3},{4,20},{20... | collective-permute-start | bytes 786440 | tf_op jit(solution)/shard_map/ppermute | solution.py:43
  14.4 1.6 copy-start.6
  14.4 7.8 %copy-start.4 = (bf16[2,256,128]{2,1,0:T(8,128)(2,1)S(1)}, bf16[2,256,128]{2,1,0:T(8,128)(2,1)}, u32[]{:S(2)}) copy-start(bf16[2,256,128]{2,1,0:T(8,128)(2,1)} %param.16) | copy-start | bytes 393220
  75.0 2.4 copy-start.7
  75.0 46.7 %copy-start.5 = (f32[2048]{0:T(1024)S(1)}, f32[2048]{0:T(1024)}, u32[]{:S(2)}) copy-start(f32[2048]{0:T(1024)} %param.22) | copy-start | bytes 24580
  75.0 119.9 %all-gather.5.cloned.1.call-start = ((), (), s32[]{:S(2)}) async-start(), calls=%async_computation.6 | async-start | bytes 2785280 | tf_op jit(solution)/shard_map/all_gather | solution.py:140
  75.2 46.8 %collective-permute-start.2 = (bf16[1,2048,384]{2,1,0:T(8,128)(2,1)}, bf16[1,2048,384]{2,1,0:T(8,128)(2,1)}, u32[]{:S(2)}, u32[]{:S(2)}) collective-permute-start(bf16[1,2048,384]{2,1,0:T(8,128)(2,1)} %param.25), channel_id=1, source_target_pairs={{0,16},{16,0},{1,17},{17,1},{2,18},{18,2},{3,19},{19,3},{4,20},{20... | collective-permute-start | bytes 4718600 | tf_op jit(solution)/shard_map/ppermute | solution.py:43
  75.6 69.8 %collective-permute-start.3 = (bf16[1,2048,384]{2,1,0:T(8,128)(2,1)}, bf16[1,2048,384]{2,1,0:T(8,128)(2,1)}, u32[]{:S(2)}, u32[]{:S(2)}) collective-permute-start(bf16[1,2048,384]{2,1,0:T(8,128)(2,1)} %param.26), channel_id=1, source_target_pairs={{0,16},{16,0},{1,17},{17,1},{2,18},{18,2},{3,19},{19,3},{4,20},{20... | collective-permute-start | bytes 4718600 | tf_op jit(solution)/shard_map/ppermute | solution.py:43
  146.3 57.6 %collective-permute-start.4 = (bf16[1,2048,384]{2,1,0:T(8,128)(2,1)}, bf16[1,2048,384]{2,1,0:T(8,128)(2,1)S(1)}, u32[]{:S(2)}, u32[]{:S(2)}) collective-permute-start(bf16[1,2048,384]{2,1,0:T(8,128)(2,1)} %param.27), channel_id=1, source_target_pairs={{0,16},{16,0},{1,17},{17,1},{2,18},{18,2},{3,19},{19,3},{4,20},{20... | collective-permute-start | bytes 4718600 | tf_op jit(solution)/shard_map/ppermute | solution.py:43
  204.0 56.4 %copy-start.10 = (bf16[1,2048,384]{2,1,0:T(8,128)(2,1)}, bf16[1,2048,384]{2,1,0:T(8,128)(2,1)S(1)}, u32[]{:S(2)}) copy-start(bf16[1,2048,384]{2,1,0:T(8,128)(2,1)S(1)} %collective-permute-done.4) | copy-start | bytes 4718596
  260.4 2.2 copy-start.1
  262.5 7.6 %copy-start.9 = (bf16[1,2048,384]{2,1,0:T(8,128)(2,1)S(1)}, bf16[1,2048,384]{2,1,0:T(8,128)(2,1)}, u32[]{:S(2)}) copy-start(bf16[1,2048,384]{2,1,0:T(8,128)(2,1)} %param.27) | copy-start | bytes 4718596
  284.0 5.2 %copy-start.2 = (bf16[512,2176]{0,1:T(8,128)(2,1)S(1)}, bf16[512,2176]{0,1:T(8,128)(2,1)}, u32[]{:S(2)}) copy-start(bf16[512,2176]{0,1:T(8,128)(2,1)} %all-gather.5.cloned.1.call-done) | copy-start | bytes 6684676
  284.0 59.0 %all-to-all-start.1 = ((bf16[4,288,2048]{2,1,0:T(8,128)(2,1)}), bf16[4,288,2048]{2,1,0:T(8,128)(2,1)}, u32[]{:S(2)}, u32[]{:S(2)}) async-start(bf16[4,288,2048]{2,1,0:T(8,128)(2,1)} %bitcast.81), calls=%async_computation.2 | async-start | bytes 9437184 | tf_op jit(solution)/shard_map/all_to_all | solution.py:181
  289.1 106.5 %reduce-scatter.5.cloned.1.call-start = ((), (), s32[]{:S(2)}) async-start(), calls=%async_computation.7 | async-start | bytes 2621440 | tf_op jit(solution)/shard_map/reduce_scatter | solution.py:191
Sparse Core Ops, SparseCore 0:
  8.9 59.4 all-gather.2
  75.1 44.5 reduce-scatter.2
  146.5 48.3 all-gather.4
  354.5 41.1 reduce-scatter.4

commit v3 on v2

--- a/solution.py
+++ b/solution.py
@@ -109,7 +109,7 @@
         .astype(jnp.bfloat16)
         .reshape(packs * row_count, head_count * HEAD_WIDTH)
     )
-    full_out_weight = lax.all_gather(out_weight, "cp", axis=1, tiled=True)
+    full_out_weight = jnp.concatenate(cp_pieces(out_weight, n_cp), axis=1)
     partial_proj = jnp.dot(
         attn, full_out_weight, preferred_element_type=jnp.float32
     ).reshape(packs, row_count, width)
@@ -118,7 +118,18 @@
     tp_index = lax.axis_index("tp")
     ep_index = lax.axis_index("ep")
     cap = capacity(share, top_count, experts)
-    projected = lax.psum_scatter(partial_proj, "tp", scatter_dimension=1, tiled=True)
+    projected = lax.psum_scatter(
+        partial_proj.astype(jnp.bfloat16), "tp", scatter_dimension=1, tiled=True
+    ).astype(jnp.float32)
+    cp_index = lax.axis_index("cp")
+    block_width = width // n_cp
+    blocks = projected.reshape(packs, share, n_cp, block_width)
+    source_block = (cp_index - jnp.arange(n_cp, dtype=jnp.int32)) % n_cp
+    picks_block = source_block[:, None] == jnp.arange(n_cp, dtype=jnp.int32)[None, :]
+    projected = jnp.sum(
+        jnp.where(picks_block[None, None, :, :, None], blocks[:, :, None, :, :], jnp.float32(0.0)),
+        axis=3,
+    ).reshape(packs, share, width)
     first_row = tp_index * share
     state = lax.dynamic_slice_in_dim(residual, first_row, share, 1).astype(jnp.float32) + projected
     local_ids = lax.dynamic_slice_in_dim(expert_ids, first_row, share, 1).reshape(

time: 405 us -> 400 us (0.988)
  waiting for transfers between devices: 254 us -> 246 us
  local copies, waits for them, and re-layouts: 3.22 us -> 7.48 us
    ppermute x5 -> x6, waiting for transfers between devices: 29.3 us -> 76.2 us  [cp_pieces(): pieces.append(lax.ppermute(x, 'cp', perm))]
    all_gather x1 -> x0, waiting for transfers between devices: 41.4 us -> none  [shards(): full_out_weight = lax.all_gather(out_weight, 'cp', axis=1, tiled=True)]
    reduce_scatter x1, waiting for transfers between devices: 42.2 us -> 29.3 us  [shards(): lax.psum_scatter(partial_proj.astype(jnp.bfloat16), 'tp', scatter_dimensi...]
  transfers between devices with their start and end apart: 10 -> 10, of which waited for: 7 -> 8; matrix products, arithmetic and copies ran while one was open for 6% -> 7% of each run, Pallas kernels for 0% -> 0%
where the time goes in v3:
time: 400 us; the launch traced here: 399 us
  waiting for transfers between devices  246 us (62%)
  blocking collectives  56.4 us (14%)
  matrix products  45.4 us (11%)
  other arithmetic  17.5 us (4%)
  between operations  13.5 us (3%)
  starting transfers between devices  13.2 us (3%)
  local copies, waits for them, and re-layouts  7.48 us (2%)
    ppermute x6, waiting for transfers between devices, cp_pieces(): pieces.append(lax.ppermute(x, 'cp', perm))  76.2 us
    all_to_all x1, blocking collectives, shards(): lax.all_to_all(buffer.reshape(n_tp, cap2, width), 'tp', split_axis=0, con...  56.4 us
    all_to_all x1, waiting for transfers between devices, shards(): lax.all_to_all(served, 'tp', split_axis=0, concat_axis=0, tiled=True)  50.8 us
    all_gather x1, waiting for transfers between devices, shards(): lax.all_gather(jnp.concatenate([normed, id_lanes], axis=1), 'ep', axis=0,...  48.2 us
    reduce_scatter x1, waiting for transfers between devices, shards(): lax.psum_scatter(partial.astype(jnp.bfloat16).reshape(n_ep, home_rows, wi...  41.3 us
    reduce_scatter x1, waiting for transfers between devices, shards(): lax.psum_scatter(partial_proj.astype(jnp.bfloat16), 'tp', scatter_dimensi...  29.3 us
    dot_general x1, matrix products, expert_rows(): jnp.einsum('rf,df->rd', hidden_act, full_down[0], preferred_element_type=...  13.8 us
  transfers between devices with their start and end apart: 10, of which 8 were waited for; matrix products, arithmetic and copies ran while one was open for 7% of the time, Pallas kernels for 0%

profile of v3, /device:TPU:0, one launch (start us, length us, event | category | flops | bytes accessed | tf_op | source)
XLA Modules:
  0.0 399.2 jit_solution(16929958345955165421)
XLA Ops:
  6.5 3.0 collective-permute-start.1
  9.5 1.0 fusion.38
  10.6 1.0 fusion.40
  11.6 0.9 pad_maximum_fusion.1
  12.7 2.0 collective-permute-start.2
  14.7 1.5 copy.73
  19.1 2.8 collective-permute-done
  21.9 2.2 fusion.1
  24.2 1.6 fusion.24
  25.7 39.7 %collective-permute-done.2 = bf16[1024,1024]{1,0:T(8,128)(2,1)} collective-permute-done((bf16[1024,1024]{1,0:T(8,128)(2,1)}, bf16[1024,1024]{1,0:T(8,128)(2,1)}, u32[]{:S(2)}, u32[]{:S(2)}) %collective-permute-start.2) | collective-permute-done | bytes 2097184 | tf_op jit(solution)/shard_map/ppermute | solution.py:43
  65.5 1.8 constant_dynamic-update-slice_fusion
  67.3 3.7 fusion.18
  71.7 1.7 collective-permute-start.4
  73.6 29.3 %reduce-scatter.3.cloned.1.call-done = bf16[2,64,2048]{2,1,0:T(8,128)(2,1)} async-done(((bf16[2,256,2048]{2,1,0:T(8,128)(2,1)}), bf16[2,64,2048]{2,1,0:T(8,128)(2,1)}) %reduce-scatter.3.cloned.1.call-update) | async-done | bytes 524304 | tf_op jit(solution)/shard_map/reduce_scatter | solution.py:121
  102.9 1.1 broadcast_in_dim.113
  104.5 1.3 multiply_reduce_fusion
  106.6 2.4 collective-permute-done.3
  109.0 31.3 %collective-permute-done.4 = bf16[1,2048,384]{2,1,0:T(8,128)(2,1)} collective-permute-done((bf16[1,2048,384]{2,1,0:T(8,128)(2,1)}, bf16[1,2048,384]{2,1,0:T(8,128)(2,1)}, u32[]{:S(2)}, u32[]{:S(2)}) %collective-permute-start.4) | collective-permute-done | bytes 1572896 | tf_op jit(solution)/shard_map/ppermute | solution.py:43
  141.9 48.2 %all-gather.2.cloned.1.call-done = bf16[512,2176]{0,1:T(8,128)(2,1)} async-done(((bf16[128,2176]{0,1:T(8,128)(2,1)}), bf16[512,2176]{0,1:T(8,128)(2,1)}) %all-gather.2.cloned.1.call-update) | async-done | bytes 2228240 | tf_op jit(solution)/shard_map/all_gather | solution.py:151
  191.1 3.5 fusion
  194.6 4.5 %convolution_convert_fusion.1 = bf16[1152,2048]{1,0:T(8,128)(2,1)S(1)} fusion(pred[1152,512]{1,0:T(8,128)(4,1)S(1)} %fusion, bf16[512,2176]{0,1:T(8,128)(2,1)} %all-gather.2.cloned.1.call-done), kind=kOutput, calls=%fused_computation.5 | convolution fusion | flops 2418278400 | bytes 7405568 | tf_op jit(solution)/shard_map/dot_general | solution.py:183
  199.1 56.4 %all_to_all.10 = bf16[4,288,2048]{2,1,0:T(8,128)(2,1)S(1)} all-to-all(bf16[4,288,2048]{2,1,0:T(8,128)(2,1)S(1)} %bitcast.92), channel_id=1, replica_groups=mesh['cp'=2,'tp'=4,'ep'=4] {'tp'}, dimensions={0} | all-to-all | bytes 9437184 | tf_op jit(solution)/shard_map/all_to_all | solution.py:188
  255.5 2.2 copy-done.1
  257.7 7.6 %fusion.11 = f32[1152,768]{1,0:T(8,128)} fusion(bf16[1152,2048]{1,0:T(8,128)(2,1)S(1)} %bitcast.90, bf16[1,2048,384]{2,1,0:T(8,128)(2,1)} %collective-permute-done.3, bf16[1,2048,384]{2,1,0:T(8,128)(2,1)} %param.25), kind=kOutput, calls=%fused_computation.18 | convolution fusion | flops 3630170112 | bytes 11403264 | tf_op jit(solution)/shard_map/dot_general | solution.py:50
  265.3 13.8 %convolution_convert_fusion = bf16[1152,2048]{1,0:T(8,128)(2,1)} fusion(bf16[1,2048,384]{2,1,0:T(8,128)(2,1)} %copy-done.10, bf16[1,2048,384]{2,1,0:T(8,128)(2,1)S(1)} %copy-done.9, bf16[1152,2048]{1,0:T(8,128)(2,1)} %bitcast.91, f32[1152,768]{1,0:T(8,128)} %fusion.11, bf16[1,2048,384]{2,1,0:T(8,128)(2,1)} %collective-permute-done.4, ...), kind=kOutput, calls=%fused_computation.4 | convolution fusion | flops 7268007936 | bytes 19267584 | tf_op jit(solution)/shard_map/rf,df->rd/dot_general | solution.py:53
  279.1 5.1 %all-to-all-start.1 = ((bf16[4,288,2048]{2,1,0:T(8,128)(2,1)}), bf16[4,288,2048]{2,1,0:T(8,128)(2,1)}, u32[]{:S(2)}, u32[]{:S(2)}) async-start(bf16[4,288,2048]{2,1,0:T(8,128)(2,1)} %bitcast.89), calls=%async_computation.2 | async-start | bytes 9437184 | tf_op jit(solution)/shard_map/all_to_all | solution.py:192
  284.8 2.5 select_reduce_fusion
  287.3 50.8 %all-to-all-done.1 = bf16[4,288,2048]{2,1,0:T(8,128)(2,1)} async-done(((bf16[4,288,2048]{2,1,0:T(8,128)(2,1)}), bf16[4,288,2048]{2,1,0:T(8,128)(2,1)}, u32[]{:S(2)}, u32[]{:S(2)}) %all-to-all-start.1) | async-done | bytes 4718624 | tf_op jit(solution)/shard_map/all_to_all | solution.py:192
  338.1 4.8 %fusion.35 = f32[512,2048]{1,0:T(8,128)S(1)} fusion(bf16[1152,2048]{1,0:T(8,128)(2,1)} %bitcast.17, f32[1152,512]{1,0:T(8,128)S(1)} %select_reduce_fusion), kind=kOutput, calls=%fused_computation.53 | convolution fusion | flops 2416508928 | bytes 11272192 | tf_op jit(solution)/shard_map/dot_general | solution.py:199
  342.8 6.5 %add_convert_fusion = bf16[512,2048]{1,0:T(8,128)(2,1)} fusion(f32[512,2048]{1,0:T(8,128)S(1)} %fusion.35, bf16[1152,2048]{1,0:T(8,128)(2,1)} %bitcast.17, f32[1152,512]{1,0:T(8,128)S(1)} %select_reduce_fusion), kind=kOutput, calls=%fused_computation.11 | convolution fusion | flops 2420375552 | bytes 13369344 | tf_op jit(solution)/shard_map/dot_general | solution.py:201
  349.4 41.3 %reduce-scatter.5.cloned.1.call-done = bf16[1,128,2048]{2,1,0:T(8,128)(2,1)} async-done(((bf16[4,128,2048]{2,1,0:T(8,128)(2,1)}), bf16[1,128,2048]{2,1,0:T(8,128)(2,1)}) %reduce-scatter.5.cloned.1.call-update) | async-done | bytes 524304 | tf_op jit(solution)/shard_map/reduce_scatter | solution.py:202
  390.7 1.9 fusion.31
  (68 shorter events, 8.2 us)
Async XLA Ops:
  6.5 277.7 %copy-start = (bf16[2048,16]{0,1:T(8,128)(2,1)S(1)}, bf16[2048,16]{0,1:T(8,128)(2,1)}, u32[]{:S(2)}) copy-start(bf16[2048,16]{0,1:T(8,128)(2,1)} %param.23) | copy-start | bytes 196612
  6.5 96.4 %reduce-scatter.3.cloned.1.call-start = ((), (), s32[]{:S(2)}) async-start(), calls=%async_computation.4 | async-start | bytes 2621440 | tf_op jit(solution)/shard_map/reduce_scatter | solution.py:121
  6.5 12.3 %collective-permute-start.1 = (s32[2,256]{1,0:T(2,128)}, s32[2,256]{1,0:T(2,128)S(1)}, u32[]{:S(2)}, u32[]{:S(2)}) collective-permute-start(s32[2,256]{1,0:T(2,128)} %param.17), channel_id=1, source_target_pairs={{0,16},{16,0},{1,17},{17,1},{2,18},{18,2},{3,19},{19,3},{4,20},{20... | collective-permute-start | bytes 6152 | tf_op jit(solution)/shard_map/ppermute | solution.py:43
  12.6 4.5 %copy-start.8 = (f32[128]{0:T(128)S(1)}, f32[128]{0:T(128)}, u32[]{:S(2)}) copy-start(f32[128]{0:T(128)} %param.18) | copy-start | bytes 1540
  12.6 9.3 %collective-permute-start = (bf16[2,256,256]{2,1,0:T(8,128)(2,1)S(1)}, bf16[2,256,256]{2,1,0:T(8,128)(2,1)S(1)}, u32[]{:S(2)}, u32[]{:S(2)}) collective-permute-start(bf16[2,256,256]{2,1,0:T(8,128)(2,1)S(1)} %pad_maximum_fusion.1), channel_id=1, source_target_pairs={{0,16},{16,0},{1,17},{17,1},{2,18},{18,2},{3,19},{19,3},{4,20},{20... | collective-permute-start | bytes 786440 | tf_op jit(solution)/shard_map/ppermute | solution.py:43
  12.7 52.8 %collective-permute-start.2 = (bf16[1024,1024]{1,0:T(8,128)(2,1)}, bf16[1024,1024]{1,0:T(8,128)(2,1)}, u32[]{:S(2)}, u32[]{:S(2)}) collective-permute-start(bf16[1024,1024]{1,0:T(8,128)(2,1)} %param.20), channel_id=1, source_target_pairs={{0,16},{16,0},{1,17},{17,1},{2,18},{18,2},{3,19},{19,3},{4,20},{20... | collective-permute-start | bytes 6291464 | tf_op jit(solution)/shard_map/ppermute | solution.py:43
  17.0 1.6 copy-start.2
  17.1 1.8 copy-start.6
  17.1 4.8 %copy-start.4 = (bf16[2,256,128]{2,1,0:T(8,128)(2,1)S(1)}, bf16[2,256,128]{2,1,0:T(8,128)(2,1)}, u32[]{:S(2)}) copy-start(bf16[2,256,128]{2,1,0:T(8,128)(2,1)} %param.16) | copy-start | bytes 393220
  67.3 6.1 %copy-start.7 = (s32[2,256,8]{1,2,0:T(8,128)S(1)}, s32[2,256,8]{1,2,0:T(8,128)}, u32[]{:S(2)}) copy-start(s32[2,256,8]{1,2,0:T(8,128)} %param.24) | copy-start | bytes 49156
  71.1 119.0 %all-gather.2.cloned.1.call-start = ((), (), s32[]{:S(2)}) async-start(), calls=%async_computation.5 | async-start | bytes 2785280 | tf_op jit(solution)/shard_map/all_gather | solution.py:151
  71.3 37.7 %collective-permute-start.3 = (bf16[1,2048,384]{2,1,0:T(8,128)(2,1)}, bf16[1,2048,384]{2,1,0:T(8,128)(2,1)}, u32[]{:S(2)}, u32[]{:S(2)}) collective-permute-start(bf16[1,2048,384]{2,1,0:T(8,128)(2,1)} %param.25), channel_id=1, source_target_pairs={{0,16},{16,0},{1,17},{17,1},{2,18},{18,2},{3,19},{19,3},{4,20},{20... | collective-permute-start | bytes 4718600 | tf_op jit(solution)/shard_map/ppermute | solution.py:43
  71.7 68.7 %collective-permute-start.4 = (bf16[1,2048,384]{2,1,0:T(8,128)(2,1)}, bf16[1,2048,384]{2,1,0:T(8,128)(2,1)}, u32[]{:S(2)}, u32[]{:S(2)}) collective-permute-start(bf16[1,2048,384]{2,1,0:T(8,128)(2,1)} %param.26), channel_id=1, source_target_pairs={{0,16},{16,0},{1,17},{17,1},{2,18},{18,2},{3,19},{19,3},{4,20},{20... | collective-permute-start | bytes 4718600 | tf_op jit(solution)/shard_map/ppermute | solution.py:43
  104.4 1.8 copy-start.5
  141.2 57.9 %collective-permute-start.5 = (bf16[1,2048,384]{2,1,0:T(8,128)(2,1)}, bf16[1,2048,384]{2,1,0:T(8,128)(2,1)S(1)}, u32[]{:S(2)}, u32[]{:S(2)}) collective-permute-start(bf16[1,2048,384]{2,1,0:T(8,128)(2,1)} %param.27), channel_id=1, source_target_pairs={{0,16},{16,0},{1,17},{17,1},{2,18},{18,2},{3,19},{19,3},{4,20},{20... | collective-permute-start | bytes 4718600 | tf_op jit(solution)/shard_map/ppermute | solution.py:43
  199.1 56.4 %copy-start.10 = (bf16[1,2048,384]{2,1,0:T(8,128)(2,1)}, bf16[1,2048,384]{2,1,0:T(8,128)(2,1)S(1)}, u32[]{:S(2)}) copy-start(bf16[1,2048,384]{2,1,0:T(8,128)(2,1)S(1)} %collective-permute-done.5) | copy-start | bytes 4718596
  255.5 2.2 copy-start.1
  257.7 7.6 %copy-start.9 = (bf16[1,2048,384]{2,1,0:T(8,128)(2,1)S(1)}, bf16[1,2048,384]{2,1,0:T(8,128)(2,1)}, u32[]{:S(2)}) copy-start(bf16[1,2048,384]{2,1,0:T(8,128)(2,1)} %param.27) | copy-start | bytes 4718596
  279.1 5.2 %copy-start.3 = (bf16[512,2176]{0,1:T(8,128)(2,1)S(1)}, bf16[512,2176]{0,1:T(8,128)(2,1)}, u32[]{:S(2)}) copy-start(bf16[512,2176]{0,1:T(8,128)(2,1)} %all-gather.2.cloned.1.call-done) | copy-start | bytes 6684676
  279.1 59.0 %all-to-all-start.1 = ((bf16[4,288,2048]{2,1,0:T(8,128)(2,1)}), bf16[4,288,2048]{2,1,0:T(8,128)(2,1)}, u32[]{:S(2)}, u32[]{:S(2)}) async-start(bf16[4,288,2048]{2,1,0:T(8,128)(2,1)} %bitcast.89), calls=%async_computation.2 | async-start | bytes 9437184 | tf_op jit(solution)/shard_map/all_to_all | solution.py:192
  284.2 106.5 %reduce-scatter.5.cloned.1.call-start = ((), (), s32[]{:S(2)}) async-start(), calls=%async_computation.6 | async-start | bytes 2621440 | tf_op jit(solution)/shard_map/reduce_scatter | solution.py:202
Sparse Core Ops, SparseCore 0:
  71.2 31.6 reduce-scatter.2
  141.3 48.6 all-gather.1
  349.5 41.1 reduce-scatter.4

commit v4 on v3

--- a/solution.py
+++ b/solution.py
@@ -144,7 +144,6 @@
     gate_pieces = cp_pieces(expert_gate, n_cp)
     up_pieces = cp_pieces(expert_up, n_cp)
     down_pieces = cp_pieces(expert_down, n_cp)
-    normed, gate_pieces, up_pieces = lax.optimization_barrier((normed, gate_pieces, up_pieces))
 
     lanes = 128
     id_lanes = jnp.pad(local_ids.astype(jnp.bfloat16), ((0, 0), (0, lanes - top_count)))
@@ -176,18 +175,19 @@
         axis=-1,
     )
     target = jnp.where(mine, dest * cap2 + rank_of, jnp.int32(-1)).T
+    target, gate_pieces, up_pieces = lax.optimization_barrier((target, gate_pieces, up_pieces))
     hit = target[:, None, :] == jnp.arange(n_slots, dtype=jnp.int32)[None, :, None]
     select = jnp.any(hit, axis=0).astype(jnp.bfloat16)
     weight = jnp.sum(jnp.where(hit, gates_all.T[:, None, :], jnp.float32(0.0)), axis=0)
 
     buffer = jnp.dot(select, normed_all, preferred_element_type=jnp.float32).astype(jnp.bfloat16)
-    buffer, down_pieces = lax.optimization_barrier((buffer, down_pieces))
     full_gate = jnp.concatenate(gate_pieces, axis=2)
     full_up = jnp.concatenate(up_pieces, axis=2)
-    full_down = jnp.concatenate(down_pieces, axis=2)
     received = lax.all_to_all(
         buffer.reshape(n_tp, cap2, width), "tp", split_axis=0, concat_axis=0, tiled=True
     )
+    received, down_pieces = lax.optimization_barrier((received, down_pieces))
+    full_down = jnp.concatenate(down_pieces, axis=2)
     served = expert_rows(received, full_gate, full_up, full_down)
     back = lax.all_to_all(served, "tp", split_axis=0, concat_axis=0, tiled=True).reshape(
         n_slots, width

time: 400 us -> 392 us (0.980)
  blocking collectives: 56.4 us -> 0 us
  waiting for transfers between devices: 246 us -> 288 us
  starting transfers between devices: 13.2 us -> 19.3 us
    all_to_all x1 -> x0, blocking collectives: 56.4 us -> none  [shards(): lax.all_to_all(buffer.reshape(n_tp, cap2, width), 'tp', split_axis=0, con...]
    ppermute x6, waiting for transfers between devices: 76.2 us -> 98.3 us  [cp_pieces(): pieces.append(lax.ppermute(x, 'cp', perm))]
    all_to_all x0 -> x1, waiting for transfers between devices: none -> 16.8 us  [shards(): lax.all_to_all(buffer.reshape(n_tp, cap2, width), 'tp', split_axis=0, con...]
    all_to_all x0 -> x1, starting transfers between devices: none -> 5.3 us  [shards(): lax.all_to_all(buffer.reshape(n_tp, cap2, width), 'tp', split_axis=0, con...]
  transfers between devices with their start and end apart: 10 -> 11, of which waited for: 8 -> 9; matrix products, arithmetic and copies ran while one was open for 7% -> 4% of each run, Pallas kernels for 0% -> 0%
where the time goes in v4:
time: 392 us
  waiting for transfers between devices  288 us (73%)
  matrix products  48.1 us (12%)
  starting transfers between devices  19.3 us (5%)
  other arithmetic  17.5 us (4%)
  between operations  13.5 us (3%)
  local copies, waits for them, and re-layouts  5.31 us (1%)
    ppermute x6, waiting for transfers between devices, cp_pieces(): pieces.append(lax.ppermute(x, 'cp', perm))  98.3 us
    all_to_all x1, waiting for transfers between devices, shards(): lax.all_to_all(served, 'tp', split_axis=0, concat_axis=0, tiled=True)  50.8 us
    all_gather x1, waiting for transfers between devices, shards(): lax.all_gather(jnp.concatenate([normed, id_lanes], axis=1), 'ep', axis=0,...  46.5 us
    reduce_scatter x1, waiting for transfers between devices, shards(): lax.psum_scatter(partial.astype(jnp.bfloat16).reshape(n_ep, home_rows, wi...  44 us
    reduce_scatter x1, waiting for transfers between devices, shards(): lax.psum_scatter(partial_proj.astype(jnp.bfloat16), 'tp', scatter_dimensi...  31.4 us
    all_to_all x1, waiting for transfers between devices, shards(): lax.all_to_all(buffer.reshape(n_tp, cap2, width), 'tp', split_axis=0, con...  16.8 us
    dot_general x1, matrix products, expert_rows(): jnp.einsum('rf,df->rd', hidden_act, full_down[0], preferred_element_type=...  14.3 us
    ppermute x6, starting transfers between devices, cp_pieces(): pieces.append(lax.ppermute(x, 'cp', perm))  8.71 us
  transfers between devices with their start and end apart: 11, of which 9 were waited for; matrix products, arithmetic and copies ran while one was open for 4% of the time, Pallas kernels for 0%

profile of v4, /device:TPU:0, one launch (start us, length us, event | category | flops | bytes accessed | tf_op | source)
XLA Modules:
  0.0 391.5 jit_solution(5047447885703281828)
XLA Ops:
  6.5 3.0 collective-permute-start.1
  9.5 1.0 fusion.38
  10.6 1.0 fusion.40
  12.7 2.0 collective-permute-start.2
  14.7 1.5 copy.73
  19.1 2.8 collective-permute-done
  21.9 2.2 fusion.1
  24.2 1.6 fusion.24
  25.7 39.7 %collective-permute-done.2 = bf16[1024,1024]{1,0:T(8,128)(2,1)} collective-permute-done((bf16[1024,1024]{1,0:T(8,128)(2,1)}, bf16[1024,1024]{1,0:T(8,128)(2,1)}, u32[]{:S(2)}, u32[]{:S(2)}) %collective-permute-start.2) | collective-permute-done | bytes 2097184 | tf_op jit(solution)/shard_map/ppermute | solution.py:43
  65.5 1.8 constant_dynamic-update-slice_fusion
  67.3 3.7 fusion.18
  71.6 31.4 %reduce-scatter.3.cloned.1.call-done = bf16[2,64,2048]{2,1,0:T(8,128)(2,1)} async-done(((bf16[2,256,2048]{2,1,0:T(8,128)(2,1)}), bf16[2,64,2048]{2,1,0:T(8,128)(2,1)}) %reduce-scatter.3.cloned.1.call-update) | async-done | bytes 524304 | tf_op jit(solution)/shard_map/reduce_scatter | solution.py:121
  103.0 1.1 broadcast_in_dim.113
  104.6 1.3 multiply_reduce_fusion
  107.5 1.5 collective-permute-start.3
  109.6 46.5 %all-gather.2.cloned.1.call-done = bf16[512,2176]{0,1:T(8,128)(2,1)} async-done(((bf16[128,2176]{0,1:T(8,128)(2,1)}), bf16[512,2176]{0,1:T(8,128)(2,1)}) %all-gather.2.cloned.1.call-update) | async-done | bytes 2228240 | tf_op jit(solution)/shard_map/all_gather | solution.py:150
  157.1 20.5 %collective-permute-done.4 = bf16[1,2048,384]{2,1,0:T(8,128)(2,1)} collective-permute-done((bf16[1,2048,384]{2,1,0:T(8,128)(2,1)}, bf16[1,2048,384]{2,1,0:T(8,128)(2,1)}, u32[]{:S(2)}, u32[]{:S(2)}) %collective-permute-start.4) | collective-permute-done | bytes 1572896 | tf_op jit(solution)/shard_map/ppermute | solution.py:43
  177.7 3.5 fusion
  181.2 5.9 %convolution_convert_fusion.1 = bf16[1152,2048]{1,0:T(8,128)(2,1)} fusion(pred[1152,512]{1,0:T(8,128)(4,1)S(1)} %fusion, bf16[512,2176]{0,1:T(8,128)(2,1)} %all-gather.2.cloned.1.call-done), kind=kOutput, calls=%fused_computation.5 | convolution fusion | flops 2418278400 | bytes 7405568 | tf_op jit(solution)/shard_map/dot_general | solution.py:183
  187.1 5.3 %all-to-all-start = ((bf16[4,288,2048]{2,1,0:T(8,128)(2,1)}), bf16[4,288,2048]{2,1,0:T(8,128)(2,1)}, u32[]{:S(2)}, u32[]{:S(2)}) async-start(bf16[4,288,2048]{2,1,0:T(8,128)(2,1)} %bitcast.90), calls=%async_computation.1 | async-start | bytes 9437184 | tf_op jit(solution)/shard_map/all_to_all | solution.py:186
  192.4 1.6 collective-permute-start.5
  194.0 35.3 %collective-permute-done.5 = bf16[1,2048,384]{2,1,0:T(8,128)(2,1)} collective-permute-done((bf16[1,2048,384]{2,1,0:T(8,128)(2,1)}, bf16[1,2048,384]{2,1,0:T(8,128)(2,1)}, u32[]{:S(2)}, u32[]{:S(2)}) %collective-permute-start.5) | collective-permute-done | bytes 1572896 | tf_op jit(solution)/shard_map/ppermute | solution.py:43
  229.3 16.8 %all-to-all-done = bf16[4,288,2048]{2,1,0:T(8,128)(2,1)} async-done(((bf16[4,288,2048]{2,1,0:T(8,128)(2,1)}), bf16[4,288,2048]{2,1,0:T(8,128)(2,1)}, u32[]{:S(2)}, u32[]{:S(2)}) %all-to-all-start) | async-done | bytes 4718624 | tf_op jit(solution)/shard_map/all_to_all | solution.py:186
  246.0 8.4 %fusion.11 = f32[1152,768]{1,0:T(8,128)} fusion(bf16[1152,2048]{1,0:T(8,128)(2,1)} %bitcast.12, bf16[1,2048,384]{2,1,0:T(8,128)(2,1)} %copy-done.9, bf16[1,2048,384]{2,1,0:T(8,128)(2,1)S(1)} %copy-done.8), kind=kOutput, calls=%fused_computation.18 | convolution fusion | flops 3630170112 | bytes 11403264 | tf_op jit(solution)/shard_map/dot_general | solution.py:50
  254.5 14.3 %convolution_convert_fusion = bf16[1152,2048]{1,0:T(8,128)(2,1)} fusion(bf16[1,2048,384]{2,1,0:T(8,128)(2,1)} %collective-permute-done.5, bf16[1,2048,384]{2,1,0:T(8,128)(2,1)} %param.27, bf16[1152,2048]{1,0:T(8,128)(2,1)} %bitcast.12, f32[1152,768]{1,0:T(8,128)} %fusion.11, bf16[1,2048,384]{2,1,0:T(8,128)(2,1)} %collective-permute-done.4, ...), kind=kOutput, calls=%fused_computation.4 | convolution fusion | flops 7268007936 | bytes 19267584 | tf_op jit(solution)/shard_map/rf,df->rd/dot_general | solution.py:53
  268.8 5.1 %all-to-all-start.1 = ((bf16[4,288,2048]{2,1,0:T(8,128)(2,1)}), bf16[4,288,2048]{2,1,0:T(8,128)(2,1)}, u32[]{:S(2)}, u32[]{:S(2)}) async-start(bf16[4,288,2048]{2,1,0:T(8,128)(2,1)} %bitcast.89), calls=%async_computation.2 | async-start | bytes 9437184 | tf_op jit(solution)/shard_map/all_to_all | solution.py:192
  274.4 2.5 select_reduce_fusion
  276.9 50.8 %all-to-all-done.1 = bf16[4,288,2048]{2,1,0:T(8,128)(2,1)} async-done(((bf16[4,288,2048]{2,1,0:T(8,128)(2,1)}), bf16[4,288,2048]{2,1,0:T(8,128)(2,1)}, u32[]{:S(2)}, u32[]{:S(2)}) %all-to-all-start.1) | async-done | bytes 4718624 | tf_op jit(solution)/shard_map/all_to_all | solution.py:192
  327.7 4.8 %fusion.35 = f32[512,2048]{1,0:T(8,128)S(1)} fusion(bf16[1152,2048]{1,0:T(8,128)(2,1)} %bitcast.17, f32[1152,512]{1,0:T(8,128)S(1)} %select_reduce_fusion), kind=kOutput, calls=%fused_computation.53 | convolution fusion | flops 2416508928 | bytes 11272192 | tf_op jit(solution)/shard_map/dot_general | solution.py:199
  332.5 6.5 %add_convert_fusion = bf16[512,2048]{1,0:T(8,128)(2,1)} fusion(f32[512,2048]{1,0:T(8,128)S(1)} %fusion.35, bf16[1152,2048]{1,0:T(8,128)(2,1)} %bitcast.17, f32[1152,512]{1,0:T(8,128)S(1)} %select_reduce_fusion), kind=kOutput, calls=%fused_computation.11 | convolution fusion | flops 2420375552 | bytes 13369344 | tf_op jit(solution)/shard_map/dot_general | solution.py:201
  339.0 44.0 %reduce-scatter.5.cloned.1.call-done = bf16[1,128,2048]{2,1,0:T(8,128)(2,1)} async-done(((bf16[4,128,2048]{2,1,0:T(8,128)(2,1)}), bf16[1,128,2048]{2,1,0:T(8,128)(2,1)}) %reduce-scatter.5.cloned.1.call-update) | async-done | bytes 524304 | tf_op jit(solution)/shard_map/reduce_scatter | solution.py:202
  383.1 1.9 fusion.31
  (67 shorter events, 8.6 us)
Async XLA Ops:
  6.5 267.4 %copy-start = (bf16[2048,16]{0,1:T(8,128)(2,1)S(1)}, bf16[2048,16]{0,1:T(8,128)(2,1)}, u32[]{:S(2)}) copy-start(bf16[2048,16]{0,1:T(8,128)(2,1)} %param.23) | copy-start | bytes 196612
  6.5 96.4 %reduce-scatter.3.cloned.1.call-start = ((), (), s32[]{:S(2)}) async-start(), calls=%async_computation.4 | async-start | bytes 2621440 | tf_op jit(solution)/shard_map/reduce_scatter | solution.py:121
  6.5 12.3 %collective-permute-start.1 = (s32[2,256]{1,0:T(2,128)}, s32[2,256]{1,0:T(2,128)S(1)}, u32[]{:S(2)}, u32[]{:S(2)}) collective-permute-start(s32[2,256]{1,0:T(2,128)} %param.17), channel_id=1, source_target_pairs={{0,16},{16,0},{1,17},{17,1},{2,18},{18,2},{3,19},{19,3},{4,20},{20... | collective-permute-start | bytes 6152 | tf_op jit(solution)/shard_map/ppermute | solution.py:43
  12.6 4.5 %copy-start.7 = (f32[128]{0:T(128)S(1)}, f32[128]{0:T(128)}, u32[]{:S(2)}) copy-start(f32[128]{0:T(128)} %param.18) | copy-start | bytes 1540
  12.6 9.3 %collective-permute-start = (bf16[2,256,256]{2,1,0:T(8,128)(2,1)S(1)}, bf16[2,256,256]{2,1,0:T(8,128)(2,1)S(1)}, u32[]{:S(2)}, u32[]{:S(2)}) collective-permute-start(bf16[2,256,256]{2,1,0:T(8,128)(2,1)S(1)} %pad_maximum_fusion.1), channel_id=1, source_target_pairs={{0,16},{16,0},{1,17},{17,1},{2,18},{18,2},{3,19},{19,3},{4,20},{20... | collective-permute-start | bytes 786440 | tf_op jit(solution)/shard_map/ppermute | solution.py:43
  12.7 52.8 %collective-permute-start.2 = (bf16[1024,1024]{1,0:T(8,128)(2,1)}, bf16[1024,1024]{1,0:T(8,128)(2,1)}, u32[]{:S(2)}, u32[]{:S(2)}) collective-permute-start(bf16[1024,1024]{1,0:T(8,128)(2,1)} %param.20), channel_id=1, source_target_pairs={{0,16},{16,0},{1,17},{17,1},{2,18},{18,2},{3,19},{19,3},{4,20},{20... | collective-permute-start | bytes 6291464 | tf_op jit(solution)/shard_map/ppermute | solution.py:43
  17.0 1.6 copy-start.1
  17.1 1.8 copy-start.5
  17.1 4.8 %copy-start.3 = (bf16[2,256,128]{2,1,0:T(8,128)(2,1)S(1)}, bf16[2,256,128]{2,1,0:T(8,128)(2,1)}, u32[]{:S(2)}) copy-start(bf16[2,256,128]{2,1,0:T(8,128)(2,1)} %param.16) | copy-start | bytes 393220
  67.3 4.0 %copy-start.6 = (s32[2,256,8]{1,2,0:T(8,128)S(1)}, s32[2,256,8]{1,2,0:T(8,128)}, u32[]{:S(2)}) copy-start(s32[2,256,8]{1,2,0:T(8,128)} %param.24) | copy-start | bytes 49156
  71.1 85.0 %all-gather.2.cloned.1.call-start = ((), (), s32[]{:S(2)}) async-start(), calls=%async_computation.5 | async-start | bytes 2785280 | tf_op jit(solution)/shard_map/all_gather | solution.py:150
  104.5 1.8 copy-start.4
  107.5 49.7 %collective-permute-start.3 = (bf16[1,2048,384]{2,1,0:T(8,128)(2,1)}, bf16[1,2048,384]{2,1,0:T(8,128)(2,1)S(1)}, u32[]{:S(2)}, u32[]{:S(2)}) collective-permute-start(bf16[1,2048,384]{2,1,0:T(8,128)(2,1)} %param.25), channel_id=1, source_target_pairs={{0,16},{16,0},{1,17},{17,1},{2,18},{18,2},{3,19},{19,3},{4,20},{20... | collective-permute-start | bytes 4718600 | tf_op jit(solution)/shard_map/ppermute | solution.py:43
  109.0 68.7 %collective-permute-start.4 = (bf16[1,2048,384]{2,1,0:T(8,128)(2,1)}, bf16[1,2048,384]{2,1,0:T(8,128)(2,1)}, u32[]{:S(2)}, u32[]{:S(2)}) collective-permute-start(bf16[1,2048,384]{2,1,0:T(8,128)(2,1)} %param.26), channel_id=1, source_target_pairs={{0,16},{16,0},{1,17},{17,1},{2,18},{18,2},{3,19},{19,3},{4,20},{20... | collective-permute-start | bytes 4718600 | tf_op jit(solution)/shard_map/ppermute | solution.py:43
  157.1 30.0 %copy-start.9 = (bf16[1,2048,384]{2,1,0:T(8,128)(2,1)}, bf16[1,2048,384]{2,1,0:T(8,128)(2,1)S(1)}, u32[]{:S(2)}) copy-start(bf16[1,2048,384]{2,1,0:T(8,128)(2,1)S(1)} %collective-permute-done.3) | copy-start | bytes 4718596
  187.1 58.9 %copy-start.8 = (bf16[1,2048,384]{2,1,0:T(8,128)(2,1)S(1)}, bf16[1,2048,384]{2,1,0:T(8,128)(2,1)}, u32[]{:S(2)}) copy-start(bf16[1,2048,384]{2,1,0:T(8,128)(2,1)} %param.25) | copy-start | bytes 4718596
  187.1 58.9 %all-to-all-start = ((bf16[4,288,2048]{2,1,0:T(8,128)(2,1)}), bf16[4,288,2048]{2,1,0:T(8,128)(2,1)}, u32[]{:S(2)}, u32[]{:S(2)}) async-start(bf16[4,288,2048]{2,1,0:T(8,128)(2,1)} %bitcast.90), calls=%async_computation.1 | async-start | bytes 9437184 | tf_op jit(solution)/shard_map/all_to_all | solution.py:186
  192.4 36.9 %collective-permute-start.5 = (bf16[1,2048,384]{2,1,0:T(8,128)(2,1)}, bf16[1,2048,384]{2,1,0:T(8,128)(2,1)}, u32[]{:S(2)}, u32[]{:S(2)}) collective-permute-start(bf16[1,2048,384]{2,1,0:T(8,128)(2,1)} %param.27), channel_id=1, source_target_pairs={{0,16},{16,0},{1,17},{17,1},{2,18},{18,2},{3,19},{19,3},{4,20},{20... | collective-permute-start | bytes 4718600 | tf_op jit(solution)/shard_map/ppermute | solution.py:43
  268.8 5.1 %copy-start.2 = (bf16[512,2176]{0,1:T(8,128)(2,1)S(1)}, bf16[512,2176]{0,1:T(8,128)(2,1)}, u32[]{:S(2)}) copy-start(bf16[512,2176]{0,1:T(8,128)(2,1)} %all-gather.2.cloned.1.call-done) | copy-start | bytes 6684676
  268.8 58.9 %all-to-all-start.1 = ((bf16[4,288,2048]{2,1,0:T(8,128)(2,1)}), bf16[4,288,2048]{2,1,0:T(8,128)(2,1)}, u32[]{:S(2)}, u32[]{:S(2)}) async-start(bf16[4,288,2048]{2,1,0:T(8,128)(2,1)} %bitcast.89), calls=%async_computation.2 | async-start | bytes 9437184 | tf_op jit(solution)/shard_map/all_to_all | solution.py:192
  273.8 109.2 %reduce-scatter.5.cloned.1.call-start = ((), (), s32[]{:S(2)}) async-start(), calls=%async_computation.6 | async-start | bytes 2621440 | tf_op jit(solution)/shard_map/reduce_scatter | solution.py:202
Sparse Core Ops, SparseCore 0:
  71.2 31.7 reduce-scatter.2
  107.6 48.3 all-gather.1
  339.2 43.8 reduce-scatter.4

commit v5 on v4

--- a/solution.py
+++ b/solution.py
@@ -109,21 +109,21 @@
         .astype(jnp.bfloat16)
         .reshape(packs * row_count, head_count * HEAD_WIDTH)
     )
-    full_out_weight = jnp.concatenate(cp_pieces(out_weight, n_cp), axis=1)
-    partial_proj = jnp.dot(
-        attn, full_out_weight, preferred_element_type=jnp.float32
-    ).reshape(packs, row_count, width)
-
     share = row_count // n_tp
     tp_index = lax.axis_index("tp")
     ep_index = lax.axis_index("ep")
+    cp_index = lax.axis_index("cp")
     cap = capacity(share, top_count, experts)
-    projected = lax.psum_scatter(
-        partial_proj.astype(jnp.bfloat16), "tp", scatter_dimension=1, tiled=True
-    ).astype(jnp.float32)
-    cp_index = lax.axis_index("cp")
-    block_width = width // n_cp
-    blocks = projected.reshape(packs, share, n_cp, block_width)
+    weight_pieces = cp_pieces(out_weight, n_cp)
+    summed_blocks = []
+    for piece in weight_pieces:
+        block = jnp.dot(attn, piece, preferred_element_type=jnp.float32).reshape(
+            packs, row_count, piece.shape[1]
+        )
+        summed_blocks.append(
+            lax.psum_scatter(block.astype(jnp.bfloat16), "tp", scatter_dimension=1, tiled=True)
+        )
+    blocks = jnp.stack(summed_blocks, axis=2).astype(jnp.float32)
     source_block = (cp_index - jnp.arange(n_cp, dtype=jnp.int32)) % n_cp
     picks_block = source_block[:, None] == jnp.arange(n_cp, dtype=jnp.int32)[None, :]
     projected = jnp.sum(
@@ -138,12 +138,13 @@
     home_rows = packs * share
     normed = root_mean_scale(state.reshape(home_rows, width), norm_gain).astype(jnp.bfloat16)
 
-    full_out_weight, expert_gate, expert_up, expert_down = lax.optimization_barrier(
-        (full_out_weight, expert_gate, expert_up, expert_down)
+    weight_pieces, expert_gate, expert_up, expert_down = lax.optimization_barrier(
+        (weight_pieces, expert_gate, expert_up, expert_down)
     )
     gate_pieces = cp_pieces(expert_gate, n_cp)
     up_pieces = cp_pieces(expert_up, n_cp)
     down_pieces = cp_pieces(expert_down, n_cp)
+    normed, gate_pieces = lax.optimization_barrier((normed, gate_pieces))
 
     lanes = 128
     id_lanes = jnp.pad(local_ids.astype(jnp.bfloat16), ((0, 0), (0, lanes - top_count)))
@@ -175,7 +176,7 @@
         axis=-1,
     )
     target = jnp.where(mine, dest * cap2 + rank_of, jnp.int32(-1)).T
-    target, gate_pieces, up_pieces = lax.optimization_barrier((target, gate_pieces, up_pieces))
+    target, up_pieces = lax.optimization_barrier((target, up_pieces))
     hit = target[:, None, :] == jnp.arange(n_slots, dtype=jnp.int32)[None, :, None]
     select = jnp.any(hit, axis=0).astype(jnp.bfloat16)
     weight = jnp.sum(jnp.where(hit, gates_all.T[:, None, :], jnp.float32(0.0)), axis=0)

time: 392 us -> 367 us (0.936)
  waiting for transfers between devices: 288 us -> 265 us
    ppermute x6, waiting for transfers between devices: 98.3 us -> 82.8 us  [cp_pieces(): pieces.append(lax.ppermute(x, 'cp', perm))]
    reduce_scatter x1 -> x2, waiting for transfers between devices: 31.4 us -> 24.4 us  [shards(): lax.psum_scatter(block.astype(jnp.bfloat16), 'tp', scatter_dimension=1, t...]
  transfers between devices with their start and end apart: 11 -> 12, of which waited for: 9 -> 9; matrix products, arithmetic and copies ran while one was open for 4% -> 7% of each run, Pallas kernels for 0% -> 0%
where the time goes in v5:
time: 367 us
  waiting for transfers between devices  265 us (72%)
  matrix products  50.5 us (14%)
  starting transfers between devices  18.3 us (5%)
  other arithmetic  17.6 us (5%)
  between operations  13.5 us (4%)
    ppermute x6, waiting for transfers between devices, cp_pieces(): pieces.append(lax.ppermute(x, 'cp', perm))  82.8 us
    all_to_all x1, waiting for transfers between devices, shards(): lax.all_to_all(served, 'tp', split_axis=0, concat_axis=0, tiled=True)  50.8 us
    all_gather x1, waiting for transfers between devices, shards(): lax.all_gather(jnp.concatenate([normed, id_lanes], axis=1), 'ep', axis=0,...  48.2 us
    reduce_scatter x1, waiting for transfers between devices, shards(): lax.psum_scatter(partial.astype(jnp.bfloat16).reshape(n_ep, home_rows, wi...  41.3 us
    reduce_scatter x2, waiting for transfers between devices, shards(): lax.psum_scatter(block.astype(jnp.bfloat16), 'tp', scatter_dimension=1, t...  24.4 us
    all_to_all x1, waiting for transfers between devices, shards(): lax.all_to_all(buffer.reshape(n_tp, cap2, width), 'tp', split_axis=0, con...  17 us
    dot_general x1, matrix products, expert_rows(): jnp.einsum('rf,df->rd', hidden_act, full_down[0], preferred_element_type=...  13.9 us
    dot_general x1, matrix products, expert_rows(): jnp.dot(flat_rows, full_gate[0], preferred_element_type=jnp.float32)  8.91 us
  transfers between devices with their start and end apart: 12, of which 9 were waited for; matrix products, arithmetic and copies ran while one was open for 7% of the time, Pallas kernels for 0%

profile of v5, /device:TPU:0, one launch (start us, length us, event | category | flops | bytes accessed | tf_op | source)
XLA Modules:
  0.0 366.8 jit_solution(2281632203789861577)
XLA Ops:
  6.5 3.0 collective-permute-start.1
  9.5 1.0 fusion.43
  10.6 1.0 fusion.45
  11.6 0.9 pad_maximum_fusion.1
  12.7 2.0 collective-permute-start.2
  14.7 1.5 copy.82
  18.0 3.8 %collective-permute-done = bf16[2,256,256]{2,1,0:T(8,128)(2,1)S(1)} collective-permute-done((bf16[2,256,256]{2,1,0:T(8,128)(2,1)S(1)}, bf16[2,256,256]{2,1,0:T(8,128)(2,1)S(1)}, u32[]{:S(2)}, u32[]{:S(2)}) %collective-permute-start) | collective-permute-done | bytes 262176 | tf_op jit(solution)/shard_map/ppermute | solution.py:43
  21.9 2.2 fusion.1
  24.2 1.6 fusion.23
  25.8 2.3 fusion.29
  28.1 37.3 %collective-permute-done.2 = bf16[1024,1024]{1,0:T(8,128)(2,1)} collective-permute-done((bf16[1024,1024]{1,0:T(8,128)(2,1)}, bf16[1024,1024]{1,0:T(8,128)(2,1)}, u32[]{:S(2)}, u32[]{:S(2)}) %collective-permute-start.2) | collective-permute-done | bytes 2097184 | tf_op jit(solution)/shard_map/ppermute | solution.py:43
  65.5 3.8 %fusion.32 = bf16[2,256,1024]{2,1,0:T(8,128)(2,1)} fusion(bf16[2,256,1024]{1,2,0:T(8,128)(2,1)S(1)} %bitcast.98, bf16[1024,1024]{1,0:T(8,128)(2,1)} %collective-permute-done.2), kind=kOutput, calls=%fused_computation.42 | convolution fusion | flops 1074266112 | bytes 4194304 | tf_op jit(solution)/shard_map/dot_general | solution.py:120
  70.2 24.4 %reduce-scatter.6.cloned.1.call-done = bf16[2,64,1024]{2,1,0:T(8,128)(2,1)} async-done(((bf16[2,256,1024]{2,1,0:T(8,128)(2,1)}), bf16[2,64,1024]{2,1,0:T(8,128)(2,1)}) %reduce-scatter.6.cloned.1.call-update) | async-done | bytes 262160 | tf_op jit(solution)/shard_map/reduce_scatter | solution.py:124
  94.6 1.5 select_reduce_fusion.1
  96.3 1.3 multiply_reduce_fusion
  98.3 6.6 %collective-permute-done.3 = bf16[1,2048,384]{2,1,0:T(8,128)(2,1)} collective-permute-done((bf16[1,2048,384]{2,1,0:T(8,128)(2,1)}, bf16[1,2048,384]{2,1,0:T(8,128)(2,1)}, u32[]{:S(2)}, u32[]{:S(2)}) %collective-permute-start.3) | collective-permute-done | bytes 1572896 | tf_op jit(solution)/shard_map/ppermute | solution.py:43
  106.4 48.2 %all-gather.2.cloned.1.call-done = bf16[512,2176]{0,1:T(8,128)(2,1)} async-done(((bf16[128,2176]{0,1:T(8,128)(2,1)}), bf16[512,2176]{0,1:T(8,128)(2,1)}) %all-gather.2.cloned.1.call-update) | async-done | bytes 2228240 | tf_op jit(solution)/shard_map/all_gather | solution.py:151
  155.7 3.5 fusion
  159.2 5.9 %convolution_convert_fusion.1 = bf16[1152,2048]{1,0:T(8,128)(2,1)} fusion(pred[1152,512]{1,0:T(8,128)(4,1)S(1)} %fusion, bf16[512,2176]{0,1:T(8,128)(2,1)} %all-gather.2.cloned.1.call-done), kind=kOutput, calls=%fused_computation.5 | convolution fusion | flops 2418278400 | bytes 7405568 | tf_op jit(solution)/shard_map/dot_general | solution.py:184
  165.1 5.3 %all-to-all-start = ((bf16[4,288,2048]{2,1,0:T(8,128)(2,1)}), bf16[4,288,2048]{2,1,0:T(8,128)(2,1)}, u32[]{:S(2)}, u32[]{:S(2)}) async-start(bf16[4,288,2048]{2,1,0:T(8,128)(2,1)} %bitcast.94), calls=%async_computation.2 | async-start | bytes 9437184 | tf_op jit(solution)/shard_map/all_to_all | solution.py:187
  170.4 1.6 collective-permute-start.5
  172.0 35.1 %collective-permute-done.5 = bf16[1,2048,384]{2,1,0:T(8,128)(2,1)} collective-permute-done((bf16[1,2048,384]{2,1,0:T(8,128)(2,1)S(1)}, bf16[1,2048,384]{2,1,0:T(8,128)(2,1)}, u32[]{:S(2)}, u32[]{:S(2)}) %collective-permute-start.5) | collective-permute-done | bytes 1572896 | tf_op jit(solution)/shard_map/ppermute | solution.py:43
  207.1 17.0 %all-to-all-done = bf16[4,288,2048]{2,1,0:T(8,128)(2,1)} async-done(((bf16[4,288,2048]{2,1,0:T(8,128)(2,1)}), bf16[4,288,2048]{2,1,0:T(8,128)(2,1)}, u32[]{:S(2)}, u32[]{:S(2)}) %all-to-all-start) | async-done | bytes 4718624 | tf_op jit(solution)/shard_map/all_to_all | solution.py:187
  224.0 8.9 %fusion.9 = f32[1152,768]{1,0:T(8,128)} fusion(bf16[1152,2048]{1,0:T(8,128)(2,1)} %bitcast.15, bf16[1,2048,384]{2,1,0:T(8,128)(2,1)} %collective-permute-done.3, bf16[1,2048,384]{2,1,0:T(8,128)(2,1)} %param.25), kind=kOutput, calls=%fused_computation.16 | convolution fusion | flops 3630170112 | bytes 11403264 | tf_op jit(solution)/shard_map/dot_general | solution.py:50
  233.0 13.9 %convolution_convert_fusion = bf16[1152,2048]{1,0:T(8,128)(2,1)} fusion(bf16[1,2048,384]{2,1,0:T(8,128)(2,1)} %collective-permute-done.5, bf16[1,2048,384]{2,1,0:T(8,128)(2,1)S(1)} %copy-done.8, bf16[1152,2048]{1,0:T(8,128)(2,1)} %bitcast.15, f32[1152,768]{1,0:T(8,128)} %fusion.9, bf16[1,2048,384]{2,1,0:T(8,128)(2,1)} %copy-done.9, ...), kind=kOutput, calls=%fused_computation.4 | convolution fusion | flops 7268007936 | bytes 19267584 | tf_op jit(solution)/shard_map/rf,df->rd/dot_general | solution.py:53
  246.8 5.1 %all-to-all-start.1 = ((bf16[4,288,2048]{2,1,0:T(8,128)(2,1)}), bf16[4,288,2048]{2,1,0:T(8,128)(2,1)}, u32[]{:S(2)}, u32[]{:S(2)}) async-start(bf16[4,288,2048]{2,1,0:T(8,128)(2,1)} %bitcast.93), calls=%async_computation.3 | async-start | bytes 9437184 | tf_op jit(solution)/shard_map/all_to_all | solution.py:193
  252.5 2.5 select_reduce_fusion
  255.0 50.8 %all-to-all-done.1 = bf16[4,288,2048]{2,1,0:T(8,128)(2,1)} async-done(((bf16[4,288,2048]{2,1,0:T(8,128)(2,1)}), bf16[4,288,2048]{2,1,0:T(8,128)(2,1)}, u32[]{:S(2)}, u32[]{:S(2)}) %all-to-all-start.1) | async-done | bytes 4718624 | tf_op jit(solution)/shard_map/all_to_all | solution.py:193
  305.7 4.8 %fusion.40 = f32[512,2048]{1,0:T(8,128)S(1)} fusion(bf16[1152,2048]{1,0:T(8,128)(2,1)} %bitcast.20, f32[1152,512]{1,0:T(8,128)S(1)} %select_reduce_fusion), kind=kOutput, calls=%fused_computation.55 | convolution fusion | flops 2416508928 | bytes 11272192 | tf_op jit(solution)/shard_map/dot_general | solution.py:200
  310.5 6.5 %add_convert_fusion = bf16[512,2048]{1,0:T(8,128)(2,1)} fusion(f32[512,2048]{1,0:T(8,128)S(1)} %fusion.40, bf16[1152,2048]{1,0:T(8,128)(2,1)} %bitcast.20, f32[1152,512]{1,0:T(8,128)S(1)} %select_reduce_fusion), kind=kOutput, calls=%fused_computation.9 | convolution fusion | flops 2420375552 | bytes 13369344 | tf_op jit(solution)/shard_map/dot_general | solution.py:202
  317.1 41.3 %reduce-scatter.8.cloned.1.call-done = bf16[1,128,2048]{2,1,0:T(8,128)(2,1)} async-done(((bf16[4,128,2048]{2,1,0:T(8,128)(2,1)}), bf16[1,128,2048]{2,1,0:T(8,128)(2,1)}) %reduce-scatter.8.cloned.1.call-update) | async-done | bytes 524304 | tf_op jit(solution)/shard_map/reduce_scatter | solution.py:203
  358.4 1.9 fusion.36
  (67 shorter events, 6.9 us)
Async XLA Ops:
  6.5 245.4 %copy-start = (bf16[2048,16]{0,1:T(8,128)(2,1)S(1)}, bf16[2048,16]{0,1:T(8,128)(2,1)}, u32[]{:S(2)}) copy-start(bf16[2048,16]{0,1:T(8,128)(2,1)} %param.23) | copy-start | bytes 196612
  6.5 63.7 %reduce-scatter.4.cloned.1.call-start = ((), (), s32[]{:S(2)}) async-start(), calls=%async_computation.5 | async-start | bytes 1310720 | tf_op jit(solution)/shard_map/reduce_scatter | solution.py:124
  6.5 11.2 %collective-permute-start.1 = (s32[2,256]{1,0:T(2,128)}, s32[2,256]{1,0:T(2,128)S(1)}, u32[]{:S(2)}, u32[]{:S(2)}) collective-permute-start(s32[2,256]{1,0:T(2,128)} %param.17), channel_id=1, source_target_pairs={{0,16},{16,0},{1,17},{17,1},{2,18},{18,2},{3,19},{19,3},{4,20},{20... | collective-permute-start | bytes 6152 | tf_op jit(solution)/shard_map/ppermute | solution.py:43
  12.6 4.5 %copy-start.7 = (f32[128]{0:T(128)S(1)}, f32[128]{0:T(128)}, u32[]{:S(2)}) copy-start(f32[128]{0:T(128)} %param.18) | copy-start | bytes 1540
  12.6 9.3 %collective-permute-start = (bf16[2,256,256]{2,1,0:T(8,128)(2,1)S(1)}, bf16[2,256,256]{2,1,0:T(8,128)(2,1)S(1)}, u32[]{:S(2)}, u32[]{:S(2)}) collective-permute-start(bf16[2,256,256]{2,1,0:T(8,128)(2,1)S(1)} %pad_maximum_fusion.1), channel_id=1, source_target_pairs={{0,16},{16,0},{1,17},{17,1},{2,18},{18,2},{3,19},{19,3},{4,20},{20... | collective-permute-start | bytes 786440 | tf_op jit(solution)/shard_map/ppermute | solution.py:43
  12.7 52.8 %collective-permute-start.2 = (bf16[1024,1024]{1,0:T(8,128)(2,1)}, bf16[1024,1024]{1,0:T(8,128)(2,1)}, u32[]{:S(2)}, u32[]{:S(2)}) collective-permute-start(bf16[1024,1024]{1,0:T(8,128)(2,1)} %param.20), channel_id=1, source_target_pairs={{0,16},{16,0},{1,17},{17,1},{2,18},{18,2},{3,19},{19,3},{4,20},{20... | collective-permute-start | bytes 6291464 | tf_op jit(solution)/shard_map/ppermute | solution.py:43
  16.2 1.6 copy-start.5
  16.2 5.7 %copy-start.3 = (bf16[2,256,128]{2,1,0:T(8,128)(2,1)S(1)}, bf16[2,256,128]{2,1,0:T(8,128)(2,1)}, u32[]{:S(2)}) copy-start(bf16[2,256,128]{2,1,0:T(8,128)(2,1)} %param.16) | copy-start | bytes 393220
  24.2 1.6 copy-start.1
  28.0 41.9 %copy-start.6 = (s32[2,256,8]{1,2,0:T(8,128)S(1)}, s32[2,256,8]{1,2,0:T(8,128)}, u32[]{:S(2)}) copy-start(s32[2,256,8]{1,2,0:T(8,128)} %param.24) | copy-start | bytes 49156
  28.1 66.6 %reduce-scatter.6.cloned.1.call-start = ((), (), s32[]{:S(2)}) async-start(), calls=%async_computation.6 | async-start | bytes 1310720 | tf_op jit(solution)/shard_map/reduce_scatter | solution.py:124
  69.3 85.3 %all-gather.2.cloned.1.call-start = ((), (), s32[]{:S(2)}) async-start(), calls=%async_computation.7 | async-start | bytes 2785280 | tf_op jit(solution)/shard_map/all_gather | solution.py:151
  69.6 35.3 %collective-permute-start.3 = (bf16[1,2048,384]{2,1,0:T(8,128)(2,1)}, bf16[1,2048,384]{2,1,0:T(8,128)(2,1)}, u32[]{:S(2)}, u32[]{:S(2)}) collective-permute-start(bf16[1,2048,384]{2,1,0:T(8,128)(2,1)} %param.25), channel_id=1, source_target_pairs={{0,16},{16,0},{1,17},{17,1},{2,18},{18,2},{3,19},{19,3},{4,20},{20... | collective-permute-start | bytes 4718600 | tf_op jit(solution)/shard_map/ppermute | solution.py:43
  96.2 1.8 copy-start.4
  105.7 49.9 %collective-permute-start.4 = (bf16[1,2048,384]{2,1,0:T(8,128)(2,1)}, bf16[1,2048,384]{2,1,0:T(8,128)(2,1)S(1)}, u32[]{:S(2)}, u32[]{:S(2)}) collective-permute-start(bf16[1,2048,384]{2,1,0:T(8,128)(2,1)} %param.26), channel_id=1, source_target_pairs={{0,16},{16,0},{1,17},{17,1},{2,18},{18,2},{3,19},{19,3},{4,20},{20... | collective-permute-start | bytes 4718600 | tf_op jit(solution)/shard_map/ppermute | solution.py:43
  155.7 9.4 %copy-start.9 = (bf16[1,2048,384]{2,1,0:T(8,128)(2,1)}, bf16[1,2048,384]{2,1,0:T(8,128)(2,1)S(1)}, u32[]{:S(2)}) copy-start(bf16[1,2048,384]{2,1,0:T(8,128)(2,1)S(1)} %collective-permute-done.4) | copy-start | bytes 4718596
  165.1 5.3 %copy-start.8 = (bf16[1,2048,384]{2,1,0:T(8,128)(2,1)S(1)}, bf16[1,2048,384]{2,1,0:T(8,128)(2,1)}, u32[]{:S(2)}) copy-start(bf16[1,2048,384]{2,1,0:T(8,128)(2,1)} %param.27) | copy-start | bytes 4718596
  165.1 58.9 %all-to-all-start = ((bf16[4,288,2048]{2,1,0:T(8,128)(2,1)}), bf16[4,288,2048]{2,1,0:T(8,128)(2,1)}, u32[]{:S(2)}, u32[]{:S(2)}) async-start(bf16[4,288,2048]{2,1,0:T(8,128)(2,1)} %bitcast.94), calls=%async_computation.2 | async-start | bytes 9437184 | tf_op jit(solution)/shard_map/all_to_all | solution.py:187
  170.4 36.6 %collective-permute-start.5 = (bf16[1,2048,384]{2,1,0:T(8,128)(2,1)S(1)}, bf16[1,2048,384]{2,1,0:T(8,128)(2,1)}, u32[]{:S(2)}, u32[]{:S(2)}) collective-permute-start(bf16[1,2048,384]{2,1,0:T(8,128)(2,1)S(1)} %copy-done.8), channel_id=1, source_target_pairs={{0,16},{16,0},{1,17},{17,1},{2,18},{18,2},{3,19},{19,3},{4,20},{20... | collective-permute-start | bytes 4718600 | tf_op jit(solution)/shard_map/ppermute | solution.py:43
  246.8 5.1 %copy-start.2 = (bf16[512,2176]{0,1:T(8,128)(2,1)S(1)}, bf16[512,2176]{0,1:T(8,128)(2,1)}, u32[]{:S(2)}) copy-start(bf16[512,2176]{0,1:T(8,128)(2,1)} %all-gather.2.cloned.1.call-done) | copy-start | bytes 6684676
  246.8 58.9 %all-to-all-start.1 = ((bf16[4,288,2048]{2,1,0:T(8,128)(2,1)}), bf16[4,288,2048]{2,1,0:T(8,128)(2,1)}, u32[]{:S(2)}, u32[]{:S(2)}) async-start(bf16[4,288,2048]{2,1,0:T(8,128)(2,1)} %bitcast.93), calls=%async_computation.3 | async-start | bytes 9437184 | tf_op jit(solution)/shard_map/all_to_all | solution.py:193
  251.9 106.5 %reduce-scatter.8.cloned.1.call-start = ((), (), s32[]{:S(2)}) async-start(), calls=%async_computation.8 | async-start | bytes 2621440 | tf_op jit(solution)/shard_map/reduce_scatter | solution.py:203
Sparse Core Ops, SparseCore 0:
  28.2 25.1 reduce-scatter.3
  69.4 25.1 reduce-scatter.5
  105.9 48.6 all-gather.1
  317.2 41.1 reduce-scatter.7

commit v6 on v5

--- a/solution.py
+++ b/solution.py
@@ -147,68 +147,77 @@
     normed, gate_pieces = lax.optimization_barrier((normed, gate_pieces))
 
     lanes = 128
-    id_lanes = jnp.pad(local_ids.astype(jnp.bfloat16), ((0, 0), (0, lanes - top_count)))
-    rows_all = lax.all_gather(
-        jnp.concatenate([normed, id_lanes], axis=1), "ep", axis=0, tiled=True
-    )
-    normed_all = rows_all[:, :width]
-    ids_all = rows_all[:, width : width + top_count].astype(jnp.int32)
-    logits = jnp.dot(normed_all, router_weight, preferred_element_type=jnp.float32)
-    picks = ids_all[:, :, None] == jnp.arange(experts, dtype=jnp.int32)[None, None, :]
-    raised = jnp.exp(jnp.sum(jnp.where(picks, logits[:, None, :], jnp.float32(0.0)), axis=-1))
-    gates_all = raised / jnp.sum(raised, axis=-1, keepdims=True)
-
-    gathered = n_ep * home_rows
-    dev_cap = packs * cap
-    cap2 = n_ep * dev_cap
+    cap2 = n_ep * cap
     n_slots = n_tp * cap2
-    mine = (ids_all % n_ep) == ep_index
-    dest = ids_all // n_ep
-    named = jnp.stack(
-        [jnp.any(mine & (dest == j), axis=1) for j in range(n_tp)], axis=1
-    ).astype(jnp.bfloat16)
+    gathered = n_ep * share
     row_iota = jnp.arange(gathered, dtype=jnp.int32)
     earlier = (row_iota[:, None] > row_iota[None, :]).astype(jnp.bfloat16)
-    rank = jnp.dot(earlier, named, preferred_element_type=jnp.float32).astype(jnp.int32)
-    rank_of = jnp.sum(
-        jnp.where(dest[:, :, None] == jnp.arange(n_tp, dtype=jnp.int32)[None, None, :],
-                  rank[:, None, :], 0),
-        axis=-1,
-    )
-    target = jnp.where(mine, dest * cap2 + rank_of, jnp.int32(-1)).T
-    target, up_pieces = lax.optimization_barrier((target, up_pieces))
-    hit = target[:, None, :] == jnp.arange(n_slots, dtype=jnp.int32)[None, :, None]
-    select = jnp.any(hit, axis=0).astype(jnp.bfloat16)
-    weight = jnp.sum(jnp.where(hit, gates_all.T[:, None, :], jnp.float32(0.0)), axis=0)
-
-    buffer = jnp.dot(select, normed_all, preferred_element_type=jnp.float32).astype(jnp.bfloat16)
-    full_gate = jnp.concatenate(gate_pieces, axis=2)
-    full_up = jnp.concatenate(up_pieces, axis=2)
-    received = lax.all_to_all(
-        buffer.reshape(n_tp, cap2, width), "tp", split_axis=0, concat_axis=0, tiled=True
-    )
-    received, down_pieces = lax.optimization_barrier((received, down_pieces))
-    full_down = jnp.concatenate(down_pieces, axis=2)
-    served = expert_rows(received, full_gate, full_up, full_down)
-    back = lax.all_to_all(served, "tp", split_axis=0, concat_axis=0, tiled=True).reshape(
-        n_slots, width
-    )
-
-    weight_hi = weight.astype(jnp.bfloat16)
-    weight_lo = (weight - weight_hi.astype(jnp.float32)).astype(jnp.bfloat16)
     contract = (((0,), (0,)), ((), ()))
-    partial = lax.dot_general(
-        weight_hi, back, contract, preferred_element_type=jnp.float32
-    ) + lax.dot_general(weight_lo, back, contract, preferred_element_type=jnp.float32)
-    mixture = lax.psum_scatter(
-        partial.astype(jnp.bfloat16).reshape(n_ep, home_rows, width),
-        "ep",
-        scatter_dimension=0,
-        tiled=True,
-    )
-    layer_out = (state + mixture.astype(jnp.float32).reshape(packs, share, width)).astype(
-        jnp.bfloat16
-    )
+    mixtures = []
+    for chunk in range(packs):
+        rows = normed[chunk * share : (chunk + 1) * share]
+        ids = local_ids[chunk * share : (chunk + 1) * share]
+        id_lanes = jnp.pad(ids.astype(jnp.bfloat16), ((0, 0), (0, lanes - top_count)))
+        rows_all = lax.all_gather(
+            jnp.concatenate([rows, id_lanes], axis=1), "ep", axis=0, tiled=True
+        )
+        normed_all = rows_all[:, :width]
+        ids_all = rows_all[:, width : width + top_count].astype(jnp.int32)
+        logits = jnp.dot(normed_all, router_weight, preferred_element_type=jnp.float32)
+        picks = ids_all[:, :, None] == jnp.arange(experts, dtype=jnp.int32)[None, None, :]
+        raised = jnp.exp(
+            jnp.sum(jnp.where(picks, logits[:, None, :], jnp.float32(0.0)), axis=-1)
+        )
+        gates_all = raised / jnp.sum(raised, axis=-1, keepdims=True)
+        mine = (ids_all % n_ep) == ep_index
+        dest = ids_all // n_ep
+        named = jnp.stack(
+            [jnp.any(mine & (dest == j), axis=1) for j in range(n_tp)], axis=1
+        ).astype(jnp.bfloat16)
+        rank = jnp.dot(earlier, named, preferred_element_type=jnp.float32).astype(jnp.int32)
+        rank_of = jnp.sum(
+            jnp.where(dest[:, :, None] == jnp.arange(n_tp, dtype=jnp.int32)[None, None, :],
+                      rank[:, None, :], 0),
+            axis=-1,
+        )
+        target = jnp.where(mine, dest * cap2 + rank_of, jnp.int32(-1)).T
+        if chunk == 0:
+            target, up_pieces = lax.optimization_barrier((target, up_pieces))
+            full_gate = jnp.concatenate(gate_pieces, axis=2)
+            full_up = jnp.concatenate(up_pieces, axis=2)
+        hit = target[:, None, :] == jnp.arange(n_slots, dtype=jnp.int32)[None, :, None]
+        select = jnp.any(hit, axis=0).astype(jnp.bfloat16)
+        weight = jnp.sum(jnp.where(hit, gates_all.T[:, None, :], jnp.float32(0.0)), axis=0)
+
+        buffer = jnp.dot(select, normed_all, preferred_element_type=jnp.float32).astype(
+            jnp.bfloat16
+        )
+        received = lax.all_to_all(
+            buffer.reshape(n_tp, cap2, width), "tp", split_axis=0, concat_axis=0, tiled=True
+        )
+        if chunk == 0:
+            received, down_pieces = lax.optimization_barrier((received, down_pieces))
+            full_down = jnp.concatenate(down_pieces, axis=2)
+        served = expert_rows(received, full_gate, full_up, full_down)
+        back = lax.all_to_all(served, "tp", split_axis=0, concat_axis=0, tiled=True).reshape(
+            n_slots, width
+        )
+
+        weight_hi = weight.astype(jnp.bfloat16)
+        weight_lo = (weight - weight_hi.astype(jnp.float32)).astype(jnp.bfloat16)
+        partial = lax.dot_general(
+            weight_hi, back, contract, preferred_element_type=jnp.float32
+        ) + lax.dot_general(weight_lo, back, contract, preferred_element_type=jnp.float32)
+        mixtures.append(
+            lax.psum_scatter(
+                partial.astype(jnp.bfloat16).reshape(n_ep, share, width),
+                "ep",
+                scatter_dimension=0,
+                tiled=True,
+            )
+        )
+    mixture = jnp.concatenate(mixtures, axis=0).astype(jnp.float32)
+    layer_out = (state + mixture).astype(jnp.bfloat16)
     return layer_out
 
 

time: 367 us -> 343 us (0.935)
  waiting for transfers between devices: 265 us -> 221 us
  matrix products: 50.5 us -> 59.4 us
  starting transfers between devices: 18.3 us -> 25.9 us
    ppermute x6, waiting for transfers between devices: 82.8 us -> 48.4 us  [cp_pieces(): pieces.append(lax.ppermute(x, 'cp', perm))]
    all_to_all x1 -> x2, waiting for transfers between devices: 50.8 us -> 31.3 us  [shards(): lax.all_to_all(served, 'tp', split_axis=0, concat_axis=0, tiled=True)]
    all_to_all x1 -> x2, waiting for transfers between devices: 17 us -> 32.5 us  [shards(): lax.all_to_all(buffer.reshape(n_tp, cap2, width), 'tp', split_axis=0, con...]
    reduce_scatter x1 -> x2, waiting for transfers between devices: 41.3 us -> 27.8 us  [shards(): lax.psum_scatter(partial.astype(jnp.bfloat16).reshape(n_ep, share, width)...]
    all_gather x1 -> x2, waiting for transfers between devices: 48.2 us -> 57.1 us  [shards(): lax.all_gather(jnp.concatenate([rows, id_lanes], axis=1), 'ep', axis=0, t...]
    dot_general x1 -> x2, matrix products: 13.9 us -> 19 us  [expert_rows(): jnp.einsum('rf,df->rd', hidden_act, full_down[0], preferred_element_type=...]
    all_to_all x1 -> x2, starting transfers between devices: 5.28 us -> 8.31 us  [shards(): lax.all_to_all(buffer.reshape(n_tp, cap2, width), 'tp', split_axis=0, con...]
    dot_general x1 -> x2, matrix products: 8.91 us -> 11 us  [expert_rows(): jnp.dot(flat_rows, full_gate[0], preferred_element_type=jnp.float32)]
  transfers between devices with their start and end apart: 12 -> 16, of which waited for: 9 -> 12; matrix products, arithmetic and copies ran while one was open for 7% -> 20% of each run, Pallas kernels for 0% -> 0%
where the time goes in v6:
time: 343 us; the launch traced here: 342 us
  waiting for transfers between devices  221 us (64%)
  matrix products  59.4 us (17%)
  starting transfers between devices  25.9 us (8%)
  other arithmetic  15.9 us (5%)
  between operations  14 us (4%)
  local copies, waits for them, and re-layouts  5.4 us (2%)
    all_gather x2, waiting for transfers between devices, shards(): lax.all_gather(jnp.concatenate([rows, id_lanes], axis=1), 'ep', axis=0, t...  57.1 us
    ppermute x6, waiting for transfers between devices, cp_pieces(): pieces.append(lax.ppermute(x, 'cp', perm))  48.4 us
    all_to_all x2, waiting for transfers between devices, shards(): lax.all_to_all(buffer.reshape(n_tp, cap2, width), 'tp', split_axis=0, con...  32.5 us
    all_to_all x2, waiting for transfers between devices, shards(): lax.all_to_all(served, 'tp', split_axis=0, concat_axis=0, tiled=True)  31.3 us
    reduce_scatter x2, waiting for transfers between devices, shards(): lax.psum_scatter(partial.astype(jnp.bfloat16).reshape(n_ep, share, width)...  27.8 us
    reduce_scatter x2, waiting for transfers between devices, shards(): lax.psum_scatter(block.astype(jnp.bfloat16), 'tp', scatter_dimension=1, t...  24.3 us
    dot_general x2, matrix products, expert_rows(): jnp.einsum('rf,df->rd', hidden_act, full_down[0], preferred_element_type=...  19 us
    dot_general x2, matrix products, expert_rows(): jnp.dot(flat_rows, full_gate[0], preferred_element_type=jnp.float32)  11 us
  transfers between devices with their start and end apart: 16, of which 12 were waited for; matrix products, arithmetic and copies ran while one was open for 20% of the time, Pallas kernels for 0%

profile of v6, /device:TPU:0, one launch (start us, length us, event | category | flops | bytes accessed | tf_op | source)
XLA Modules:
  0.0 342.0 jit_solution(8752805374858603834)
XLA Ops:
  9.6 3.0 collective-permute-start
  12.7 1.9 collective-permute-start.2
  17.8 2.0 collective-permute-done.1
  20.1 2.2 fusion
  24.0 2.3 fusion.25
  26.3 37.7 %collective-permute-done.2 = bf16[1024,1024]{1,0:T(8,128)(2,1)} collective-permute-done((bf16[1024,1024]{1,0:T(8,128)(2,1)}, bf16[1024,1024]{1,0:T(8,128)(2,1)}, u32[]{:S(2)}, u32[]{:S(2)}) %collective-permute-start.2) | collective-permute-done | bytes 2097184 | tf_op jit(solution)/shard_map/ppermute | solution.py:43
  64.1 3.8 %fusion.28 = bf16[2,256,1024]{2,1,0:T(8,128)(2,1)} fusion(bf16[2,256,1024]{1,2,0:T(8,128)(2,1)S(1)} %bitcast.129, bf16[1024,1024]{1,0:T(8,128)(2,1)} %collective-permute-done.2), kind=kOutput, calls=%fused_computation.43 | convolution fusion | flops 1074266112 | bytes 4194304 | tf_op jit(solution)/shard_map/dot_general | solution.py:120
  70.1 24.3 %reduce-scatter.7.cloned.1.call-done = bf16[2,64,1024]{2,1,0:T(8,128)(2,1)} async-done(((bf16[2,256,1024]{2,1,0:T(8,128)(2,1)}), bf16[2,64,1024]{2,1,0:T(8,128)(2,1)}) %reduce-scatter.7.cloned.1.call-update) | async-done | bytes 262160 | tf_op jit(solution)/shard_map/reduce_scatter | solution.py:124
  97.6 6.4 %collective-permute-done.3 = bf16[1,2048,384]{2,1,0:T(8,128)(2,1)} collective-permute-done((bf16[1,2048,384]{2,1,0:T(8,128)(2,1)S(1)}, bf16[1,2048,384]{2,1,0:T(8,128)(2,1)}, u32[]{:S(2)}, u32[]{:S(2)}) %collective-permute-start.3) | collective-permute-done | bytes 1572896 | tf_op jit(solution)/shard_map/ppermute | solution.py:43
  107.1 28.0 %all-gather.3.cloned.1.call-done = bf16[256,2176]{1,0:T(8,128)(2,1)} async-done(((bf16[64,2176]{1,0:T(8,128)(2,1)}), bf16[256,2176]{1,0:T(8,128)(2,1)}) %all-gather.3.cloned.1.call-update) | async-done | bytes 1114128 | tf_op jit(solution)/shard_map/all_gather | solution.py:161
  136.0 29.0 %all-gather.5.cloned.1.call-done = bf16[256,2176]{1,0:T(8,128)(2,1)} async-done(((bf16[64,2176]{1,0:T(8,128)(2,1)}), bf16[256,2176]{1,0:T(8,128)(2,1)}) %all-gather.5.cloned.1.call-update) | async-done | bytes 1114128 | tf_op jit(solution)/shard_map/all_gather | solution.py:161
  167.1 3.4 convolution_convert_fusion.3
  170.5 3.6 %all-to-all-start = ((bf16[4,144,2048]{2,1,0:T(8,128)(2,1)}), bf16[4,144,2048]{2,1,0:T(8,128)(2,1)S(1)}, u32[]{:S(2)}, u32[]{:S(2)}) async-start(bf16[4,144,2048]{2,1,0:T(8,128)(2,1)} %bitcast.15), calls=%async_computation.2 | async-start | bytes 4718592 | tf_op jit(solution)/shard_map/all_to_all | solution.py:195
  176.7 3.4 %convolution_convert_fusion.2 = bf16[576,2048]{1,0:T(8,128)(2,1)} fusion(pred[576,256]{1,0:T(8,128)(4,1)S(1)} %fusion.2, bf16[256,2176]{1,0:T(8,128)(2,1)} %all-gather.5.cloned.1.call-done), kind=kOutput, calls=%fused_computation.18 | convolution fusion | flops 605159424 | bytes 3555328 | tf_op jit(solution)/shard_map/dot_general | solution.py:192
  180.1 22.5 %all-to-all-done = bf16[4,144,2048]{2,1,0:T(8,128)(2,1)S(1)} async-done(((bf16[4,144,2048]{2,1,0:T(8,128)(2,1)}), bf16[4,144,2048]{2,1,0:T(8,128)(2,1)S(1)}, u32[]{:S(2)}, u32[]{:S(2)}) %all-to-all-start) | async-done | bytes 2359328 | tf_op jit(solution)/shard_map/all_to_all | solution.py:195
  202.6 4.7 %all-to-all-start.2 = ((bf16[4,144,2048]{2,1,0:T(8,128)(2,1)}), bf16[4,144,2048]{2,1,0:T(8,128)(2,1)}, u32[]{:S(2)}, u32[]{:S(2)}) async-start(bf16[4,144,2048]{2,1,0:T(8,128)(2,1)} %bitcast.26), calls=%async_computation.5 | async-start | bytes 4718592 | tf_op jit(solution)/shard_map/all_to_all | solution.py:195
  209.0 2.3 collective-permute-done.5
  211.2 5.2 %fusion.22 = f32[576,768]{1,0:T(8,128)} fusion(bf16[576,2048]{1,0:T(8,128)(2,1)S(1)} %bitcast.130, bf16[1,2048,384]{2,1,0:T(8,128)(2,1)} %collective-permute-done.3, bf16[1,2048,384]{2,1,0:T(8,128)(2,1)} %param.25), kind=kOutput, calls=%fused_computation.39 | convolution fusion | flops 1818230784 | bytes 7274496 | tf_op jit(solution)/shard_map/dot_general | solution.py:50
  216.4 9.2 %convolution_convert_fusion.1 = bf16[576,2048]{1,0:T(8,128)(2,1)} fusion(bf16[1,2048,384]{2,1,0:T(8,128)(2,1)} %collective-permute-done.5, bf16[1,2048,384]{2,1,0:T(8,128)(2,1)} %param.27, f32[576,768]{1,0:T(8,128)} %fusion.22, bf16[576,2048]{1,0:T(8,128)(2,1)S(1)} %bitcast.131, bf16[1,2048,384]{2,1,0:T(8,128)(2,1)} %collective-permute-done.4, ...), kind=kOutput, calls=%fused_computation.17 | convolution fusion | flops 3640295424 | bytes 12779520 | tf_op jit(solution)/shard_map/rf,df->rd/dot_general | solution.py:53
  225.6 10.1 %all-to-all-done.2 = bf16[4,144,2048]{2,1,0:T(8,128)(2,1)} async-done(((bf16[4,144,2048]{2,1,0:T(8,128)(2,1)}), bf16[4,144,2048]{2,1,0:T(8,128)(2,1)}, u32[]{:S(2)}, u32[]{:S(2)}) %all-to-all-start.2) | async-done | bytes 2359328 | tf_op jit(solution)/shard_map/all_to_all | solution.py:195
  235.7 3.6 %all-to-all-start.1 = ((bf16[4,144,2048]{2,1,0:T(8,128)(2,1)}), bf16[4,144,2048]{2,1,0:T(8,128)(2,1)S(1)}, u32[]{:S(2)}, u32[]{:S(2)}) async-start(bf16[4,144,2048]{2,1,0:T(8,128)(2,1)} %bitcast.133), calls=%async_computation.3 | async-start | bytes 4718592 | tf_op jit(solution)/shard_map/all_to_all | solution.py:202
  240.8 5.9 %fusion.21 = f32[576,768]{1,0:T(8,128)} fusion(bf16[576,2048]{1,0:T(8,128)(2,1)} %bitcast.27, bf16[1,2048,384]{2,1,0:T(8,128)(2,1)} %collective-permute-done.3, bf16[1,2048,384]{2,1,0:T(8,128)(2,1)} %param.25), kind=kOutput, calls=%fused_computation.38 | convolution fusion | flops 1818230784 | bytes 7274496 | tf_op jit(solution)/shard_map/dot_general | solution.py:50
  246.7 9.8 %convolution_convert_fusion = bf16[576,2048]{1,0:T(8,128)(2,1)} fusion(bf16[1,2048,384]{2,1,0:T(8,128)(2,1)} %collective-permute-done.5, bf16[1,2048,384]{2,1,0:T(8,128)(2,1)} %param.27, f32[576,768]{1,0:T(8,128)} %fusion.21, bf16[576,2048]{1,0:T(8,128)(2,1)} %bitcast.27, bf16[1,2048,384]{2,1,0:T(8,128)(2,1)} %collective-permute-done.4, ...), kind=kOutput, calls=%fused_computation.16 | convolution fusion | flops 3640295424 | bytes 12779520 | tf_op jit(solution)/shard_map/rf,df->rd/dot_general | solution.py:53
  256.5 11.3 %all-to-all-done.1 = bf16[4,144,2048]{2,1,0:T(8,128)(2,1)S(1)} async-done(((bf16[4,144,2048]{2,1,0:T(8,128)(2,1)}), bf16[4,144,2048]{2,1,0:T(8,128)(2,1)S(1)}, u32[]{:S(2)}, u32[]{:S(2)}) %all-to-all-start.1) | async-done | bytes 2359328 | tf_op jit(solution)/shard_map/all_to_all | solution.py:202
  269.2 3.6 %all-to-all-start.3 = ((bf16[4,144,2048]{2,1,0:T(8,128)(2,1)}), bf16[4,144,2048]{2,1,0:T(8,128)(2,1)S(1)}, u32[]{:S(2)}, u32[]{:S(2)}) async-start(bf16[4,144,2048]{2,1,0:T(8,128)(2,1)} %bitcast.132), calls=%async_computation.6 | async-start | bytes 4718592 | tf_op jit(solution)/shard_map/all_to_all | solution.py:202
  273.1 3.0 fusion.52
  276.1 2.0 fusion.9
  281.3 20.0 %all-to-all-done.3 = bf16[4,144,2048]{2,1,0:T(8,128)(2,1)S(1)} async-done(((bf16[4,144,2048]{2,1,0:T(8,128)(2,1)}), bf16[4,144,2048]{2,1,0:T(8,128)(2,1)S(1)}, u32[]{:S(2)}, u32[]{:S(2)}) %all-to-all-start.3) | async-done | bytes 2359328 | tf_op jit(solution)/shard_map/all_to_all | solution.py:202
  301.3 2.1 fusion.49
  303.4 2.0 fusion.10
  305.5 27.7 %reduce-scatter.11.cloned.1.call-done = bf16[1,64,2048]{2,1,0:T(8,128)(2,1)} async-done(((bf16[4,64,2048]{2,1,0:T(8,128)(2,1)}), bf16[1,64,2048]{2,1,0:T(8,128)(2,1)}) %reduce-scatter.11.cloned.1.call-update) | async-done | bytes 262160 | tf_op jit(solution)/shard_map/reduce_scatter | solution.py:212
  333.3 1.9 add_convert_fusion
  (108 shorter events, 29.9 us)
Async XLA Ops:
  6.5 200.8 %copy-start = (bf16[2048,16]{0,1:T(8,128)(2,1)S(1)}, bf16[2048,16]{0,1:T(8,128)(2,1)}, u32[]{:S(2)}) copy-start(bf16[2048,16]{0,1:T(8,128)(2,1)} %param.23) | copy-start | bytes 196612
  6.5 63.6 %reduce-scatter.5.cloned.1.call-start = ((), (), s32[]{:S(2)}) async-start(), calls=%async_computation.8 | async-start | bytes 1310720 | tf_op jit(solution)/shard_map/reduce_scatter | solution.py:124
  9.6 10.4 %collective-permute-start = (bf16[2,256,256]{2,1,0:T(8,128)(2,1)S(1)}, bf16[2,256,256]{2,1,0:T(8,128)(2,1)S(1)}, u32[]{:S(2)}, u32[]{:S(2)}) collective-permute-start(bf16[2,256,256]{2,1,0:T(8,128)(2,1)S(1)} %pad_maximum_fusion.1), channel_id=1, source_target_pairs={{0,16},{16,0},{1,17},{17,1},{2,18},{18,2},{3,19},{19,3},{4,20},{20... | collective-permute-start | bytes 786440 | tf_op jit(solution)/shard_map/ppermute | solution.py:43
  12.7 7.2 %collective-permute-start.1 = (s32[2,256]{1,0:T(2,128)}, s32[2,256]{1,0:T(2,128)S(1)}, u32[]{:S(2)}, u32[]{:S(2)}) collective-permute-start(s32[2,256]{1,0:T(2,128)} %param.17), channel_id=1, source_target_pairs={{0,16},{16,0},{1,17},{17,1},{2,18},{18,2},{3,19},{19,3},{4,20},{20... | collective-permute-start | bytes 6152 | tf_op jit(solution)/shard_map/ppermute | solution.py:43
  12.7 51.3 %collective-permute-start.2 = (bf16[1024,1024]{1,0:T(8,128)(2,1)}, bf16[1024,1024]{1,0:T(8,128)(2,1)}, u32[]{:S(2)}, u32[]{:S(2)}) collective-permute-start(bf16[1024,1024]{1,0:T(8,128)(2,1)} %param.20), channel_id=1, source_target_pairs={{0,16},{16,0},{1,17},{17,1},{2,18},{18,2},{3,19},{19,3},{4,20},{20... | collective-permute-start | bytes 6291464 | tf_op jit(solution)/shard_map/ppermute | solution.py:43
  14.7 2.4 copy-start.10
  16.8 3.0 copy-start.8
  16.8 3.2 copy-start.6
  22.4 1.6 copy-start.5
  26.3 41.7 %copy-start.9 = (s32[2,256,8]{1,2,0:T(8,128)S(1)}, s32[2,256,8]{1,2,0:T(8,128)}, u32[]{:S(2)}) copy-start(s32[2,256,8]{1,2,0:T(8,128)} %param.24) | copy-start | bytes 49156
  26.3 41.9 %copy-start.11 = (bf16[1,2048,384]{2,1,0:T(8,128)(2,1)S(1)}, bf16[1,2048,384]{2,1,0:T(8,128)(2,1)}, u32[]{:S(2)}) copy-start(bf16[1,2048,384]{2,1,0:T(8,128)(2,1)} %param.25) | copy-start | bytes 4718596
  26.3 68.1 %reduce-scatter.7.cloned.1.call-start = ((), (), s32[]{:S(2)}) async-start(), calls=%async_computation.9 | async-start | bytes 1310720 | tf_op jit(solution)/shard_map/reduce_scatter | solution.py:124
  67.9 67.2 %all-gather.3.cloned.1.call-start = ((), (), s32[]{:S(2)}) async-start(), calls=%async_computation.10 | async-start | bytes 1392640 | tf_op jit(solution)/shard_map/all_gather | solution.py:161
  68.2 35.8 %collective-permute-start.3 = (bf16[1,2048,384]{2,1,0:T(8,128)(2,1)S(1)}, bf16[1,2048,384]{2,1,0:T(8,128)(2,1)}, u32[]{:S(2)}, u32[]{:S(2)}) collective-permute-start(bf16[1,2048,384]{2,1,0:T(8,128)(2,1)S(1)} %copy-done.11), channel_id=1, source_target_pairs={{0,16},{16,0},{1,17},{17,1},{2,18},{18,2},{3,19},{19,3},{4,20},{20... | collective-permute-start | bytes 4718600 | tf_op jit(solution)/shard_map/ppermute | solution.py:43
  96.0 1.5 copy-start.7
  104.0 1.6 copy-start.12
  104.8 60.3 %all-gather.5.cloned.1.call-start = ((), (), s32[]{:S(2)}) async-start(), calls=%async_computation.12 | async-start | bytes 1392640 | tf_op jit(solution)/shard_map/all_gather | solution.py:161
  105.6 60.7 %collective-permute-start.4 = (bf16[1,2048,384]{2,1,0:T(8,128)(2,1)S(1)}, bf16[1,2048,384]{2,1,0:T(8,128)(2,1)}, u32[]{:S(2)}, u32[]{:S(2)}) collective-permute-start(bf16[1,2048,384]{2,1,0:T(8,128)(2,1)S(1)} %copy-done.12), channel_id=1, source_target_pairs={{0,16},{16,0},{1,17},{17,1},{2,18},{18,2},{3,19},{19,3},{4,20},{20... | collective-permute-start | bytes 4718600 | tf_op jit(solution)/shard_map/ppermute | solution.py:43
  170.5 32.1 %all-to-all-start = ((bf16[4,144,2048]{2,1,0:T(8,128)(2,1)}), bf16[4,144,2048]{2,1,0:T(8,128)(2,1)S(1)}, u32[]{:S(2)}, u32[]{:S(2)}) async-start(bf16[4,144,2048]{2,1,0:T(8,128)(2,1)} %bitcast.15), calls=%async_computation.2 | async-start | bytes 4718592 | tf_op jit(solution)/shard_map/all_to_all | solution.py:195
  174.1 37.1 %collective-permute-start.5 = (bf16[1,2048,384]{2,1,0:T(8,128)(2,1)}, bf16[1,2048,384]{2,1,0:T(8,128)(2,1)}, u32[]{:S(2)}, u32[]{:S(2)}) collective-permute-start(bf16[1,2048,384]{2,1,0:T(8,128)(2,1)} %param.27), channel_id=1, source_target_pairs={{0,16},{16,0},{1,17},{17,1},{2,18},{18,2},{3,19},{19,3},{4,20},{20... | collective-permute-start | bytes 4718600 | tf_op jit(solution)/shard_map/ppermute | solution.py:43
  202.6 33.1 %all-to-all-start.2 = ((bf16[4,144,2048]{2,1,0:T(8,128)(2,1)}), bf16[4,144,2048]{2,1,0:T(8,128)(2,1)}, u32[]{:S(2)}, u32[]{:S(2)}) async-start(bf16[4,144,2048]{2,1,0:T(8,128)(2,1)} %bitcast.26), calls=%async_computation.5 | async-start | bytes 4718592 | tf_op jit(solution)/shard_map/all_to_all | solution.py:195
  235.7 32.1 %all-to-all-start.1 = ((bf16[4,144,2048]{2,1,0:T(8,128)(2,1)}), bf16[4,144,2048]{2,1,0:T(8,128)(2,1)S(1)}, u32[]{:S(2)}, u32[]{:S(2)}) async-start(bf16[4,144,2048]{2,1,0:T(8,128)(2,1)} %bitcast.133), calls=%async_computation.3 | async-start | bytes 4718592 | tf_op jit(solution)/shard_map/all_to_all | solution.py:202
  267.8 1.4 copy-start.1
  269.2 32.1 %all-to-all-start.3 = ((bf16[4,144,2048]{2,1,0:T(8,128)(2,1)}), bf16[4,144,2048]{2,1,0:T(8,128)(2,1)S(1)}, u32[]{:S(2)}, u32[]{:S(2)}) async-start(bf16[4,144,2048]{2,1,0:T(8,128)(2,1)} %bitcast.132), calls=%async_computation.6 | async-start | bytes 4718592 | tf_op jit(solution)/shard_map/all_to_all | solution.py:202
  272.8 32.7 %reduce-scatter.9.cloned.1.call-start = ((), (), s32[]{:S(2)}) async-start(), calls=%async_computation.11 | async-start | bytes 1310720 | tf_op jit(solution)/shard_map/reduce_scatter | solution.py:212
  273.1 3.0 copy-start.2
  273.1 3.0 copy-start.3
  278.1 55.1 %reduce-scatter.11.cloned.1.call-start = ((), (), s32[]{:S(2)}) async-start(), calls=%async_computation.13 | async-start | bytes 1310720 | tf_op jit(solution)/shard_map/reduce_scatter | solution.py:212
  301.3 2.1 copy-start.4
Sparse Core Ops, SparseCore 0:
  26.4 26.6 reduce-scatter.4
  68.0 26.3 reduce-scatter.6
  104.9 30.1 all-gather.2
  136.5 28.4 all-gather.4
  278.2 26.8 reduce-scatter.8
  307.4 25.8 reduce-scatter.10

commit v7 on v6

--- a/solution.py
+++ b/solution.py
@@ -157,6 +157,8 @@
     for chunk in range(packs):
         rows = normed[chunk * share : (chunk + 1) * share]
         ids = local_ids[chunk * share : (chunk + 1) * share]
+        if chunk > 0:
+            rows, ids, _ = lax.optimization_barrier((rows, ids, buffer))
         id_lanes = jnp.pad(ids.astype(jnp.bfloat16), ((0, 0), (0, lanes - top_count)))
         rows_all = lax.all_gather(
             jnp.concatenate([rows, id_lanes], axis=1), "ep", axis=0, tiled=True

time: 343 us -> 320 us (0.933)
  waiting for transfers between devices: 221 us -> 199 us
    all_to_all x2, waiting for transfers between devices: 32.5 us -> 12.3 us  [shards(): lax.all_to_all(buffer.reshape(n_tp, cap2, width), 'tp', split_axis=0, con...]
  transfers between devices with their start and end apart: 16 -> 16, of which waited for: 12 -> 11; matrix products, arithmetic and copies ran while one was open for 20% -> 21% of each run, Pallas kernels for 0% -> 0%
where the time goes in v7:
time: 320 us
  waiting for transfers between devices  199 us (62%)
  matrix products  59.4 us (19%)
  starting transfers between devices  25.5 us (8%)
  other arithmetic  15.9 us (5%)
  between operations  14 us (4%)
  local copies, waits for them, and re-layouts  5.48 us (2%)
    all_gather x2, waiting for transfers between devices, shards(): lax.all_gather(jnp.concatenate([rows, id_lanes], axis=1), 'ep', axis=0, t...  53.9 us
    ppermute x6, waiting for transfers between devices, cp_pieces(): pieces.append(lax.ppermute(x, 'cp', perm))  49.5 us
    all_to_all x2, waiting for transfers between devices, shards(): lax.all_to_all(served, 'tp', split_axis=0, concat_axis=0, tiled=True)  31.3 us
    reduce_scatter x2, waiting for transfers between devices, shards(): lax.psum_scatter(partial.astype(jnp.bfloat16).reshape(n_ep, share, width)...  27.8 us
    reduce_scatter x2, waiting for transfers between devices, shards(): lax.psum_scatter(block.astype(jnp.bfloat16), 'tp', scatter_dimension=1, t...  24.4 us
    dot_general x2, matrix products, expert_rows(): jnp.einsum('rf,df->rd', hidden_act, full_down[0], preferred_element_type=...  19 us
    all_to_all x2, waiting for transfers between devices, shards(): lax.all_to_all(buffer.reshape(n_tp, cap2, width), 'tp', split_axis=0, con...  12.3 us
    dot_general x2, matrix products, expert_rows(): jnp.dot(flat_rows, full_gate[0], preferred_element_type=jnp.float32)  11 us
  transfers between devices with their start and end apart: 16, of which 11 were waited for; matrix products, arithmetic and copies ran while one was open for 21% of the time, Pallas kernels for 0%

profile of v7, /device:TPU:0, one launch (start us, length us, event | category | flops | bytes accessed | tf_op | source)
XLA Modules:
  0.0 319.6 jit_solution(3185376150049281821)
XLA Ops:
  9.6 3.0 collective-permute-start
  12.7 1.9 collective-permute-start.2
  17.8 2.0 collective-permute-done.1
  20.1 2.2 fusion
  24.0 2.3 fusion.25
  26.3 37.7 %collective-permute-done.2 = bf16[1024,1024]{1,0:T(8,128)(2,1)} collective-permute-done((bf16[1024,1024]{1,0:T(8,128)(2,1)}, bf16[1024,1024]{1,0:T(8,128)(2,1)}, u32[]{:S(2)}, u32[]{:S(2)}) %collective-permute-start.2) | collective-permute-done | bytes 2097184 | tf_op jit(solution)/shard_map/ppermute | solution.py:43
  64.1 3.8 %fusion.28 = bf16[2,256,1024]{2,1,0:T(8,128)(2,1)} fusion(bf16[2,256,1024]{1,2,0:T(8,128)(2,1)S(1)} %bitcast.128, bf16[1024,1024]{1,0:T(8,128)(2,1)} %collective-permute-done.2), kind=kOutput, calls=%fused_computation.43 | convolution fusion | flops 1074266112 | bytes 4194304 | tf_op jit(solution)/shard_map/dot_general | solution.py:120
  68.2 1.8 collective-permute-start.3
  70.1 24.4 %reduce-scatter.7.cloned.1.call-done = bf16[2,64,1024]{2,1,0:T(8,128)(2,1)} async-done(((bf16[2,256,1024]{2,1,0:T(8,128)(2,1)}), bf16[2,64,1024]{2,1,0:T(8,128)(2,1)}) %reduce-scatter.7.cloned.1.call-update) | async-done | bytes 262160 | tf_op jit(solution)/shard_map/reduce_scatter | solution.py:124
  97.6 6.4 %collective-permute-done.3 = bf16[1,2048,384]{2,1,0:T(8,128)(2,1)} collective-permute-done((bf16[1,2048,384]{2,1,0:T(8,128)(2,1)S(1)}, bf16[1,2048,384]{2,1,0:T(8,128)(2,1)}, u32[]{:S(2)}, u32[]{:S(2)}) %collective-permute-start.3) | collective-permute-done | bytes 1572896 | tf_op jit(solution)/shard_map/ppermute | solution.py:43
  106.3 28.7 %all-gather.3.cloned.1.call-done = bf16[256,2176]{1,0:T(8,128)(2,1)} async-done(((bf16[64,2176]{1,0:T(8,128)(2,1)}), bf16[256,2176]{1,0:T(8,128)(2,1)}) %all-gather.3.cloned.1.call-update) | async-done | bytes 1114128 | tf_op jit(solution)/shard_map/all_gather | solution.py:163
  136.3 3.4 %collective-permute-done.4 = bf16[1,2048,384]{2,1,0:T(8,128)(2,1)S(1)} collective-permute-done((bf16[1,2048,384]{2,1,0:T(8,128)(2,1)}, bf16[1,2048,384]{2,1,0:T(8,128)(2,1)S(1)}, u32[]{:S(2)}, u32[]{:S(2)}) %collective-permute-start.4) | collective-permute-done | bytes 1572896 | tf_op jit(solution)/shard_map/ppermute | solution.py:43
  140.5 3.4 %convolution_convert_fusion.3 = bf16[576,2048]{1,0:T(8,128)(2,1)} fusion(pred[576,256]{1,0:T(8,128)(4,1)S(1)} %fusion.3, bf16[256,2176]{1,0:T(8,128)(2,1)} %all-gather.3.cloned.1.call-done), kind=kOutput, calls=%fused_computation.19 | convolution fusion | flops 605159424 | bytes 3555328 | tf_op jit(solution)/shard_map/dot_general | solution.py:194
  144.7 3.6 %all-to-all-start = ((bf16[4,144,2048]{2,1,0:T(8,128)(2,1)}), bf16[4,144,2048]{2,1,0:T(8,128)(2,1)S(1)}, u32[]{:S(2)}, u32[]{:S(2)}) async-start(bf16[4,144,2048]{2,1,0:T(8,128)(2,1)} %bitcast.15), calls=%async_computation.2 | async-start | bytes 4718592 | tf_op jit(solution)/shard_map/all_to_all | solution.py:197
  149.5 25.2 %all-gather.5.cloned.1.call-done = bf16[256,2176]{1,0:T(8,128)(2,1)} async-done(((bf16[64,2176]{1,0:T(8,128)(2,1)}), bf16[256,2176]{1,0:T(8,128)(2,1)}) %all-gather.5.cloned.1.call-update) | async-done | bytes 1114128 | tf_op jit(solution)/shard_map/all_gather | solution.py:163
  176.7 3.4 %convolution_convert_fusion.2 = bf16[576,2048]{1,0:T(8,128)(2,1)} fusion(pred[576,256]{1,0:T(8,128)(4,1)S(1)} %fusion.2, bf16[256,2176]{1,0:T(8,128)(2,1)} %all-gather.5.cloned.1.call-done), kind=kOutput, calls=%fused_computation.18 | convolution fusion | flops 605159424 | bytes 3555328 | tf_op jit(solution)/shard_map/dot_general | solution.py:194
  180.1 4.7 %all-to-all-start.2 = ((bf16[4,144,2048]{2,1,0:T(8,128)(2,1)}), bf16[4,144,2048]{2,1,0:T(8,128)(2,1)}, u32[]{:S(2)}, u32[]{:S(2)}) async-start(bf16[4,144,2048]{2,1,0:T(8,128)(2,1)} %bitcast.26), calls=%async_computation.5 | async-start | bytes 4718592 | tf_op jit(solution)/shard_map/all_to_all | solution.py:197
  186.5 5.2 %fusion.22 = f32[576,768]{1,0:T(8,128)} fusion(bf16[576,2048]{1,0:T(8,128)(2,1)S(1)} %bitcast.129, bf16[1,2048,384]{2,1,0:T(8,128)(2,1)} %collective-permute-done.3, bf16[1,2048,384]{2,1,0:T(8,128)(2,1)} %param.25), kind=kOutput, calls=%fused_computation.39 | convolution fusion | flops 1818230784 | bytes 7274496 | tf_op jit(solution)/shard_map/dot_general | solution.py:50
  191.7 9.2 %convolution_convert_fusion.1 = bf16[576,2048]{1,0:T(8,128)(2,1)} fusion(bf16[1,2048,384]{2,1,0:T(8,128)(2,1)} %collective-permute-done.5, bf16[1,2048,384]{2,1,0:T(8,128)(2,1)} %param.27, f32[576,768]{1,0:T(8,128)} %fusion.22, bf16[576,2048]{1,0:T(8,128)(2,1)S(1)} %bitcast.130, bf16[1,2048,384]{2,1,0:T(8,128)(2,1)} %copy-done.12, ...), kind=kOutput, calls=%fused_computation.17 | convolution fusion | flops 3640295424 | bytes 12779520 | tf_op jit(solution)/shard_map/rf,df->rd/dot_general | solution.py:53
  200.9 12.3 %all-to-all-done.2 = bf16[4,144,2048]{2,1,0:T(8,128)(2,1)} async-done(((bf16[4,144,2048]{2,1,0:T(8,128)(2,1)}), bf16[4,144,2048]{2,1,0:T(8,128)(2,1)}, u32[]{:S(2)}, u32[]{:S(2)}) %all-to-all-start.2) | async-done | bytes 2359328 | tf_op jit(solution)/shard_map/all_to_all | solution.py:197
  213.2 3.6 %all-to-all-start.1 = ((bf16[4,144,2048]{2,1,0:T(8,128)(2,1)}), bf16[4,144,2048]{2,1,0:T(8,128)(2,1)S(1)}, u32[]{:S(2)}, u32[]{:S(2)}) async-start(bf16[4,144,2048]{2,1,0:T(8,128)(2,1)} %bitcast.132), calls=%async_computation.3 | async-start | bytes 4718592 | tf_op jit(solution)/shard_map/all_to_all | solution.py:204
  218.3 5.9 %fusion.21 = f32[576,768]{1,0:T(8,128)} fusion(bf16[576,2048]{1,0:T(8,128)(2,1)} %bitcast.27, bf16[1,2048,384]{2,1,0:T(8,128)(2,1)} %collective-permute-done.3, bf16[1,2048,384]{2,1,0:T(8,128)(2,1)} %param.25), kind=kOutput, calls=%fused_computation.38 | convolution fusion | flops 1818230784 | bytes 7274496 | tf_op jit(solution)/shard_map/dot_general | solution.py:50
  224.2 9.8 %convolution_convert_fusion = bf16[576,2048]{1,0:T(8,128)(2,1)} fusion(bf16[1,2048,384]{2,1,0:T(8,128)(2,1)} %collective-permute-done.5, bf16[1,2048,384]{2,1,0:T(8,128)(2,1)} %param.27, f32[576,768]{1,0:T(8,128)} %fusion.21, bf16[576,2048]{1,0:T(8,128)(2,1)} %bitcast.27, bf16[1,2048,384]{2,1,0:T(8,128)(2,1)} %copy-done.12, bf16[1,2048,384]{2,1,0:T(8,128)(2,1)} %param.26), kind=kOutput, calls=%fused_computation.16 | convolution fusion | flops 3640295424 | bytes 12779520 | tf_op jit(solution)/shard_map/rf,df->rd/dot_general | solution.py:53
  234.0 11.3 %all-to-all-done.1 = bf16[4,144,2048]{2,1,0:T(8,128)(2,1)S(1)} async-done(((bf16[4,144,2048]{2,1,0:T(8,128)(2,1)}), bf16[4,144,2048]{2,1,0:T(8,128)(2,1)S(1)}, u32[]{:S(2)}, u32[]{:S(2)}) %all-to-all-start.1) | async-done | bytes 2359328 | tf_op jit(solution)/shard_map/all_to_all | solution.py:204
  246.7 3.6 %all-to-all-start.3 = ((bf16[4,144,2048]{2,1,0:T(8,128)(2,1)}), bf16[4,144,2048]{2,1,0:T(8,128)(2,1)S(1)}, u32[]{:S(2)}, u32[]{:S(2)}) async-start(bf16[4,144,2048]{2,1,0:T(8,128)(2,1)} %bitcast.131), calls=%async_computation.6 | async-start | bytes 4718592 | tf_op jit(solution)/shard_map/all_to_all | solution.py:204
  250.7 3.0 fusion.52
  253.7 2.0 fusion.9
  258.8 20.0 %all-to-all-done.3 = bf16[4,144,2048]{2,1,0:T(8,128)(2,1)S(1)} async-done(((bf16[4,144,2048]{2,1,0:T(8,128)(2,1)}), bf16[4,144,2048]{2,1,0:T(8,128)(2,1)S(1)}, u32[]{:S(2)}, u32[]{:S(2)}) %all-to-all-start.3) | async-done | bytes 2359328 | tf_op jit(solution)/shard_map/all_to_all | solution.py:204
  278.8 2.1 fusion.49
  281.0 2.0 fusion.10
  283.1 27.7 %reduce-scatter.11.cloned.1.call-done = bf16[1,64,2048]{2,1,0:T(8,128)(2,1)} async-done(((bf16[4,64,2048]{2,1,0:T(8,128)(2,1)}), bf16[1,64,2048]{2,1,0:T(8,128)(2,1)}) %reduce-scatter.11.cloned.1.call-update) | async-done | bytes 262160 | tf_op jit(solution)/shard_map/reduce_scatter | solution.py:214
  310.8 1.9 add_convert_fusion
  (111 shorter events, 27.9 us)
Async XLA Ops:
  6.5 178.3 %copy-start = (bf16[2048,16]{0,1:T(8,128)(2,1)S(1)}, bf16[2048,16]{0,1:T(8,128)(2,1)}, u32[]{:S(2)}) copy-start(bf16[2048,16]{0,1:T(8,128)(2,1)} %param.23) | copy-start | bytes 196612
  6.5 63.5 %reduce-scatter.5.cloned.1.call-start = ((), (), s32[]{:S(2)}) async-start(), calls=%async_computation.8 | async-start | bytes 1310720 | tf_op jit(solution)/shard_map/reduce_scatter | solution.py:124
  9.6 10.4 %collective-permute-start = (bf16[2,256,256]{2,1,0:T(8,128)(2,1)S(1)}, bf16[2,256,256]{2,1,0:T(8,128)(2,1)S(1)}, u32[]{:S(2)}, u32[]{:S(2)}) collective-permute-start(bf16[2,256,256]{2,1,0:T(8,128)(2,1)S(1)} %pad_maximum_fusion.1), channel_id=1, source_target_pairs={{0,16},{16,0},{1,17},{17,1},{2,18},{18,2},{3,19},{19,3},{4,20},{20... | collective-permute-start | bytes 786440 | tf_op jit(solution)/shard_map/ppermute | solution.py:43
  12.7 7.2 %collective-permute-start.1 = (s32[2,256]{1,0:T(2,128)}, s32[2,256]{1,0:T(2,128)S(1)}, u32[]{:S(2)}, u32[]{:S(2)}) collective-permute-start(s32[2,256]{1,0:T(2,128)} %param.17), channel_id=1, source_target_pairs={{0,16},{16,0},{1,17},{17,1},{2,18},{18,2},{3,19},{19,3},{4,20},{20... | collective-permute-start | bytes 6152 | tf_op jit(solution)/shard_map/ppermute | solution.py:43
  12.7 51.3 %collective-permute-start.2 = (bf16[1024,1024]{1,0:T(8,128)(2,1)}, bf16[1024,1024]{1,0:T(8,128)(2,1)}, u32[]{:S(2)}, u32[]{:S(2)}) collective-permute-start(bf16[1024,1024]{1,0:T(8,128)(2,1)} %param.20), channel_id=1, source_target_pairs={{0,16},{16,0},{1,17},{17,1},{2,18},{18,2},{3,19},{19,3},{4,20},{20... | collective-permute-start | bytes 6291464 | tf_op jit(solution)/shard_map/ppermute | solution.py:43
  14.7 2.4 copy-start.10
  16.8 3.0 copy-start.8
  16.8 3.2 %copy-start.6 = (bf16[2,256,128]{2,1,0:T(8,128)(2,1)S(1)}, bf16[2,256,128]{2,1,0:T(8,128)(2,1)}, u32[]{:S(2)}) copy-start(bf16[2,256,128]{2,1,0:T(8,128)(2,1)} %param.16) | copy-start | bytes 393220
  22.4 1.6 copy-start.5
  26.3 41.7 %copy-start.9 = (s32[2,256,8]{1,2,0:T(8,128)S(1)}, s32[2,256,8]{1,2,0:T(8,128)}, u32[]{:S(2)}) copy-start(s32[2,256,8]{1,2,0:T(8,128)} %param.24) | copy-start | bytes 49156
  26.3 41.9 %copy-start.11 = (bf16[1,2048,384]{2,1,0:T(8,128)(2,1)S(1)}, bf16[1,2048,384]{2,1,0:T(8,128)(2,1)}, u32[]{:S(2)}) copy-start(bf16[1,2048,384]{2,1,0:T(8,128)(2,1)} %param.25) | copy-start | bytes 4718596
  26.3 68.1 %reduce-scatter.7.cloned.1.call-start = ((), (), s32[]{:S(2)}) async-start(), calls=%async_computation.9 | async-start | bytes 1310720 | tf_op jit(solution)/shard_map/reduce_scatter | solution.py:124
  67.9 67.1 %all-gather.3.cloned.1.call-start = ((), (), s32[]{:S(2)}) async-start(), calls=%async_computation.10 | async-start | bytes 1392640 | tf_op jit(solution)/shard_map/all_gather | solution.py:163
  68.2 35.8 %collective-permute-start.3 = (bf16[1,2048,384]{2,1,0:T(8,128)(2,1)S(1)}, bf16[1,2048,384]{2,1,0:T(8,128)(2,1)}, u32[]{:S(2)}, u32[]{:S(2)}) collective-permute-start(bf16[1,2048,384]{2,1,0:T(8,128)(2,1)S(1)} %copy-done.11), channel_id=1, source_target_pairs={{0,16},{16,0},{1,17},{17,1},{2,18},{18,2},{3,19},{19,3},{4,20},{20... | collective-permute-start | bytes 4718600 | tf_op jit(solution)/shard_map/ppermute | solution.py:43
  96.0 1.5 copy-start.7
  104.7 70.0 %all-gather.5.cloned.1.call-start = ((), (), s32[]{:S(2)}) async-start(), calls=%async_computation.12 | async-start | bytes 1392640 | tf_op jit(solution)/shard_map/all_gather | solution.py:163
  104.8 34.9 %collective-permute-start.4 = (bf16[1,2048,384]{2,1,0:T(8,128)(2,1)}, bf16[1,2048,384]{2,1,0:T(8,128)(2,1)S(1)}, u32[]{:S(2)}, u32[]{:S(2)}) collective-permute-start(bf16[1,2048,384]{2,1,0:T(8,128)(2,1)} %param.26), channel_id=1, source_target_pairs={{0,16},{16,0},{1,17},{17,1},{2,18},{18,2},{3,19},{19,3},{4,20},{20... | collective-permute-start | bytes 4718600 | tf_op jit(solution)/shard_map/ppermute | solution.py:43
  139.7 5.0 %copy-start.12 = (bf16[1,2048,384]{2,1,0:T(8,128)(2,1)}, bf16[1,2048,384]{2,1,0:T(8,128)(2,1)S(1)}, u32[]{:S(2)}) copy-start(bf16[1,2048,384]{2,1,0:T(8,128)(2,1)S(1)} %collective-permute-done.4) | copy-start | bytes 4718596
  144.7 35.5 %all-to-all-start = ((bf16[4,144,2048]{2,1,0:T(8,128)(2,1)}), bf16[4,144,2048]{2,1,0:T(8,128)(2,1)S(1)}, u32[]{:S(2)}, u32[]{:S(2)}) async-start(bf16[4,144,2048]{2,1,0:T(8,128)(2,1)} %bitcast.15), calls=%async_computation.2 | async-start | bytes 4718592 | tf_op jit(solution)/shard_map/all_to_all | solution.py:197
  148.3 38.2 %collective-permute-start.5 = (bf16[1,2048,384]{2,1,0:T(8,128)(2,1)}, bf16[1,2048,384]{2,1,0:T(8,128)(2,1)}, u32[]{:S(2)}, u32[]{:S(2)}) collective-permute-start(bf16[1,2048,384]{2,1,0:T(8,128)(2,1)} %param.27), channel_id=1, source_target_pairs={{0,16},{16,0},{1,17},{17,1},{2,18},{18,2},{3,19},{19,3},{4,20},{20... | collective-permute-start | bytes 4718600 | tf_op jit(solution)/shard_map/ppermute | solution.py:43
  180.1 33.1 %all-to-all-start.2 = ((bf16[4,144,2048]{2,1,0:T(8,128)(2,1)}), bf16[4,144,2048]{2,1,0:T(8,128)(2,1)}, u32[]{:S(2)}, u32[]{:S(2)}) async-start(bf16[4,144,2048]{2,1,0:T(8,128)(2,1)} %bitcast.26), calls=%async_computation.5 | async-start | bytes 4718592 | tf_op jit(solution)/shard_map/all_to_all | solution.py:197
  213.2 32.1 %all-to-all-start.1 = ((bf16[4,144,2048]{2,1,0:T(8,128)(2,1)}), bf16[4,144,2048]{2,1,0:T(8,128)(2,1)S(1)}, u32[]{:S(2)}, u32[]{:S(2)}) async-start(bf16[4,144,2048]{2,1,0:T(8,128)(2,1)} %bitcast.132), calls=%async_computation.3 | async-start | bytes 4718592 | tf_op jit(solution)/shard_map/all_to_all | solution.py:204
  245.3 1.4 copy-start.1
  246.7 32.1 %all-to-all-start.3 = ((bf16[4,144,2048]{2,1,0:T(8,128)(2,1)}), bf16[4,144,2048]{2,1,0:T(8,128)(2,1)S(1)}, u32[]{:S(2)}, u32[]{:S(2)}) async-start(bf16[4,144,2048]{2,1,0:T(8,128)(2,1)} %bitcast.131), calls=%async_computation.6 | async-start | bytes 4718592 | tf_op jit(solution)/shard_map/all_to_all | solution.py:204
  250.4 32.7 %reduce-scatter.9.cloned.1.call-start = ((), (), s32[]{:S(2)}) async-start(), calls=%async_computation.11 | async-start | bytes 1310720 | tf_op jit(solution)/shard_map/reduce_scatter | solution.py:214
  250.6 3.0 copy-start.2
  250.6 3.0 copy-start.3
  255.7 55.1 %reduce-scatter.11.cloned.1.call-start = ((), (), s32[]{:S(2)}) async-start(), calls=%async_computation.13 | async-start | bytes 1310720 | tf_op jit(solution)/shard_map/reduce_scatter | solution.py:214
  278.8 2.1 copy-start.4
Sparse Core Ops, SparseCore 0:
  26.4 26.6 reduce-scatter.4
  68.0 26.3 reduce-scatter.6
  104.8 30.1 all-gather.2
  144.8 29.8 all-gather.4
  255.8 26.8 reduce-scatter.8
  284.9 25.8 reduce-scatter.10

commit v8 on v7

--- a/solution.py
+++ b/solution.py
@@ -42,6 +42,13 @@
         perm = [(i, (i + shift) % n_cp) for i in range(n_cp)]
         pieces.append(lax.ppermute(x, "cp", perm))
     return pieces
+
+
+def sum_scatter(x, axis, size, dim):
+    shape = x.shape
+    parts = x.reshape(shape[:dim] + (size, shape[dim] // size) + shape[dim + 1 :])
+    arrived = lax.all_to_all(parts, axis, split_axis=dim, concat_axis=dim, tiled=True)
+    return jnp.sum(arrived.astype(jnp.float32), axis=dim)
 
 
 def expert_rows(received, full_gate, full_up, full_down):
@@ -116,13 +123,16 @@
     cap = capacity(share, top_count, experts)
     weight_pieces = cp_pieces(out_weight, n_cp)
     summed_blocks = []
-    for piece in weight_pieces:
+    for j, piece in enumerate(weight_pieces):
         block = jnp.dot(attn, piece, preferred_element_type=jnp.float32).reshape(
             packs, row_count, piece.shape[1]
         )
-        summed_blocks.append(
-            lax.psum_scatter(block.astype(jnp.bfloat16), "tp", scatter_dimension=1, tiled=True)
-        )
+        if j == 0:
+            summed_blocks.append(
+                lax.psum_scatter(block.astype(jnp.bfloat16), "tp", scatter_dimension=1, tiled=True)
+            )
+        else:
+            summed_blocks.append(sum_scatter(block.astype(jnp.bfloat16), "tp", n_tp, 1))
     blocks = jnp.stack(summed_blocks, axis=2).astype(jnp.float32)
     source_block = (cp_index - jnp.arange(n_cp, dtype=jnp.int32)) % n_cp
     picks_block = source_block[:, None] == jnp.arange(n_cp, dtype=jnp.int32)[None, :]
@@ -210,14 +220,15 @@
         partial = lax.dot_general(
             weight_hi, back, contract, preferred_element_type=jnp.float32
         ) + lax.dot_general(weight_lo, back, contract, preferred_element_type=jnp.float32)
-        mixtures.append(
-            lax.psum_scatter(
-                partial.astype(jnp.bfloat16).reshape(n_ep, share, width),
-                "ep",
-                scatter_dimension=0,
-                tiled=True,
+        partial = partial.astype(jnp.bfloat16).reshape(n_ep, share, width)
+        if chunk < packs - 1:
+            mixtures.append(
+                lax.psum_scatter(partial, "ep", scatter_dimension=0, tiled=True).astype(
+                    jnp.float32
+                )
             )
-        )
+        else:
+            mixtures.append(sum_scatter(partial, "ep", n_ep, 0))
     mixture = jnp.concatenate(mixtures, axis=0).astype(jnp.float32)
     layer_out = (state + mixture).astype(jnp.bfloat16)
     return layer_out

time: 320 us -> 329 us (1.028)
  starting transfers between devices: 25.5 us -> 34.4 us
    all_to_all x0 -> x2, waiting for transfers between devices: none -> 36.2 us  [sum_scatter(): lax.all_to_all(parts, axis, split_axis=dim, concat_axis=dim, tiled=True)]
    reduce_scatter x2 -> x1, waiting for transfers between devices: 27.8 us -> 0.02 us  [shards(): lax.psum_scatter(partial, 'ep', scatter_dimension=0, tiled=True)]
    reduce_scatter x2 -> x1, waiting for transfers between devices: 24.4 us -> 0.01 us  [shards(): lax.psum_scatter(block.astype(jnp.bfloat16), 'tp', scatter_dimension=1, t...]
    ppermute x6, waiting for transfers between devices: 49.5 us -> 64.3 us  [cp_pieces(): pieces.append(lax.ppermute(x, 'cp', perm))]
    all_to_all x0 -> x2, starting transfers between devices: none -> 7.03 us  [sum_scatter(): lax.all_to_all(parts, axis, split_axis=dim, concat_axis=dim, tiled=True)]
where the time goes in v8:
time: 329 us; the launch traced here: 328 us
  waiting for transfers between devices  201 us (61%)
  matrix products  58.9 us (18%)
  starting transfers between devices  34.4 us (10%)
  other arithmetic  15.7 us (5%)
  between operations  13.6 us (4%)
  local copies, waits for them, and re-layouts  5.14 us (2%)
    ppermute x6, waiting for transfers between devices, cp_pieces(): pieces.append(lax.ppermute(x, 'cp', perm))  64.3 us
    all_gather x2, waiting for transfers between devices, shards(): lax.all_gather(jnp.concatenate([rows, id_lanes], axis=1), 'ep', axis=0, t...  53.3 us
    all_to_all x2, waiting for transfers between devices, sum_scatter(): lax.all_to_all(parts, axis, split_axis=dim, concat_axis=dim, tiled=True)  36.2 us
    all_to_all x2, waiting for transfers between devices, shards(): lax.all_to_all(served, 'tp', split_axis=0, concat_axis=0, tiled=True)  34.2 us
    dot_general x2, matrix products, expert_rows(): jnp.einsum('rf,df->rd', hidden_act, full_down[0], preferred_element_type=...  19 us
    all_to_all x2, waiting for transfers between devices, shards(): lax.all_to_all(buffer.reshape(n_tp, cap2, width), 'tp', split_axis=0, con...  12.4 us
    dot_general x2, matrix products, expert_rows(): jnp.dot(flat_rows, full_gate[0], preferred_element_type=jnp.float32)  11 us
    ppermute x6, starting transfers between devices, cp_pieces(): pieces.append(lax.ppermute(x, 'cp', perm))  10.5 us
  transfers between devices with their start and end apart: 16, of which 11 were waited for; matrix products, arithmetic and copies ran while one was open for 21% of the time, Pallas kernels for 0%

profile of v8, /device:TPU:0, one launch (start us, length us, event | category | flops | bytes accessed | tf_op | source)
XLA Modules:
  0.0 328.3 jit_solution(15999448799461664594)
XLA Ops:
  9.6 3.0 collective-permute-start
  12.7 1.9 collective-permute-start.2
  17.8 2.0 collective-permute-done.1
  20.1 2.2 fusion
  24.0 2.3 fusion.25
  26.5 37.6 %collective-permute-done.2 = bf16[1024,1024]{1,0:T(8,128)(2,1)} collective-permute-done((bf16[1024,1024]{1,0:T(8,128)(2,1)}, bf16[1024,1024]{1,0:T(8,128)(2,1)}, u32[]{:S(2)}, u32[]{:S(2)}) %collective-permute-start.2) | collective-permute-done | bytes 2097184 | tf_op jit(solution)/shard_map/ppermute | solution.py:43
  64.1 2.9 fusion.28
  68.0 3.5 %all-to-all-start = ((bf16[2,4,64,1024]{3,2,0,1:T(8,128)(2,1)}), bf16[2,4,64,1024]{3,2,0,1:T(8,128)(2,1)S(1)}, u32[]{:S(2)}, u32[]{:S(2)}) async-start(bf16[2,4,64,1024]{3,2,0,1:T(8,128)(2,1)} %copy.97), calls=%async_computation.1 | async-start | bytes 2097152 | tf_op jit(solution)/shard_map/all_to_all | solution.py:50
  71.6 1.8 collective-permute-start.3
  74.5 11.5 %all-to-all-done = bf16[2,4,64,1024]{3,2,0,1:T(8,128)(2,1)S(1)} async-done(((bf16[2,4,64,1024]{3,2,0,1:T(8,128)(2,1)}), bf16[2,4,64,1024]{3,2,0,1:T(8,128)(2,1)S(1)}, u32[]{:S(2)}, u32[]{:S(2)}) %all-to-all-start) | async-done | bytes 1048608 | tf_op jit(solution)/shard_map/all_to_all | solution.py:50
  88.0 20.5 %collective-permute-done.3 = bf16[1,2048,384]{2,1,0:T(8,128)(2,1)} collective-permute-done((bf16[1,2048,384]{2,1,0:T(8,128)(2,1)S(1)}, bf16[1,2048,384]{2,1,0:T(8,128)(2,1)}, u32[]{:S(2)}, u32[]{:S(2)}) %collective-permute-start.3) | collective-permute-done | bytes 1572896 | tf_op jit(solution)/shard_map/ppermute | solution.py:43
  111.2 28.9 %all-gather.3.cloned.1.call-done = bf16[256,2176]{1,0:T(8,128)(2,1)} async-done(((bf16[64,2176]{1,0:T(8,128)(2,1)}), bf16[256,2176]{1,0:T(8,128)(2,1)}) %all-gather.3.cloned.1.call-update) | async-done | bytes 1114128 | tf_op jit(solution)/shard_map/all_gather | solution.py:173
  141.3 4.2 %collective-permute-done.4 = bf16[1,2048,384]{2,1,0:T(8,128)(2,1)S(1)} collective-permute-done((bf16[1,2048,384]{2,1,0:T(8,128)(2,1)}, bf16[1,2048,384]{2,1,0:T(8,128)(2,1)S(1)}, u32[]{:S(2)}, u32[]{:S(2)}) %collective-permute-start.4) | collective-permute-done | bytes 1572896 | tf_op jit(solution)/shard_map/ppermute | solution.py:43
  146.4 3.4 %convolution_convert_fusion.3 = bf16[576,2048]{1,0:T(8,128)(2,1)} fusion(pred[576,256]{1,0:T(8,128)(4,1)S(1)} %fusion.3, bf16[256,2176]{1,0:T(8,128)(2,1)} %all-gather.3.cloned.1.call-done), kind=kOutput, calls=%fused_computation.19 | convolution fusion | flops 605159424 | bytes 3555328 | tf_op jit(solution)/shard_map/dot_general | solution.py:204
  150.6 3.6 %all-to-all-start.1 = ((bf16[4,144,2048]{2,1,0:T(8,128)(2,1)}), bf16[4,144,2048]{2,1,0:T(8,128)(2,1)S(1)}, u32[]{:S(2)}, u32[]{:S(2)}) async-start(bf16[4,144,2048]{2,1,0:T(8,128)(2,1)} %bitcast.16), calls=%async_computation.2 | async-start | bytes 4718592 | tf_op jit(solution)/shard_map/all_to_all | solution.py:207
  156.6 24.4 %all-gather.5.cloned.1.call-done = bf16[256,2176]{1,0:T(8,128)(2,1)} async-done(((bf16[64,2176]{1,0:T(8,128)(2,1)}), bf16[256,2176]{1,0:T(8,128)(2,1)}) %all-gather.5.cloned.1.call-update) | async-done | bytes 1114128 | tf_op jit(solution)/shard_map/all_gather | solution.py:173
  183.1 3.4 %convolution_convert_fusion.2 = bf16[576,2048]{1,0:T(8,128)(2,1)} fusion(pred[576,256]{1,0:T(8,128)(4,1)S(1)} %fusion.2, bf16[256,2176]{1,0:T(8,128)(2,1)} %all-gather.5.cloned.1.call-done), kind=kOutput, calls=%fused_computation.18 | convolution fusion | flops 605159424 | bytes 3555328 | tf_op jit(solution)/shard_map/dot_general | solution.py:204
  186.5 4.8 %all-to-all-start.3 = ((bf16[4,144,2048]{2,1,0:T(8,128)(2,1)}), bf16[4,144,2048]{2,1,0:T(8,128)(2,1)}, u32[]{:S(2)}, u32[]{:S(2)}) async-start(bf16[4,144,2048]{2,1,0:T(8,128)(2,1)} %bitcast.27), calls=%async_computation.5 | async-start | bytes 4718592 | tf_op jit(solution)/shard_map/all_to_all | solution.py:207
  192.9 5.2 %fusion.22 = f32[576,768]{1,0:T(8,128)} fusion(bf16[576,2048]{1,0:T(8,128)(2,1)S(1)} %bitcast.133, bf16[1,2048,384]{2,1,0:T(8,128)(2,1)} %collective-permute-done.3, bf16[1,2048,384]{2,1,0:T(8,128)(2,1)} %param.25), kind=kOutput, calls=%fused_computation.41 | convolution fusion | flops 1818230784 | bytes 7274496 | tf_op jit(solution)/shard_map/dot_general | solution.py:57
  198.1 9.2 %convolution_convert_fusion.1 = bf16[576,2048]{1,0:T(8,128)(2,1)} fusion(bf16[1,2048,384]{2,1,0:T(8,128)(2,1)} %collective-permute-done.5, bf16[1,2048,384]{2,1,0:T(8,128)(2,1)} %param.27, f32[576,768]{1,0:T(8,128)} %fusion.22, bf16[576,2048]{1,0:T(8,128)(2,1)S(1)} %bitcast.134, bf16[1,2048,384]{2,1,0:T(8,128)(2,1)} %copy-done.10, ...), kind=kOutput, calls=%fused_computation.17 | convolution fusion | flops 3640295424 | bytes 12779520 | tf_op jit(solution)/shard_map/rf,df->rd/dot_general | solution.py:60
  207.3 12.4 %all-to-all-done.3 = bf16[4,144,2048]{2,1,0:T(8,128)(2,1)} async-done(((bf16[4,144,2048]{2,1,0:T(8,128)(2,1)}), bf16[4,144,2048]{2,1,0:T(8,128)(2,1)}, u32[]{:S(2)}, u32[]{:S(2)}) %all-to-all-start.3) | async-done | bytes 2359328 | tf_op jit(solution)/shard_map/all_to_all | solution.py:207
  219.7 3.6 %all-to-all-start.2 = ((bf16[4,144,2048]{2,1,0:T(8,128)(2,1)}), bf16[4,144,2048]{2,1,0:T(8,128)(2,1)S(1)}, u32[]{:S(2)}, u32[]{:S(2)}) async-start(bf16[4,144,2048]{2,1,0:T(8,128)(2,1)} %bitcast.136), calls=%async_computation.3 | async-start | bytes 4718592 | tf_op jit(solution)/shard_map/all_to_all | solution.py:214
  223.3 5.9 %fusion.21 = f32[576,768]{1,0:T(8,128)} fusion(bf16[576,2048]{1,0:T(8,128)(2,1)} %bitcast.28, bf16[1,2048,384]{2,1,0:T(8,128)(2,1)} %collective-permute-done.3, bf16[1,2048,384]{2,1,0:T(8,128)(2,1)} %param.25), kind=kOutput, calls=%fused_computation.40 | convolution fusion | flops 1818230784 | bytes 7274496 | tf_op jit(solution)/shard_map/dot_general | solution.py:57
  229.2 9.8 %convolution_convert_fusion = bf16[576,2048]{1,0:T(8,128)(2,1)} fusion(bf16[1,2048,384]{2,1,0:T(8,128)(2,1)} %collective-permute-done.5, bf16[1,2048,384]{2,1,0:T(8,128)(2,1)} %param.27, f32[576,768]{1,0:T(8,128)} %fusion.21, bf16[576,2048]{1,0:T(8,128)(2,1)} %bitcast.28, bf16[1,2048,384]{2,1,0:T(8,128)(2,1)} %copy-done.10, bf16[1,2048,384]{2,1,0:T(8,128)(2,1)} %param.26), kind=kOutput, calls=%fused_computation.16 | convolution fusion | flops 3640295424 | bytes 12779520 | tf_op jit(solution)/shard_map/rf,df->rd/dot_general | solution.py:60
  239.0 12.8 %all-to-all-done.2 = bf16[4,144,2048]{2,1,0:T(8,128)(2,1)S(1)} async-done(((bf16[4,144,2048]{2,1,0:T(8,128)(2,1)}), bf16[4,144,2048]{2,1,0:T(8,128)(2,1)S(1)}, u32[]{:S(2)}, u32[]{:S(2)}) %all-to-all-start.2) | async-done | bytes 2359328 | tf_op jit(solution)/shard_map/all_to_all | solution.py:214
  251.8 4.5 %all-to-all-start.4 = ((bf16[4,144,2048]{2,1,0:T(8,128)(2,1)}), bf16[4,144,2048]{2,1,0:T(8,128)(2,1)}, u32[]{:S(2)}, u32[]{:S(2)}) async-start(bf16[4,144,2048]{2,1,0:T(8,128)(2,1)} %bitcast.135), calls=%async_computation.6 | async-start | bytes 4718592 | tf_op jit(solution)/shard_map/all_to_all | solution.py:214
  261.3 2.0 fusion.9
  263.3 21.5 %all-to-all-done.4 = bf16[4,144,2048]{2,1,0:T(8,128)(2,1)} async-done(((bf16[4,144,2048]{2,1,0:T(8,128)(2,1)}), bf16[4,144,2048]{2,1,0:T(8,128)(2,1)}, u32[]{:S(2)}, u32[]{:S(2)}) %all-to-all-start.4) | async-done | bytes 2359328 | tf_op jit(solution)/shard_map/all_to_all | solution.py:214
  284.8 2.9 fusion.50
  287.8 3.7 %fusion.10 = bf16[256,2048]{1,0:T(8,128)(2,1)} fusion(f32[256,2048]{1,0:T(8,128)S(1)} %fusion.50, bf16[576,2048]{1,0:T(8,128)(2,1)} %bitcast.30, f32[576,256]{1,0:T(8,128)S(1)} %copy-done.1), kind=kOutput, calls=%fused_computation.23 | convolution fusion | flops 605618176 | bytes 6094848 | tf_op jit(solution)/shard_map/dot_general | solution.py:222
  291.4 3.5 %all-to-all-start.5 = ((bf16[4,1,64,2048]{3,2,1,0:T(8,128)(2,1)}), bf16[4,1,64,2048]{3,2,1,0:T(8,128)(2,1)S(1)}, u32[]{:S(2)}, u32[]{:S(2)}) async-start(bf16[4,1,64,2048]{3,2,1,0:T(8,128)(2,1)} %bitcast.32), calls=%async_computation.7 | async-start | bytes 2097152 | tf_op jit(solution)/shard_map/all_to_all | solution.py:50
  296.0 24.8 %all-to-all-done.5 = bf16[4,1,64,2048]{3,2,1,0:T(8,128)(2,1)S(1)} async-done(((bf16[4,1,64,2048]{3,2,1,0:T(8,128)(2,1)}), bf16[4,1,64,2048]{3,2,1,0:T(8,128)(2,1)S(1)}, u32[]{:S(2)}, u32[]{:S(2)}) %all-to-all-start.5) | async-done | bytes 1048608 | tf_op jit(solution)/shard_map/all_to_all | solution.py:50
  (110 shorter events, 31.1 us)
Async XLA Ops:
  6.5 184.7 %copy-start = (bf16[2048,16]{0,1:T(8,128)(2,1)S(1)}, bf16[2048,16]{0,1:T(8,128)(2,1)}, u32[]{:S(2)}) copy-start(bf16[2048,16]{0,1:T(8,128)(2,1)} %param.23) | copy-start | bytes 196612
  6.5 66.9 %reduce-scatter.3.cloned.1.call-start = ((), (), s32[]{:S(2)}) async-start(), calls=%async_computation.8 | async-start | bytes 1310720 | tf_op jit(solution)/shard_map/reduce_scatter | solution.py:132
  9.6 10.4 %collective-permute-start = (bf16[2,256,256]{2,1,0:T(8,128)(2,1)S(1)}, bf16[2,256,256]{2,1,0:T(8,128)(2,1)S(1)}, u32[]{:S(2)}, u32[]{:S(2)}) collective-permute-start(bf16[2,256,256]{2,1,0:T(8,128)(2,1)S(1)} %pad_maximum_fusion.2), channel_id=1, source_target_pairs={{0,16},{16,0},{1,17},{17,1},{2,18},{18,2},{3,19},{19,3},{4,20},{20... | collective-permute-start | bytes 786440 | tf_op jit(solution)/shard_map/ppermute | solution.py:43
  12.7 7.2 %collective-permute-start.1 = (s32[2,256]{1,0:T(2,128)}, s32[2,256]{1,0:T(2,128)S(1)}, u32[]{:S(2)}, u32[]{:S(2)}) collective-permute-start(s32[2,256]{1,0:T(2,128)} %param.17), channel_id=1, source_target_pairs={{0,16},{16,0},{1,17},{17,1},{2,18},{18,2},{3,19},{19,3},{4,20},{20... | collective-permute-start | bytes 6152 | tf_op jit(solution)/shard_map/ppermute | solution.py:43
  12.7 51.3 %collective-permute-start.2 = (bf16[1024,1024]{1,0:T(8,128)(2,1)}, bf16[1024,1024]{1,0:T(8,128)(2,1)}, u32[]{:S(2)}, u32[]{:S(2)}) collective-permute-start(bf16[1024,1024]{1,0:T(8,128)(2,1)} %param.20), channel_id=1, source_target_pairs={{0,16},{16,0},{1,17},{17,1},{2,18},{18,2},{3,19},{19,3},{4,20},{20... | collective-permute-start | bytes 6291464 | tf_op jit(solution)/shard_map/ppermute | solution.py:43
  14.7 2.4 copy-start.8
  16.8 3.0 copy-start.6
  16.8 3.2 copy-start.3
  22.4 1.6 copy-start.2
  24.0 2.3 copy-start.7
  66.9 4.7 %copy-start.9 = (bf16[1,2048,384]{2,1,0:T(8,128)(2,1)S(1)}, bf16[1,2048,384]{2,1,0:T(8,128)(2,1)}, u32[]{:S(2)}) copy-start(bf16[1,2048,384]{2,1,0:T(8,128)(2,1)} %param.25) | copy-start | bytes 4718596
  68.0 18.0 %all-to-all-start = ((bf16[2,4,64,1024]{3,2,0,1:T(8,128)(2,1)}), bf16[2,4,64,1024]{3,2,0,1:T(8,128)(2,1)S(1)}, u32[]{:S(2)}, u32[]{:S(2)}) async-start(bf16[2,4,64,1024]{3,2,0,1:T(8,128)(2,1)} %copy.97), calls=%async_computation.1 | async-start | bytes 2097152 | tf_op jit(solution)/shard_map/all_to_all | solution.py:50
  71.5 68.6 %all-gather.3.cloned.1.call-start = ((), (), s32[]{:S(2)}) async-start(), calls=%async_computation.9 | async-start | bytes 1392640 | tf_op jit(solution)/shard_map/all_gather | solution.py:173
  71.6 36.9 %collective-permute-start.3 = (bf16[1,2048,384]{2,1,0:T(8,128)(2,1)S(1)}, bf16[1,2048,384]{2,1,0:T(8,128)(2,1)}, u32[]{:S(2)}, u32[]{:S(2)}) collective-permute-start(bf16[1,2048,384]{2,1,0:T(8,128)(2,1)S(1)} %copy-done.9), channel_id=1, source_target_pairs={{0,16},{16,0},{1,17},{17,1},{2,18},{18,2},{3,19},{19,3},{4,20},{20... | collective-permute-start | bytes 4718600 | tf_op jit(solution)/shard_map/ppermute | solution.py:43
  86.4 1.5 copy-start.5
  109.3 71.7 %all-gather.5.cloned.1.call-start = ((), (), s32[]{:S(2)}) async-start(), calls=%async_computation.11 | async-start | bytes 1392640 | tf_op jit(solution)/shard_map/all_gather | solution.py:173
  109.3 36.2 %collective-permute-start.4 = (bf16[1,2048,384]{2,1,0:T(8,128)(2,1)}, bf16[1,2048,384]{2,1,0:T(8,128)(2,1)S(1)}, u32[]{:S(2)}, u32[]{:S(2)}) collective-permute-start(bf16[1,2048,384]{2,1,0:T(8,128)(2,1)} %param.26), channel_id=1, source_target_pairs={{0,16},{16,0},{1,17},{17,1},{2,18},{18,2},{3,19},{19,3},{4,20},{20... | collective-permute-start | bytes 4718600 | tf_op jit(solution)/shard_map/ppermute | solution.py:43
  145.6 5.0 %copy-start.10 = (bf16[1,2048,384]{2,1,0:T(8,128)(2,1)}, bf16[1,2048,384]{2,1,0:T(8,128)(2,1)S(1)}, u32[]{:S(2)}) copy-start(bf16[1,2048,384]{2,1,0:T(8,128)(2,1)S(1)} %collective-permute-done.4) | copy-start | bytes 4718596
  150.6 35.9 %all-to-all-start.1 = ((bf16[4,144,2048]{2,1,0:T(8,128)(2,1)}), bf16[4,144,2048]{2,1,0:T(8,128)(2,1)S(1)}, u32[]{:S(2)}, u32[]{:S(2)}) async-start(bf16[4,144,2048]{2,1,0:T(8,128)(2,1)} %bitcast.16), calls=%async_computation.2 | async-start | bytes 4718592 | tf_op jit(solution)/shard_map/all_to_all | solution.py:207
  154.2 38.7 %collective-permute-start.5 = (bf16[1,2048,384]{2,1,0:T(8,128)(2,1)}, bf16[1,2048,384]{2,1,0:T(8,128)(2,1)}, u32[]{:S(2)}, u32[]{:S(2)}) collective-permute-start(bf16[1,2048,384]{2,1,0:T(8,128)(2,1)} %param.27), channel_id=1, source_target_pairs={{0,16},{16,0},{1,17},{17,1},{2,18},{18,2},{3,19},{19,3},{4,20},{20... | collective-permute-start | bytes 4718600 | tf_op jit(solution)/shard_map/ppermute | solution.py:43
  186.5 6.4 %copy-start.4 = (s32[256,8]{0,1:T(8,128)S(1)}, s32[256,8]{0,1:T(8,128)}, u32[]{:S(2)}) copy-start(s32[256,8]{0,1:T(8,128)} %convert_element_type.121) | copy-start | bytes 24580
  186.5 33.2 %all-to-all-start.3 = ((bf16[4,144,2048]{2,1,0:T(8,128)(2,1)}), bf16[4,144,2048]{2,1,0:T(8,128)(2,1)}, u32[]{:S(2)}, u32[]{:S(2)}) async-start(bf16[4,144,2048]{2,1,0:T(8,128)(2,1)} %bitcast.27), calls=%async_computation.5 | async-start | bytes 4718592 | tf_op jit(solution)/shard_map/all_to_all | solution.py:207
  219.7 32.1 %all-to-all-start.2 = ((bf16[4,144,2048]{2,1,0:T(8,128)(2,1)}), bf16[4,144,2048]{2,1,0:T(8,128)(2,1)S(1)}, u32[]{:S(2)}, u32[]{:S(2)}) async-start(bf16[4,144,2048]{2,1,0:T(8,128)(2,1)} %bitcast.136), calls=%async_computation.3 | async-start | bytes 4718592 | tf_op jit(solution)/shard_map/all_to_all | solution.py:214
  251.8 33.1 %all-to-all-start.4 = ((bf16[4,144,2048]{2,1,0:T(8,128)(2,1)}), bf16[4,144,2048]{2,1,0:T(8,128)(2,1)}, u32[]{:S(2)}, u32[]{:S(2)}) async-start(bf16[4,144,2048]{2,1,0:T(8,128)(2,1)} %bitcast.135), calls=%async_computation.6 | async-start | bytes 4718592 | tf_op jit(solution)/shard_map/all_to_all | solution.py:214
  256.3 38.7 %reduce-scatter.5.cloned.1.call-start = ((), (), s32[]{:S(2)}) async-start(), calls=%async_computation.10 | async-start | bytes 1310720 | tf_op jit(solution)/shard_map/reduce_scatter | solution.py:226
  284.8 2.9 copy-start.1
  291.4 29.3 %all-to-all-start.5 = ((bf16[4,1,64,2048]{3,2,1,0:T(8,128)(2,1)}), bf16[4,1,64,2048]{3,2,1,0:T(8,128)(2,1)S(1)}, u32[]{:S(2)}, u32[]{:S(2)}) async-start(bf16[4,1,64,2048]{3,2,1,0:T(8,128)(2,1)} %bitcast.32), calls=%async_computation.7 | async-start | bytes 2097152 | tf_op jit(solution)/shard_map/all_to_all | solution.py:50
Sparse Core Ops, SparseCore 0:
  26.4 26.6 reduce-scatter.2
  109.4 30.6 all-gather.2
  150.7 30.3 all-gather.4
  263.5 26.8 reduce-scatter.4

commit v9 on v7

--- a/solution.py
+++ b/solution.py
@@ -114,17 +114,22 @@
     ep_index = lax.axis_index("ep")
     cp_index = lax.axis_index("cp")
     cap = capacity(share, top_count, experts)
-    weight_pieces = cp_pieces(out_weight, n_cp)
-    summed_blocks = []
-    for piece in weight_pieces:
-        block = jnp.dot(attn, piece, preferred_element_type=jnp.float32).reshape(
-            packs, row_count, piece.shape[1]
-        )
-        summed_blocks.append(
-            lax.psum_scatter(block.astype(jnp.bfloat16), "tp", scatter_dimension=1, tiled=True)
-        )
-    blocks = jnp.stack(summed_blocks, axis=2).astype(jnp.float32)
-    source_block = (cp_index - jnp.arange(n_cp, dtype=jnp.int32)) % n_cp
+    attn_pieces = cp_pieces(attn, n_cp)
+    received_blocks = []
+    for j, piece in enumerate(attn_pieces):
+        if j > 0:
+            piece, received_blocks[0] = lax.optimization_barrier((piece, received_blocks[0]))
+        block = jnp.dot(piece, out_weight, preferred_element_type=jnp.float32).reshape(
+            packs, row_count, out_weight.shape[1]
+        )
+        summed = lax.psum_scatter(
+            block.astype(jnp.bfloat16), "tp", scatter_dimension=1, tiled=True
+        )
+        if j > 0:
+            summed = lax.ppermute(summed, "cp", [(i, (i - j) % n_cp) for i in range(n_cp)])
+        received_blocks.append(summed)
+    blocks = jnp.stack(received_blocks, axis=2).astype(jnp.float32)
+    source_block = (jnp.arange(n_cp, dtype=jnp.int32) - cp_index) % n_cp
     picks_block = source_block[:, None] == jnp.arange(n_cp, dtype=jnp.int32)[None, :]
     projected = jnp.sum(
         jnp.where(picks_block[None, None, :, :, None], blocks[:, :, None, :, :], jnp.float32(0.0)),
@@ -138,8 +143,8 @@
     home_rows = packs * share
     normed = root_mean_scale(state.reshape(home_rows, width), norm_gain).astype(jnp.bfloat16)
 
-    weight_pieces, expert_gate, expert_up, expert_down = lax.optimization_barrier(
-        (weight_pieces, expert_gate, expert_up, expert_down)
+    attn_pieces, expert_gate, expert_up, expert_down = lax.optimization_barrier(
+        (attn_pieces, expert_gate, expert_up, expert_down)
     )
     gate_pieces = cp_pieces(expert_gate, n_cp)
     up_pieces = cp_pieces(expert_up, n_cp)

time: 320 us -> 318 us (level)
  waiting for transfers between devices: 199 us -> 188 us
  starting transfers between devices: 25.5 us -> 29.7 us
    ppermute x6, waiting for transfers between devices: 49.5 us -> 30.5 us  [cp_pieces(): pieces.append(lax.ppermute(x, 'cp', perm))]
    ppermute x0 -> x1, waiting for transfers between devices: none -> 14.3 us  [shards(): lax.ppermute(summed, 'cp', [(i, (i - j) % n_cp) for i in range(n_cp)])]
    dot_general x2, matrix products: 3.99 us -> 7.83 us  [shards(): lax.dot_general(weight_lo, back, contract, preferred_element_type=jnp.flo...]
    all_gather x2, waiting for transfers between devices: 53.9 us -> 50.2 us  [shards(): lax.all_gather(jnp.concatenate([rows, id_lanes], axis=1), 'ep', axis=0, t...]
  transfers between devices with their start and end apart: 16 -> 17, of which waited for: 11 -> 12; matrix products, arithmetic and copies ran while one was open for 21% -> 20% of each run, Pallas kernels for 0% -> 0%
where the time goes in v9:
time: 318 us; the launch traced here: 317 us
  waiting for transfers between devices  188 us (59%)
  matrix products  61.9 us (19%)
  starting transfers between devices  29.7 us (9%)
  other arithmetic  15.3 us (5%)
  between operations  14 us (4%)
  local copies, waits for them, and re-layouts  8.44 us (3%)
    all_gather x2, waiting for transfers between devices, shards(): lax.all_gather(jnp.concatenate([rows, id_lanes], axis=1), 'ep', axis=0, t...  50.2 us
    all_to_all x2, waiting for transfers between devices, shards(): lax.all_to_all(served, 'tp', split_axis=0, concat_axis=0, tiled=True)  31.1 us
    ppermute x6, waiting for transfers between devices, cp_pieces(): pieces.append(lax.ppermute(x, 'cp', perm))  30.5 us
    reduce_scatter x2, waiting for transfers between devices, shards(): lax.psum_scatter(partial.astype(jnp.bfloat16).reshape(n_ep, share, width)...  26.5 us
    reduce_scatter x2, waiting for transfers between devices, shards(): lax.psum_scatter(block.astype(jnp.bfloat16), 'tp', scatter_dimension=1, t...  24.5 us
    dot_general x2, matrix products, expert_rows(): jnp.einsum('rf,df->rd', hidden_act, full_down[0], preferred_element_type=...  19.3 us
    ppermute x1, waiting for transfers between devices, shards(): lax.ppermute(summed, 'cp', [(i, (i - j) % n_cp) for i in range(n_cp)])  14.3 us
    dot_general x2, matrix products, expert_rows(): jnp.dot(flat_rows, full_gate[0], preferred_element_type=jnp.float32)  11.7 us
  transfers between devices with their start and end apart: 17, of which 12 were waited for; matrix products, arithmetic and copies ran while one was open for 20% of the time, Pallas kernels for 0%

profile of v9, /device:TPU:0, one launch (start us, length us, event | category | flops | bytes accessed | tf_op | source)
XLA Modules:
  0.0 317.0 jit_solution(17901882507598583596)
XLA Ops:
  9.7 3.0 collective-permute-start
  16.6 1.9 fusion.13
  19.4 2.2 fusion
  24.2 2.3 fusion.23
  28.6 1.8 collective-permute-start.2
  30.4 22.6 %collective-permute-done.2 = bf16[512,1024]{1,0:T(8,128)(2,1)S(1)} collective-permute-done((bf16[512,1024]{1,0:T(8,128)(2,1)S(1)}, bf16[512,1024]{1,0:T(8,128)(2,1)S(1)}, u32[]{:S(2)}, u32[]{:S(2)}) %collective-permute-start.2) | collective-permute-done | bytes 1048608 | tf_op jit(solution)/shard_map/ppermute | solution.py:43
  53.1 2.2 convolution_convert_fusion.4
  57.0 24.5 %reduce-scatter.7.cloned.1.call-done = bf16[2,64,1024]{2,1,0:T(8,128)(2,1)} async-done(((bf16[2,256,1024]{2,1,0:T(8,128)(2,1)}), bf16[2,64,1024]{2,1,0:T(8,128)(2,1)}) %reduce-scatter.7.cloned.1.call-update) | async-done | bytes 262160 | tf_op jit(solution)/shard_map/reduce_scatter | solution.py:125
  83.1 14.3 %collective-permute-done.3 = bf16[2,64,1024]{2,1,0:T(8,128)(2,1)S(1)} collective-permute-done((bf16[2,64,1024]{2,1,0:T(8,128)(2,1)}, bf16[2,64,1024]{2,1,0:T(8,128)(2,1)S(1)}, u32[]{:S(2)}, u32[]{:S(2)}) %collective-permute-start.3) | collective-permute-done | bytes 262176 | tf_op jit(solution)/shard_map/ppermute | solution.py:129
  102.0 27.5 %all-gather.3.cloned.1.call-done = bf16[256,2176]{1,0:T(8,128)(2,1)} async-done(((bf16[64,2176]{1,0:T(8,128)(2,1)}), bf16[256,2176]{1,0:T(8,128)(2,1)}) %all-gather.3.cloned.1.call-update) | async-done | bytes 1114128 | tf_op jit(solution)/shard_map/all_gather | solution.py:168
  130.8 5.3 %collective-permute-done.5 = bf16[1,2048,384]{2,1,0:T(8,128)(2,1)} collective-permute-done((bf16[1,2048,384]{2,1,0:T(8,128)(2,1)}, bf16[1,2048,384]{2,1,0:T(8,128)(2,1)}, u32[]{:S(2)}, u32[]{:S(2)}) %collective-permute-start.5) | collective-permute-done | bytes 1572896 | tf_op jit(solution)/shard_map/ppermute | solution.py:43
  136.9 3.4 %convolution_convert_fusion.3 = bf16[576,2048]{1,0:T(8,128)(2,1)} fusion(pred[576,256]{1,0:T(8,128)(4,1)S(1)} %fusion.3, bf16[256,2176]{1,0:T(8,128)(2,1)} %all-gather.3.cloned.1.call-done), kind=kOutput, calls=%fused_computation.19 | convolution fusion | flops 605159424 | bytes 3555328 | tf_op jit(solution)/shard_map/dot_general | solution.py:199
  141.0 4.7 %all-to-all-start = ((bf16[4,144,2048]{2,1,0:T(8,128)(2,1)}), bf16[4,144,2048]{2,1,0:T(8,128)(2,1)}, u32[]{:S(2)}, u32[]{:S(2)}) async-start(bf16[4,144,2048]{2,1,0:T(8,128)(2,1)} %bitcast.121), calls=%async_computation.2 | async-start | bytes 4718592 | tf_op jit(solution)/shard_map/all_to_all | solution.py:202
  147.3 22.7 %all-gather.5.cloned.1.call-done = bf16[256,2176]{1,0:T(8,128)(2,1)} async-done(((bf16[64,2176]{1,0:T(8,128)(2,1)}), bf16[256,2176]{1,0:T(8,128)(2,1)}) %all-gather.5.cloned.1.call-update) | async-done | bytes 1114128 | tf_op jit(solution)/shard_map/all_gather | solution.py:168
  172.0 3.5 %convolution_convert_fusion.2 = bf16[576,2048]{1,0:T(8,128)(2,1)} fusion(pred[576,256]{1,0:T(8,128)(4,1)S(1)} %fusion.2, bf16[256,2176]{1,0:T(8,128)(2,1)} %all-gather.5.cloned.1.call-done), kind=kOutput, calls=%fused_computation.18 | convolution fusion | flops 605159424 | bytes 3555328 | tf_op jit(solution)/shard_map/dot_general | solution.py:199
  175.5 4.6 %all-to-all-start.2 = ((bf16[4,144,2048]{2,1,0:T(8,128)(2,1)}), bf16[4,144,2048]{2,1,0:T(8,128)(2,1)}, u32[]{:S(2)}, u32[]{:S(2)}) async-start(bf16[4,144,2048]{2,1,0:T(8,128)(2,1)} %bitcast.122), calls=%async_computation.5 | async-start | bytes 4718592 | tf_op jit(solution)/shard_map/all_to_all | solution.py:202
  180.6 2.0 collective-permute-done.6
  182.6 5.8 %fusion.20 = f32[576,768]{1,0:T(8,128)} fusion(bf16[576,2048]{1,0:T(8,128)(2,1)} %bitcast.16, bf16[1,2048,384]{2,1,0:T(8,128)(2,1)} %collective-permute-done.4, bf16[1,2048,384]{2,1,0:T(8,128)(2,1)} %param.25), kind=kOutput, calls=%fused_computation.37 | convolution fusion | flops 1818230784 | bytes 7274496 | tf_op jit(solution)/shard_map/dot_general | solution.py:50
  188.4 9.9 %convolution_convert_fusion.1 = bf16[576,2048]{1,0:T(8,128)(2,1)} fusion(bf16[1,2048,384]{2,1,0:T(8,128)(2,1)} %collective-permute-done.6, bf16[1,2048,384]{2,1,0:T(8,128)(2,1)} %param.27, f32[576,768]{1,0:T(8,128)} %fusion.20, bf16[576,2048]{1,0:T(8,128)(2,1)} %bitcast.16, bf16[1,2048,384]{2,1,0:T(8,128)(2,1)} %collective-permute-done.5, ...), kind=kOutput, calls=%fused_computation.17 | convolution fusion | flops 3640295424 | bytes 12779520 | tf_op jit(solution)/shard_map/rf,df->rd/dot_general | solution.py:53
  198.3 10.4 %all-to-all-done.2 = bf16[4,144,2048]{2,1,0:T(8,128)(2,1)} async-done(((bf16[4,144,2048]{2,1,0:T(8,128)(2,1)}), bf16[4,144,2048]{2,1,0:T(8,128)(2,1)}, u32[]{:S(2)}, u32[]{:S(2)}) %all-to-all-start.2) | async-done | bytes 2359328 | tf_op jit(solution)/shard_map/all_to_all | solution.py:202
  208.7 4.7 %all-to-all-start.1 = ((bf16[4,144,2048]{2,1,0:T(8,128)(2,1)}), bf16[4,144,2048]{2,1,0:T(8,128)(2,1)}, u32[]{:S(2)}, u32[]{:S(2)}) async-start(bf16[4,144,2048]{2,1,0:T(8,128)(2,1)} %bitcast.130), calls=%async_computation.3 | async-start | bytes 4718592 | tf_op jit(solution)/shard_map/all_to_all | solution.py:209
  214.9 5.9 %fusion.19 = f32[576,768]{1,0:T(8,128)} fusion(bf16[576,2048]{1,0:T(8,128)(2,1)} %bitcast.27, bf16[1,2048,384]{2,1,0:T(8,128)(2,1)} %collective-permute-done.4, bf16[1,2048,384]{2,1,0:T(8,128)(2,1)} %param.25), kind=kOutput, calls=%fused_computation.36 | convolution fusion | flops 1818230784 | bytes 7274496 | tf_op jit(solution)/shard_map/dot_general | solution.py:50
  220.8 9.4 %convolution_convert_fusion = bf16[576,2048]{1,0:T(8,128)(2,1)} fusion(bf16[1,2048,384]{2,1,0:T(8,128)(2,1)} %collective-permute-done.6, bf16[1,2048,384]{2,1,0:T(8,128)(2,1)S(1)} %copy-done.13, f32[576,768]{1,0:T(8,128)} %fusion.19, bf16[576,2048]{1,0:T(8,128)(2,1)} %bitcast.27, bf16[1,2048,384]{2,1,0:T(8,128)(2,1)} %collective-permute-done.5, ...), kind=kOutput, calls=%fused_computation.16 | convolution fusion | flops 3640295424 | bytes 12779520 | tf_op jit(solution)/shard_map/rf,df->rd/dot_general | solution.py:53
  230.2 11.6 %all-to-all-done.1 = bf16[4,144,2048]{2,1,0:T(8,128)(2,1)} async-done(((bf16[4,144,2048]{2,1,0:T(8,128)(2,1)}), bf16[4,144,2048]{2,1,0:T(8,128)(2,1)}, u32[]{:S(2)}, u32[]{:S(2)}) %all-to-all-start.1) | async-done | bytes 2359328 | tf_op jit(solution)/shard_map/all_to_all | solution.py:209
  241.8 4.5 %all-to-all-start.3 = ((bf16[4,144,2048]{2,1,0:T(8,128)(2,1)}), bf16[4,144,2048]{2,1,0:T(8,128)(2,1)}, u32[]{:S(2)}, u32[]{:S(2)}) async-start(bf16[4,144,2048]{2,1,0:T(8,128)(2,1)} %bitcast.129), calls=%async_computation.6 | async-start | bytes 4718592 | tf_op jit(solution)/shard_map/all_to_all | solution.py:209
  246.3 2.9 fusion.47
  249.2 3.6 %fusion.9 = bf16[256,2048]{1,0:T(8,128)(2,1)} fusion(f32[256,2048]{1,0:T(8,128)S(1)} %fusion.47, bf16[576,2048]{1,0:T(8,128)(2,1)} %bitcast.21, f32[576,256]{1,0:T(8,128)S(1)} %copy-done.3), kind=kOutput, calls=%fused_computation.22 | convolution fusion | flops 605618176 | bytes 6094848 | tf_op jit(solution)/shard_map/dot_general | solution.py:217
  255.3 19.5 %all-to-all-done.3 = bf16[4,144,2048]{2,1,0:T(8,128)(2,1)} async-done(((bf16[4,144,2048]{2,1,0:T(8,128)(2,1)}), bf16[4,144,2048]{2,1,0:T(8,128)(2,1)}, u32[]{:S(2)}, u32[]{:S(2)}) %all-to-all-start.3) | async-done | bytes 2359328 | tf_op jit(solution)/shard_map/all_to_all | solution.py:209
  274.8 2.7 fusion.44
  277.5 4.2 %fusion.10 = bf16[256,2048]{1,0:T(8,128)(2,1)} fusion(f32[256,2048]{1,0:T(8,128)S(1)} %fusion.44, bf16[576,2048]{1,0:T(8,128)(2,1)} %bitcast.29, f32[576,256]{1,0:T(8,128)} %copy-done.4), kind=kOutput, calls=%fused_computation.23 | convolution fusion | flops 605618176 | bytes 6094848 | tf_op jit(solution)/shard_map/dot_general | solution.py:217
  281.8 26.5 %reduce-scatter.11.cloned.1.call-done = bf16[1,64,2048]{2,1,0:T(8,128)(2,1)} async-done(((bf16[4,64,2048]{2,1,0:T(8,128)(2,1)}), bf16[1,64,2048]{2,1,0:T(8,128)(2,1)}) %reduce-scatter.11.cloned.1.call-update) | async-done | bytes 262160 | tf_op jit(solution)/shard_map/reduce_scatter | solution.py:219
  308.2 1.9 add_convert_fusion
  (119 shorter events, 30.8 us)
Async XLA Ops:
  6.5 17.7 %copy-start = (bf16[1024,1024]{1,0:T(8,128)(2,1)S(1)}, bf16[1024,1024]{1,0:T(8,128)(2,1)}, u32[]{:S(2)}) copy-start(bf16[1024,1024]{1,0:T(8,128)(2,1)} %param.20) | copy-start | bytes 6291460
  6.5 46.5 %reduce-scatter.5.cloned.1.call-start = ((), (), s32[]{:S(2)}) async-start(), calls=%async_computation.8 | async-start | bytes 1310720 | tf_op jit(solution)/shard_map/reduce_scatter | solution.py:125
  9.7 9.6 %collective-permute-start = (bf16[2,256,256]{2,1,0:T(8,128)(2,1)S(1)}, bf16[2,256,256]{2,1,0:T(8,128)(2,1)S(1)}, u32[]{:S(2)}, u32[]{:S(2)}) collective-permute-start(bf16[2,256,256]{2,1,0:T(8,128)(2,1)S(1)} %pad_maximum_fusion.1), channel_id=1, source_target_pairs={{0,16},{16,0},{1,17},{17,1},{2,18},{18,2},{3,19},{19,3},{4,20},{20... | collective-permute-start | bytes 786440 | tf_op jit(solution)/shard_map/ppermute | solution.py:43
  12.8 6.3 %collective-permute-start.1 = (s32[2,256]{1,0:T(2,128)}, s32[2,256]{1,0:T(2,128)S(1)}, u32[]{:S(2)}, u32[]{:S(2)}) collective-permute-start(s32[2,256]{1,0:T(2,128)} %param.17), channel_id=1, source_target_pairs={{0,16},{16,0},{1,17},{17,1},{2,18},{18,2},{3,19},{19,3},{4,20},{20... | collective-permute-start | bytes 6152 | tf_op jit(solution)/shard_map/ppermute | solution.py:43
  12.9 3.8 %copy-start.12 = (f32[128]{0:T(128)S(1)}, f32[128]{0:T(128)}, u32[]{:S(2)}) copy-start(f32[128]{0:T(128)} %param.18) | copy-start | bytes 1540
  14.4 1.4 copy-start.2
  16.3 2.8 copy-start.10
  16.3 3.0 copy-start.7
  23.3 1.0 copy-start.5
  26.6 54.9 %reduce-scatter.7.cloned.1.call-start = ((), (), s32[]{:S(2)}) async-start(), calls=%async_computation.9 | async-start | bytes 1310720 | tf_op jit(solution)/shard_map/reduce_scatter | solution.py:125
  28.6 26.8 %copy-start.11 = (s32[2,256,8]{1,2,0:T(8,128)S(1)}, s32[2,256,8]{1,2,0:T(8,128)}, u32[]{:S(2)}) copy-start(s32[2,256,8]{1,2,0:T(8,128)} %param.24) | copy-start | bytes 49156
  28.6 24.4 %collective-permute-start.2 = (bf16[512,1024]{1,0:T(8,128)(2,1)S(1)}, bf16[512,1024]{1,0:T(8,128)(2,1)S(1)}, u32[]{:S(2)}, u32[]{:S(2)}) collective-permute-start(bf16[512,1024]{1,0:T(8,128)(2,1)S(1)} %bitcast.133), channel_id=1, source_target_pairs={{0,16},{16,0},{1,17},{17,1},{2,18},{18,2},{3,19},{19,3},{4,20},{20... | collective-permute-start | bytes 3145736 | tf_op jit(solution)/shard_map/ppermute | solution.py:43
  53.1 44.4 %copy-start.8 = (bf16[2,64,1024]{2,1,0:T(8,128)(2,1)S(1)}, bf16[2,64,1024]{2,1,0:T(8,128)(2,1)}, u32[]{:S(2)}) copy-start(bf16[2,64,1024]{2,1,0:T(8,128)(2,1)} %reduce-scatter.5.cloned.1.call-done) | copy-start | bytes 786436
  55.3 74.2 %all-gather.3.cloned.1.call-start = ((), (), s32[]{:S(2)}) async-start(), calls=%async_computation.10 | async-start | bytes 1392640 | tf_op jit(solution)/shard_map/all_gather | solution.py:168
  55.5 44.0 %collective-permute-start.4 = (bf16[1,2048,384]{2,1,0:T(8,128)(2,1)}, bf16[1,2048,384]{2,1,0:T(8,128)(2,1)}, u32[]{:S(2)}, u32[]{:S(2)}) collective-permute-start(bf16[1,2048,384]{2,1,0:T(8,128)(2,1)} %param.25), channel_id=1, source_target_pairs={{0,16},{16,0},{1,17},{17,1},{2,18},{18,2},{3,19},{19,3},{4,20},{20... | collective-permute-start | bytes 4718600 | tf_op jit(solution)/shard_map/ppermute | solution.py:43
  81.5 16.0 %collective-permute-start.3 = (bf16[2,64,1024]{2,1,0:T(8,128)(2,1)}, bf16[2,64,1024]{2,1,0:T(8,128)(2,1)S(1)}, u32[]{:S(2)}, u32[]{:S(2)}) collective-permute-start(bf16[2,64,1024]{2,1,0:T(8,128)(2,1)} %reduce-scatter.7.cloned.1.call-done), channel_id=1, source_target_pairs={{0,16},{16,0},{1,17},{17,1},{2,18},{18,2},{3,19},{19,3},{4,20},{20... | collective-permute-start | bytes 786440 | tf_op jit(solution)/shard_map/ppermute | solution.py:129
  97.9 1.5 copy-start.9
  100.4 69.6 %all-gather.5.cloned.1.call-start = ((), (), s32[]{:S(2)}) async-start(), calls=%async_computation.12 | async-start | bytes 1392640 | tf_op jit(solution)/shard_map/all_gather | solution.py:168
  100.4 35.6 %collective-permute-start.5 = (bf16[1,2048,384]{2,1,0:T(8,128)(2,1)}, bf16[1,2048,384]{2,1,0:T(8,128)(2,1)}, u32[]{:S(2)}, u32[]{:S(2)}) collective-permute-start(bf16[1,2048,384]{2,1,0:T(8,128)(2,1)} %param.26), channel_id=1, source_target_pairs={{0,16},{16,0},{1,17},{17,1},{2,18},{18,2},{3,19},{19,3},{4,20},{20... | collective-permute-start | bytes 4718600 | tf_op jit(solution)/shard_map/ppermute | solution.py:43
  141.0 34.4 %all-to-all-start = ((bf16[4,144,2048]{2,1,0:T(8,128)(2,1)}), bf16[4,144,2048]{2,1,0:T(8,128)(2,1)}, u32[]{:S(2)}, u32[]{:S(2)}) async-start(bf16[4,144,2048]{2,1,0:T(8,128)(2,1)} %bitcast.121), calls=%async_computation.2 | async-start | bytes 4718592 | tf_op jit(solution)/shard_map/all_to_all | solution.py:202
  145.7 36.9 %collective-permute-start.6 = (bf16[1,2048,384]{2,1,0:T(8,128)(2,1)}, bf16[1,2048,384]{2,1,0:T(8,128)(2,1)}, u32[]{:S(2)}, u32[]{:S(2)}) collective-permute-start(bf16[1,2048,384]{2,1,0:T(8,128)(2,1)} %param.27), channel_id=1, source_target_pairs={{0,16},{16,0},{1,17},{17,1},{2,18},{18,2},{3,19},{19,3},{4,20},{20... | collective-permute-start | bytes 4718600 | tf_op jit(solution)/shard_map/ppermute | solution.py:43
  175.5 4.6 %copy-start.6 = (bf16[256,2176]{1,0:T(8,128)(2,1)S(1)}, bf16[256,2176]{1,0:T(8,128)(2,1)}, u32[]{:S(2)}) copy-start(bf16[256,2176]{1,0:T(8,128)(2,1)} %all-gather.3.cloned.1.call-done) | copy-start | bytes 3342340
  175.5 4.6 %copy-start.14 = (bf16[2048,16]{0,1:T(8,128)(2,1)S(1)}, bf16[2048,16]{0,1:T(8,128)(2,1)}, u32[]{:S(2)}) copy-start(bf16[2048,16]{0,1:T(8,128)(2,1)} %param.23) | copy-start | bytes 196612
  175.5 33.2 %all-to-all-start.2 = ((bf16[4,144,2048]{2,1,0:T(8,128)(2,1)}), bf16[4,144,2048]{2,1,0:T(8,128)(2,1)}, u32[]{:S(2)}, u32[]{:S(2)}) async-start(bf16[4,144,2048]{2,1,0:T(8,128)(2,1)} %bitcast.122), calls=%async_computation.5 | async-start | bytes 4718592 | tf_op jit(solution)/shard_map/all_to_all | solution.py:202
  208.7 33.1 %all-to-all-start.1 = ((bf16[4,144,2048]{2,1,0:T(8,128)(2,1)}), bf16[4,144,2048]{2,1,0:T(8,128)(2,1)}, u32[]{:S(2)}, u32[]{:S(2)}) async-start(bf16[4,144,2048]{2,1,0:T(8,128)(2,1)} %bitcast.130), calls=%async_computation.3 | async-start | bytes 4718592 | tf_op jit(solution)/shard_map/all_to_all | solution.py:209
  214.9 5.9 %copy-start.13 = (bf16[1,2048,384]{2,1,0:T(8,128)(2,1)S(1)}, bf16[1,2048,384]{2,1,0:T(8,128)(2,1)}, u32[]{:S(2)}) copy-start(bf16[1,2048,384]{2,1,0:T(8,128)(2,1)} %param.27) | copy-start | bytes 4718596
  241.8 33.1 %all-to-all-start.3 = ((bf16[4,144,2048]{2,1,0:T(8,128)(2,1)}), bf16[4,144,2048]{2,1,0:T(8,128)(2,1)}, u32[]{:S(2)}, u32[]{:S(2)}) async-start(bf16[4,144,2048]{2,1,0:T(8,128)(2,1)} %bitcast.129), calls=%async_computation.6 | async-start | bytes 4718592 | tf_op jit(solution)/shard_map/all_to_all | solution.py:209
  246.3 35.5 %reduce-scatter.9.cloned.1.call-start = ((), (), s32[]{:S(2)}) async-start(), calls=%async_computation.11 | async-start | bytes 1310720 | tf_op jit(solution)/shard_map/reduce_scatter | solution.py:219
  246.3 2.9 copy-start.3
  252.9 55.3 %reduce-scatter.11.cloned.1.call-start = ((), (), s32[]{:S(2)}) async-start(), calls=%async_computation.13 | async-start | bytes 1310720 | tf_op jit(solution)/shard_map/reduce_scatter | solution.py:219
  255.3 19.6 %copy-start.4 = (f32[576,256]{1,0:T(8,128)}, f32[576,256]{1,0:T(8,128)S(1)}, u32[]{:S(2)}) copy-start(f32[576,256]{1,0:T(8,128)S(1)} %select_reduce_fusion) | copy-start | bytes 1769476
  277.5 32.6 %copy-start.1 = (bf16[1024,1024]{1,0:T(8,128)(2,1)S(1)}, bf16[1024,1024]{1,0:T(8,128)(2,1)}, u32[]{:S(2)}) copy-start(bf16[1024,1024]{1,0:T(8,128)(2,1)} %param.20) | copy-start | bytes 6291460
Sparse Core Ops, SparseCore 0:
  26.7 26.3 reduce-scatter.4
  55.8 25.7 reduce-scatter.6
  100.5 29.0 all-gather.2
  141.2 28.7 all-gather.4
  253.0 27.0 reduce-scatter.8
  282.4 25.7 reduce-scatter.10

commit v10 on v9

--- a/solution.py
+++ b/solution.py
@@ -114,6 +114,10 @@
     ep_index = lax.axis_index("ep")
     cp_index = lax.axis_index("cp")
     cap = capacity(share, top_count, experts)
+    gate_head = expert_gate[:, :, : expert_gate.shape[2] // 2]
+    gate_tail = expert_gate[:, :, expert_gate.shape[2] // 2 :]
+    gate_head_pieces = cp_pieces(gate_head, n_cp)
+    attn, gate_head_pieces = lax.optimization_barrier((attn, gate_head_pieces))
     attn_pieces = cp_pieces(attn, n_cp)
     received_blocks = []
     for j, piece in enumerate(attn_pieces):
@@ -143,10 +147,14 @@
     home_rows = packs * share
     normed = root_mean_scale(state.reshape(home_rows, width), norm_gain).astype(jnp.bfloat16)
 
-    attn_pieces, expert_gate, expert_up, expert_down = lax.optimization_barrier(
-        (attn_pieces, expert_gate, expert_up, expert_down)
-    )
-    gate_pieces = cp_pieces(expert_gate, n_cp)
+    attn_pieces, gate_tail, expert_up, expert_down = lax.optimization_barrier(
+        (attn_pieces, gate_tail, expert_up, expert_down)
+    )
+    gate_tail_pieces = cp_pieces(gate_tail, n_cp)
+    gate_pieces = [
+        jnp.concatenate([head, tail], axis=2)
+        for head, tail in zip(gate_head_pieces, gate_tail_pieces)
+    ]
     up_pieces = cp_pieces(expert_up, n_cp)
     down_pieces = cp_pieces(expert_down, n_cp)
     normed, gate_pieces = lax.optimization_barrier((normed, gate_pieces))

time: 318 us -> 323 us (1.016)
  waiting for transfers between devices: 188 us -> 179 us
  other arithmetic: 15.3 us -> 20 us
  local copies, waits for them, and re-layouts: 8.44 us -> 12.3 us
    ppermute x1, waiting for transfers between devices: 14.3 us -> 4.35 us  [shards(): lax.ppermute(summed, 'cp', [(i, (i - j) % n_cp) for i in range(n_cp)])]
    concatenate x0 -> x2, other arithmetic: none -> 3.79 us  [shards(): jnp.concatenate([head, tail], axis=2)]
    ppermute x6 -> x7, starting transfers between devices: 9.48 us -> 11.4 us  [cp_pieces(): pieces.append(lax.ppermute(x, 'cp', perm))]
    ppermute x6 -> x7, waiting for transfers between devices: 30.5 us -> 31.8 us  [cp_pieces(): pieces.append(lax.ppermute(x, 'cp', perm))]
  transfers between devices with their start and end apart: 17 -> 18, of which waited for: 12 -> 13; matrix products, arithmetic and copies ran while one was open for 20% -> 24% of each run, Pallas kernels for 0% -> 0%
where the time goes in v10:
time: 323 us; the launch traced here: 322 us
  waiting for transfers between devices  179 us (55%)
  matrix products  64.8 us (20%)
  starting transfers between devices  31.6 us (10%)
  other arithmetic  20 us (6%)
  between operations  14 us (4%)
  local copies, waits for them, and re-layouts  12.3 us (4%)
    all_gather x2, waiting for transfers between devices, shards(): lax.all_gather(jnp.concatenate([rows, id_lanes], axis=1), 'ep', axis=0, t...  50.4 us
    ppermute x7, waiting for transfers between devices, cp_pieces(): pieces.append(lax.ppermute(x, 'cp', perm))  31.8 us
    all_to_all x2, waiting for transfers between devices, shards(): lax.all_to_all(served, 'tp', split_axis=0, concat_axis=0, tiled=True)  31.2 us
    reduce_scatter x2, waiting for transfers between devices, shards(): lax.psum_scatter(partial.astype(jnp.bfloat16).reshape(n_ep, share, width)...  26.5 us
    reduce_scatter x2, waiting for transfers between devices, shards(): lax.psum_scatter(block.astype(jnp.bfloat16), 'tp', scatter_dimension=1, t...  23.5 us
    dot_general x2, matrix products, expert_rows(): jnp.einsum('rf,df->rd', hidden_act, full_down[0], preferred_element_type=...  19.7 us
    ppermute x7, starting transfers between devices, cp_pieces(): pieces.append(lax.ppermute(x, 'cp', perm))  11.4 us
    all_to_all x2, waiting for transfers between devices, shards(): lax.all_to_all(buffer.reshape(n_tp, cap2, width), 'tp', split_axis=0, con...  11 us
  transfers between devices with their start and end apart: 18, of which 13 were waited for; matrix products, arithmetic and copies ran while one was open for 24% of the time, Pallas kernels for 0%

profile of v10, /device:TPU:0, one launch (start us, length us, event | category | flops | bytes accessed | tf_op | source)
XLA Modules:
  0.0 321.7 jit_solution(1861624092134071130)
XLA Ops:
  9.7 3.0 collective-permute-start
  12.9 3.0 fusion.79
  28.3 2.6 fusion.14
  32.9 3.6 %collective-permute-done.2 = bf16[1,2048,192]{1,2,0:T(8,128)(2,1)} collective-permute-done((bf16[1,2048,192]{1,2,0:T(8,128)(2,1)}, bf16[1,2048,192]{1,2,0:T(8,128)(2,1)}, u32[]{:S(2)}, u32[]{:S(2)}) %collective-permute-start.2) | collective-permute-done | bytes 786464 | tf_op jit(solution)/shard_map/ppermute | solution.py:43
  36.4 2.2 convolution_convert_fusion.5
  40.5 22.4 %collective-permute-done.3 = bf16[512,1024]{1,0:T(8,128)(2,1)} collective-permute-done((bf16[512,1024]{1,0:T(8,128)(2,1)}, bf16[512,1024]{1,0:T(8,128)(2,1)}, u32[]{:S(2)}, u32[]{:S(2)}) %collective-permute-start.3) | collective-permute-done | bytes 1048608 | tf_op jit(solution)/shard_map/ppermute | solution.py:43
  62.9 2.3 reduce-scatter.5.cloned.1.call-done
  65.2 3.5 %convolution_convert_fusion.4 = bf16[512,1024]{1,0:T(8,128)(2,1)} fusion(bf16[512,1024]{1,0:T(8,128)(2,1)} %collective-permute-done.3, bf16[1024,1024]{1,0:T(8,128)(2,1)S(1)} %copy-done), kind=kOutput, calls=%fused_computation.40 | convolution fusion | flops 1074266112 | bytes 4194304 | tf_op jit(solution)/shard_map/dot_general | solution.py:126
  72.5 21.3 %reduce-scatter.7.cloned.1.call-done = bf16[2,64,1024]{2,1,0:T(8,128)(2,1)} async-done(((bf16[2,256,1024]{2,1,0:T(8,128)(2,1)}), bf16[2,64,1024]{2,1,0:T(8,128)(2,1)}) %reduce-scatter.7.cloned.1.call-update) | async-done | bytes 262160 | tf_op jit(solution)/shard_map/reduce_scatter | solution.py:129
  95.2 2.4 pad_maximum_fusion.1
  97.6 4.3 %collective-permute-done.4 = bf16[2,64,1024]{2,1,0:T(8,128)(2,1)S(1)} collective-permute-done((bf16[2,64,1024]{2,1,0:T(8,128)(2,1)}, bf16[2,64,1024]{2,1,0:T(8,128)(2,1)S(1)}, u32[]{:S(2)}, u32[]{:S(2)}) %collective-permute-start.4) | collective-permute-done | bytes 262176 | tf_op jit(solution)/shard_map/ppermute | solution.py:133
  106.5 27.5 %all-gather.3.cloned.1.call-done = bf16[256,2176]{1,0:T(8,128)(2,1)} async-done(((bf16[64,2176]{1,0:T(8,128)(2,1)}), bf16[256,2176]{1,0:T(8,128)(2,1)}) %all-gather.3.cloned.1.call-update) | async-done | bytes 1114128 | tf_op jit(solution)/shard_map/all_gather | solution.py:176
  135.2 5.3 %collective-permute-done.6 = bf16[1,2048,384]{2,1,0:T(8,128)(2,1)} collective-permute-done((bf16[1,2048,384]{2,1,0:T(8,128)(2,1)}, bf16[1,2048,384]{2,1,0:T(8,128)(2,1)}, u32[]{:S(2)}, u32[]{:S(2)}) %collective-permute-start.6) | collective-permute-done | bytes 1572896 | tf_op jit(solution)/shard_map/ppermute | solution.py:43
  141.3 3.4 %convolution_convert_fusion.3 = bf16[576,2048]{1,0:T(8,128)(2,1)} fusion(pred[576,256]{1,0:T(8,128)(4,1)S(1)} %fusion.3, bf16[256,2176]{1,0:T(8,128)(2,1)} %all-gather.3.cloned.1.call-done), kind=kOutput, calls=%fused_computation.19 | convolution fusion | flops 605159424 | bytes 3555328 | tf_op jit(solution)/shard_map/dot_general | solution.py:207
  145.5 4.7 %all-to-all-start = ((bf16[4,144,2048]{2,1,0:T(8,128)(2,1)}), bf16[4,144,2048]{2,1,0:T(8,128)(2,1)}, u32[]{:S(2)}, u32[]{:S(2)}) async-start(bf16[4,144,2048]{2,1,0:T(8,128)(2,1)} %bitcast.117), calls=%async_computation.2 | async-start | bytes 4718592 | tf_op jit(solution)/shard_map/all_to_all | solution.py:210
  151.7 22.9 %all-gather.5.cloned.1.call-done = bf16[256,2176]{1,0:T(8,128)(2,1)} async-done(((bf16[64,2176]{1,0:T(8,128)(2,1)}), bf16[256,2176]{1,0:T(8,128)(2,1)}) %all-gather.5.cloned.1.call-update) | async-done | bytes 1114128 | tf_op jit(solution)/shard_map/all_gather | solution.py:176
  176.7 3.5 %convolution_convert_fusion.2 = bf16[576,2048]{1,0:T(8,128)(2,1)} fusion(pred[576,256]{1,0:T(8,128)(4,1)S(1)} %fusion.2, bf16[256,2176]{1,0:T(8,128)(2,1)} %all-gather.5.cloned.1.call-done), kind=kOutput, calls=%fused_computation.18 | convolution fusion | flops 605159424 | bytes 3555328 | tf_op jit(solution)/shard_map/dot_general | solution.py:207
  180.2 4.6 %all-to-all-start.2 = ((bf16[4,144,2048]{2,1,0:T(8,128)(2,1)}), bf16[4,144,2048]{2,1,0:T(8,128)(2,1)}, u32[]{:S(2)}, u32[]{:S(2)}) async-start(bf16[4,144,2048]{2,1,0:T(8,128)(2,1)} %bitcast.118), calls=%async_computation.5 | async-start | bytes 4718592 | tf_op jit(solution)/shard_map/all_to_all | solution.py:210
  187.1 5.4 %fusion.18 = f32[576,768]{1,0:T(8,128)} fusion(bf16[576,2048]{1,0:T(8,128)(2,1)} %bitcast.15, bf16[1,2048,384]{1,2,0:T(8,128)(2,1)} %pad_maximum_fusion.1, bf16[1,2048,384]{1,2,0:T(8,128)(2,1)S(1)} %copy-done.7), kind=kOutput, calls=%fused_computation.35 | convolution fusion | flops 1818230784 | bytes 7274496 | tf_op jit(solution)/shard_map/dot_general | solution.py:50
  192.4 9.9 %convolution_convert_fusion.1 = bf16[576,2048]{1,0:T(8,128)(2,1)} fusion(bf16[1,2048,384]{2,1,0:T(8,128)(2,1)} %collective-permute-done.7, bf16[1,2048,384]{2,1,0:T(8,128)(2,1)} %param.27, f32[576,768]{1,0:T(8,128)} %fusion.18, bf16[576,2048]{1,0:T(8,128)(2,1)} %bitcast.15, bf16[1,2048,384]{2,1,0:T(8,128)(2,1)} %collective-permute-done.6, ...), kind=kOutput, calls=%fused_computation.17 | convolution fusion | flops 3640295424 | bytes 12779520 | tf_op jit(solution)/shard_map/rf,df->rd/dot_general | solution.py:53
  202.3 11.0 %all-to-all-done.2 = bf16[4,144,2048]{2,1,0:T(8,128)(2,1)} async-done(((bf16[4,144,2048]{2,1,0:T(8,128)(2,1)}), bf16[4,144,2048]{2,1,0:T(8,128)(2,1)}, u32[]{:S(2)}, u32[]{:S(2)}) %all-to-all-start.2) | async-done | bytes 2359328 | tf_op jit(solution)/shard_map/all_to_all | solution.py:210
  213.4 4.7 %all-to-all-start.1 = ((bf16[4,144,2048]{2,1,0:T(8,128)(2,1)}), bf16[4,144,2048]{2,1,0:T(8,128)(2,1)}, u32[]{:S(2)}, u32[]{:S(2)}) async-start(bf16[4,144,2048]{2,1,0:T(8,128)(2,1)} %bitcast.125), calls=%async_computation.3 | async-start | bytes 4718592 | tf_op jit(solution)/shard_map/all_to_all | solution.py:217
  219.5 5.4 %fusion.17 = f32[576,768]{1,0:T(8,128)} fusion(bf16[576,2048]{1,0:T(8,128)(2,1)} %bitcast.26, bf16[1,2048,384]{1,2,0:T(8,128)(2,1)} %pad_maximum_fusion.1, bf16[1,2048,384]{1,2,0:T(8,128)(2,1)S(1)} %copy-done.7), kind=kOutput, calls=%fused_computation.34 | convolution fusion | flops 1818230784 | bytes 7274496 | tf_op jit(solution)/shard_map/dot_general | solution.py:50
  224.9 9.9 %convolution_convert_fusion = bf16[576,2048]{1,0:T(8,128)(2,1)} fusion(bf16[1,2048,384]{2,1,0:T(8,128)(2,1)} %collective-permute-done.7, bf16[1,2048,384]{2,1,0:T(8,128)(2,1)} %param.27, f32[576,768]{1,0:T(8,128)} %fusion.17, bf16[576,2048]{1,0:T(8,128)(2,1)} %bitcast.26, bf16[1,2048,384]{2,1,0:T(8,128)(2,1)} %collective-permute-done.6, ...), kind=kOutput, calls=%fused_computation.16 | convolution fusion | flops 3640295424 | bytes 12779520 | tf_op jit(solution)/shard_map/rf,df->rd/dot_general | solution.py:53
  234.7 11.7 %all-to-all-done.1 = bf16[4,144,2048]{2,1,0:T(8,128)(2,1)} async-done(((bf16[4,144,2048]{2,1,0:T(8,128)(2,1)}), bf16[4,144,2048]{2,1,0:T(8,128)(2,1)}, u32[]{:S(2)}, u32[]{:S(2)}) %all-to-all-start.1) | async-done | bytes 2359328 | tf_op jit(solution)/shard_map/all_to_all | solution.py:217
  246.4 4.5 %all-to-all-start.3 = ((bf16[4,144,2048]{2,1,0:T(8,128)(2,1)}), bf16[4,144,2048]{2,1,0:T(8,128)(2,1)}, u32[]{:S(2)}, u32[]{:S(2)}) async-start(bf16[4,144,2048]{2,1,0:T(8,128)(2,1)} %bitcast.124), calls=%async_computation.6 | async-start | bytes 4718592 | tf_op jit(solution)/shard_map/all_to_all | solution.py:217
  251.0 2.9 fusion.42
  253.9 3.6 %fusion.9 = bf16[256,2048]{1,0:T(8,128)(2,1)} fusion(f32[256,2048]{1,0:T(8,128)S(1)} %fusion.42, bf16[576,2048]{1,0:T(8,128)(2,1)} %bitcast.20, f32[576,256]{1,0:T(8,128)S(1)} %copy-done.3), kind=kOutput, calls=%fused_computation.22 | convolution fusion | flops 605618176 | bytes 6094848 | tf_op jit(solution)/shard_map/dot_general | solution.py:225
  259.9 19.5 %all-to-all-done.3 = bf16[4,144,2048]{2,1,0:T(8,128)(2,1)} async-done(((bf16[4,144,2048]{2,1,0:T(8,128)(2,1)}), bf16[4,144,2048]{2,1,0:T(8,128)(2,1)}, u32[]{:S(2)}, u32[]{:S(2)}) %all-to-all-start.3) | async-done | bytes 2359328 | tf_op jit(solution)/shard_map/all_to_all | solution.py:217
  279.5 2.7 fusion.39
  282.2 4.2 %fusion.10 = bf16[256,2048]{1,0:T(8,128)(2,1)} fusion(f32[256,2048]{1,0:T(8,128)S(1)} %fusion.39, bf16[576,2048]{1,0:T(8,128)(2,1)} %bitcast.28, f32[576,256]{1,0:T(8,128)} %copy-done.4), kind=kOutput, calls=%fused_computation.23 | convolution fusion | flops 605618176 | bytes 6094848 | tf_op jit(solution)/shard_map/dot_general | solution.py:225
  286.4 26.5 %reduce-scatter.11.cloned.1.call-done = bf16[1,64,2048]{2,1,0:T(8,128)(2,1)} async-done(((bf16[4,64,2048]{2,1,0:T(8,128)(2,1)}), bf16[1,64,2048]{2,1,0:T(8,128)(2,1)}) %reduce-scatter.11.cloned.1.call-update) | async-done | bytes 262160 | tf_op jit(solution)/shard_map/reduce_scatter | solution.py:227
  (128 shorter events, 43.5 us)
Async XLA Ops:
  6.5 29.9 %copy-start = (bf16[1024,1024]{1,0:T(8,128)(2,1)S(1)}, bf16[1024,1024]{1,0:T(8,128)(2,1)}, u32[]{:S(2)}) copy-start(bf16[1024,1024]{1,0:T(8,128)(2,1)} %param.20) | copy-start | bytes 6291460
  6.5 58.6 %reduce-scatter.5.cloned.1.call-start = ((), (), s32[]{:S(2)}) async-start(), calls=%async_computation.8 | async-start | bytes 1310720 | tf_op jit(solution)/shard_map/reduce_scatter | solution.py:129
  9.7 15.3 %collective-permute-start = (bf16[2,256,256]{2,1,0:T(8,128)(2,1)S(1)}, bf16[2,256,256]{2,1,0:T(8,128)(2,1)}, u32[]{:S(2)}, u32[]{:S(2)}) collective-permute-start(bf16[2,256,256]{2,1,0:T(8,128)(2,1)S(1)} %pad_maximum_fusion.3), channel_id=1, source_target_pairs={{0,16},{16,0},{1,17},{17,1},{2,18},{18,2},{3,19},{19,3},{4,20},{20... | collective-permute-start | bytes 786440 | tf_op jit(solution)/shard_map/ppermute | solution.py:43
  12.8 12.0 %collective-permute-start.1 = (s32[2,256]{1,0:T(2,128)}, s32[2,256]{1,0:T(2,128)S(1)}, u32[]{:S(2)}, u32[]{:S(2)}) collective-permute-start(s32[2,256]{1,0:T(2,128)} %param.17), channel_id=1, source_target_pairs={{0,16},{16,0},{1,17},{17,1},{2,18},{18,2},{3,19},{19,3},{4,20},{20... | collective-permute-start | bytes 6152 | tf_op jit(solution)/shard_map/ppermute | solution.py:43
  17.1 19.3 %collective-permute-start.2 = (bf16[1,2048,192]{1,2,0:T(8,128)(2,1)}, bf16[1,2048,192]{1,2,0:T(8,128)(2,1)}, u32[]{:S(2)}, u32[]{:S(2)}) collective-permute-start(bf16[1,2048,192]{1,2,0:T(8,128)(2,1)} %copy.101), channel_id=1, source_target_pairs={{0,16},{16,0},{1,17},{17,1},{2,18},{18,2},{3,19},{19,3},{4,20},{20... | collective-permute-start | bytes 2359304 | tf_op jit(solution)/shard_map/ppermute | solution.py:43
  19.1 3.8 %copy-start.14 = (f32[128]{0:T(128)S(1)}, f32[128]{0:T(128)}, u32[]{:S(2)}) copy-start(f32[128]{0:T(128)} %param.18) | copy-start | bytes 1540
  22.5 2.2 copy-start.12
  22.6 2.5 copy-start.9
  32.9 5.8 %copy-start.8 = (bf16[64,8,8,128]{3,1,2,0:T(8,128)(2,1)}, bf16[64,8,8,128]{3,1,2,0:T(8,128)(2,1)S(1)}, u32[]{:S(2)}) copy-start(bf16[64,8,8,128]{3,1,2,0:T(8,128)(2,1)S(1)} %copy.118) | copy-start | bytes 3145732
  38.7 30.0 %copy-start.5 = (bf16[1,2048,192]{2,1,0:T(8,128)(2,1)S(1)}, bf16[1,2048,192]{2,1,0:T(8,128)(2,1)}, u32[]{:S(2)}) copy-start(bf16[1,2048,192]{2,1,0:T(8,128)(2,1)} %get-tuple-element.57) | copy-start | bytes 2359300
  38.7 55.0 %reduce-scatter.7.cloned.1.call-start = ((), (), s32[]{:S(2)}) async-start(), calls=%async_computation.9 | async-start | bytes 1310720 | tf_op jit(solution)/shard_map/reduce_scatter | solution.py:129
  38.8 24.1 %collective-permute-start.3 = (bf16[512,1024]{1,0:T(8,128)(2,1)}, bf16[512,1024]{1,0:T(8,128)(2,1)}, u32[]{:S(2)}, u32[]{:S(2)}) collective-permute-start(bf16[512,1024]{1,0:T(8,128)(2,1)} %bitcast.129), channel_id=1, source_target_pairs={{0,16},{16,0},{1,17},{17,1},{2,18},{18,2},{3,19},{19,3},{4,20},{20... | collective-permute-start | bytes 3145736 | tf_op jit(solution)/shard_map/ppermute | solution.py:43
  68.6 2.5 copy-start.6
  68.7 65.3 %all-gather.3.cloned.1.call-start = ((), (), s32[]{:S(2)}) async-start(), calls=%async_computation.10 | async-start | bytes 1392640 | tf_op jit(solution)/shard_map/all_gather | solution.py:176
  69.5 25.7 %collective-permute-start.5 = (bf16[1,2048,192]{1,2,0:T(8,128)(2,1)S(1)}, bf16[1,2048,192]{1,2,0:T(8,128)(2,1)S(1)}, u32[]{:S(2)}, u32[]{:S(2)}) collective-permute-start(bf16[1,2048,192]{1,2,0:T(8,128)(2,1)S(1)} %copy.102), channel_id=1, source_target_pairs={{0,16},{16,0},{1,17},{17,1},{2,18},{18,2},{3,19},{19,3},{4,20},{20... | collective-permute-start | bytes 2359304 | tf_op jit(solution)/shard_map/ppermute | solution.py:43
  72.5 29.5 %copy-start.10 = (bf16[2,64,1024]{2,1,0:T(8,128)(2,1)S(1)}, bf16[2,64,1024]{2,1,0:T(8,128)(2,1)}, u32[]{:S(2)}) copy-start(bf16[2,64,1024]{2,1,0:T(8,128)(2,1)} %reduce-scatter.5.cloned.1.call-done) | copy-start | bytes 786436
  93.7 8.2 %collective-permute-start.4 = (bf16[2,64,1024]{2,1,0:T(8,128)(2,1)}, bf16[2,64,1024]{2,1,0:T(8,128)(2,1)S(1)}, u32[]{:S(2)}, u32[]{:S(2)}) collective-permute-start(bf16[2,64,1024]{2,1,0:T(8,128)(2,1)} %reduce-scatter.7.cloned.1.call-done), channel_id=1, source_target_pairs={{0,16},{16,0},{1,17},{17,1},{2,18},{18,2},{3,19},{19,3},{4,20},{20... | collective-permute-start | bytes 786440 | tf_op jit(solution)/shard_map/ppermute | solution.py:133
  102.3 1.5 copy-start.11
  104.8 69.8 %all-gather.5.cloned.1.call-start = ((), (), s32[]{:S(2)}) async-start(), calls=%async_computation.12 | async-start | bytes 1392640 | tf_op jit(solution)/shard_map/all_gather | solution.py:176
  104.9 35.6 %collective-permute-start.6 = (bf16[1,2048,384]{2,1,0:T(8,128)(2,1)}, bf16[1,2048,384]{2,1,0:T(8,128)(2,1)}, u32[]{:S(2)}, u32[]{:S(2)}) collective-permute-start(bf16[1,2048,384]{2,1,0:T(8,128)(2,1)} %param.26), channel_id=1, source_target_pairs={{0,16},{16,0},{1,17},{17,1},{2,18},{18,2},{3,19},{19,3},{4,20},{20... | collective-permute-start | bytes 4718600 | tf_op jit(solution)/shard_map/ppermute | solution.py:43
  145.5 34.7 %all-to-all-start = ((bf16[4,144,2048]{2,1,0:T(8,128)(2,1)}), bf16[4,144,2048]{2,1,0:T(8,128)(2,1)}, u32[]{:S(2)}, u32[]{:S(2)}) async-start(bf16[4,144,2048]{2,1,0:T(8,128)(2,1)} %bitcast.117), calls=%async_computation.2 | async-start | bytes 4718592 | tf_op jit(solution)/shard_map/all_to_all | solution.py:210
  150.2 36.9 %collective-permute-start.7 = (bf16[1,2048,384]{2,1,0:T(8,128)(2,1)}, bf16[1,2048,384]{2,1,0:T(8,128)(2,1)}, u32[]{:S(2)}, u32[]{:S(2)}) collective-permute-start(bf16[1,2048,384]{2,1,0:T(8,128)(2,1)} %param.27), channel_id=1, source_target_pairs={{0,16},{16,0},{1,17},{17,1},{2,18},{18,2},{3,19},{19,3},{4,20},{20... | collective-permute-start | bytes 4718600 | tf_op jit(solution)/shard_map/ppermute | solution.py:43
  180.1 4.6 %copy-start.15 = (bf16[2048,16]{0,1:T(8,128)(2,1)S(1)}, bf16[2048,16]{0,1:T(8,128)(2,1)}, u32[]{:S(2)}) copy-start(bf16[2048,16]{0,1:T(8,128)(2,1)} %param.23) | copy-start | bytes 196612
  180.1 6.9 %copy-start.7 = (bf16[1,2048,384]{1,2,0:T(8,128)(2,1)S(1)}, bf16[1,2048,384]{1,2,0:T(8,128)(2,1)}, u32[]{:S(2)}) copy-start(bf16[1,2048,384]{1,2,0:T(8,128)(2,1)} %pad_maximum_fusion) | copy-start | bytes 4718596
  180.2 33.2 %all-to-all-start.2 = ((bf16[4,144,2048]{2,1,0:T(8,128)(2,1)}), bf16[4,144,2048]{2,1,0:T(8,128)(2,1)}, u32[]{:S(2)}, u32[]{:S(2)}) async-start(bf16[4,144,2048]{2,1,0:T(8,128)(2,1)} %bitcast.118), calls=%async_computation.5 | async-start | bytes 4718592 | tf_op jit(solution)/shard_map/all_to_all | solution.py:210
  213.4 33.1 %all-to-all-start.1 = ((bf16[4,144,2048]{2,1,0:T(8,128)(2,1)}), bf16[4,144,2048]{2,1,0:T(8,128)(2,1)}, u32[]{:S(2)}, u32[]{:S(2)}) async-start(bf16[4,144,2048]{2,1,0:T(8,128)(2,1)} %bitcast.125), calls=%async_computation.3 | async-start | bytes 4718592 | tf_op jit(solution)/shard_map/all_to_all | solution.py:217
  246.4 33.1 %all-to-all-start.3 = ((bf16[4,144,2048]{2,1,0:T(8,128)(2,1)}), bf16[4,144,2048]{2,1,0:T(8,128)(2,1)}, u32[]{:S(2)}, u32[]{:S(2)}) async-start(bf16[4,144,2048]{2,1,0:T(8,128)(2,1)} %bitcast.124), calls=%async_computation.6 | async-start | bytes 4718592 | tf_op jit(solution)/shard_map/all_to_all | solution.py:217
  250.9 35.5 %reduce-scatter.9.cloned.1.call-start = ((), (), s32[]{:S(2)}) async-start(), calls=%async_computation.11 | async-start | bytes 1310720 | tf_op jit(solution)/shard_map/reduce_scatter | solution.py:227
  251.0 2.9 copy-start.3
  257.6 55.3 %reduce-scatter.11.cloned.1.call-start = ((), (), s32[]{:S(2)}) async-start(), calls=%async_computation.13 | async-start | bytes 1310720 | tf_op jit(solution)/shard_map/reduce_scatter | solution.py:227
  259.9 19.6 %copy-start.4 = (f32[576,256]{1,0:T(8,128)}, f32[576,256]{1,0:T(8,128)S(1)}, u32[]{:S(2)}) copy-start(f32[576,256]{1,0:T(8,128)S(1)} %select_reduce_fusion) | copy-start | bytes 1769476
  282.2 32.6 %copy-start.1 = (bf16[1024,1024]{1,0:T(8,128)(2,1)S(1)}, bf16[1024,1024]{1,0:T(8,128)(2,1)}, u32[]{:S(2)}) copy-start(bf16[1024,1024]{1,0:T(8,128)(2,1)} %param.20) | copy-start | bytes 6291460
  (2 other events, 2.1 us)
Sparse Core Ops, SparseCore 0:
  38.8 26.2 reduce-scatter.4
  68.8 24.8 reduce-scatter.6
  104.9 29.0 all-gather.2
  145.6 29.0 all-gather.4
  257.7 27.0 reduce-scatter.8
  287.0 25.8 reduce-scatter.10

commit v11 on v9

--- a/solution.py
+++ b/solution.py
@@ -147,9 +147,10 @@
         (attn_pieces, expert_gate, expert_up, expert_down)
     )
     gate_pieces = cp_pieces(expert_gate, n_cp)
-    up_pieces = cp_pieces(expert_up, n_cp)
-    down_pieces = cp_pieces(expert_down, n_cp)
     normed, gate_pieces = lax.optimization_barrier((normed, gate_pieces))
+    up_down = jnp.concatenate([expert_up, expert_down], axis=2)
+    gate_pieces, up_down = lax.optimization_barrier((gate_pieces, up_down))
+    up_down_pieces = cp_pieces(up_down, n_cp)
 
     lanes = 128
     cap2 = n_ep * cap
@@ -189,9 +190,7 @@
         )
         target = jnp.where(mine, dest * cap2 + rank_of, jnp.int32(-1)).T
         if chunk == 0:
-            target, up_pieces = lax.optimization_barrier((target, up_pieces))
             full_gate = jnp.concatenate(gate_pieces, axis=2)
-            full_up = jnp.concatenate(up_pieces, axis=2)
         hit = target[:, None, :] == jnp.arange(n_slots, dtype=jnp.int32)[None, :, None]
         select = jnp.any(hit, axis=0).astype(jnp.bfloat16)
         weight = jnp.sum(jnp.where(hit, gates_all.T[:, None, :], jnp.float32(0.0)), axis=0)
@@ -203,8 +202,10 @@
             buffer.reshape(n_tp, cap2, width), "tp", split_axis=0, concat_axis=0, tiled=True
         )
         if chunk == 0:
-            received, down_pieces = lax.optimization_barrier((received, down_pieces))
-            full_down = jnp.concatenate(down_pieces, axis=2)
+            received, up_down_pieces = lax.optimization_barrier((received, up_down_pieces))
+            units = expert_up.shape[2]
+            full_up = jnp.concatenate([p[:, :, :units] for p in up_down_pieces], axis=2)
+            full_down = jnp.concatenate([p[:, :, units:] for p in up_down_pieces], axis=2)
         served = expert_rows(received, full_gate, full_up, full_down)
         back = lax.all_to_all(served, "tp", split_axis=0, concat_axis=0, tiled=True).reshape(
             n_slots, width

time: 318 us -> 312 us (0.981)
  waiting for transfers between devices: 188 us -> 177 us
  local copies, waits for them, and re-layouts: 8.44 us -> 13.9 us
  other arithmetic: 15.3 us -> 18.5 us
    ppermute x6 -> x5, waiting for transfers between devices: 30.5 us -> 24.9 us  [cp_pieces(): pieces.append(lax.ppermute(x, 'cp', perm))]
    slice x0 -> x1, local copies, waits for them, and re-layouts: none -> 5.2 us  [shards(): full_up = jnp.concatenate([p[:, :, :units] for p in up_down_pieces], axis=2)]
    concatenate x0 -> x1, other arithmetic: none -> 3.32 us  [shards(): up_down = jnp.concatenate([expert_up, expert_down], axis=2)]
    ppermute x6 -> x5, starting transfers between devices: 9.48 us -> 6.17 us  [cp_pieces(): pieces.append(lax.ppermute(x, 'cp', perm))]
  transfers between devices with their start and end apart: 17 -> 16, of which waited for: 12 -> 10; matrix products, arithmetic and copies ran while one was open for 20% -> 26% of each run, Pallas kernels for 0% -> 0%
where the time goes in v11:
time: 312 us; the launch traced here: 311 us
  waiting for transfers between devices  177 us (57%)
  matrix products  60.9 us (20%)
  starting transfers between devices  26.6 us (9%)
  other arithmetic  18.5 us (6%)
  between operations  14 us (4%)
  local copies, waits for them, and re-layouts  13.9 us (4%)
    all_gather x2, waiting for transfers between devices, shards(): lax.all_gather(jnp.concatenate([rows, id_lanes], axis=1), 'ep', axis=0, t...  47.3 us
    all_to_all x2, waiting for transfers between devices, shards(): lax.all_to_all(served, 'tp', split_axis=0, concat_axis=0, tiled=True)  31.1 us
    reduce_scatter x2, waiting for transfers between devices, shards(): lax.psum_scatter(partial.astype(jnp.bfloat16).reshape(n_ep, share, width)...  26.5 us
    ppermute x5, waiting for transfers between devices, cp_pieces(): pieces.append(lax.ppermute(x, 'cp', perm))  24.9 us
    reduce_scatter x2, waiting for transfers between devices, shards(): lax.psum_scatter(block.astype(jnp.bfloat16), 'tp', scatter_dimension=1, t...  24.5 us
    dot_general x2, matrix products, expert_rows(): jnp.einsum('rf,df->rd', hidden_act, full_down[0], preferred_element_type=...  18.8 us
    ppermute x1, waiting for transfers between devices, shards(): lax.ppermute(summed, 'cp', [(i, (i - j) % n_cp) for i in range(n_cp)])  14.4 us
    dot_general x2, matrix products, expert_rows(): jnp.dot(flat_rows, full_gate[0], preferred_element_type=jnp.float32)  11.2 us
  transfers between devices with their start and end apart: 16, of which 10 were waited for; matrix products, arithmetic and copies ran while one was open for 26% of the time, Pallas kernels for 0%

profile of v11, /device:TPU:0, one launch (start us, length us, event | category | flops | bytes accessed | tf_op | source)
XLA Modules:
  0.0 311.3 jit_solution(12733667623735496090)
XLA Ops:
  6.5 3.0 collective-permute-start.1
  16.5 1.9 fusion.13
  20.4 2.2 fusion
  25.3 2.3 fusion.23
  27.6 1.7 copy.86
  30.1 23.3 %collective-permute-done.2 = bf16[512,1024]{1,0:T(8,128)(2,1)S(1)} collective-permute-done((bf16[512,1024]{1,0:T(8,128)(2,1)S(1)}, bf16[512,1024]{1,0:T(8,128)(2,1)S(1)}, u32[]{:S(2)}, u32[]{:S(2)}) %collective-permute-start.2) | collective-permute-done | bytes 1048608 | tf_op jit(solution)/shard_map/ppermute | solution.py:43
  53.4 2.2 convolution_convert_fusion.4
  56.8 24.5 %reduce-scatter.7.cloned.1.call-done = bf16[2,64,1024]{2,1,0:T(8,128)(2,1)} async-done(((bf16[2,256,1024]{2,1,0:T(8,128)(2,1)}), bf16[2,64,1024]{2,1,0:T(8,128)(2,1)}) %reduce-scatter.7.cloned.1.call-update) | async-done | bytes 262160 | tf_op jit(solution)/shard_map/reduce_scatter | solution.py:125
  82.9 14.4 %collective-permute-done.3 = bf16[2,64,1024]{2,1,0:T(8,128)(2,1)S(1)} collective-permute-done((bf16[2,64,1024]{2,1,0:T(8,128)(2,1)}, bf16[2,64,1024]{2,1,0:T(8,128)(2,1)S(1)}, u32[]{:S(2)}, u32[]{:S(2)}) %collective-permute-start.3) | collective-permute-done | bytes 262176 | tf_op jit(solution)/shard_map/ppermute | solution.py:129
  100.6 3.3 %pad_maximum_fusion = bf16[1,2048,768]{2,1,0:T(8,128)(2,1)} fusion(bf16[1,2048,384]{2,1,0:T(8,128)(2,1)S(1)} %copy-done.6, bf16[1,2048,384]{2,1,0:T(8,128)(2,1)} %param.26), kind=kLoop, calls=%fused_computation.13 | loop fusion | flops 6291456 | bytes 6291456 | tf_op jit(solution)/shard_map/concatenate | solution.py:151
  105.4 24.0 %all-gather.3.cloned.1.call-done = bf16[256,2176]{1,0:T(8,128)(2,1)} async-done(((bf16[64,2176]{1,0:T(8,128)(2,1)}), bf16[256,2176]{1,0:T(8,128)(2,1)}) %all-gather.3.cloned.1.call-update) | async-done | bytes 1114128 | tf_op jit(solution)/shard_map/all_gather | solution.py:169
  131.4 3.4 %convolution_convert_fusion.3 = bf16[576,2048]{1,0:T(8,128)(2,1)} fusion(pred[576,256]{1,0:T(8,128)(4,1)S(1)} %fusion.3, bf16[256,2176]{1,0:T(8,128)(2,1)} %all-gather.3.cloned.1.call-done), kind=kOutput, calls=%fused_computation.20 | convolution fusion | flops 605159424 | bytes 3555328 | tf_op jit(solution)/shard_map/dot_general | solution.py:198
  135.6 4.8 %all-to-all-start = ((bf16[4,144,2048]{2,1,0:T(8,128)(2,1)}), bf16[4,144,2048]{2,1,0:T(8,128)(2,1)}, u32[]{:S(2)}, u32[]{:S(2)}) async-start(bf16[4,144,2048]{2,1,0:T(8,128)(2,1)} %bitcast.121), calls=%async_computation.2 | async-start | bytes 4718592 | tf_op jit(solution)/shard_map/all_to_all | solution.py:201
  140.9 23.3 %all-gather.5.cloned.1.call-done = bf16[256,2176]{1,0:T(8,128)(2,1)} async-done(((bf16[64,2176]{1,0:T(8,128)(2,1)}), bf16[256,2176]{1,0:T(8,128)(2,1)}) %all-gather.5.cloned.1.call-update) | async-done | bytes 1114128 | tf_op jit(solution)/shard_map/all_gather | solution.py:169
  166.3 3.4 %convolution_convert_fusion.2 = bf16[576,2048]{1,0:T(8,128)(2,1)} fusion(pred[576,256]{1,0:T(8,128)(4,1)S(1)} %fusion.2, bf16[256,2176]{1,0:T(8,128)(2,1)} %all-gather.5.cloned.1.call-done), kind=kOutput, calls=%fused_computation.19 | convolution fusion | flops 605159424 | bytes 3555328 | tf_op jit(solution)/shard_map/dot_general | solution.py:198
  169.7 4.6 %all-to-all-start.2 = ((bf16[4,144,2048]{2,1,0:T(8,128)(2,1)}), bf16[4,144,2048]{2,1,0:T(8,128)(2,1)}, u32[]{:S(2)}, u32[]{:S(2)}) async-start(bf16[4,144,2048]{2,1,0:T(8,128)(2,1)} %bitcast.122), calls=%async_computation.5 | async-start | bytes 4718592 | tf_op jit(solution)/shard_map/all_to_all | solution.py:201
  174.4 5.4 %fusion.20 = f32[576,768]{1,0:T(8,128)} fusion(bf16[576,2048]{1,0:T(8,128)(2,1)} %bitcast.16, bf16[1,2048,384]{2,1,0:T(8,128)(2,1)} %collective-permute-done.4, bf16[1,2048,384]{2,1,0:T(8,128)(2,1)S(1)} %copy-done.14), kind=kOutput, calls=%fused_computation.38 | convolution fusion | flops 1818230784 | bytes 7274496 | tf_op jit(solution)/shard_map/dot_general | solution.py:50
  179.7 5.2 %fusion.84 = (bf16[1,2048,384]{2,1,0:T(8,128)(2,1)S(1)}, bf16[1,2048,384]{2,1,0:T(8,128)(2,1)}, bf16[1,2048,384]{2,1,0:T(8,128)(2,1)}, bf16[1,2048,384]{2,1,0:T(8,128)(2,1)}) fusion(bf16[1,2048,768]{2,1,0:T(8,128)(2,1)} %pad_maximum_fusion, bf16[1,2048,768]{2,1,0:T(8,128)(2,1)} %collective-permute-done.5), kind=kLoop, calls=%fused_computation.160 | loop fusion | bytes 12582912 | tf_op jit(solution)/shard_map/slice | solution.py:207
  184.9 9.4 %convolution_convert_fusion.1 = bf16[576,2048]{1,0:T(8,128)(2,1)} fusion(bf16[1,2048,384]{2,1,0:T(8,128)(2,1)} %get-tuple-element.61, bf16[1,2048,384]{2,1,0:T(8,128)(2,1)} %get-tuple-element.52, f32[576,768]{1,0:T(8,128)} %fusion.20, bf16[576,2048]{1,0:T(8,128)(2,1)} %bitcast.16, bf16[1,2048,384]{2,1,0:T(8,128)(2,1)} %get-tuple-element.62, ...), kind=kOutput, calls=%fused_computation.18 | convolution fusion | flops 3640295424 | bytes 12779520 | tf_op jit(solution)/shard_map/rf,df->rd/dot_general | solution.py:53
  194.3 8.6 %all-to-all-done.2 = bf16[4,144,2048]{2,1,0:T(8,128)(2,1)} async-done(((bf16[4,144,2048]{2,1,0:T(8,128)(2,1)}), bf16[4,144,2048]{2,1,0:T(8,128)(2,1)}, u32[]{:S(2)}, u32[]{:S(2)}) %all-to-all-start.2) | async-done | bytes 2359328 | tf_op jit(solution)/shard_map/all_to_all | solution.py:201
  202.9 4.7 %all-to-all-start.1 = ((bf16[4,144,2048]{2,1,0:T(8,128)(2,1)}), bf16[4,144,2048]{2,1,0:T(8,128)(2,1)}, u32[]{:S(2)}, u32[]{:S(2)}) async-start(bf16[4,144,2048]{2,1,0:T(8,128)(2,1)} %bitcast.130), calls=%async_computation.3 | async-start | bytes 4718592 | tf_op jit(solution)/shard_map/all_to_all | solution.py:210
  209.1 5.8 %fusion.19 = f32[576,768]{1,0:T(8,128)} fusion(bf16[576,2048]{1,0:T(8,128)(2,1)} %bitcast.27, bf16[1,2048,384]{2,1,0:T(8,128)(2,1)} %collective-permute-done.4, bf16[1,2048,384]{2,1,0:T(8,128)(2,1)} %param.25), kind=kOutput, calls=%fused_computation.37 | convolution fusion | flops 1818230784 | bytes 7274496 | tf_op jit(solution)/shard_map/dot_general | solution.py:50
  214.9 9.4 %convolution_convert_fusion = bf16[576,2048]{1,0:T(8,128)(2,1)} fusion(bf16[1,2048,384]{2,1,0:T(8,128)(2,1)} %get-tuple-element.61, bf16[1,2048,384]{2,1,0:T(8,128)(2,1)} %get-tuple-element.52, f32[576,768]{1,0:T(8,128)} %fusion.19, bf16[576,2048]{1,0:T(8,128)(2,1)} %bitcast.27, bf16[1,2048,384]{2,1,0:T(8,128)(2,1)} %get-tuple-element.62, ...), kind=kOutput, calls=%fused_computation.17 | convolution fusion | flops 3640295424 | bytes 12779520 | tf_op jit(solution)/shard_map/rf,df->rd/dot_general | solution.py:53
  224.3 11.6 %all-to-all-done.1 = bf16[4,144,2048]{2,1,0:T(8,128)(2,1)} async-done(((bf16[4,144,2048]{2,1,0:T(8,128)(2,1)}), bf16[4,144,2048]{2,1,0:T(8,128)(2,1)}, u32[]{:S(2)}, u32[]{:S(2)}) %all-to-all-start.1) | async-done | bytes 2359328 | tf_op jit(solution)/shard_map/all_to_all | solution.py:210
  236.0 4.5 %all-to-all-start.3 = ((bf16[4,144,2048]{2,1,0:T(8,128)(2,1)}), bf16[4,144,2048]{2,1,0:T(8,128)(2,1)}, u32[]{:S(2)}, u32[]{:S(2)}) async-start(bf16[4,144,2048]{2,1,0:T(8,128)(2,1)} %bitcast.129), calls=%async_computation.6 | async-start | bytes 4718592 | tf_op jit(solution)/shard_map/all_to_all | solution.py:210
  240.6 2.9 fusion.47
  243.5 3.7 %fusion.9 = bf16[256,2048]{1,0:T(8,128)(2,1)} fusion(f32[256,2048]{1,0:T(8,128)S(1)} %fusion.47, bf16[576,2048]{1,0:T(8,128)(2,1)} %bitcast.21, f32[576,256]{1,0:T(8,128)S(1)} %copy-done.3), kind=kOutput, calls=%fused_computation.23 | convolution fusion | flops 605618176 | bytes 6094848 | tf_op jit(solution)/shard_map/dot_general | solution.py:218
  249.6 19.5 %all-to-all-done.3 = bf16[4,144,2048]{2,1,0:T(8,128)(2,1)} async-done(((bf16[4,144,2048]{2,1,0:T(8,128)(2,1)}), bf16[4,144,2048]{2,1,0:T(8,128)(2,1)}, u32[]{:S(2)}, u32[]{:S(2)}) %all-to-all-start.3) | async-done | bytes 2359328 | tf_op jit(solution)/shard_map/all_to_all | solution.py:210
  269.1 2.7 fusion.44
  271.8 4.2 %fusion.10 = bf16[256,2048]{1,0:T(8,128)(2,1)} fusion(f32[256,2048]{1,0:T(8,128)S(1)} %fusion.44, bf16[576,2048]{1,0:T(8,128)(2,1)} %bitcast.29, f32[576,256]{1,0:T(8,128)} %copy-done.4), kind=kOutput, calls=%fused_computation.24 | convolution fusion | flops 605618176 | bytes 6094848 | tf_op jit(solution)/shard_map/dot_general | solution.py:218
  276.0 26.5 %reduce-scatter.11.cloned.1.call-done = bf16[1,64,2048]{2,1,0:T(8,128)(2,1)} async-done(((bf16[4,64,2048]{2,1,0:T(8,128)(2,1)}), bf16[1,64,2048]{2,1,0:T(8,128)(2,1)}) %reduce-scatter.11.cloned.1.call-update) | async-done | bytes 262160 | tf_op jit(solution)/shard_map/reduce_scatter | solution.py:220
  302.5 1.9 add_convert_fusion
  (121 shorter events, 28.8 us)
Async XLA Ops:
  6.5 18.7 %copy-start = (bf16[1024,1024]{1,0:T(8,128)(2,1)S(1)}, bf16[1024,1024]{1,0:T(8,128)(2,1)}, u32[]{:S(2)}) copy-start(bf16[1024,1024]{1,0:T(8,128)(2,1)} %param.20) | copy-start | bytes 6291460
  6.5 46.8 %reduce-scatter.5.cloned.1.call-start = ((), (), s32[]{:S(2)}) async-start(), calls=%async_computation.8 | async-start | bytes 1310720 | tf_op jit(solution)/shard_map/reduce_scatter | solution.py:125
  6.5 12.0 %collective-permute-start.1 = (s32[2,256]{1,0:T(2,128)}, s32[2,256]{1,0:T(2,128)S(1)}, u32[]{:S(2)}, u32[]{:S(2)}) collective-permute-start(s32[2,256]{1,0:T(2,128)} %param.17), channel_id=1, source_target_pairs={{0,16},{16,0},{1,17},{17,1},{2,18},{18,2},{3,19},{19,3},{4,20},{20... | collective-permute-start | bytes 6152 | tf_op jit(solution)/shard_map/ppermute | solution.py:43
  12.6 7.8 %collective-permute-start = (bf16[2,256,256]{2,1,0:T(8,128)(2,1)S(1)}, bf16[2,256,256]{2,1,0:T(8,128)(2,1)S(1)}, u32[]{:S(2)}, u32[]{:S(2)}) collective-permute-start(bf16[2,256,256]{2,1,0:T(8,128)(2,1)S(1)} %pad_maximum_fusion.2), channel_id=1, source_target_pairs={{0,16},{16,0},{1,17},{17,1},{2,18},{18,2},{3,19},{19,3},{4,20},{20... | collective-permute-start | bytes 786440 | tf_op jit(solution)/shard_map/ppermute | solution.py:43
  12.8 3.8 %copy-start.13 = (f32[128]{0:T(128)S(1)}, f32[128]{0:T(128)}, u32[]{:S(2)}) copy-start(f32[128]{0:T(128)} %param.18) | copy-start | bytes 1540
  14.3 1.4 copy-start.2
  16.3 2.2 copy-start.11
  16.3 4.1 %copy-start.8 = (bf16[2,256,128]{2,1,0:T(8,128)(2,1)S(1)}, bf16[2,256,128]{2,1,0:T(8,128)(2,1)}, u32[]{:S(2)}) copy-start(bf16[2,256,128]{2,1,0:T(8,128)(2,1)} %param.16) | copy-start | bytes 393220
  24.3 1.0 copy-start.5
  27.5 53.8 %reduce-scatter.7.cloned.1.call-start = ((), (), s32[]{:S(2)}) async-start(), calls=%async_computation.9 | async-start | bytes 1310720 | tf_op jit(solution)/shard_map/reduce_scatter | solution.py:125
  29.6 26.1 %copy-start.12 = (s32[2,256,8]{1,2,0:T(8,128)S(1)}, s32[2,256,8]{1,2,0:T(8,128)}, u32[]{:S(2)}) copy-start(s32[2,256,8]{1,2,0:T(8,128)} %param.24) | copy-start | bytes 49156
  29.6 23.8 %collective-permute-start.2 = (bf16[512,1024]{1,0:T(8,128)(2,1)S(1)}, bf16[512,1024]{1,0:T(8,128)(2,1)S(1)}, u32[]{:S(2)}, u32[]{:S(2)}) collective-permute-start(bf16[512,1024]{1,0:T(8,128)(2,1)S(1)} %bitcast.133), channel_id=1, source_target_pairs={{0,16},{16,0},{1,17},{17,1},{2,18},{18,2},{3,19},{19,3},{4,20},{20... | collective-permute-start | bytes 3145736 | tf_op jit(solution)/shard_map/ppermute | solution.py:43
  53.4 44.0 %copy-start.9 = (bf16[2,64,1024]{2,1,0:T(8,128)(2,1)S(1)}, bf16[2,64,1024]{2,1,0:T(8,128)(2,1)}, u32[]{:S(2)}) copy-start(bf16[2,64,1024]{2,1,0:T(8,128)(2,1)} %reduce-scatter.5.cloned.1.call-done) | copy-start | bytes 786436
  55.6 73.7 %all-gather.3.cloned.1.call-start = ((), (), s32[]{:S(2)}) async-start(), calls=%async_computation.10 | async-start | bytes 1392640 | tf_op jit(solution)/shard_map/all_gather | solution.py:169
  55.8 43.6 %collective-permute-start.4 = (bf16[1,2048,384]{2,1,0:T(8,128)(2,1)}, bf16[1,2048,384]{2,1,0:T(8,128)(2,1)}, u32[]{:S(2)}, u32[]{:S(2)}) collective-permute-start(bf16[1,2048,384]{2,1,0:T(8,128)(2,1)} %param.25), channel_id=1, source_target_pairs={{0,16},{16,0},{1,17},{17,1},{2,18},{18,2},{3,19},{19,3},{4,20},{20... | collective-permute-start | bytes 4718600 | tf_op jit(solution)/shard_map/ppermute | solution.py:43
  81.3 16.0 %collective-permute-start.3 = (bf16[2,64,1024]{2,1,0:T(8,128)(2,1)}, bf16[2,64,1024]{2,1,0:T(8,128)(2,1)S(1)}, u32[]{:S(2)}, u32[]{:S(2)}) collective-permute-start(bf16[2,64,1024]{2,1,0:T(8,128)(2,1)} %reduce-scatter.7.cloned.1.call-done), channel_id=1, source_target_pairs={{0,16},{16,0},{1,17},{17,1},{2,18},{18,2},{3,19},{19,3},{4,20},{20... | collective-permute-start | bytes 786440 | tf_op jit(solution)/shard_map/ppermute | solution.py:129
  97.7 1.5 copy-start.10
  99.1 1.5 copy-start.6
  100.2 64.1 %all-gather.5.cloned.1.call-start = ((), (), s32[]{:S(2)}) async-start(), calls=%async_computation.12 | async-start | bytes 1392640 | tf_op jit(solution)/shard_map/all_gather | solution.py:169
  104.0 70.4 %collective-permute-start.5 = (bf16[1,2048,768]{2,1,0:T(8,128)(2,1)}, bf16[1,2048,768]{2,1,0:T(8,128)(2,1)}, u32[]{:S(2)}, u32[]{:S(2)}) collective-permute-start(bf16[1,2048,768]{2,1,0:T(8,128)(2,1)} %pad_maximum_fusion), channel_id=1, source_target_pairs={{0,16},{16,0},{1,17},{17,1},{2,18},{18,2},{3,19},{19,3},{4,20},{20... | collective-permute-start | bytes 9437192 | tf_op jit(solution)/shard_map/ppermute | solution.py:43
  135.6 4.9 %copy-start.7 = (bf16[256,2176]{1,0:T(8,128)(2,1)S(1)}, bf16[256,2176]{1,0:T(8,128)(2,1)}, u32[]{:S(2)}) copy-start(bf16[256,2176]{1,0:T(8,128)(2,1)} %all-gather.3.cloned.1.call-done) | copy-start | bytes 3342340
  135.6 4.9 %copy-start.15 = (bf16[2048,16]{0,1:T(8,128)(2,1)S(1)}, bf16[2048,16]{0,1:T(8,128)(2,1)}, u32[]{:S(2)}) copy-start(bf16[2048,16]{0,1:T(8,128)(2,1)} %param.23) | copy-start | bytes 196612
  135.6 34.1 %all-to-all-start = ((bf16[4,144,2048]{2,1,0:T(8,128)(2,1)}), bf16[4,144,2048]{2,1,0:T(8,128)(2,1)}, u32[]{:S(2)}, u32[]{:S(2)}) async-start(bf16[4,144,2048]{2,1,0:T(8,128)(2,1)} %bitcast.121), calls=%async_computation.2 | async-start | bytes 4718592 | tf_op jit(solution)/shard_map/all_to_all | solution.py:201
  169.7 4.7 %copy-start.14 = (bf16[1,2048,384]{2,1,0:T(8,128)(2,1)S(1)}, bf16[1,2048,384]{2,1,0:T(8,128)(2,1)}, u32[]{:S(2)}) copy-start(bf16[1,2048,384]{2,1,0:T(8,128)(2,1)} %param.25) | copy-start | bytes 4718596
  169.7 33.2 %all-to-all-start.2 = ((bf16[4,144,2048]{2,1,0:T(8,128)(2,1)}), bf16[4,144,2048]{2,1,0:T(8,128)(2,1)}, u32[]{:S(2)}, u32[]{:S(2)}) async-start(bf16[4,144,2048]{2,1,0:T(8,128)(2,1)} %bitcast.122), calls=%async_computation.5 | async-start | bytes 4718592 | tf_op jit(solution)/shard_map/all_to_all | solution.py:201
  202.9 33.1 %all-to-all-start.1 = ((bf16[4,144,2048]{2,1,0:T(8,128)(2,1)}), bf16[4,144,2048]{2,1,0:T(8,128)(2,1)}, u32[]{:S(2)}, u32[]{:S(2)}) async-start(bf16[4,144,2048]{2,1,0:T(8,128)(2,1)} %bitcast.130), calls=%async_computation.3 | async-start | bytes 4718592 | tf_op jit(solution)/shard_map/all_to_all | solution.py:210
  236.0 33.1 %all-to-all-start.3 = ((bf16[4,144,2048]{2,1,0:T(8,128)(2,1)}), bf16[4,144,2048]{2,1,0:T(8,128)(2,1)}, u32[]{:S(2)}, u32[]{:S(2)}) async-start(bf16[4,144,2048]{2,1,0:T(8,128)(2,1)} %bitcast.129), calls=%async_computation.6 | async-start | bytes 4718592 | tf_op jit(solution)/shard_map/all_to_all | solution.py:210
  240.5 35.5 %reduce-scatter.9.cloned.1.call-start = ((), (), s32[]{:S(2)}) async-start(), calls=%async_computation.11 | async-start | bytes 1310720 | tf_op jit(solution)/shard_map/reduce_scatter | solution.py:220
  240.6 2.9 copy-start.3
  247.2 55.3 %reduce-scatter.11.cloned.1.call-start = ((), (), s32[]{:S(2)}) async-start(), calls=%async_computation.13 | async-start | bytes 1310720 | tf_op jit(solution)/shard_map/reduce_scatter | solution.py:220
  249.6 19.5 %copy-start.4 = (f32[576,256]{1,0:T(8,128)}, f32[576,256]{1,0:T(8,128)S(1)}, u32[]{:S(2)}) copy-start(f32[576,256]{1,0:T(8,128)S(1)} %select_reduce_fusion) | copy-start | bytes 1769476
  271.8 32.7 %copy-start.1 = (bf16[1024,1024]{1,0:T(8,128)(2,1)S(1)}, bf16[1024,1024]{1,0:T(8,128)(2,1)}, u32[]{:S(2)}) copy-start(bf16[1024,1024]{1,0:T(8,128)(2,1)} %param.20) | copy-start | bytes 6291460
Sparse Core Ops, SparseCore 0:
  27.7 25.2 reduce-scatter.4
  55.8 25.4 reduce-scatter.6
  100.3 29.0 all-gather.2
  135.7 28.4 all-gather.4
  247.3 27.0 reduce-scatter.8
  276.7 25.7 reduce-scatter.10

commit v12 on v11

--- a/solution.py
+++ b/solution.py
@@ -211,11 +211,13 @@
             n_slots, width
         )
 
-        weight_hi = weight.astype(jnp.bfloat16)
-        weight_lo = (weight - weight_hi.astype(jnp.float32)).astype(jnp.bfloat16)
         partial = lax.dot_general(
-            weight_hi, back, contract, preferred_element_type=jnp.float32
-        ) + lax.dot_general(weight_lo, back, contract, preferred_element_type=jnp.float32)
+            weight,
+            back.astype(jnp.float32),
+            contract,
+            precision=lax.Precision.HIGHEST,
+            preferred_element_type=jnp.float32,
+        )
         mixtures.append(
             lax.psum_scatter(
                 partial.astype(jnp.bfloat16).reshape(n_ep, share, width),

time: 312 us -> 326 us (1.045)
  waiting for transfers between devices: 177 us -> 194 us
    all_to_all x2, waiting for transfers between devices: 31.1 us -> 47.9 us  [shards(): lax.all_to_all(served, 'tp', split_axis=0, concat_axis=0, tiled=True)]
    dot_general x4 -> x2, matrix products: 13.5 us -> 10.9 us  [shards(): lax.dot_general(weight, back.astype(jnp.float32), contract, precision=lax...]
  transfers between devices with their start and end apart: 16 -> 16, of which waited for: 10 -> 10; matrix products, arithmetic and copies ran while one was open for 26% -> 22% of each run, Pallas kernels for 0% -> 0%
where the time goes in v12:
time: 326 us; the launch traced here: 325 us
  waiting for transfers between devices  194 us (60%)
  matrix products  59.4 us (18%)
  starting transfers between devices  26.6 us (8%)
  other arithmetic  18.5 us (6%)
  between operations  14 us (4%)
  local copies, waits for them, and re-layouts  12.9 us (4%)
    all_to_all x2, waiting for transfers between devices, shards(): lax.all_to_all(served, 'tp', split_axis=0, concat_axis=0, tiled=True)  47.9 us
    all_gather x2, waiting for transfers between devices, shards(): lax.all_gather(jnp.concatenate([rows, id_lanes], axis=1), 'ep', axis=0, t...  47.9 us
    reduce_scatter x2, waiting for transfers between devices, shards(): lax.psum_scatter(partial.astype(jnp.bfloat16).reshape(n_ep, share, width)...  25.9 us
    ppermute x5, waiting for transfers between devices, cp_pieces(): pieces.append(lax.ppermute(x, 'cp', perm))  25 us
    reduce_scatter x2, waiting for transfers between devices, shards(): lax.psum_scatter(block.astype(jnp.bfloat16), 'tp', scatter_dimension=1, t...  24.6 us
    dot_general x2, matrix products, expert_rows(): jnp.einsum('rf,df->rd', hidden_act, full_down[0], preferred_element_type=...  19.8 us
    ppermute x1, waiting for transfers between devices, shards(): lax.ppermute(summed, 'cp', [(i, (i - j) % n_cp) for i in range(n_cp)])  14.3 us
    dot_general x2, matrix products, expert_rows(): jnp.dot(flat_rows, full_gate[0], preferred_element_type=jnp.float32)  11.1 us
  transfers between devices with their start and end apart: 16, of which 10 were waited for; matrix products, arithmetic and copies ran while one was open for 22% of the time, Pallas kernels for 0%

profile of v12, /device:TPU:0, one launch (start us, length us, event | category | flops | bytes accessed | tf_op | source)
XLA Modules:
  0.0 325.1 jit_solution(10638604013821000751)
XLA Ops:
  6.5 3.0 collective-permute-start.1
  16.5 1.9 fusion.11
  18.7 1.7 collective-permute-done
  20.4 2.2 fusion
  22.7 1.6 fusion.14
  24.3 2.3 fusion.21
  26.6 1.7 copy.86
  29.1 23.4 %collective-permute-done.2 = bf16[512,1024]{1,0:T(8,128)(2,1)} collective-permute-done((bf16[512,1024]{1,0:T(8,128)(2,1)S(1)}, bf16[512,1024]{1,0:T(8,128)(2,1)}, u32[]{:S(2)}, u32[]{:S(2)}) %collective-permute-start.2) | collective-permute-done | bytes 1048608 | tf_op jit(solution)/shard_map/ppermute | solution.py:43
  52.5 3.5 %convolution_convert_fusion.6 = bf16[512,1024]{1,0:T(8,128)(2,1)} fusion(bf16[512,1024]{1,0:T(8,128)(2,1)} %collective-permute-done.2, bf16[1024,1024]{1,0:T(8,128)(2,1)S(1)} %copy-done), kind=kOutput, calls=%fused_computation.40 | convolution fusion | flops 1074266112 | bytes 4194304 | tf_op jit(solution)/shard_map/dot_general | solution.py:122
  57.1 24.6 %reduce-scatter.7.cloned.1.call-done = bf16[2,64,1024]{2,1,0:T(8,128)(2,1)} async-done(((bf16[2,256,1024]{2,1,0:T(8,128)(2,1)}), bf16[2,64,1024]{2,1,0:T(8,128)(2,1)}) %reduce-scatter.7.cloned.1.call-update) | async-done | bytes 262160 | tf_op jit(solution)/shard_map/reduce_scatter | solution.py:125
  83.3 14.3 %collective-permute-done.3 = bf16[2,64,1024]{2,1,0:T(8,128)(2,1)S(1)} collective-permute-done((bf16[2,64,1024]{2,1,0:T(8,128)(2,1)}, bf16[2,64,1024]{2,1,0:T(8,128)(2,1)S(1)}, u32[]{:S(2)}, u32[]{:S(2)}) %collective-permute-start.3) | collective-permute-done | bytes 262176 | tf_op jit(solution)/shard_map/ppermute | solution.py:129
  100.9 3.3 %pad_maximum_fusion = bf16[1,2048,768]{2,1,0:T(8,128)(2,1)} fusion(bf16[1,2048,384]{2,1,0:T(8,128)(2,1)S(1)} %copy-done.5, bf16[1,2048,384]{2,1,0:T(8,128)(2,1)} %param.26), kind=kLoop, calls=%fused_computation.13 | loop fusion | flops 6291456 | bytes 6291456 | tf_op jit(solution)/shard_map/concatenate | solution.py:151
  105.8 23.9 %all-gather.3.cloned.1.call-done = bf16[256,2176]{1,0:T(8,128)(2,1)} async-done(((bf16[64,2176]{1,0:T(8,128)(2,1)}), bf16[256,2176]{1,0:T(8,128)(2,1)}) %all-gather.3.cloned.1.call-update) | async-done | bytes 1114128 | tf_op jit(solution)/shard_map/all_gather | solution.py:169
  131.7 3.4 %convolution_convert_fusion.3 = bf16[576,2048]{1,0:T(8,128)(2,1)} fusion(pred[576,256]{1,0:T(8,128)(4,1)S(1)} %fusion.3, bf16[256,2176]{1,0:T(8,128)(2,1)} %all-gather.3.cloned.1.call-done), kind=kOutput, calls=%fused_computation.20 | convolution fusion | flops 605159424 | bytes 3555328 | tf_op jit(solution)/shard_map/dot_general | solution.py:198
  135.9 4.7 %all-to-all-start = ((bf16[4,144,2048]{2,1,0:T(8,128)(2,1)}), bf16[4,144,2048]{2,1,0:T(8,128)(2,1)}, u32[]{:S(2)}, u32[]{:S(2)}) async-start(bf16[4,144,2048]{2,1,0:T(8,128)(2,1)} %bitcast.121), calls=%async_computation.2 | async-start | bytes 4718592 | tf_op jit(solution)/shard_map/all_to_all | solution.py:201
  140.6 23.9 %all-gather.5.cloned.1.call-done = bf16[256,2176]{1,0:T(8,128)(2,1)} async-done(((bf16[64,2176]{1,0:T(8,128)(2,1)}), bf16[256,2176]{1,0:T(8,128)(2,1)}) %all-gather.5.cloned.1.call-update) | async-done | bytes 1114128 | tf_op jit(solution)/shard_map/all_gather | solution.py:169
  166.6 3.5 %convolution_convert_fusion.2 = bf16[576,2048]{1,0:T(8,128)(2,1)} fusion(pred[576,256]{1,0:T(8,128)(4,1)S(1)} %fusion.2, bf16[256,2176]{1,0:T(8,128)(2,1)} %all-gather.5.cloned.1.call-done), kind=kOutput, calls=%fused_computation.19 | convolution fusion | flops 605159424 | bytes 3555328 | tf_op jit(solution)/shard_map/dot_general | solution.py:198
  170.1 4.6 %all-to-all-start.2 = ((bf16[4,144,2048]{2,1,0:T(8,128)(2,1)}), bf16[4,144,2048]{2,1,0:T(8,128)(2,1)}, u32[]{:S(2)}, u32[]{:S(2)}) async-start(bf16[4,144,2048]{2,1,0:T(8,128)(2,1)} %bitcast.122), calls=%async_computation.5 | async-start | bytes 4718592 | tf_op jit(solution)/shard_map/all_to_all | solution.py:201
  174.7 5.3 %fusion.18 = f32[576,768]{1,0:T(8,128)} fusion(bf16[576,2048]{1,0:T(8,128)(2,1)} %bitcast.16, bf16[1,2048,384]{2,1,0:T(8,128)(2,1)} %collective-permute-done.4, bf16[1,2048,384]{2,1,0:T(8,128)(2,1)S(1)} %copy-done.14), kind=kOutput, calls=%fused_computation.36 | convolution fusion | flops 1818230784 | bytes 7274496 | tf_op jit(solution)/shard_map/dot_general | solution.py:50
  180.0 5.1 %fusion.76 = (bf16[1,2048,384]{2,1,0:T(8,128)(2,1)S(1)}, bf16[1,2048,384]{2,1,0:T(8,128)(2,1)}, bf16[1,2048,384]{2,1,0:T(8,128)(2,1)}, bf16[1,2048,384]{2,1,0:T(8,128)(2,1)}) fusion(bf16[1,2048,768]{2,1,0:T(8,128)(2,1)} %pad_maximum_fusion, bf16[1,2048,768]{2,1,0:T(8,128)(2,1)} %collective-permute-done.5), kind=kLoop, calls=%fused_computation.150 | loop fusion | bytes 12582912 | tf_op jit(solution)/shard_map/slice | solution.py:207
  185.1 10.0 %convolution_convert_fusion.1 = bf16[576,2048]{1,0:T(8,128)(2,1)} fusion(bf16[1,2048,384]{2,1,0:T(8,128)(2,1)} %get-tuple-element.61, bf16[1,2048,384]{2,1,0:T(8,128)(2,1)} %get-tuple-element.52, f32[576,768]{1,0:T(8,128)} %fusion.18, bf16[576,2048]{1,0:T(8,128)(2,1)} %bitcast.16, bf16[1,2048,384]{2,1,0:T(8,128)(2,1)} %get-tuple-element.62, ...), kind=kOutput, calls=%fused_computation.18 | convolution fusion | flops 3640295424 | bytes 12779520 | tf_op jit(solution)/shard_map/rf,df->rd/dot_general | solution.py:53
  195.1 8.2 %all-to-all-done.2 = bf16[4,144,2048]{2,1,0:T(8,128)(2,1)} async-done(((bf16[4,144,2048]{2,1,0:T(8,128)(2,1)}), bf16[4,144,2048]{2,1,0:T(8,128)(2,1)}, u32[]{:S(2)}, u32[]{:S(2)}) %all-to-all-start.2) | async-done | bytes 2359328 | tf_op jit(solution)/shard_map/all_to_all | solution.py:201
  203.3 4.6 %all-to-all-start.1 = ((bf16[4,144,2048]{2,1,0:T(8,128)(2,1)}), bf16[4,144,2048]{2,1,0:T(8,128)(2,1)}, u32[]{:S(2)}, u32[]{:S(2)}) async-start(bf16[4,144,2048]{2,1,0:T(8,128)(2,1)} %bitcast.129), calls=%async_computation.3 | async-start | bytes 4718592 | tf_op jit(solution)/shard_map/all_to_all | solution.py:210
  209.3 5.8 %fusion.17 = f32[576,768]{1,0:T(8,128)} fusion(bf16[576,2048]{1,0:T(8,128)(2,1)} %bitcast.27, bf16[1,2048,384]{2,1,0:T(8,128)(2,1)} %collective-permute-done.4, bf16[1,2048,384]{2,1,0:T(8,128)(2,1)} %param.25), kind=kOutput, calls=%fused_computation.35 | convolution fusion | flops 1818230784 | bytes 7274496 | tf_op jit(solution)/shard_map/dot_general | solution.py:50
  215.2 21.3 %all-to-all-done.1 = bf16[4,144,2048]{2,1,0:T(8,128)(2,1)} async-done(((bf16[4,144,2048]{2,1,0:T(8,128)(2,1)}), bf16[4,144,2048]{2,1,0:T(8,128)(2,1)}, u32[]{:S(2)}, u32[]{:S(2)}) %all-to-all-start.1) | async-done | bytes 2359328 | tf_op jit(solution)/shard_map/all_to_all | solution.py:210
  236.5 5.3 %convolution_convert_fusion.5 = bf16[256,2048]{1,0:T(8,128)(2,1)} fusion(f32[576,256]{1,0:T(8,128)S(1)} %select_reduce_fusion.1, bf16[576,2048]{1,0:T(8,128)(2,1)} %bitcast.21), kind=kOutput, calls=%fused_computation.22 | convolution fusion | flops 3624402944 | bytes 3997696 | tf_op jit(solution)/shard_map/dot_general | solution.py:214
  241.8 9.8 %convolution_convert_fusion = bf16[576,2048]{1,0:T(8,128)(2,1)} fusion(bf16[1,2048,384]{2,1,0:T(8,128)(2,1)} %get-tuple-element.61, bf16[1,2048,384]{2,1,0:T(8,128)(2,1)} %get-tuple-element.52, f32[576,768]{1,0:T(8,128)} %fusion.17, bf16[576,2048]{1,0:T(8,128)(2,1)} %bitcast.27, bf16[1,2048,384]{2,1,0:T(8,128)(2,1)} %get-tuple-element.62, ...), kind=kOutput, calls=%fused_computation.17 | convolution fusion | flops 3640295424 | bytes 12779520 | tf_op jit(solution)/shard_map/rf,df->rd/dot_general | solution.py:53
  251.6 4.6 %all-to-all-start.3 = ((bf16[4,144,2048]{2,1,0:T(8,128)(2,1)}), bf16[4,144,2048]{2,1,0:T(8,128)(2,1)}, u32[]{:S(2)}, u32[]{:S(2)}) async-start(bf16[4,144,2048]{2,1,0:T(8,128)(2,1)} %bitcast.130), calls=%async_computation.6 | async-start | bytes 4718592 | tf_op jit(solution)/shard_map/all_to_all | solution.py:210
  258.3 26.6 %all-to-all-done.3 = bf16[4,144,2048]{2,1,0:T(8,128)(2,1)} async-done(((bf16[4,144,2048]{2,1,0:T(8,128)(2,1)}), bf16[4,144,2048]{2,1,0:T(8,128)(2,1)}, u32[]{:S(2)}, u32[]{:S(2)}) %all-to-all-start.3) | async-done | bytes 2359328 | tf_op jit(solution)/shard_map/all_to_all | solution.py:210
  284.8 5.6 %convolution_convert_fusion.4 = bf16[256,2048]{1,0:T(8,128)(2,1)} fusion(f32[576,256]{1,0:T(8,128)} %select_reduce_fusion, bf16[576,2048]{1,0:T(8,128)(2,1)} %bitcast.29), kind=kOutput, calls=%fused_computation.21 | convolution fusion | flops 3624402944 | bytes 3997696 | tf_op jit(solution)/shard_map/dot_general | solution.py:214
  290.5 25.8 %reduce-scatter.11.cloned.1.call-done = bf16[1,64,2048]{2,1,0:T(8,128)(2,1)} async-done(((bf16[4,64,2048]{2,1,0:T(8,128)(2,1)}), bf16[1,64,2048]{2,1,0:T(8,128)(2,1)}) %reduce-scatter.11.cloned.1.call-update) | async-done | bytes 262160 | tf_op jit(solution)/shard_map/reduce_scatter | solution.py:222
  316.4 1.9 add_convert_fusion
  (119 shorter events, 23.5 us)
Async XLA Ops:
  6.5 17.7 %copy-start = (bf16[1024,1024]{1,0:T(8,128)(2,1)S(1)}, bf16[1024,1024]{1,0:T(8,128)(2,1)}, u32[]{:S(2)}) copy-start(bf16[1024,1024]{1,0:T(8,128)(2,1)} %param.20) | copy-start | bytes 6291460
  6.5 46.0 %reduce-scatter.5.cloned.1.call-start = ((), (), s32[]{:S(2)}) async-start(), calls=%async_computation.8 | async-start | bytes 1310720 | tf_op jit(solution)/shard_map/reduce_scatter | solution.py:125
  6.5 12.0 %collective-permute-start.1 = (s32[2,256]{1,0:T(2,128)}, s32[2,256]{1,0:T(2,128)S(1)}, u32[]{:S(2)}, u32[]{:S(2)}) collective-permute-start(s32[2,256]{1,0:T(2,128)} %param.17), channel_id=1, source_target_pairs={{0,16},{16,0},{1,17},{17,1},{2,18},{18,2},{3,19},{19,3},{4,20},{20... | collective-permute-start | bytes 6152 | tf_op jit(solution)/shard_map/ppermute | solution.py:43
  12.6 7.8 %collective-permute-start = (bf16[2,256,256]{2,1,0:T(8,128)(2,1)S(1)}, bf16[2,256,256]{2,1,0:T(8,128)(2,1)S(1)}, u32[]{:S(2)}, u32[]{:S(2)}) collective-permute-start(bf16[2,256,256]{2,1,0:T(8,128)(2,1)S(1)} %pad_maximum_fusion.2), channel_id=1, source_target_pairs={{0,16},{16,0},{1,17},{17,1},{2,18},{18,2},{3,19},{19,3},{4,20},{20... | collective-permute-start | bytes 786440 | tf_op jit(solution)/shard_map/ppermute | solution.py:43
  12.8 3.8 %copy-start.13 = (f32[128]{0:T(128)S(1)}, f32[128]{0:T(128)}, u32[]{:S(2)}) copy-start(f32[128]{0:T(128)} %param.18) | copy-start | bytes 1540
  14.3 1.4 copy-start.2
  16.3 2.2 copy-start.11
  16.3 4.1 %copy-start.8 = (bf16[2,256,128]{2,1,0:T(8,128)(2,1)S(1)}, bf16[2,256,128]{2,1,0:T(8,128)(2,1)}, u32[]{:S(2)}) copy-start(bf16[2,256,128]{2,1,0:T(8,128)(2,1)} %param.16) | copy-start | bytes 393220
  24.3 2.3 copy-start.3
  26.6 55.1 %reduce-scatter.7.cloned.1.call-start = ((), (), s32[]{:S(2)}) async-start(), calls=%async_computation.9 | async-start | bytes 1310720 | tf_op jit(solution)/shard_map/reduce_scatter | solution.py:125
  28.6 27.5 %copy-start.12 = (s32[2,256,8]{1,2,0:T(8,128)S(1)}, s32[2,256,8]{1,2,0:T(8,128)}, u32[]{:S(2)}) copy-start(s32[2,256,8]{1,2,0:T(8,128)} %param.24) | copy-start | bytes 49156
  28.6 23.9 %collective-permute-start.2 = (bf16[512,1024]{1,0:T(8,128)(2,1)S(1)}, bf16[512,1024]{1,0:T(8,128)(2,1)}, u32[]{:S(2)}, u32[]{:S(2)}) collective-permute-start(bf16[512,1024]{1,0:T(8,128)(2,1)S(1)} %bitcast.133), channel_id=1, source_target_pairs={{0,16},{16,0},{1,17},{17,1},{2,18},{18,2},{3,19},{19,3},{4,20},{20... | collective-permute-start | bytes 3145736 | tf_op jit(solution)/shard_map/ppermute | solution.py:43
  52.5 45.1 %copy-start.9 = (bf16[2,64,1024]{2,1,0:T(8,128)(2,1)S(1)}, bf16[2,64,1024]{2,1,0:T(8,128)(2,1)}, u32[]{:S(2)}) copy-start(bf16[2,64,1024]{2,1,0:T(8,128)(2,1)} %reduce-scatter.5.cloned.1.call-done) | copy-start | bytes 786436
  56.1 73.6 %all-gather.3.cloned.1.call-start = ((), (), s32[]{:S(2)}) async-start(), calls=%async_computation.10 | async-start | bytes 1392640 | tf_op jit(solution)/shard_map/all_gather | solution.py:169
  56.2 43.5 %collective-permute-start.4 = (bf16[1,2048,384]{2,1,0:T(8,128)(2,1)}, bf16[1,2048,384]{2,1,0:T(8,128)(2,1)}, u32[]{:S(2)}, u32[]{:S(2)}) collective-permute-start(bf16[1,2048,384]{2,1,0:T(8,128)(2,1)} %param.25), channel_id=1, source_target_pairs={{0,16},{16,0},{1,17},{17,1},{2,18},{18,2},{3,19},{19,3},{4,20},{20... | collective-permute-start | bytes 4718600 | tf_op jit(solution)/shard_map/ppermute | solution.py:43
  81.7 15.9 %collective-permute-start.3 = (bf16[2,64,1024]{2,1,0:T(8,128)(2,1)}, bf16[2,64,1024]{2,1,0:T(8,128)(2,1)S(1)}, u32[]{:S(2)}, u32[]{:S(2)}) collective-permute-start(bf16[2,64,1024]{2,1,0:T(8,128)(2,1)} %reduce-scatter.7.cloned.1.call-done), channel_id=1, source_target_pairs={{0,16},{16,0},{1,17},{17,1},{2,18},{18,2},{3,19},{19,3},{4,20},{20... | collective-permute-start | bytes 786440 | tf_op jit(solution)/shard_map/ppermute | solution.py:129
  98.0 1.5 copy-start.10
  99.4 1.5 copy-start.5
  100.5 64.1 %all-gather.5.cloned.1.call-start = ((), (), s32[]{:S(2)}) async-start(), calls=%async_computation.12 | async-start | bytes 1392640 | tf_op jit(solution)/shard_map/all_gather | solution.py:169
  104.3 70.5 %collective-permute-start.5 = (bf16[1,2048,768]{2,1,0:T(8,128)(2,1)}, bf16[1,2048,768]{2,1,0:T(8,128)(2,1)}, u32[]{:S(2)}, u32[]{:S(2)}) collective-permute-start(bf16[1,2048,768]{2,1,0:T(8,128)(2,1)} %pad_maximum_fusion), channel_id=1, source_target_pairs={{0,16},{16,0},{1,17},{17,1},{2,18},{18,2},{3,19},{19,3},{4,20},{20... | collective-permute-start | bytes 9437192 | tf_op jit(solution)/shard_map/ppermute | solution.py:43
  135.9 34.2 %all-to-all-start = ((bf16[4,144,2048]{2,1,0:T(8,128)(2,1)}), bf16[4,144,2048]{2,1,0:T(8,128)(2,1)}, u32[]{:S(2)}, u32[]{:S(2)}) async-start(bf16[4,144,2048]{2,1,0:T(8,128)(2,1)} %bitcast.121), calls=%async_computation.2 | async-start | bytes 4718592 | tf_op jit(solution)/shard_map/all_to_all | solution.py:201
  170.1 4.6 %copy-start.14 = (bf16[1,2048,384]{2,1,0:T(8,128)(2,1)S(1)}, bf16[1,2048,384]{2,1,0:T(8,128)(2,1)}, u32[]{:S(2)}) copy-start(bf16[1,2048,384]{2,1,0:T(8,128)(2,1)} %param.25) | copy-start | bytes 4718596
  170.1 33.2 %all-to-all-start.2 = ((bf16[4,144,2048]{2,1,0:T(8,128)(2,1)}), bf16[4,144,2048]{2,1,0:T(8,128)(2,1)}, u32[]{:S(2)}, u32[]{:S(2)}) async-start(bf16[4,144,2048]{2,1,0:T(8,128)(2,1)} %bitcast.122), calls=%async_computation.5 | async-start | bytes 4718592 | tf_op jit(solution)/shard_map/all_to_all | solution.py:201
  185.1 10.0 %copy-start.4 = (bf16[1,2048,384]{2,1,0:T(8,128)(2,1)}, bf16[1,2048,384]{2,1,0:T(8,128)(2,1)S(1)}, u32[]{:S(2)}) copy-start(bf16[1,2048,384]{2,1,0:T(8,128)(2,1)S(1)} %get-tuple-element.51) | copy-start | bytes 4718596
  203.3 4.9 %copy-start.6 = (bf16[256,2176]{1,0:T(8,128)(2,1)S(1)}, bf16[256,2176]{1,0:T(8,128)(2,1)}, u32[]{:S(2)}) copy-start(bf16[256,2176]{1,0:T(8,128)(2,1)} %all-gather.3.cloned.1.call-done) | copy-start | bytes 3342340
  203.3 4.9 %copy-start.15 = (bf16[2048,16]{0,1:T(8,128)(2,1)S(1)}, bf16[2048,16]{0,1:T(8,128)(2,1)}, u32[]{:S(2)}) copy-start(bf16[2048,16]{0,1:T(8,128)(2,1)} %param.23) | copy-start | bytes 196612
  203.3 33.2 %all-to-all-start.1 = ((bf16[4,144,2048]{2,1,0:T(8,128)(2,1)}), bf16[4,144,2048]{2,1,0:T(8,128)(2,1)}, u32[]{:S(2)}, u32[]{:S(2)}) async-start(bf16[4,144,2048]{2,1,0:T(8,128)(2,1)} %bitcast.129), calls=%async_computation.3 | async-start | bytes 4718592 | tf_op jit(solution)/shard_map/all_to_all | solution.py:210
  207.9 82.6 %reduce-scatter.9.cloned.1.call-start = ((), (), s32[]{:S(2)}) async-start(), calls=%async_computation.11 | async-start | bytes 1310720 | tf_op jit(solution)/shard_map/reduce_scatter | solution.py:222
  251.6 4.7 %copy-start.7 = (bf16[256,2176]{1,0:T(8,128)(2,1)S(1)}, bf16[256,2176]{1,0:T(8,128)(2,1)}, u32[]{:S(2)}) copy-start(bf16[256,2176]{1,0:T(8,128)(2,1)} %all-gather.5.cloned.1.call-done) | copy-start | bytes 3342340
  251.6 33.2 %all-to-all-start.3 = ((bf16[4,144,2048]{2,1,0:T(8,128)(2,1)}), bf16[4,144,2048]{2,1,0:T(8,128)(2,1)}, u32[]{:S(2)}, u32[]{:S(2)}) async-start(bf16[4,144,2048]{2,1,0:T(8,128)(2,1)} %bitcast.130), calls=%async_computation.6 | async-start | bytes 4718592 | tf_op jit(solution)/shard_map/all_to_all | solution.py:210
  256.3 60.1 %reduce-scatter.11.cloned.1.call-start = ((), (), s32[]{:S(2)}) async-start(), calls=%async_computation.13 | async-start | bytes 1310720 | tf_op jit(solution)/shard_map/reduce_scatter | solution.py:222
  284.8 33.5 %copy-start.1 = (bf16[1024,1024]{1,0:T(8,128)(2,1)S(1)}, bf16[1024,1024]{1,0:T(8,128)(2,1)}, u32[]{:S(2)}) copy-start(bf16[1024,1024]{1,0:T(8,128)(2,1)} %param.20) | copy-start | bytes 6291460
Sparse Core Ops, SparseCore 0:
  26.7 25.2 reduce-scatter.4
  56.2 25.4 reduce-scatter.6
  100.6 29.0 all-gather.2
  136.0 28.4 all-gather.4
  241.9 25.7 reduce-scatter.8
  290.6 25.6 reduce-scatter.10

commit v13 on v11

--- a/solution.py
+++ b/solution.py
@@ -84,41 +84,47 @@
     top_count = expert_ids.shape[2]
     score_scale = HEAD_WIDTH ** (-0.5)
 
-    query_rows_normed = root_mean_scale(
-        query.astype(jnp.float32).reshape(packs, row_count, head_count, HEAD_WIDTH), query_norm_gain
-    ).astype(jnp.bfloat16)
+    query_pieces = cp_pieces(query, n_cp)
     key_rows_normed = root_mean_scale(keys.astype(jnp.float32), key_norm_gain).astype(jnp.bfloat16)
     key_value = jnp.concatenate([key_rows_normed, values], axis=-1)
+    doc_pieces = cp_pieces(segment_ids, n_cp)
     kv_all = jnp.concatenate(cp_pieces(key_value, n_cp), axis=1)
-    doc_all = jnp.concatenate(cp_pieces(segment_ids, n_cp), axis=1)
+    doc_all = jnp.concatenate(doc_pieces, axis=1)
     key_piece = kv_all[..., :HEAD_WIDTH]
     value_piece = kv_all[..., HEAD_WIDTH:]
-    scores = (
-        jnp.einsum(
-            "pshd,pnd->phsn", query_rows_normed, key_piece, preferred_element_type=jnp.float32
-        )
-        * score_scale
-    )
-    same_doc = segment_ids[:, :, None] == doc_all[:, None, :]
-    probs = jnp.where(same_doc[:, None], jnp.exp(scores), jnp.float32(0.0))
-    denom = jnp.sum(probs, axis=-1)
-    probs_b = probs.astype(jnp.bfloat16)
-    summed = jnp.einsum("phsn,pnd->pshd", probs_b, value_piece, preferred_element_type=jnp.float32)
-    attn = (
-        (summed / jnp.transpose(denom, (0, 2, 1))[:, :, :, None])
-        .astype(jnp.bfloat16)
-        .reshape(packs * row_count, head_count * HEAD_WIDTH)
-    )
+
+    def attention(query_rows, docs):
+        query_rows_normed = root_mean_scale(
+            query_rows.astype(jnp.float32).reshape(packs, row_count, head_count, HEAD_WIDTH),
+            query_norm_gain,
+        ).astype(jnp.bfloat16)
+        scores = (
+            jnp.einsum(
+                "pshd,pnd->phsn", query_rows_normed, key_piece, preferred_element_type=jnp.float32
+            )
+            * score_scale
+        )
+        same_doc = docs[:, :, None] == doc_all[:, None, :]
+        probs = jnp.where(same_doc[:, None], jnp.exp(scores), jnp.float32(0.0))
+        denom = jnp.sum(probs, axis=-1)
+        probs_b = probs.astype(jnp.bfloat16)
+        summed = jnp.einsum(
+            "phsn,pnd->pshd", probs_b, value_piece, preferred_element_type=jnp.float32
+        )
+        return (
+            (summed / jnp.transpose(denom, (0, 2, 1))[:, :, :, None])
+            .astype(jnp.bfloat16)
+            .reshape(packs * row_count, head_count * HEAD_WIDTH)
+        )
+
     share = row_count // n_tp
     tp_index = lax.axis_index("tp")
     ep_index = lax.axis_index("ep")
     cp_index = lax.axis_index("cp")
     cap = capacity(share, top_count, experts)
-    attn_pieces = cp_pieces(attn, n_cp)
     received_blocks = []
-    for j, piece in enumerate(attn_pieces):
-        if j > 0:
-            piece, received_blocks[0] = lax.optimization_barrier((piece, received_blocks[0]))
+    for j in range(n_cp):
+        piece = attention(query_pieces[j], doc_pieces[j])
         block = jnp.dot(piece, out_weight, preferred_element_type=jnp.float32).reshape(
             packs, row_count, out_weight.shape[1]
         )
@@ -143,8 +149,8 @@
     home_rows = packs * share
     normed = root_mean_scale(state.reshape(home_rows, width), norm_gain).astype(jnp.bfloat16)
 
-    attn_pieces, expert_gate, expert_up, expert_down = lax.optimization_barrier(
-        (attn_pieces, expert_gate, expert_up, expert_down)
+    query_pieces, expert_gate, expert_up, expert_down = lax.optimization_barrier(
+        (query_pieces, expert_gate, expert_up, expert_down)
     )
     gate_pieces = cp_pieces(expert_gate, n_cp)
     normed, gate_pieces = lax.optimization_barrier((normed, gate_pieces))

time: 312 us -> 323 us (1.035)
  other arithmetic: 18.5 us -> 27.3 us
  matrix products: 60.9 us -> 65.6 us
    reduce_scatter x2, waiting for transfers between devices: 24.5 us -> 43.5 us  [shards(): lax.psum_scatter(block.astype(jnp.bfloat16), 'tp', scatter_dimension=1, t...]
    ppermute x1, waiting for transfers between devices: 14.4 us -> 0.01 us  [shards(): lax.ppermute(summed, 'cp', [(i, (i - j) % n_cp) for i in range(n_cp)])]
    ppermute x5, waiting for transfers between devices: 24.9 us -> 17.2 us  [cp_pieces(): pieces.append(lax.ppermute(x, 'cp', perm))]
    dot_general x2 -> x4, matrix products: 3.81 us -> 8.49 us  [the longest x2 5.35 us: attention(): jnp.einsum('pshd,pnd->phsn', query_rows_normed, key_piece, preferred_elem...]
  transfers between devices with their start and end apart: 16 -> 16, of which waited for: 10 -> 9; matrix products, arithmetic and copies ran while one was open for 26% -> 28% of each run, Pallas kernels for 0% -> 0%
where the time goes in v13:
time: 323 us; the launch traced here: 322 us
  waiting for transfers between devices  175 us (54%)
  matrix products  65.6 us (20%)
  other arithmetic  27.3 us (8%)
  starting transfers between devices  27.2 us (8%)
  between operations  14 us (4%)
  local copies, waits for them, and re-layouts  13.5 us (4%)
    all_gather x2, waiting for transfers between devices, shards(): lax.all_gather(jnp.concatenate([rows, id_lanes], axis=1), 'ep', axis=0, t...  47.5 us
    reduce_scatter x2, waiting for transfers between devices, shards(): lax.psum_scatter(block.astype(jnp.bfloat16), 'tp', scatter_dimension=1, t...  43.5 us
    all_to_all x2, waiting for transfers between devices, shards(): lax.all_to_all(served, 'tp', split_axis=0, concat_axis=0, tiled=True)  31.1 us
    reduce_scatter x2, waiting for transfers between devices, shards(): lax.psum_scatter(partial.astype(jnp.bfloat16).reshape(n_ep, share, width)...  26.5 us
    dot_general x2, matrix products, expert_rows(): jnp.einsum('rf,df->rd', hidden_act, full_down[0], preferred_element_type=...  18.8 us
    ppermute x5, waiting for transfers between devices, cp_pieces(): pieces.append(lax.ppermute(x, 'cp', perm))  17.2 us
    dot_general x2, matrix products, expert_rows(): jnp.dot(flat_rows, full_gate[0], preferred_element_type=jnp.float32)  11.2 us
    all_to_all x2, starting transfers between devices, shards(): lax.all_to_all(buffer.reshape(n_tp, cap2, width), 'tp', split_axis=0, con...  9.28 us
  transfers between devices with their start and end apart: 16, of which 9 were waited for; matrix products, arithmetic and copies ran while one was open for 28% of the time, Pallas kernels for 0%

profile of v13, /device:TPU:0, one launch (start us, length us, event | category | flops | bytes accessed | tf_op | source)
XLA Modules:
  0.0 322.2 jit_solution(13094077192391829150)
XLA Ops:
  6.5 3.0 collective-permute-start.1
  13.3 2.0 collective-permute-start
  22.8 17.2 %collective-permute-done = bf16[2,256,256]{2,1,0:T(8,128)(2,1)} collective-permute-done((bf16[2,256,256]{2,1,0:T(8,128)(2,1)}, bf16[2,256,256]{2,1,0:T(8,128)(2,1)}, u32[]{:S(2)}, u32[]{:S(2)}) %collective-permute-start) | collective-permute-done | bytes 262176 | tf_op jit(solution)/shard_map/ppermute | solution.py:43
  44.4 3.6 %fusion.23 = (bf16[2,256,8,128]{3,2,1,0:T(8,128)(2,1)}, bf16[2,256,8,128]{3,2,1,0:T(8,128)(2,1)S(1)}) fusion(f32[128]{0:T(128)S(1)} %copy-done.15, f32[2,256,8]{2,1,0:T(8,128)S(1)} %copy.101, f32[2,256,8]{2,1,0:T(8,128)S(1)} %copy.107, f32[2,256,8,128]{3,2,1,0:T(8,128)} %bitcast.153, f32[2,256,8,128]{3,2,1,0:T(8,128)} %bitcast.155), kind=kLoop, calls=%fused_computation.41 | loop fusion | flops 3145728 | bytes 6324736 | tf_op jit(solution)/shard_map/convert_element_type | solution.py:100
  48.1 2.2 fusion.2
  51.9 2.3 fusion.39
  54.3 3.1 fusion
  59.0 2.2 fusion.36
  62.0 17.6 %reduce-scatter.7.cloned.1.call-done = bf16[2,64,1024]{2,1,0:T(8,128)(2,1)} async-done(((bf16[2,256,1024]{2,1,0:T(8,128)(2,1)}), bf16[2,64,1024]{2,1,0:T(8,128)(2,1)}) %reduce-scatter.7.cloned.1.call-update) | async-done | bytes 262160 | tf_op jit(solution)/shard_map/reduce_scatter | solution.py:131
  81.2 25.9 %reduce-scatter.5.cloned.1.call-done = bf16[2,64,1024]{2,1,0:T(8,128)(2,1)} async-done(((bf16[2,256,1024]{2,1,0:T(8,128)(2,1)}), bf16[2,64,1024]{2,1,0:T(8,128)(2,1)}) %reduce-scatter.5.cloned.1.call-update) | async-done | bytes 262160 | tf_op jit(solution)/shard_map/reduce_scatter | solution.py:131
  111.5 3.3 %pad_maximum_fusion = bf16[1,2048,768]{2,1,0:T(8,128)(2,1)} fusion(bf16[1,2048,384]{2,1,0:T(8,128)(2,1)S(1)} %copy-done.6, bf16[1,2048,384]{2,1,0:T(8,128)(2,1)} %param.26), kind=kLoop, calls=%fused_computation.20 | loop fusion | flops 6291456 | bytes 6291456 | tf_op jit(solution)/shard_map/concatenate | solution.py:157
  116.3 23.9 %all-gather.3.cloned.1.call-done = bf16[256,2176]{1,0:T(8,128)(2,1)} async-done(((bf16[64,2176]{1,0:T(8,128)(2,1)}), bf16[256,2176]{1,0:T(8,128)(2,1)}) %all-gather.3.cloned.1.call-update) | async-done | bytes 1114128 | tf_op jit(solution)/shard_map/all_gather | solution.py:175
  142.3 3.4 %convolution_convert_fusion.3 = bf16[576,2048]{1,0:T(8,128)(2,1)} fusion(pred[576,256]{1,0:T(8,128)(4,1)S(1)} %fusion.5, bf16[256,2176]{1,0:T(8,128)(2,1)} %all-gather.3.cloned.1.call-done), kind=kOutput, calls=%fused_computation.27 | convolution fusion | flops 605159424 | bytes 3555328 | tf_op jit(solution)/shard_map/dot_general | solution.py:204
  146.5 4.6 %all-to-all-start = ((bf16[4,144,2048]{2,1,0:T(8,128)(2,1)}), bf16[4,144,2048]{2,1,0:T(8,128)(2,1)}, u32[]{:S(2)}, u32[]{:S(2)}) async-start(bf16[4,144,2048]{2,1,0:T(8,128)(2,1)} %bitcast.156), calls=%async_computation.2 | async-start | bytes 4718592 | tf_op jit(solution)/shard_map/all_to_all | solution.py:207
  151.7 23.5 %all-gather.5.cloned.1.call-done = bf16[256,2176]{1,0:T(8,128)(2,1)} async-done(((bf16[64,2176]{1,0:T(8,128)(2,1)}), bf16[256,2176]{1,0:T(8,128)(2,1)}) %all-gather.5.cloned.1.call-update) | async-done | bytes 1114128 | tf_op jit(solution)/shard_map/all_gather | solution.py:175
  177.2 3.4 %convolution_convert_fusion.2 = bf16[576,2048]{1,0:T(8,128)(2,1)} fusion(pred[576,256]{1,0:T(8,128)(4,1)S(1)} %fusion.4, bf16[256,2176]{1,0:T(8,128)(2,1)} %all-gather.5.cloned.1.call-done), kind=kOutput, calls=%fused_computation.26 | convolution fusion | flops 605159424 | bytes 3555328 | tf_op jit(solution)/shard_map/dot_general | solution.py:204
  180.6 4.6 %all-to-all-start.2 = ((bf16[4,144,2048]{2,1,0:T(8,128)(2,1)}), bf16[4,144,2048]{2,1,0:T(8,128)(2,1)}, u32[]{:S(2)}, u32[]{:S(2)}) async-start(bf16[4,144,2048]{2,1,0:T(8,128)(2,1)} %bitcast.157), calls=%async_computation.5 | async-start | bytes 4718592 | tf_op jit(solution)/shard_map/all_to_all | solution.py:207
  185.3 5.4 %fusion.33 = f32[576,768]{1,0:T(8,128)} fusion(bf16[576,2048]{1,0:T(8,128)(2,1)} %bitcast.21, bf16[1,2048,384]{2,1,0:T(8,128)(2,1)} %collective-permute-done.4, bf16[1,2048,384]{2,1,0:T(8,128)(2,1)S(1)} %copy-done.16), kind=kOutput, calls=%fused_computation.54 | convolution fusion | flops 1818230784 | bytes 7274496 | tf_op jit(solution)/shard_map/dot_general | solution.py:50
  190.6 5.2 %fusion.106 = (bf16[1,2048,384]{2,1,0:T(8,128)(2,1)S(1)}, bf16[1,2048,384]{2,1,0:T(8,128)(2,1)}, bf16[1,2048,384]{2,1,0:T(8,128)(2,1)}, bf16[1,2048,384]{2,1,0:T(8,128)(2,1)}) fusion(bf16[1,2048,768]{2,1,0:T(8,128)(2,1)} %pad_maximum_fusion, bf16[1,2048,768]{2,1,0:T(8,128)(2,1)} %collective-permute-done.5), kind=kLoop, calls=%fused_computation.181 | loop fusion | bytes 12582912 | tf_op jit(solution)/shard_map/slice | solution.py:213
  195.8 9.4 %convolution_convert_fusion.1 = bf16[576,2048]{1,0:T(8,128)(2,1)} fusion(bf16[1,2048,384]{2,1,0:T(8,128)(2,1)} %get-tuple-element.63, bf16[1,2048,384]{2,1,0:T(8,128)(2,1)} %get-tuple-element.48, f32[576,768]{1,0:T(8,128)} %fusion.33, bf16[576,2048]{1,0:T(8,128)(2,1)} %bitcast.21, bf16[1,2048,384]{2,1,0:T(8,128)(2,1)} %get-tuple-element.64, ...), kind=kOutput, calls=%fused_computation.25 | convolution fusion | flops 3640295424 | bytes 12779520 | tf_op jit(solution)/shard_map/rf,df->rd/dot_general | solution.py:53
  205.2 8.6 %all-to-all-done.2 = bf16[4,144,2048]{2,1,0:T(8,128)(2,1)} async-done(((bf16[4,144,2048]{2,1,0:T(8,128)(2,1)}), bf16[4,144,2048]{2,1,0:T(8,128)(2,1)}, u32[]{:S(2)}, u32[]{:S(2)}) %all-to-all-start.2) | async-done | bytes 2359328 | tf_op jit(solution)/shard_map/all_to_all | solution.py:207
  213.8 4.7 %all-to-all-start.1 = ((bf16[4,144,2048]{2,1,0:T(8,128)(2,1)}), bf16[4,144,2048]{2,1,0:T(8,128)(2,1)}, u32[]{:S(2)}, u32[]{:S(2)}) async-start(bf16[4,144,2048]{2,1,0:T(8,128)(2,1)} %bitcast.163), calls=%async_computation.3 | async-start | bytes 4718592 | tf_op jit(solution)/shard_map/all_to_all | solution.py:216
  220.0 5.8 %fusion.32 = f32[576,768]{1,0:T(8,128)} fusion(bf16[576,2048]{1,0:T(8,128)(2,1)} %bitcast.32, bf16[1,2048,384]{2,1,0:T(8,128)(2,1)} %collective-permute-done.4, bf16[1,2048,384]{2,1,0:T(8,128)(2,1)} %param.25), kind=kOutput, calls=%fused_computation.53 | convolution fusion | flops 1818230784 | bytes 7274496 | tf_op jit(solution)/shard_map/dot_general | solution.py:50
  225.8 9.4 %convolution_convert_fusion = bf16[576,2048]{1,0:T(8,128)(2,1)} fusion(bf16[1,2048,384]{2,1,0:T(8,128)(2,1)} %get-tuple-element.63, bf16[1,2048,384]{2,1,0:T(8,128)(2,1)} %get-tuple-element.48, f32[576,768]{1,0:T(8,128)} %fusion.32, bf16[576,2048]{1,0:T(8,128)(2,1)} %bitcast.32, bf16[1,2048,384]{2,1,0:T(8,128)(2,1)} %get-tuple-element.64, ...), kind=kOutput, calls=%fused_computation.24 | convolution fusion | flops 3640295424 | bytes 12779520 | tf_op jit(solution)/shard_map/rf,df->rd/dot_general | solution.py:53
  235.3 11.6 %all-to-all-done.1 = bf16[4,144,2048]{2,1,0:T(8,128)(2,1)} async-done(((bf16[4,144,2048]{2,1,0:T(8,128)(2,1)}), bf16[4,144,2048]{2,1,0:T(8,128)(2,1)}, u32[]{:S(2)}, u32[]{:S(2)}) %all-to-all-start.1) | async-done | bytes 2359328 | tf_op jit(solution)/shard_map/all_to_all | solution.py:216
  246.9 4.5 %all-to-all-start.3 = ((bf16[4,144,2048]{2,1,0:T(8,128)(2,1)}), bf16[4,144,2048]{2,1,0:T(8,128)(2,1)}, u32[]{:S(2)}, u32[]{:S(2)}) async-start(bf16[4,144,2048]{2,1,0:T(8,128)(2,1)} %bitcast.162), calls=%async_computation.6 | async-start | bytes 4718592 | tf_op jit(solution)/shard_map/all_to_all | solution.py:216
  251.5 2.9 fusion.67
  254.4 3.7 %fusion.16 = bf16[256,2048]{1,0:T(8,128)(2,1)} fusion(f32[256,2048]{1,0:T(8,128)S(1)} %fusion.67, bf16[576,2048]{1,0:T(8,128)(2,1)} %bitcast.26, f32[576,256]{1,0:T(8,128)S(1)} %copy-done.4), kind=kOutput, calls=%fused_computation.30 | convolution fusion | flops 605618176 | bytes 6094848 | tf_op jit(solution)/shard_map/dot_general | solution.py:224
  260.5 19.5 %all-to-all-done.3 = bf16[4,144,2048]{2,1,0:T(8,128)(2,1)} async-done(((bf16[4,144,2048]{2,1,0:T(8,128)(2,1)}), bf16[4,144,2048]{2,1,0:T(8,128)(2,1)}, u32[]{:S(2)}, u32[]{:S(2)}) %all-to-all-start.3) | async-done | bytes 2359328 | tf_op jit(solution)/shard_map/all_to_all | solution.py:216
  280.0 2.7 fusion.64
  282.7 4.2 %fusion.17 = bf16[256,2048]{1,0:T(8,128)(2,1)} fusion(f32[256,2048]{1,0:T(8,128)S(1)} %fusion.64, bf16[576,2048]{1,0:T(8,128)(2,1)} %bitcast.34, f32[576,256]{1,0:T(8,128)} %copy-done.5), kind=kOutput, calls=%fused_computation.31 | convolution fusion | flops 605618176 | bytes 6094848 | tf_op jit(solution)/shard_map/dot_general | solution.py:224
  287.0 26.5 %reduce-scatter.11.cloned.1.call-done = bf16[1,64,2048]{2,1,0:T(8,128)(2,1)} async-done(((bf16[4,64,2048]{2,1,0:T(8,128)(2,1)}), bf16[1,64,2048]{2,1,0:T(8,128)(2,1)}) %reduce-scatter.11.cloned.1.call-update) | async-done | bytes 262160 | tf_op jit(solution)/shard_map/reduce_scatter | solution.py:226
  (130 shorter events, 37.9 us)
Async XLA Ops:
  6.5 45.4 %copy-start = (bf16[1024,1024]{1,0:T(8,128)(2,1)S(1)}, bf16[1024,1024]{1,0:T(8,128)(2,1)}, u32[]{:S(2)}) copy-start(bf16[1024,1024]{1,0:T(8,128)(2,1)} %param.20) | copy-start | bytes 6291460
  6.5 73.0 %reduce-scatter.7.cloned.1.call-start = ((), (), s32[]{:S(2)}) async-start(), calls=%async_computation.9 | async-start | bytes 1310720 | tf_op jit(solution)/shard_map/reduce_scatter | solution.py:131
  6.5 13.8 %collective-permute-start.1 = (s32[2,256]{1,0:T(2,128)}, s32[2,256]{1,0:T(2,128)}, u32[]{:S(2)}, u32[]{:S(2)}) collective-permute-start(s32[2,256]{1,0:T(2,128)} %param.17), channel_id=1, source_target_pairs={{0,16},{16,0},{1,17},{17,1},{2,18},{18,2},{3,19},{19,3},{4,20},{20... | collective-permute-start | bytes 6152 | tf_op jit(solution)/shard_map/ppermute | solution.py:43
  9.5 32.4 %collective-permute-start.2 = (bf16[2,256,1024]{2,1,0:T(8,128)(2,1)}, bf16[2,256,1024]{2,1,0:T(8,128)(2,1)S(1)}, u32[]{:S(2)}, u32[]{:S(2)}) collective-permute-start(bf16[2,256,1024]{2,1,0:T(8,128)(2,1)} %param.14), channel_id=1, source_target_pairs={{0,16},{16,0},{1,17},{17,1},{2,18},{18,2},{3,19},{19,3},{4,20},{20... | collective-permute-start | bytes 3145736 | tf_op jit(solution)/shard_map/ppermute | solution.py:43
  13.3 26.8 %collective-permute-start = (bf16[2,256,256]{2,1,0:T(8,128)(2,1)}, bf16[2,256,256]{2,1,0:T(8,128)(2,1)}, u32[]{:S(2)}, u32[]{:S(2)}) collective-permute-start(bf16[2,256,256]{2,1,0:T(8,128)(2,1)} %pad_maximum_fusion.2), channel_id=1, source_target_pairs={{0,16},{16,0},{1,17},{17,1},{2,18},{18,2},{3,19},{19,3},{4,20},{20... | collective-permute-start | bytes 786440 | tf_op jit(solution)/shard_map/ppermute | solution.py:43
  41.9 2.5 copy-start.15
  44.4 3.7 %copy-start.9 = (bf16[2,512,256]{2,1,0:T(8,128)(2,1)S(1)}, bf16[2,512,256]{2,1,0:T(8,128)(2,1)}, u32[]{:S(2)}) copy-start(bf16[2,512,256]{2,1,0:T(8,128)(2,1)} %pad_maximum_fusion.1) | copy-start | bytes 1572868
  44.4 3.7 %copy-start.12 = (pred[2,256,512]{1,2,0:T(8,128)(4,1)S(1)}, pred[2,256,512]{1,2,0:T(8,128)(4,1)}, u32[]{:S(2)}) copy-start(pred[2,256,512]{1,2,0:T(8,128)(4,1)} %get-tuple-element.56) | copy-start | bytes 786436
  51.9 2.4 copy-start.8
  51.9 2.4 copy-start.11
  54.2 53.0 %reduce-scatter.5.cloned.1.call-start = ((), (), s32[]{:S(2)}) async-start(), calls=%async_computation.8 | async-start | bytes 1310720 | tf_op jit(solution)/shard_map/reduce_scatter | solution.py:131
  54.3 3.1 copy-start.10
  59.0 2.5 copy-start.14
  61.3 79.0 %all-gather.3.cloned.1.call-start = ((), (), s32[]{:S(2)}) async-start(), calls=%async_computation.10 | async-start | bytes 1392640 | tf_op jit(solution)/shard_map/all_gather | solution.py:175
  61.7 48.6 %collective-permute-start.4 = (bf16[1,2048,384]{2,1,0:T(8,128)(2,1)}, bf16[1,2048,384]{2,1,0:T(8,128)(2,1)}, u32[]{:S(2)}, u32[]{:S(2)}) collective-permute-start(bf16[1,2048,384]{2,1,0:T(8,128)(2,1)} %param.25), channel_id=1, source_target_pairs={{0,16},{16,0},{1,17},{17,1},{2,18},{18,2},{3,19},{19,3},{4,20},{20... | collective-permute-start | bytes 4718600 | tf_op jit(solution)/shard_map/ppermute | solution.py:43
  79.6 27.6 %collective-permute-start.3 = (bf16[2,64,1024]{2,1,0:T(8,128)(2,1)}, bf16[2,64,1024]{2,1,0:T(8,128)(2,1)S(1)}, u32[]{:S(2)}, u32[]{:S(2)}) collective-permute-start(bf16[2,64,1024]{2,1,0:T(8,128)(2,1)} %reduce-scatter.7.cloned.1.call-done), channel_id=1, source_target_pairs={{0,16},{16,0},{1,17},{17,1},{2,18},{18,2},{3,19},{19,3},{4,20},{20... | collective-permute-start | bytes 786440 | tf_op jit(solution)/shard_map/ppermute | solution.py:135
  108.6 1.5 copy-start.13
  110.0 1.5 copy-start.6
  111.1 64.1 %all-gather.5.cloned.1.call-start = ((), (), s32[]{:S(2)}) async-start(), calls=%async_computation.12 | async-start | bytes 1392640 | tf_op jit(solution)/shard_map/all_gather | solution.py:175
  114.8 70.4 %collective-permute-start.5 = (bf16[1,2048,768]{2,1,0:T(8,128)(2,1)}, bf16[1,2048,768]{2,1,0:T(8,128)(2,1)}, u32[]{:S(2)}, u32[]{:S(2)}) collective-permute-start(bf16[1,2048,768]{2,1,0:T(8,128)(2,1)} %pad_maximum_fusion), channel_id=1, source_target_pairs={{0,16},{16,0},{1,17},{17,1},{2,18},{18,2},{3,19},{19,3},{4,20},{20... | collective-permute-start | bytes 9437192 | tf_op jit(solution)/shard_map/ppermute | solution.py:43
  146.5 4.7 %copy-start.7 = (bf16[256,2176]{1,0:T(8,128)(2,1)S(1)}, bf16[256,2176]{1,0:T(8,128)(2,1)}, u32[]{:S(2)}) copy-start(bf16[256,2176]{1,0:T(8,128)(2,1)} %all-gather.3.cloned.1.call-done) | copy-start | bytes 3342340
  146.5 4.7 %copy-start.17 = (bf16[2048,16]{0,1:T(8,128)(2,1)S(1)}, bf16[2048,16]{0,1:T(8,128)(2,1)}, u32[]{:S(2)}) copy-start(bf16[2048,16]{0,1:T(8,128)(2,1)} %param.23) | copy-start | bytes 196612
  146.5 34.1 %all-to-all-start = ((bf16[4,144,2048]{2,1,0:T(8,128)(2,1)}), bf16[4,144,2048]{2,1,0:T(8,128)(2,1)}, u32[]{:S(2)}, u32[]{:S(2)}) async-start(bf16[4,144,2048]{2,1,0:T(8,128)(2,1)} %bitcast.156), calls=%async_computation.2 | async-start | bytes 4718592 | tf_op jit(solution)/shard_map/all_to_all | solution.py:207
  180.6 4.7 %copy-start.16 = (bf16[1,2048,384]{2,1,0:T(8,128)(2,1)S(1)}, bf16[1,2048,384]{2,1,0:T(8,128)(2,1)}, u32[]{:S(2)}) copy-start(bf16[1,2048,384]{2,1,0:T(8,128)(2,1)} %param.25) | copy-start | bytes 4718596
  180.6 33.2 %all-to-all-start.2 = ((bf16[4,144,2048]{2,1,0:T(8,128)(2,1)}), bf16[4,144,2048]{2,1,0:T(8,128)(2,1)}, u32[]{:S(2)}, u32[]{:S(2)}) async-start(bf16[4,144,2048]{2,1,0:T(8,128)(2,1)} %bitcast.157), calls=%async_computation.5 | async-start | bytes 4718592 | tf_op jit(solution)/shard_map/all_to_all | solution.py:207
  213.8 33.1 %all-to-all-start.1 = ((bf16[4,144,2048]{2,1,0:T(8,128)(2,1)}), bf16[4,144,2048]{2,1,0:T(8,128)(2,1)}, u32[]{:S(2)}, u32[]{:S(2)}) async-start(bf16[4,144,2048]{2,1,0:T(8,128)(2,1)} %bitcast.163), calls=%async_computation.3 | async-start | bytes 4718592 | tf_op jit(solution)/shard_map/all_to_all | solution.py:216
  246.9 33.1 %all-to-all-start.3 = ((bf16[4,144,2048]{2,1,0:T(8,128)(2,1)}), bf16[4,144,2048]{2,1,0:T(8,128)(2,1)}, u32[]{:S(2)}, u32[]{:S(2)}) async-start(bf16[4,144,2048]{2,1,0:T(8,128)(2,1)} %bitcast.162), calls=%async_computation.6 | async-start | bytes 4718592 | tf_op jit(solution)/shard_map/all_to_all | solution.py:216
  251.4 35.5 %reduce-scatter.9.cloned.1.call-start = ((), (), s32[]{:S(2)}) async-start(), calls=%async_computation.11 | async-start | bytes 1310720 | tf_op jit(solution)/shard_map/reduce_scatter | solution.py:226
  251.5 2.9 copy-start.4
  258.1 55.3 %reduce-scatter.11.cloned.1.call-start = ((), (), s32[]{:S(2)}) async-start(), calls=%async_computation.13 | async-start | bytes 1310720 | tf_op jit(solution)/shard_map/reduce_scatter | solution.py:226
  260.5 19.5 %copy-start.5 = (f32[576,256]{1,0:T(8,128)}, f32[576,256]{1,0:T(8,128)S(1)}, u32[]{:S(2)}) copy-start(f32[576,256]{1,0:T(8,128)S(1)} %select_reduce_fusion) | copy-start | bytes 1769476
  282.7 32.7 %copy-start.1 = (bf16[1024,1024]{1,0:T(8,128)(2,1)S(1)}, bf16[1024,1024]{1,0:T(8,128)(2,1)}, u32[]{:S(2)}) copy-start(bf16[1024,1024]{1,0:T(8,128)(2,1)} %param.20) | copy-start | bytes 6291460
  (2 other events, 2.7 us)
Sparse Core Ops, SparseCore 0:
  54.3 25.1 reduce-scatter.6
  82.3 24.8 reduce-scatter.4
  111.2 29.0 all-gather.2
  146.6 28.5 all-gather.4
  258.3 27.0 reduce-scatter.8
  287.6 25.7 reduce-scatter.10

commit v14 on v11

--- a/solution.py
+++ b/solution.py
@@ -158,7 +158,6 @@
     gathered = n_ep * share
     row_iota = jnp.arange(gathered, dtype=jnp.int32)
     earlier = (row_iota[:, None] > row_iota[None, :]).astype(jnp.bfloat16)
-    contract = (((0,), (0,)), ((), ()))
     mixtures = []
     for chunk in range(packs):
         rows = normed[chunk * share : (chunk + 1) * share]
@@ -193,7 +192,10 @@
             full_gate = jnp.concatenate(gate_pieces, axis=2)
         hit = target[:, None, :] == jnp.arange(n_slots, dtype=jnp.int32)[None, :, None]
         select = jnp.any(hit, axis=0).astype(jnp.bfloat16)
-        weight = jnp.sum(jnp.where(hit, gates_all.T[:, None, :], jnp.float32(0.0)), axis=0)
+        hit_by_token = target[:, :, None] == jnp.arange(n_slots, dtype=jnp.int32)[None, None, :]
+        weight = jnp.sum(
+            jnp.where(hit_by_token, gates_all.T[:, :, None], jnp.float32(0.0)), axis=0
+        )
 
         buffer = jnp.dot(select, normed_all, preferred_element_type=jnp.float32).astype(
             jnp.bfloat16
@@ -213,9 +215,9 @@
 
         weight_hi = weight.astype(jnp.bfloat16)
         weight_lo = (weight - weight_hi.astype(jnp.float32)).astype(jnp.bfloat16)
-        partial = lax.dot_general(
-            weight_hi, back, contract, preferred_element_type=jnp.float32
-        ) + lax.dot_general(weight_lo, back, contract, preferred_element_type=jnp.float32)
+        partial = jnp.dot(weight_hi, back, preferred_element_type=jnp.float32) + jnp.dot(
+            weight_lo, back, preferred_element_type=jnp.float32
+        )
         mixtures.append(
             lax.psum_scatter(
                 partial.astype(jnp.bfloat16).reshape(n_ep, share, width),

time: 312 us -> 312 us (level)
  no operation moved by 1% of the time
where the time goes in v14:
time: 312 us; the launch traced here: 311 us
  waiting for transfers between devices  177 us (57%)
  matrix products  60.9 us (20%)
  starting transfers between devices  26.6 us (9%)
  other arithmetic  18.5 us (6%)
  between operations  14 us (4%)
  local copies, waits for them, and re-layouts  13.9 us (4%)
    all_gather x2, waiting for transfers between devices, shards(): lax.all_gather(jnp.concatenate([rows, id_lanes], axis=1), 'ep', axis=0, t...  47.3 us
    all_to_all x2, waiting for transfers between devices, shards(): lax.all_to_all(served, 'tp', split_axis=0, concat_axis=0, tiled=True)  31.1 us
    reduce_scatter x2, waiting for transfers between devices, shards(): lax.psum_scatter(partial.astype(jnp.bfloat16).reshape(n_ep, share, width)...  26.5 us
    ppermute x5, waiting for transfers between devices, cp_pieces(): pieces.append(lax.ppermute(x, 'cp', perm))  24.9 us
    reduce_scatter x2, waiting for transfers between devices, shards(): lax.psum_scatter(block.astype(jnp.bfloat16), 'tp', scatter_dimension=1, t...  24.5 us
    dot_general x2, matrix products, expert_rows(): jnp.einsum('rf,df->rd', hidden_act, full_down[0], preferred_element_type=...  18.8 us
    ppermute x1, waiting for transfers between devices, shards(): lax.ppermute(summed, 'cp', [(i, (i - j) % n_cp) for i in range(n_cp)])  14.4 us
    dot_general x2, matrix products, expert_rows(): jnp.dot(flat_rows, full_gate[0], preferred_element_type=jnp.float32)  11.2 us
  transfers between devices with their start and end apart: 16, of which 10 were waited for; matrix products, arithmetic and copies ran while one was open for 26% of the time, Pallas kernels for 0%

profile of v14, /device:TPU:0, one launch (start us, length us, event | category | flops | bytes accessed | tf_op | source)
XLA Modules:
  0.0 311.3 jit_solution(12733667623735496090)
XLA Ops:
  6.5 3.0 collective-permute-start.1
  16.5 1.9 fusion.13
  20.4 2.2 fusion
  25.3 2.3 fusion.23
  27.6 1.7 copy.92
  30.1 23.3 %collective-permute-done.2 = bf16[512,1024]{1,0:T(8,128)(2,1)S(1)} collective-permute-done((bf16[512,1024]{1,0:T(8,128)(2,1)S(1)}, bf16[512,1024]{1,0:T(8,128)(2,1)S(1)}, u32[]{:S(2)}, u32[]{:S(2)}) %collective-permute-start.2) | collective-permute-done | bytes 1048608 | tf_op jit(solution)/shard_map/ppermute | solution.py:43
  53.4 2.2 convolution_convert_fusion.4
  56.8 24.5 %reduce-scatter.7.cloned.1.call-done = bf16[2,64,1024]{2,1,0:T(8,128)(2,1)} async-done(((bf16[2,256,1024]{2,1,0:T(8,128)(2,1)}), bf16[2,64,1024]{2,1,0:T(8,128)(2,1)}) %reduce-scatter.7.cloned.1.call-update) | async-done | bytes 262160 | tf_op jit(solution)/shard_map/reduce_scatter | solution.py:125
  82.9 14.4 %collective-permute-done.3 = bf16[2,64,1024]{2,1,0:T(8,128)(2,1)S(1)} collective-permute-done((bf16[2,64,1024]{2,1,0:T(8,128)(2,1)}, bf16[2,64,1024]{2,1,0:T(8,128)(2,1)S(1)}, u32[]{:S(2)}, u32[]{:S(2)}) %collective-permute-start.3) | collective-permute-done | bytes 262176 | tf_op jit(solution)/shard_map/ppermute | solution.py:129
  100.6 3.3 %pad_maximum_fusion = bf16[1,2048,768]{2,1,0:T(8,128)(2,1)} fusion(bf16[1,2048,384]{2,1,0:T(8,128)(2,1)S(1)} %copy-done.6, bf16[1,2048,384]{2,1,0:T(8,128)(2,1)} %param.26), kind=kLoop, calls=%fused_computation.15 | loop fusion | flops 6291456 | bytes 6291456 | tf_op jit(solution)/shard_map/concatenate | solution.py:151
  105.4 24.0 %all-gather.3.cloned.1.call-done = bf16[256,2176]{1,0:T(8,128)(2,1)} async-done(((bf16[64,2176]{1,0:T(8,128)(2,1)}), bf16[256,2176]{1,0:T(8,128)(2,1)}) %all-gather.3.cloned.1.call-update) | async-done | bytes 1114128 | tf_op jit(solution)/shard_map/all_gather | solution.py:168
  131.4 3.4 %convolution_convert_fusion.3 = bf16[576,2048]{1,0:T(8,128)(2,1)} fusion(pred[576,256]{1,0:T(8,128)(4,1)S(1)} %fusion.2, bf16[256,2176]{1,0:T(8,128)(2,1)} %all-gather.3.cloned.1.call-done), kind=kOutput, calls=%fused_computation.22 | convolution fusion | flops 605159424 | bytes 3555328 | tf_op jit(solution)/shard_map/dot_general | solution.py:200
  135.6 4.8 %all-to-all-start = ((bf16[4,144,2048]{2,1,0:T(8,128)(2,1)}), bf16[4,144,2048]{2,1,0:T(8,128)(2,1)}, u32[]{:S(2)}, u32[]{:S(2)}) async-start(bf16[4,144,2048]{2,1,0:T(8,128)(2,1)} %bitcast.121), calls=%async_computation.2 | async-start | bytes 4718592 | tf_op jit(solution)/shard_map/all_to_all | solution.py:203
  140.9 23.3 %all-gather.5.cloned.1.call-done = bf16[256,2176]{1,0:T(8,128)(2,1)} async-done(((bf16[64,2176]{1,0:T(8,128)(2,1)}), bf16[256,2176]{1,0:T(8,128)(2,1)}) %all-gather.5.cloned.1.call-update) | async-done | bytes 1114128 | tf_op jit(solution)/shard_map/all_gather | solution.py:168
  166.3 3.4 %convolution_convert_fusion.2 = bf16[576,2048]{1,0:T(8,128)(2,1)} fusion(pred[576,256]{1,0:T(8,128)(4,1)S(1)} %fusion.3, bf16[256,2176]{1,0:T(8,128)(2,1)} %all-gather.5.cloned.1.call-done), kind=kOutput, calls=%fused_computation.21 | convolution fusion | flops 605159424 | bytes 3555328 | tf_op jit(solution)/shard_map/dot_general | solution.py:200
  169.7 4.6 %all-to-all-start.2 = ((bf16[4,144,2048]{2,1,0:T(8,128)(2,1)}), bf16[4,144,2048]{2,1,0:T(8,128)(2,1)}, u32[]{:S(2)}, u32[]{:S(2)}) async-start(bf16[4,144,2048]{2,1,0:T(8,128)(2,1)} %bitcast.122), calls=%async_computation.5 | async-start | bytes 4718592 | tf_op jit(solution)/shard_map/all_to_all | solution.py:203
  174.4 5.4 %fusion.20 = f32[576,768]{1,0:T(8,128)} fusion(bf16[576,2048]{1,0:T(8,128)(2,1)} %bitcast.16, bf16[1,2048,384]{2,1,0:T(8,128)(2,1)} %collective-permute-done.4, bf16[1,2048,384]{2,1,0:T(8,128)(2,1)S(1)} %copy-done.14), kind=kOutput, calls=%fused_computation.40 | convolution fusion | flops 1818230784 | bytes 7274496 | tf_op jit(solution)/shard_map/dot_general | solution.py:50
  179.7 5.2 %fusion.84 = (bf16[1,2048,384]{2,1,0:T(8,128)(2,1)S(1)}, bf16[1,2048,384]{2,1,0:T(8,128)(2,1)}, bf16[1,2048,384]{2,1,0:T(8,128)(2,1)}, bf16[1,2048,384]{2,1,0:T(8,128)(2,1)}) fusion(bf16[1,2048,768]{2,1,0:T(8,128)(2,1)} %pad_maximum_fusion, bf16[1,2048,768]{2,1,0:T(8,128)(2,1)} %collective-permute-done.5), kind=kLoop, calls=%fused_computation.162 | loop fusion | bytes 12582912 | tf_op jit(solution)/shard_map/slice | solution.py:209
  184.9 9.4 %convolution_convert_fusion.1 = bf16[576,2048]{1,0:T(8,128)(2,1)} fusion(bf16[1,2048,384]{2,1,0:T(8,128)(2,1)} %get-tuple-element.61, bf16[1,2048,384]{2,1,0:T(8,128)(2,1)} %get-tuple-element.52, f32[576,768]{1,0:T(8,128)} %fusion.20, bf16[576,2048]{1,0:T(8,128)(2,1)} %bitcast.16, bf16[1,2048,384]{2,1,0:T(8,128)(2,1)} %get-tuple-element.62, ...), kind=kOutput, calls=%fused_computation.20 | convolution fusion | flops 3640295424 | bytes 12779520 | tf_op jit(solution)/shard_map/rf,df->rd/dot_general | solution.py:53
  194.3 8.6 %all-to-all-done.2 = bf16[4,144,2048]{2,1,0:T(8,128)(2,1)} async-done(((bf16[4,144,2048]{2,1,0:T(8,128)(2,1)}), bf16[4,144,2048]{2,1,0:T(8,128)(2,1)}, u32[]{:S(2)}, u32[]{:S(2)}) %all-to-all-start.2) | async-done | bytes 2359328 | tf_op jit(solution)/shard_map/all_to_all | solution.py:203
  202.9 4.7 %all-to-all-start.1 = ((bf16[4,144,2048]{2,1,0:T(8,128)(2,1)}), bf16[4,144,2048]{2,1,0:T(8,128)(2,1)}, u32[]{:S(2)}, u32[]{:S(2)}) async-start(bf16[4,144,2048]{2,1,0:T(8,128)(2,1)} %bitcast.130), calls=%async_computation.3 | async-start | bytes 4718592 | tf_op jit(solution)/shard_map/all_to_all | solution.py:212
  209.1 5.8 %fusion.19 = f32[576,768]{1,0:T(8,128)} fusion(bf16[576,2048]{1,0:T(8,128)(2,1)} %bitcast.27, bf16[1,2048,384]{2,1,0:T(8,128)(2,1)} %collective-permute-done.4, bf16[1,2048,384]{2,1,0:T(8,128)(2,1)} %param.25), kind=kOutput, calls=%fused_computation.39 | convolution fusion | flops 1818230784 | bytes 7274496 | tf_op jit(solution)/shard_map/dot_general | solution.py:50
  214.9 9.4 %convolution_convert_fusion = bf16[576,2048]{1,0:T(8,128)(2,1)} fusion(bf16[1,2048,384]{2,1,0:T(8,128)(2,1)} %get-tuple-element.61, bf16[1,2048,384]{2,1,0:T(8,128)(2,1)} %get-tuple-element.52, f32[576,768]{1,0:T(8,128)} %fusion.19, bf16[576,2048]{1,0:T(8,128)(2,1)} %bitcast.27, bf16[1,2048,384]{2,1,0:T(8,128)(2,1)} %get-tuple-element.62, ...), kind=kOutput, calls=%fused_computation.19 | convolution fusion | flops 3640295424 | bytes 12779520 | tf_op jit(solution)/shard_map/rf,df->rd/dot_general | solution.py:53
  224.3 11.6 %all-to-all-done.1 = bf16[4,144,2048]{2,1,0:T(8,128)(2,1)} async-done(((bf16[4,144,2048]{2,1,0:T(8,128)(2,1)}), bf16[4,144,2048]{2,1,0:T(8,128)(2,1)}, u32[]{:S(2)}, u32[]{:S(2)}) %all-to-all-start.1) | async-done | bytes 2359328 | tf_op jit(solution)/shard_map/all_to_all | solution.py:212
  236.0 4.5 %all-to-all-start.3 = ((bf16[4,144,2048]{2,1,0:T(8,128)(2,1)}), bf16[4,144,2048]{2,1,0:T(8,128)(2,1)}, u32[]{:S(2)}, u32[]{:S(2)}) async-start(bf16[4,144,2048]{2,1,0:T(8,128)(2,1)} %bitcast.129), calls=%async_computation.6 | async-start | bytes 4718592 | tf_op jit(solution)/shard_map/all_to_all | solution.py:212
  240.6 2.9 fusion.47
  243.5 3.7 %fusion.9 = bf16[256,2048]{1,0:T(8,128)(2,1)} fusion(f32[256,2048]{1,0:T(8,128)S(1)} %fusion.47, bf16[576,2048]{1,0:T(8,128)(2,1)} %bitcast.21, f32[256,576]{0,1:T(8,128)S(1)} %copy-done.3), kind=kOutput, calls=%fused_computation.25 | convolution fusion | flops 605618176 | bytes 6094848 | tf_op jit(solution)/shard_map/dot_general | solution.py:218
  249.6 19.5 %all-to-all-done.3 = bf16[4,144,2048]{2,1,0:T(8,128)(2,1)} async-done(((bf16[4,144,2048]{2,1,0:T(8,128)(2,1)}), bf16[4,144,2048]{2,1,0:T(8,128)(2,1)}, u32[]{:S(2)}, u32[]{:S(2)}) %all-to-all-start.3) | async-done | bytes 2359328 | tf_op jit(solution)/shard_map/all_to_all | solution.py:212
  269.1 2.7 fusion.44
  271.8 4.2 %fusion.10 = bf16[256,2048]{1,0:T(8,128)(2,1)} fusion(f32[256,2048]{1,0:T(8,128)S(1)} %fusion.44, bf16[576,2048]{1,0:T(8,128)(2,1)} %bitcast.29, f32[256,576]{0,1:T(8,128)} %copy-done.4), kind=kOutput, calls=%fused_computation.26 | convolution fusion | flops 605618176 | bytes 6094848 | tf_op jit(solution)/shard_map/dot_general | solution.py:218
  276.0 26.5 %reduce-scatter.11.cloned.1.call-done = bf16[1,64,2048]{2,1,0:T(8,128)(2,1)} async-done(((bf16[4,64,2048]{2,1,0:T(8,128)(2,1)}), bf16[1,64,2048]{2,1,0:T(8,128)(2,1)}) %reduce-scatter.11.cloned.1.call-update) | async-done | bytes 262160 | tf_op jit(solution)/shard_map/reduce_scatter | solution.py:222
  302.5 1.9 add_convert_fusion
  (121 shorter events, 28.8 us)
Async XLA Ops:
  6.5 18.7 %copy-start = (bf16[1024,1024]{1,0:T(8,128)(2,1)S(1)}, bf16[1024,1024]{1,0:T(8,128)(2,1)}, u32[]{:S(2)}) copy-start(bf16[1024,1024]{1,0:T(8,128)(2,1)} %param.20) | copy-start | bytes 6291460
  6.5 46.8 %reduce-scatter.5.cloned.1.call-start = ((), (), s32[]{:S(2)}) async-start(), calls=%async_computation.8 | async-start | bytes 1310720 | tf_op jit(solution)/shard_map/reduce_scatter | solution.py:125
  6.5 12.0 %collective-permute-start.1 = (s32[2,256]{1,0:T(2,128)}, s32[2,256]{1,0:T(2,128)S(1)}, u32[]{:S(2)}, u32[]{:S(2)}) collective-permute-start(s32[2,256]{1,0:T(2,128)} %param.17), channel_id=1, source_target_pairs={{0,16},{16,0},{1,17},{17,1},{2,18},{18,2},{3,19},{19,3},{4,20},{20... | collective-permute-start | bytes 6152 | tf_op jit(solution)/shard_map/ppermute | solution.py:43
  12.6 7.8 %collective-permute-start = (bf16[2,256,256]{2,1,0:T(8,128)(2,1)S(1)}, bf16[2,256,256]{2,1,0:T(8,128)(2,1)S(1)}, u32[]{:S(2)}, u32[]{:S(2)}) collective-permute-start(bf16[2,256,256]{2,1,0:T(8,128)(2,1)S(1)} %pad_maximum_fusion.2), channel_id=1, source_target_pairs={{0,16},{16,0},{1,17},{17,1},{2,18},{18,2},{3,19},{19,3},{4,20},{20... | collective-permute-start | bytes 786440 | tf_op jit(solution)/shard_map/ppermute | solution.py:43
  12.8 3.8 %copy-start.13 = (f32[128]{0:T(128)S(1)}, f32[128]{0:T(128)}, u32[]{:S(2)}) copy-start(f32[128]{0:T(128)} %param.18) | copy-start | bytes 1540
  14.3 1.4 copy-start.2
  16.3 2.2 copy-start.11
  16.3 4.1 %copy-start.8 = (bf16[2,256,128]{2,1,0:T(8,128)(2,1)S(1)}, bf16[2,256,128]{2,1,0:T(8,128)(2,1)}, u32[]{:S(2)}) copy-start(bf16[2,256,128]{2,1,0:T(8,128)(2,1)} %param.16) | copy-start | bytes 393220
  24.3 1.0 copy-start.5
  27.5 53.8 %reduce-scatter.7.cloned.1.call-start = ((), (), s32[]{:S(2)}) async-start(), calls=%async_computation.9 | async-start | bytes 1310720 | tf_op jit(solution)/shard_map/reduce_scatter | solution.py:125
  29.6 26.1 %copy-start.12 = (s32[2,256,8]{1,2,0:T(8,128)S(1)}, s32[2,256,8]{1,2,0:T(8,128)}, u32[]{:S(2)}) copy-start(s32[2,256,8]{1,2,0:T(8,128)} %param.24) | copy-start | bytes 49156
  29.6 23.8 %collective-permute-start.2 = (bf16[512,1024]{1,0:T(8,128)(2,1)S(1)}, bf16[512,1024]{1,0:T(8,128)(2,1)S(1)}, u32[]{:S(2)}, u32[]{:S(2)}) collective-permute-start(bf16[512,1024]{1,0:T(8,128)(2,1)S(1)} %bitcast.133), channel_id=1, source_target_pairs={{0,16},{16,0},{1,17},{17,1},{2,18},{18,2},{3,19},{19,3},{4,20},{20... | collective-permute-start | bytes 3145736 | tf_op jit(solution)/shard_map/ppermute | solution.py:43
  53.4 44.0 %copy-start.9 = (bf16[2,64,1024]{2,1,0:T(8,128)(2,1)S(1)}, bf16[2,64,1024]{2,1,0:T(8,128)(2,1)}, u32[]{:S(2)}) copy-start(bf16[2,64,1024]{2,1,0:T(8,128)(2,1)} %reduce-scatter.5.cloned.1.call-done) | copy-start | bytes 786436
  55.6 73.7 %all-gather.3.cloned.1.call-start = ((), (), s32[]{:S(2)}) async-start(), calls=%async_computation.10 | async-start | bytes 1392640 | tf_op jit(solution)/shard_map/all_gather | solution.py:168
  55.8 43.6 %collective-permute-start.4 = (bf16[1,2048,384]{2,1,0:T(8,128)(2,1)}, bf16[1,2048,384]{2,1,0:T(8,128)(2,1)}, u32[]{:S(2)}, u32[]{:S(2)}) collective-permute-start(bf16[1,2048,384]{2,1,0:T(8,128)(2,1)} %param.25), channel_id=1, source_target_pairs={{0,16},{16,0},{1,17},{17,1},{2,18},{18,2},{3,19},{19,3},{4,20},{20... | collective-permute-start | bytes 4718600 | tf_op jit(solution)/shard_map/ppermute | solution.py:43
  81.3 16.0 %collective-permute-start.3 = (bf16[2,64,1024]{2,1,0:T(8,128)(2,1)}, bf16[2,64,1024]{2,1,0:T(8,128)(2,1)S(1)}, u32[]{:S(2)}, u32[]{:S(2)}) collective-permute-start(bf16[2,64,1024]{2,1,0:T(8,128)(2,1)} %reduce-scatter.7.cloned.1.call-done), channel_id=1, source_target_pairs={{0,16},{16,0},{1,17},{17,1},{2,18},{18,2},{3,19},{19,3},{4,20},{20... | collective-permute-start | bytes 786440 | tf_op jit(solution)/shard_map/ppermute | solution.py:129
  97.7 1.5 copy-start.10
  99.1 1.5 copy-start.6
  100.2 64.1 %all-gather.5.cloned.1.call-start = ((), (), s32[]{:S(2)}) async-start(), calls=%async_computation.12 | async-start | bytes 1392640 | tf_op jit(solution)/shard_map/all_gather | solution.py:168
  104.0 70.4 %collective-permute-start.5 = (bf16[1,2048,768]{2,1,0:T(8,128)(2,1)}, bf16[1,2048,768]{2,1,0:T(8,128)(2,1)}, u32[]{:S(2)}, u32[]{:S(2)}) collective-permute-start(bf16[1,2048,768]{2,1,0:T(8,128)(2,1)} %pad_maximum_fusion), channel_id=1, source_target_pairs={{0,16},{16,0},{1,17},{17,1},{2,18},{18,2},{3,19},{19,3},{4,20},{20... | collective-permute-start | bytes 9437192 | tf_op jit(solution)/shard_map/ppermute | solution.py:43
  135.6 4.9 %copy-start.7 = (bf16[256,2176]{1,0:T(8,128)(2,1)S(1)}, bf16[256,2176]{1,0:T(8,128)(2,1)}, u32[]{:S(2)}) copy-start(bf16[256,2176]{1,0:T(8,128)(2,1)} %all-gather.3.cloned.1.call-done) | copy-start | bytes 3342340
  135.6 4.9 %copy-start.15 = (bf16[2048,16]{0,1:T(8,128)(2,1)S(1)}, bf16[2048,16]{0,1:T(8,128)(2,1)}, u32[]{:S(2)}) copy-start(bf16[2048,16]{0,1:T(8,128)(2,1)} %param.23) | copy-start | bytes 196612
  135.6 34.1 %all-to-all-start = ((bf16[4,144,2048]{2,1,0:T(8,128)(2,1)}), bf16[4,144,2048]{2,1,0:T(8,128)(2,1)}, u32[]{:S(2)}, u32[]{:S(2)}) async-start(bf16[4,144,2048]{2,1,0:T(8,128)(2,1)} %bitcast.121), calls=%async_computation.2 | async-start | bytes 4718592 | tf_op jit(solution)/shard_map/all_to_all | solution.py:203
  169.7 4.7 %copy-start.14 = (bf16[1,2048,384]{2,1,0:T(8,128)(2,1)S(1)}, bf16[1,2048,384]{2,1,0:T(8,128)(2,1)}, u32[]{:S(2)}) copy-start(bf16[1,2048,384]{2,1,0:T(8,128)(2,1)} %param.25) | copy-start | bytes 4718596
  169.7 33.2 %all-to-all-start.2 = ((bf16[4,144,2048]{2,1,0:T(8,128)(2,1)}), bf16[4,144,2048]{2,1,0:T(8,128)(2,1)}, u32[]{:S(2)}, u32[]{:S(2)}) async-start(bf16[4,144,2048]{2,1,0:T(8,128)(2,1)} %bitcast.122), calls=%async_computation.5 | async-start | bytes 4718592 | tf_op jit(solution)/shard_map/all_to_all | solution.py:203
  202.9 33.1 %all-to-all-start.1 = ((bf16[4,144,2048]{2,1,0:T(8,128)(2,1)}), bf16[4,144,2048]{2,1,0:T(8,128)(2,1)}, u32[]{:S(2)}, u32[]{:S(2)}) async-start(bf16[4,144,2048]{2,1,0:T(8,128)(2,1)} %bitcast.130), calls=%async_computation.3 | async-start | bytes 4718592 | tf_op jit(solution)/shard_map/all_to_all | solution.py:212
  236.0 33.1 %all-to-all-start.3 = ((bf16[4,144,2048]{2,1,0:T(8,128)(2,1)}), bf16[4,144,2048]{2,1,0:T(8,128)(2,1)}, u32[]{:S(2)}, u32[]{:S(2)}) async-start(bf16[4,144,2048]{2,1,0:T(8,128)(2,1)} %bitcast.129), calls=%async_computation.6 | async-start | bytes 4718592 | tf_op jit(solution)/shard_map/all_to_all | solution.py:212
  240.5 35.5 %reduce-scatter.9.cloned.1.call-start = ((), (), s32[]{:S(2)}) async-start(), calls=%async_computation.11 | async-start | bytes 1310720 | tf_op jit(solution)/shard_map/reduce_scatter | solution.py:222
  240.6 2.9 copy-start.3
  247.2 55.3 %reduce-scatter.11.cloned.1.call-start = ((), (), s32[]{:S(2)}) async-start(), calls=%async_computation.13 | async-start | bytes 1310720 | tf_op jit(solution)/shard_map/reduce_scatter | solution.py:222
  249.6 19.5 %copy-start.4 = (f32[256,576]{0,1:T(8,128)}, f32[256,576]{0,1:T(8,128)S(1)}, u32[]{:S(2)}) copy-start(f32[256,576]{0,1:T(8,128)S(1)} %select_reduce_fusion) | copy-start | bytes 1769476
  271.8 32.7 %copy-start.1 = (bf16[1024,1024]{1,0:T(8,128)(2,1)S(1)}, bf16[1024,1024]{1,0:T(8,128)(2,1)}, u32[]{:S(2)}) copy-start(bf16[1024,1024]{1,0:T(8,128)(2,1)} %param.20) | copy-start | bytes 6291460
Sparse Core Ops, SparseCore 0:
  27.7 25.2 reduce-scatter.4
  55.8 25.4 reduce-scatter.6
  100.3 29.0 all-gather.2
  135.7 28.4 all-gather.4
  247.3 27.0 reduce-scatter.8
  276.7 25.7 reduce-scatter.10

commit v15 on v11

--- a/solution.py
+++ b/solution.py
@@ -159,16 +159,14 @@
     row_iota = jnp.arange(gathered, dtype=jnp.int32)
     earlier = (row_iota[:, None] > row_iota[None, :]).astype(jnp.bfloat16)
     contract = (((0,), (0,)), ((), ()))
+    id_lanes = jnp.pad(local_ids.astype(jnp.bfloat16), ((0, 0), (0, lanes - top_count)))
+    rows_with_ids = jnp.concatenate([normed, id_lanes], axis=1)
     mixtures = []
     for chunk in range(packs):
-        rows = normed[chunk * share : (chunk + 1) * share]
-        ids = local_ids[chunk * share : (chunk + 1) * share]
+        rows = rows_with_ids[chunk * share : (chunk + 1) * share]
         if chunk > 0:
-            rows, ids, _ = lax.optimization_barrier((rows, ids, buffer))
-        id_lanes = jnp.pad(ids.astype(jnp.bfloat16), ((0, 0), (0, lanes - top_count)))
-        rows_all = lax.all_gather(
-            jnp.concatenate([rows, id_lanes], axis=1), "ep", axis=0, tiled=True
-        )
+            rows, _ = lax.optimization_barrier((rows, buffer))
+        rows_all = lax.all_gather(rows, "ep", axis=0, tiled=True)
         normed_all = rows_all[:, :width]
         ids_all = rows_all[:, width : width + top_count].astype(jnp.int32)
         logits = jnp.dot(normed_all, router_weight, preferred_element_type=jnp.float32)

time: 312 us -> 312 us (level)
  transfers between devices with their start and end apart: 16 -> 16, of which waited for: 10 -> 10; matrix products, arithmetic and copies ran while one was open for 26% -> 25% of each run, Pallas kernels for 0% -> 0%
where the time goes in v15:
time: 312 us; the launch traced here: 311 us
  waiting for transfers between devices  177 us (57%)
  matrix products  60.9 us (20%)
  starting transfers between devices  26.6 us (9%)
  other arithmetic  17.6 us (6%)
  local copies, waits for them, and re-layouts  14.3 us (5%)
  between operations  14 us (4%)
    all_gather x2, waiting for transfers between devices, shards(): rows_all = lax.all_gather(rows, 'ep', axis=0, tiled=True)  47.2 us
    all_to_all x2, waiting for transfers between devices, shards(): lax.all_to_all(served, 'tp', split_axis=0, concat_axis=0, tiled=True)  31.1 us
    reduce_scatter x2, waiting for transfers between devices, shards(): lax.psum_scatter(partial.astype(jnp.bfloat16).reshape(n_ep, share, width)...  26.5 us
    ppermute x5, waiting for transfers between devices, cp_pieces(): pieces.append(lax.ppermute(x, 'cp', perm))  24.9 us
    reduce_scatter x2, waiting for transfers between devices, shards(): lax.psum_scatter(block.astype(jnp.bfloat16), 'tp', scatter_dimension=1, t...  24.5 us
    dot_general x2, matrix products, expert_rows(): jnp.einsum('rf,df->rd', hidden_act, full_down[0], preferred_element_type=...  18.8 us
    ppermute x1, waiting for transfers between devices, shards(): lax.ppermute(summed, 'cp', [(i, (i - j) % n_cp) for i in range(n_cp)])  14.3 us
    dot_general x2, matrix products, expert_rows(): jnp.dot(flat_rows, full_gate[0], preferred_element_type=jnp.float32)  11.2 us
  transfers between devices with their start and end apart: 16, of which 10 were waited for; matrix products, arithmetic and copies ran while one was open for 25% of the time, Pallas kernels for 0%

profile of v15, /device:TPU:0, one launch (start us, length us, event | category | flops | bytes accessed | tf_op | source)
XLA Modules:
  0.0 310.7 jit_solution(364503522960644901)
XLA Ops:
  6.5 3.0 collective-permute-start.1
  16.5 1.9 fusion.13
  20.4 2.2 fusion
  25.3 2.3 fusion.23
  27.6 1.7 copy.87
  30.1 23.3 %collective-permute-done.2 = bf16[512,1024]{1,0:T(8,128)(2,1)S(1)} collective-permute-done((bf16[512,1024]{1,0:T(8,128)(2,1)S(1)}, bf16[512,1024]{1,0:T(8,128)(2,1)S(1)}, u32[]{:S(2)}, u32[]{:S(2)}) %collective-permute-start.2) | collective-permute-done | bytes 1048608 | tf_op jit(solution)/shard_map/ppermute | solution.py:43
  53.4 2.3 convolution_convert_fusion.4
  56.9 24.5 %reduce-scatter.7.cloned.1.call-done = bf16[2,64,1024]{2,1,0:T(8,128)(2,1)} async-done(((bf16[2,256,1024]{2,1,0:T(8,128)(2,1)}), bf16[2,64,1024]{2,1,0:T(8,128)(2,1)}) %reduce-scatter.7.cloned.1.call-update) | async-done | bytes 262160 | tf_op jit(solution)/shard_map/reduce_scatter | solution.py:125
  83.0 14.3 %collective-permute-done.3 = bf16[2,64,1024]{2,1,0:T(8,128)(2,1)S(1)} collective-permute-done((bf16[2,64,1024]{2,1,0:T(8,128)(2,1)}, bf16[2,64,1024]{2,1,0:T(8,128)(2,1)S(1)}, u32[]{:S(2)}, u32[]{:S(2)}) %collective-permute-start.3) | collective-permute-done | bytes 262176 | tf_op jit(solution)/shard_map/ppermute | solution.py:129
  100.3 3.8 %pad_maximum_fusion = bf16[1,2048,768]{2,1,0:T(8,128)(2,1)} fusion(bf16[1,2048,384]{2,1,0:T(8,128)(2,1)} %param.27, bf16[1,2048,384]{2,1,0:T(8,128)(2,1)} %param.26), kind=kLoop, calls=%fused_computation.13 | loop fusion | flops 6291456 | bytes 6291456 | tf_op jit(solution)/shard_map/concatenate | solution.py:151
  105.6 23.9 %all-gather.3.cloned.1.call-done = bf16[256,2176]{1,0:T(8,128)(2,1)} async-done(((bf16[64,2176]{1,0:T(8,128)(2,1)}), bf16[256,2176]{1,0:T(8,128)(2,1)}) %all-gather.3.cloned.1.call-update) | async-done | bytes 1114128 | tf_op jit(solution)/shard_map/all_gather | solution.py:169
  131.5 3.4 %convolution_convert_fusion.3 = bf16[576,2048]{1,0:T(8,128)(2,1)} fusion(pred[576,256]{1,0:T(8,128)(4,1)S(1)} %fusion.3, bf16[256,2176]{1,0:T(8,128)(2,1)} %all-gather.3.cloned.1.call-done), kind=kOutput, calls=%fused_computation.20 | convolution fusion | flops 605159424 | bytes 3555328 | tf_op jit(solution)/shard_map/dot_general | solution.py:196
  135.0 4.8 %all-to-all-start = ((bf16[4,144,2048]{2,1,0:T(8,128)(2,1)}), bf16[4,144,2048]{2,1,0:T(8,128)(2,1)}, u32[]{:S(2)}, u32[]{:S(2)}) async-start(bf16[4,144,2048]{2,1,0:T(8,128)(2,1)} %bitcast.119), calls=%async_computation.2 | async-start | bytes 4718592 | tf_op jit(solution)/shard_map/all_to_all | solution.py:199
  140.3 23.3 %all-gather.5.cloned.1.call-done = bf16[256,2176]{1,0:T(8,128)(2,1)} async-done(((bf16[64,2176]{1,0:T(8,128)(2,1)}), bf16[256,2176]{1,0:T(8,128)(2,1)}) %all-gather.5.cloned.1.call-update) | async-done | bytes 1114128 | tf_op jit(solution)/shard_map/all_gather | solution.py:169
  165.6 3.4 %convolution_convert_fusion.2 = bf16[576,2048]{1,0:T(8,128)(2,1)} fusion(pred[576,256]{1,0:T(8,128)(4,1)S(1)} %fusion.2, bf16[256,2176]{1,0:T(8,128)(2,1)} %all-gather.5.cloned.1.call-done), kind=kOutput, calls=%fused_computation.19 | convolution fusion | flops 605159424 | bytes 3555328 | tf_op jit(solution)/shard_map/dot_general | solution.py:196
  169.0 4.6 %all-to-all-start.2 = ((bf16[4,144,2048]{2,1,0:T(8,128)(2,1)}), bf16[4,144,2048]{2,1,0:T(8,128)(2,1)}, u32[]{:S(2)}, u32[]{:S(2)}) async-start(bf16[4,144,2048]{2,1,0:T(8,128)(2,1)} %bitcast.120), calls=%async_computation.5 | async-start | bytes 4718592 | tf_op jit(solution)/shard_map/all_to_all | solution.py:199
  173.7 5.4 %fusion.20 = f32[576,768]{1,0:T(8,128)} fusion(bf16[576,2048]{1,0:T(8,128)(2,1)} %bitcast.16, bf16[1,2048,384]{2,1,0:T(8,128)(2,1)} %collective-permute-done.4, bf16[1,2048,384]{2,1,0:T(8,128)(2,1)S(1)} %copy-done.13), kind=kOutput, calls=%fused_computation.38 | convolution fusion | flops 1818230784 | bytes 7274496 | tf_op jit(solution)/shard_map/dot_general | solution.py:50
  179.1 5.2 %fusion.82 = (bf16[1,2048,384]{2,1,0:T(8,128)(2,1)S(1)}, bf16[1,2048,384]{2,1,0:T(8,128)(2,1)}, bf16[1,2048,384]{2,1,0:T(8,128)(2,1)}, bf16[1,2048,384]{2,1,0:T(8,128)(2,1)}) fusion(bf16[1,2048,768]{2,1,0:T(8,128)(2,1)} %pad_maximum_fusion, bf16[1,2048,768]{2,1,0:T(8,128)(2,1)} %collective-permute-done.5), kind=kLoop, calls=%fused_computation.157 | loop fusion | bytes 12582912 | tf_op jit(solution)/shard_map/slice | solution.py:205
  184.3 9.4 %convolution_convert_fusion.1 = bf16[576,2048]{1,0:T(8,128)(2,1)} fusion(bf16[1,2048,384]{2,1,0:T(8,128)(2,1)} %get-tuple-element.57, bf16[1,2048,384]{2,1,0:T(8,128)(2,1)} %get-tuple-element.50, f32[576,768]{1,0:T(8,128)} %fusion.20, bf16[576,2048]{1,0:T(8,128)(2,1)} %bitcast.16, bf16[1,2048,384]{2,1,0:T(8,128)(2,1)} %get-tuple-element.58, ...), kind=kOutput, calls=%fused_computation.18 | convolution fusion | flops 3640295424 | bytes 12779520 | tf_op jit(solution)/shard_map/rf,df->rd/dot_general | solution.py:53
  193.6 8.6 %all-to-all-done.2 = bf16[4,144,2048]{2,1,0:T(8,128)(2,1)} async-done(((bf16[4,144,2048]{2,1,0:T(8,128)(2,1)}), bf16[4,144,2048]{2,1,0:T(8,128)(2,1)}, u32[]{:S(2)}, u32[]{:S(2)}) %all-to-all-start.2) | async-done | bytes 2359328 | tf_op jit(solution)/shard_map/all_to_all | solution.py:199
  202.2 4.7 %all-to-all-start.1 = ((bf16[4,144,2048]{2,1,0:T(8,128)(2,1)}), bf16[4,144,2048]{2,1,0:T(8,128)(2,1)}, u32[]{:S(2)}, u32[]{:S(2)}) async-start(bf16[4,144,2048]{2,1,0:T(8,128)(2,1)} %bitcast.128), calls=%async_computation.3 | async-start | bytes 4718592 | tf_op jit(solution)/shard_map/all_to_all | solution.py:208
  208.4 5.8 %fusion.19 = f32[576,768]{1,0:T(8,128)} fusion(bf16[576,2048]{1,0:T(8,128)(2,1)} %bitcast.26, bf16[1,2048,384]{2,1,0:T(8,128)(2,1)} %collective-permute-done.4, bf16[1,2048,384]{2,1,0:T(8,128)(2,1)} %param.25), kind=kOutput, calls=%fused_computation.37 | convolution fusion | flops 1818230784 | bytes 7274496 | tf_op jit(solution)/shard_map/dot_general | solution.py:50
  214.2 9.4 %convolution_convert_fusion = bf16[576,2048]{1,0:T(8,128)(2,1)} fusion(bf16[1,2048,384]{2,1,0:T(8,128)(2,1)} %get-tuple-element.57, bf16[1,2048,384]{2,1,0:T(8,128)(2,1)} %get-tuple-element.50, f32[576,768]{1,0:T(8,128)} %fusion.19, bf16[576,2048]{1,0:T(8,128)(2,1)} %bitcast.26, bf16[1,2048,384]{2,1,0:T(8,128)(2,1)} %get-tuple-element.58, ...), kind=kOutput, calls=%fused_computation.17 | convolution fusion | flops 3640295424 | bytes 12779520 | tf_op jit(solution)/shard_map/rf,df->rd/dot_general | solution.py:53
  223.7 11.6 %all-to-all-done.1 = bf16[4,144,2048]{2,1,0:T(8,128)(2,1)} async-done(((bf16[4,144,2048]{2,1,0:T(8,128)(2,1)}), bf16[4,144,2048]{2,1,0:T(8,128)(2,1)}, u32[]{:S(2)}, u32[]{:S(2)}) %all-to-all-start.1) | async-done | bytes 2359328 | tf_op jit(solution)/shard_map/all_to_all | solution.py:208
  235.3 4.5 %all-to-all-start.3 = ((bf16[4,144,2048]{2,1,0:T(8,128)(2,1)}), bf16[4,144,2048]{2,1,0:T(8,128)(2,1)}, u32[]{:S(2)}, u32[]{:S(2)}) async-start(bf16[4,144,2048]{2,1,0:T(8,128)(2,1)} %bitcast.127), calls=%async_computation.6 | async-start | bytes 4718592 | tf_op jit(solution)/shard_map/all_to_all | solution.py:208
  239.9 2.9 fusion.45
  242.8 3.7 %fusion.9 = bf16[256,2048]{1,0:T(8,128)(2,1)} fusion(f32[256,2048]{1,0:T(8,128)S(1)} %fusion.45, bf16[576,2048]{1,0:T(8,128)(2,1)} %bitcast.21, f32[576,256]{1,0:T(8,128)S(1)} %copy-done.3), kind=kOutput, calls=%fused_computation.23 | convolution fusion | flops 605618176 | bytes 6094848 | tf_op jit(solution)/shard_map/dot_general | solution.py:216
  248.9 19.5 %all-to-all-done.3 = bf16[4,144,2048]{2,1,0:T(8,128)(2,1)} async-done(((bf16[4,144,2048]{2,1,0:T(8,128)(2,1)}), bf16[4,144,2048]{2,1,0:T(8,128)(2,1)}, u32[]{:S(2)}, u32[]{:S(2)}) %all-to-all-start.3) | async-done | bytes 2359328 | tf_op jit(solution)/shard_map/all_to_all | solution.py:208
  268.4 2.7 fusion.42
  271.1 4.2 %fusion.10 = bf16[256,2048]{1,0:T(8,128)(2,1)} fusion(f32[256,2048]{1,0:T(8,128)S(1)} %fusion.42, bf16[576,2048]{1,0:T(8,128)(2,1)} %bitcast.28, f32[576,256]{1,0:T(8,128)} %copy-done.4), kind=kOutput, calls=%fused_computation.24 | convolution fusion | flops 605618176 | bytes 6094848 | tf_op jit(solution)/shard_map/dot_general | solution.py:216
  275.4 26.5 %reduce-scatter.11.cloned.1.call-done = bf16[1,64,2048]{2,1,0:T(8,128)(2,1)} async-done(((bf16[4,64,2048]{2,1,0:T(8,128)(2,1)}), bf16[1,64,2048]{2,1,0:T(8,128)(2,1)}) %reduce-scatter.11.cloned.1.call-update) | async-done | bytes 262160 | tf_op jit(solution)/shard_map/reduce_scatter | solution.py:218
  301.9 1.9 add_convert_fusion
  (114 shorter events, 27.9 us)
Async XLA Ops:
  6.5 18.7 %copy-start = (bf16[1024,1024]{1,0:T(8,128)(2,1)S(1)}, bf16[1024,1024]{1,0:T(8,128)(2,1)}, u32[]{:S(2)}) copy-start(bf16[1024,1024]{1,0:T(8,128)(2,1)} %param.20) | copy-start | bytes 6291460
  6.5 46.8 %reduce-scatter.5.cloned.1.call-start = ((), (), s32[]{:S(2)}) async-start(), calls=%async_computation.8 | async-start | bytes 1310720 | tf_op jit(solution)/shard_map/reduce_scatter | solution.py:125
  6.5 12.0 %collective-permute-start.1 = (s32[2,256]{1,0:T(2,128)}, s32[2,256]{1,0:T(2,128)S(1)}, u32[]{:S(2)}, u32[]{:S(2)}) collective-permute-start(s32[2,256]{1,0:T(2,128)} %param.17), channel_id=1, source_target_pairs={{0,16},{16,0},{1,17},{17,1},{2,18},{18,2},{3,19},{19,3},{4,20},{20... | collective-permute-start | bytes 6152 | tf_op jit(solution)/shard_map/ppermute | solution.py:43
  12.6 7.8 %collective-permute-start = (bf16[2,256,256]{2,1,0:T(8,128)(2,1)S(1)}, bf16[2,256,256]{2,1,0:T(8,128)(2,1)S(1)}, u32[]{:S(2)}, u32[]{:S(2)}) collective-permute-start(bf16[2,256,256]{2,1,0:T(8,128)(2,1)S(1)} %pad_maximum_fusion.2), channel_id=1, source_target_pairs={{0,16},{16,0},{1,17},{17,1},{2,18},{18,2},{3,19},{19,3},{4,20},{20... | collective-permute-start | bytes 786440 | tf_op jit(solution)/shard_map/ppermute | solution.py:43
  12.8 3.8 %copy-start.12 = (f32[128]{0:T(128)S(1)}, f32[128]{0:T(128)}, u32[]{:S(2)}) copy-start(f32[128]{0:T(128)} %param.18) | copy-start | bytes 1540
  14.3 1.4 copy-start.2
  16.3 2.2 copy-start.10
  16.3 4.1 %copy-start.7 = (bf16[2,256,128]{2,1,0:T(8,128)(2,1)S(1)}, bf16[2,256,128]{2,1,0:T(8,128)(2,1)}, u32[]{:S(2)}) copy-start(bf16[2,256,128]{2,1,0:T(8,128)(2,1)} %param.16) | copy-start | bytes 393220
  24.3 1.0 copy-start.5
  27.5 53.8 %reduce-scatter.7.cloned.1.call-start = ((), (), s32[]{:S(2)}) async-start(), calls=%async_computation.9 | async-start | bytes 1310720 | tf_op jit(solution)/shard_map/reduce_scatter | solution.py:125
  29.6 27.2 %copy-start.11 = (s32[2,256,8]{1,2,0:T(8,128)S(1)}, s32[2,256,8]{1,2,0:T(8,128)}, u32[]{:S(2)}) copy-start(s32[2,256,8]{1,2,0:T(8,128)} %param.24) | copy-start | bytes 49156
  29.6 23.8 %collective-permute-start.2 = (bf16[512,1024]{1,0:T(8,128)(2,1)S(1)}, bf16[512,1024]{1,0:T(8,128)(2,1)S(1)}, u32[]{:S(2)}, u32[]{:S(2)}) collective-permute-start(bf16[512,1024]{1,0:T(8,128)(2,1)S(1)} %bitcast.131), channel_id=1, source_target_pairs={{0,16},{16,0},{1,17},{17,1},{2,18},{18,2},{3,19},{19,3},{4,20},{20... | collective-permute-start | bytes 3145736 | tf_op jit(solution)/shard_map/ppermute | solution.py:43
  53.4 43.9 %copy-start.8 = (bf16[2,64,1024]{2,1,0:T(8,128)(2,1)S(1)}, bf16[2,64,1024]{2,1,0:T(8,128)(2,1)}, u32[]{:S(2)}) copy-start(bf16[2,64,1024]{2,1,0:T(8,128)(2,1)} %reduce-scatter.5.cloned.1.call-done) | copy-start | bytes 786436
  55.7 73.8 %all-gather.3.cloned.1.call-start = ((), (), s32[]{:S(2)}) async-start(), calls=%async_computation.10 | async-start | bytes 1392640 | tf_op jit(solution)/shard_map/all_gather | solution.py:169
  55.7 43.6 %collective-permute-start.4 = (bf16[1,2048,384]{2,1,0:T(8,128)(2,1)}, bf16[1,2048,384]{2,1,0:T(8,128)(2,1)}, u32[]{:S(2)}, u32[]{:S(2)}) collective-permute-start(bf16[1,2048,384]{2,1,0:T(8,128)(2,1)} %param.25), channel_id=1, source_target_pairs={{0,16},{16,0},{1,17},{17,1},{2,18},{18,2},{3,19},{19,3},{4,20},{20... | collective-permute-start | bytes 4718600 | tf_op jit(solution)/shard_map/ppermute | solution.py:43
  81.3 16.0 %collective-permute-start.3 = (bf16[2,64,1024]{2,1,0:T(8,128)(2,1)}, bf16[2,64,1024]{2,1,0:T(8,128)(2,1)S(1)}, u32[]{:S(2)}, u32[]{:S(2)}) collective-permute-start(bf16[2,64,1024]{2,1,0:T(8,128)(2,1)} %reduce-scatter.7.cloned.1.call-done), channel_id=1, source_target_pairs={{0,16},{16,0},{1,17},{17,1},{2,18},{18,2},{3,19},{19,3},{4,20},{20... | collective-permute-start | bytes 786440 | tf_op jit(solution)/shard_map/ppermute | solution.py:129
  97.7 1.5 copy-start.9
  100.3 63.3 %all-gather.5.cloned.1.call-start = ((), (), s32[]{:S(2)}) async-start(), calls=%async_computation.12 | async-start | bytes 1392640 | tf_op jit(solution)/shard_map/all_gather | solution.py:169
  104.1 69.6 %collective-permute-start.5 = (bf16[1,2048,768]{2,1,0:T(8,128)(2,1)}, bf16[1,2048,768]{2,1,0:T(8,128)(2,1)}, u32[]{:S(2)}, u32[]{:S(2)}) collective-permute-start(bf16[1,2048,768]{2,1,0:T(8,128)(2,1)} %pad_maximum_fusion), channel_id=1, source_target_pairs={{0,16},{16,0},{1,17},{17,1},{2,18},{18,2},{3,19},{19,3},{4,20},{20... | collective-permute-start | bytes 9437192 | tf_op jit(solution)/shard_map/ppermute | solution.py:43
  134.9 4.9 %copy-start.6 = (bf16[256,2176]{1,0:T(8,128)(2,1)S(1)}, bf16[256,2176]{1,0:T(8,128)(2,1)}, u32[]{:S(2)}) copy-start(bf16[256,2176]{1,0:T(8,128)(2,1)} %all-gather.3.cloned.1.call-done) | copy-start | bytes 3342340
  134.9 4.9 %copy-start.14 = (bf16[2048,16]{0,1:T(8,128)(2,1)S(1)}, bf16[2048,16]{0,1:T(8,128)(2,1)}, u32[]{:S(2)}) copy-start(bf16[2048,16]{0,1:T(8,128)(2,1)} %param.23) | copy-start | bytes 196612
  135.0 34.1 %all-to-all-start = ((bf16[4,144,2048]{2,1,0:T(8,128)(2,1)}), bf16[4,144,2048]{2,1,0:T(8,128)(2,1)}, u32[]{:S(2)}, u32[]{:S(2)}) async-start(bf16[4,144,2048]{2,1,0:T(8,128)(2,1)} %bitcast.119), calls=%async_computation.2 | async-start | bytes 4718592 | tf_op jit(solution)/shard_map/all_to_all | solution.py:199
  169.0 4.7 %copy-start.13 = (bf16[1,2048,384]{2,1,0:T(8,128)(2,1)S(1)}, bf16[1,2048,384]{2,1,0:T(8,128)(2,1)}, u32[]{:S(2)}) copy-start(bf16[1,2048,384]{2,1,0:T(8,128)(2,1)} %param.25) | copy-start | bytes 4718596
  169.0 33.2 %all-to-all-start.2 = ((bf16[4,144,2048]{2,1,0:T(8,128)(2,1)}), bf16[4,144,2048]{2,1,0:T(8,128)(2,1)}, u32[]{:S(2)}, u32[]{:S(2)}) async-start(bf16[4,144,2048]{2,1,0:T(8,128)(2,1)} %bitcast.120), calls=%async_computation.5 | async-start | bytes 4718592 | tf_op jit(solution)/shard_map/all_to_all | solution.py:199
  202.2 33.1 %all-to-all-start.1 = ((bf16[4,144,2048]{2,1,0:T(8,128)(2,1)}), bf16[4,144,2048]{2,1,0:T(8,128)(2,1)}, u32[]{:S(2)}, u32[]{:S(2)}) async-start(bf16[4,144,2048]{2,1,0:T(8,128)(2,1)} %bitcast.128), calls=%async_computation.3 | async-start | bytes 4718592 | tf_op jit(solution)/shard_map/all_to_all | solution.py:208
  235.3 33.1 %all-to-all-start.3 = ((bf16[4,144,2048]{2,1,0:T(8,128)(2,1)}), bf16[4,144,2048]{2,1,0:T(8,128)(2,1)}, u32[]{:S(2)}, u32[]{:S(2)}) async-start(bf16[4,144,2048]{2,1,0:T(8,128)(2,1)} %bitcast.127), calls=%async_computation.6 | async-start | bytes 4718592 | tf_op jit(solution)/shard_map/all_to_all | solution.py:208
  239.8 35.5 %reduce-scatter.9.cloned.1.call-start = ((), (), s32[]{:S(2)}) async-start(), calls=%async_computation.11 | async-start | bytes 1310720 | tf_op jit(solution)/shard_map/reduce_scatter | solution.py:218
  239.9 2.9 copy-start.3
  246.6 55.3 %reduce-scatter.11.cloned.1.call-start = ((), (), s32[]{:S(2)}) async-start(), calls=%async_computation.13 | async-start | bytes 1310720 | tf_op jit(solution)/shard_map/reduce_scatter | solution.py:218
  248.9 19.5 %copy-start.4 = (f32[576,256]{1,0:T(8,128)}, f32[576,256]{1,0:T(8,128)S(1)}, u32[]{:S(2)}) copy-start(f32[576,256]{1,0:T(8,128)S(1)} %select_reduce_fusion) | copy-start | bytes 1769476
  271.1 32.7 %copy-start.1 = (bf16[1024,1024]{1,0:T(8,128)(2,1)S(1)}, bf16[1024,1024]{1,0:T(8,128)(2,1)}, u32[]{:S(2)}) copy-start(bf16[1024,1024]{1,0:T(8,128)(2,1)} %param.20) | copy-start | bytes 6291460
Sparse Core Ops, SparseCore 0:
  27.7 25.2 reduce-scatter.4
  55.8 25.5 reduce-scatter.6
  100.4 29.0 all-gather.2
  135.1 28.4 all-gather.4
  246.7 27.0 reduce-scatter.8
  276.0 25.7 reduce-scatter.10

commit v16 on v15

--- a/solution.py
+++ b/solution.py
@@ -104,11 +104,7 @@
     denom = jnp.sum(probs, axis=-1)
     probs_b = probs.astype(jnp.bfloat16)
     summed = jnp.einsum("phsn,pnd->pshd", probs_b, value_piece, preferred_element_type=jnp.float32)
-    attn = (
-        (summed / jnp.transpose(denom, (0, 2, 1))[:, :, :, None])
-        .astype(jnp.bfloat16)
-        .reshape(packs * row_count, head_count * HEAD_WIDTH)
-    )
+    attn = (summed / jnp.transpose(denom, (0, 2, 1))[:, :, :, None]).astype(jnp.bfloat16)
     share = row_count // n_tp
     tp_index = lax.axis_index("tp")
     ep_index = lax.axis_index("ep")
@@ -119,9 +115,11 @@
     for j, piece in enumerate(attn_pieces):
         if j > 0:
             piece, received_blocks[0] = lax.optimization_barrier((piece, received_blocks[0]))
-        block = jnp.dot(piece, out_weight, preferred_element_type=jnp.float32).reshape(
-            packs, row_count, out_weight.shape[1]
-        )
+        block = jnp.dot(
+            piece.reshape(packs * row_count, head_count * HEAD_WIDTH),
+            out_weight,
+            preferred_element_type=jnp.float32,
+        ).reshape(packs, row_count, out_weight.shape[1])
         summed = lax.psum_scatter(
             block.astype(jnp.bfloat16), "tp", scatter_dimension=1, tiled=True
         )

time: 312 us -> 312 us (level)
  transfers between devices with their start and end apart: 16 -> 16, of which waited for: 10 -> 11; matrix products, arithmetic and copies ran while one was open for 25% -> 25% of each run, Pallas kernels for 0% -> 0%
where the time goes in v16:
time: 312 us; the launch traced here: 311 us
  waiting for transfers between devices  179 us (57%)
  matrix products  62.2 us (20%)
  starting transfers between devices  27.1 us (9%)
  other arithmetic  17.6 us (6%)
  between operations  14 us (4%)
  local copies, waits for them, and re-layouts  11.3 us (4%)
    all_gather x2, waiting for transfers between devices, shards(): rows_all = lax.all_gather(rows, 'ep', axis=0, tiled=True)  47.4 us
    all_to_all x2, waiting for transfers between devices, shards(): lax.all_to_all(served, 'tp', split_axis=0, concat_axis=0, tiled=True)  31.1 us
    reduce_scatter x2, waiting for transfers between devices, shards(): lax.psum_scatter(partial.astype(jnp.bfloat16).reshape(n_ep, share, width)...  26.5 us
    ppermute x5, waiting for transfers between devices, cp_pieces(): pieces.append(lax.ppermute(x, 'cp', perm))  25 us
    reduce_scatter x2, waiting for transfers between devices, shards(): lax.psum_scatter(block.astype(jnp.bfloat16), 'tp', scatter_dimension=1, t...  24.8 us
    dot_general x2, matrix products, expert_rows(): jnp.einsum('rf,df->rd', hidden_act, full_down[0], preferred_element_type=...  18.8 us
    ppermute x1, waiting for transfers between devices, shards(): lax.ppermute(summed, 'cp', [(i, (i - j) % n_cp) for i in range(n_cp)])  15.4 us
    dot_general x2, matrix products, expert_rows(): jnp.dot(flat_rows, full_gate[0], preferred_element_type=jnp.float32)  11.2 us
  transfers between devices with their start and end apart: 16, of which 11 were waited for; matrix products, arithmetic and copies ran while one was open for 25% of the time, Pallas kernels for 0%

profile of v16, /device:TPU:0, one launch (start us, length us, event | category | flops | bytes accessed | tf_op | source)
XLA Modules:
  0.0 311.1 jit_solution(2507355340327791802)
XLA Ops:
  6.5 3.0 collective-permute-start.1
  16.5 1.9 fusion.13
  18.7 1.7 collective-permute-done
  20.4 2.2 fusion
  24.3 2.3 fusion.25
  27.1 23.4 %collective-permute-done.2 = bf16[2,256,8,128]{1,3,2,0:T(8,128)(2,1)} collective-permute-done((bf16[2,256,8,128]{1,3,2,0:T(8,128)(2,1)S(1)}, bf16[2,256,8,128]{1,3,2,0:T(8,128)(2,1)}, u32[]{:S(2)}, u32[]{:S(2)}) %collective-permute-start.2) | collective-permute-done | bytes 1048608 | tf_op jit(solution)/shard_map/ppermute | solution.py:43
  52.0 3.5 %fusion.28 = bf16[2,256,1024]{2,1,0:T(8,128)(2,1)} fusion(bf16[2,256,1024]{1,2,0:T(8,128)(2,1)} %bitcast.9, bf16[1024,1024]{1,0:T(8,128)(2,1)S(1)} %copy-done), kind=kOutput, calls=%fused_computation.44 | convolution fusion | flops 1074266112 | bytes 4194304 | tf_op jit(solution)/shard_map/dot_general | solution.py:118
  57.2 23.4 %reduce-scatter.7.cloned.1.call-done = bf16[2,64,1024]{2,1,0:T(8,128)(2,1)} async-done(((bf16[2,256,1024]{2,1,0:T(8,128)(2,1)}), bf16[2,64,1024]{2,1,0:T(8,128)(2,1)}) %reduce-scatter.7.cloned.1.call-update) | async-done | bytes 262160 | tf_op jit(solution)/shard_map/reduce_scatter | solution.py:123
  82.2 15.4 %collective-permute-done.3 = bf16[2,64,1024]{2,1,0:T(8,128)(2,1)S(1)} collective-permute-done((bf16[2,64,1024]{2,1,0:T(8,128)(2,1)}, bf16[2,64,1024]{2,1,0:T(8,128)(2,1)S(1)}, u32[]{:S(2)}, u32[]{:S(2)}) %collective-permute-start.3) | collective-permute-done | bytes 262176 | tf_op jit(solution)/shard_map/ppermute | solution.py:127
  100.6 3.8 %pad_maximum_fusion = bf16[1,2048,768]{2,1,0:T(8,128)(2,1)} fusion(bf16[1,2048,384]{2,1,0:T(8,128)(2,1)} %param.27, bf16[1,2048,384]{2,1,0:T(8,128)(2,1)} %param.26), kind=kLoop, calls=%fused_computation.13 | loop fusion | flops 6291456 | bytes 6291456 | tf_op jit(solution)/shard_map/concatenate | solution.py:149
  105.9 23.9 %all-gather.3.cloned.1.call-done = bf16[256,2176]{1,0:T(8,128)(2,1)} async-done(((bf16[64,2176]{1,0:T(8,128)(2,1)}), bf16[256,2176]{1,0:T(8,128)(2,1)}) %all-gather.3.cloned.1.call-update) | async-done | bytes 1114128 | tf_op jit(solution)/shard_map/all_gather | solution.py:167
  131.8 3.4 %convolution_convert_fusion.3 = bf16[576,2048]{1,0:T(8,128)(2,1)} fusion(pred[576,256]{1,0:T(8,128)(4,1)S(1)} %fusion.3, bf16[256,2176]{1,0:T(8,128)(2,1)} %all-gather.3.cloned.1.call-done), kind=kOutput, calls=%fused_computation.20 | convolution fusion | flops 605159424 | bytes 3555328 | tf_op jit(solution)/shard_map/dot_general | solution.py:194
  135.2 4.6 %all-to-all-start = ((bf16[4,144,2048]{2,1,0:T(8,128)(2,1)}), bf16[4,144,2048]{2,1,0:T(8,128)(2,1)}, u32[]{:S(2)}, u32[]{:S(2)}) async-start(bf16[4,144,2048]{2,1,0:T(8,128)(2,1)} %bitcast.117), calls=%async_computation.2 | async-start | bytes 4718592 | tf_op jit(solution)/shard_map/all_to_all | solution.py:197
  140.4 23.5 %all-gather.5.cloned.1.call-done = bf16[256,2176]{1,0:T(8,128)(2,1)} async-done(((bf16[64,2176]{1,0:T(8,128)(2,1)}), bf16[256,2176]{1,0:T(8,128)(2,1)}) %all-gather.5.cloned.1.call-update) | async-done | bytes 1114128 | tf_op jit(solution)/shard_map/all_gather | solution.py:167
  165.9 3.4 %convolution_convert_fusion.2 = bf16[576,2048]{1,0:T(8,128)(2,1)} fusion(pred[576,256]{1,0:T(8,128)(4,1)S(1)} %fusion.2, bf16[256,2176]{1,0:T(8,128)(2,1)} %all-gather.5.cloned.1.call-done), kind=kOutput, calls=%fused_computation.19 | convolution fusion | flops 605159424 | bytes 3555328 | tf_op jit(solution)/shard_map/dot_general | solution.py:194
  169.4 4.8 %all-to-all-start.2 = ((bf16[4,144,2048]{2,1,0:T(8,128)(2,1)}), bf16[4,144,2048]{2,1,0:T(8,128)(2,1)}, u32[]{:S(2)}, u32[]{:S(2)}) async-start(bf16[4,144,2048]{2,1,0:T(8,128)(2,1)} %bitcast.118), calls=%async_computation.5 | async-start | bytes 4718592 | tf_op jit(solution)/shard_map/all_to_all | solution.py:197
  174.2 5.4 %fusion.22 = f32[576,768]{1,0:T(8,128)} fusion(bf16[576,2048]{1,0:T(8,128)(2,1)} %bitcast.16, bf16[1,2048,384]{2,1,0:T(8,128)(2,1)} %collective-permute-done.4, bf16[1,2048,384]{2,1,0:T(8,128)(2,1)S(1)} %copy-done.12), kind=kOutput, calls=%fused_computation.40 | convolution fusion | flops 1818230784 | bytes 7274496 | tf_op jit(solution)/shard_map/dot_general | solution.py:50
  179.6 5.2 %fusion.87 = (bf16[1,2048,384]{2,1,0:T(8,128)(2,1)S(1)}, bf16[1,2048,384]{2,1,0:T(8,128)(2,1)}, bf16[1,2048,384]{2,1,0:T(8,128)(2,1)}, bf16[1,2048,384]{2,1,0:T(8,128)(2,1)}) fusion(bf16[1,2048,768]{2,1,0:T(8,128)(2,1)} %pad_maximum_fusion, bf16[1,2048,768]{2,1,0:T(8,128)(2,1)} %collective-permute-done.5), kind=kLoop, calls=%fused_computation.158 | loop fusion | bytes 12582912 | tf_op jit(solution)/shard_map/slice | solution.py:203
  184.8 9.4 %convolution_convert_fusion.1 = bf16[576,2048]{1,0:T(8,128)(2,1)} fusion(bf16[1,2048,384]{2,1,0:T(8,128)(2,1)} %get-tuple-element.57, bf16[1,2048,384]{2,1,0:T(8,128)(2,1)} %get-tuple-element.50, f32[576,768]{1,0:T(8,128)} %fusion.22, bf16[576,2048]{1,0:T(8,128)(2,1)} %bitcast.16, bf16[1,2048,384]{2,1,0:T(8,128)(2,1)} %get-tuple-element.58, ...), kind=kOutput, calls=%fused_computation.18 | convolution fusion | flops 3640295424 | bytes 12779520 | tf_op jit(solution)/shard_map/rf,df->rd/dot_general | solution.py:53
  194.1 8.6 %all-to-all-done.2 = bf16[4,144,2048]{2,1,0:T(8,128)(2,1)} async-done(((bf16[4,144,2048]{2,1,0:T(8,128)(2,1)}), bf16[4,144,2048]{2,1,0:T(8,128)(2,1)}, u32[]{:S(2)}, u32[]{:S(2)}) %all-to-all-start.2) | async-done | bytes 2359328 | tf_op jit(solution)/shard_map/all_to_all | solution.py:197
  202.7 4.5 %all-to-all-start.1 = ((bf16[4,144,2048]{2,1,0:T(8,128)(2,1)}), bf16[4,144,2048]{2,1,0:T(8,128)(2,1)}, u32[]{:S(2)}, u32[]{:S(2)}) async-start(bf16[4,144,2048]{2,1,0:T(8,128)(2,1)} %bitcast.124), calls=%async_computation.3 | async-start | bytes 4718592 | tf_op jit(solution)/shard_map/all_to_all | solution.py:206
  208.7 5.8 %fusion.21 = f32[576,768]{1,0:T(8,128)} fusion(bf16[576,2048]{1,0:T(8,128)(2,1)} %bitcast.26, bf16[1,2048,384]{2,1,0:T(8,128)(2,1)} %collective-permute-done.4, bf16[1,2048,384]{2,1,0:T(8,128)(2,1)} %param.25), kind=kOutput, calls=%fused_computation.39 | convolution fusion | flops 1818230784 | bytes 7274496 | tf_op jit(solution)/shard_map/dot_general | solution.py:50
  214.5 9.4 %convolution_convert_fusion = bf16[576,2048]{1,0:T(8,128)(2,1)} fusion(bf16[1,2048,384]{2,1,0:T(8,128)(2,1)} %get-tuple-element.57, bf16[1,2048,384]{2,1,0:T(8,128)(2,1)} %get-tuple-element.50, f32[576,768]{1,0:T(8,128)} %fusion.21, bf16[576,2048]{1,0:T(8,128)(2,1)} %bitcast.26, bf16[1,2048,384]{2,1,0:T(8,128)(2,1)} %get-tuple-element.58, ...), kind=kOutput, calls=%fused_computation.17 | convolution fusion | flops 3640295424 | bytes 12779520 | tf_op jit(solution)/shard_map/rf,df->rd/dot_general | solution.py:53
  224.0 11.9 %all-to-all-done.1 = bf16[4,144,2048]{2,1,0:T(8,128)(2,1)} async-done(((bf16[4,144,2048]{2,1,0:T(8,128)(2,1)}), bf16[4,144,2048]{2,1,0:T(8,128)(2,1)}, u32[]{:S(2)}, u32[]{:S(2)}) %all-to-all-start.1) | async-done | bytes 2359328 | tf_op jit(solution)/shard_map/all_to_all | solution.py:206
  235.8 4.5 %all-to-all-start.3 = ((bf16[4,144,2048]{2,1,0:T(8,128)(2,1)}), bf16[4,144,2048]{2,1,0:T(8,128)(2,1)}, u32[]{:S(2)}, u32[]{:S(2)}) async-start(bf16[4,144,2048]{2,1,0:T(8,128)(2,1)} %bitcast.123), calls=%async_computation.6 | async-start | bytes 4718592 | tf_op jit(solution)/shard_map/all_to_all | solution.py:206
  240.6 2.9 fusion.50
  243.5 3.7 %fusion.9 = bf16[256,2048]{1,0:T(8,128)(2,1)} fusion(f32[256,2048]{1,0:T(8,128)S(1)} %fusion.50, bf16[576,2048]{1,0:T(8,128)(2,1)} %bitcast.21, f32[576,256]{1,0:T(8,128)S(1)} %copy-done.3), kind=kOutput, calls=%fused_computation.23 | convolution fusion | flops 605618176 | bytes 6094848 | tf_op jit(solution)/shard_map/dot_general | solution.py:214
  249.6 19.3 %all-to-all-done.3 = bf16[4,144,2048]{2,1,0:T(8,128)(2,1)} async-done(((bf16[4,144,2048]{2,1,0:T(8,128)(2,1)}), bf16[4,144,2048]{2,1,0:T(8,128)(2,1)}, u32[]{:S(2)}, u32[]{:S(2)}) %all-to-all-start.3) | async-done | bytes 2359328 | tf_op jit(solution)/shard_map/all_to_all | solution.py:206
  268.9 2.7 fusion.47
  271.6 4.2 %fusion.10 = bf16[256,2048]{1,0:T(8,128)(2,1)} fusion(f32[256,2048]{1,0:T(8,128)S(1)} %fusion.47, bf16[576,2048]{1,0:T(8,128)(2,1)} %bitcast.28, f32[576,256]{1,0:T(8,128)} %copy-done.4), kind=kOutput, calls=%fused_computation.24 | convolution fusion | flops 605618176 | bytes 6094848 | tf_op jit(solution)/shard_map/dot_general | solution.py:214
  275.9 26.5 %reduce-scatter.11.cloned.1.call-done = bf16[1,64,2048]{2,1,0:T(8,128)(2,1)} async-done(((bf16[4,64,2048]{2,1,0:T(8,128)(2,1)}), bf16[1,64,2048]{2,1,0:T(8,128)(2,1)}) %reduce-scatter.11.cloned.1.call-update) | async-done | bytes 262160 | tf_op jit(solution)/shard_map/reduce_scatter | solution.py:216
  302.3 1.9 add_convert_fusion
  (110 shorter events, 27.1 us)
Async XLA Ops:
  6.5 17.7 %copy-start = (bf16[1024,1024]{1,0:T(8,128)(2,1)S(1)}, bf16[1024,1024]{1,0:T(8,128)(2,1)}, u32[]{:S(2)}) copy-start(bf16[1024,1024]{1,0:T(8,128)(2,1)} %param.20) | copy-start | bytes 6291460
  6.5 45.4 %reduce-scatter.5.cloned.1.call-start = ((), (), s32[]{:S(2)}) async-start(), calls=%async_computation.8 | async-start | bytes 1310720 | tf_op jit(solution)/shard_map/reduce_scatter | solution.py:123
  6.5 12.0 %collective-permute-start.1 = (s32[2,256]{1,0:T(2,128)}, s32[2,256]{1,0:T(2,128)S(1)}, u32[]{:S(2)}, u32[]{:S(2)}) collective-permute-start(s32[2,256]{1,0:T(2,128)} %param.17), channel_id=1, source_target_pairs={{0,16},{16,0},{1,17},{17,1},{2,18},{18,2},{3,19},{19,3},{4,20},{20... | collective-permute-start | bytes 6152 | tf_op jit(solution)/shard_map/ppermute | solution.py:43
  12.6 7.8 %collective-permute-start = (bf16[2,256,256]{2,1,0:T(8,128)(2,1)S(1)}, bf16[2,256,256]{2,1,0:T(8,128)(2,1)S(1)}, u32[]{:S(2)}, u32[]{:S(2)}) collective-permute-start(bf16[2,256,256]{2,1,0:T(8,128)(2,1)S(1)} %pad_maximum_fusion.2), channel_id=1, source_target_pairs={{0,16},{16,0},{1,17},{17,1},{2,18},{18,2},{3,19},{19,3},{4,20},{20... | collective-permute-start | bytes 786440 | tf_op jit(solution)/shard_map/ppermute | solution.py:43
  12.8 3.8 %copy-start.11 = (f32[128]{0:T(128)S(1)}, f32[128]{0:T(128)}, u32[]{:S(2)}) copy-start(f32[128]{0:T(128)} %param.18) | copy-start | bytes 1540
  14.3 1.4 copy-start.2
  16.3 2.2 copy-start.9
  16.3 4.1 %copy-start.6 = (bf16[2,256,128]{2,1,0:T(8,128)(2,1)S(1)}, bf16[2,256,128]{2,1,0:T(8,128)(2,1)}, u32[]{:S(2)}) copy-start(bf16[2,256,128]{2,1,0:T(8,128)(2,1)} %param.16) | copy-start | bytes 393220
  26.6 54.0 %reduce-scatter.7.cloned.1.call-start = ((), (), s32[]{:S(2)}) async-start(), calls=%async_computation.9 | async-start | bytes 1310720 | tf_op jit(solution)/shard_map/reduce_scatter | solution.py:123
  26.6 23.9 %collective-permute-start.2 = (bf16[2,256,8,128]{1,3,2,0:T(8,128)(2,1)S(1)}, bf16[2,256,8,128]{1,3,2,0:T(8,128)(2,1)}, u32[]{:S(2)}, u32[]{:S(2)}) collective-permute-start(bf16[2,256,8,128]{1,3,2,0:T(8,128)(2,1)S(1)} %fusion.18), channel_id=1, source_target_pairs={{0,16},{16,0},{1,17},{17,1},{2,18},{18,2},{3,19},{19,3},{4,20},{20... | collective-permute-start | bytes 3145736 | tf_op jit(solution)/shard_map/ppermute | solution.py:43
  52.0 5.1 %copy-start.10 = (s32[2,256,8]{1,2,0:T(8,128)S(1)}, s32[2,256,8]{1,2,0:T(8,128)}, u32[]{:S(2)}) copy-start(s32[2,256,8]{1,2,0:T(8,128)} %param.24) | copy-start | bytes 49156
  52.0 45.7 %copy-start.7 = (bf16[2,64,1024]{2,1,0:T(8,128)(2,1)S(1)}, bf16[2,64,1024]{2,1,0:T(8,128)(2,1)}, u32[]{:S(2)}) copy-start(bf16[2,64,1024]{2,1,0:T(8,128)(2,1)} %reduce-scatter.5.cloned.1.call-done) | copy-start | bytes 786436
  55.5 74.2 %all-gather.3.cloned.1.call-start = ((), (), s32[]{:S(2)}) async-start(), calls=%async_computation.10 | async-start | bytes 1392640 | tf_op jit(solution)/shard_map/all_gather | solution.py:167
  55.6 44.1 %collective-permute-start.4 = (bf16[1,2048,384]{2,1,0:T(8,128)(2,1)}, bf16[1,2048,384]{2,1,0:T(8,128)(2,1)}, u32[]{:S(2)}, u32[]{:S(2)}) collective-permute-start(bf16[1,2048,384]{2,1,0:T(8,128)(2,1)} %param.25), channel_id=1, source_target_pairs={{0,16},{16,0},{1,17},{17,1},{2,18},{18,2},{3,19},{19,3},{4,20},{20... | collective-permute-start | bytes 4718600 | tf_op jit(solution)/shard_map/ppermute | solution.py:43
  80.5 17.1 %collective-permute-start.3 = (bf16[2,64,1024]{2,1,0:T(8,128)(2,1)}, bf16[2,64,1024]{2,1,0:T(8,128)(2,1)S(1)}, u32[]{:S(2)}, u32[]{:S(2)}) collective-permute-start(bf16[2,64,1024]{2,1,0:T(8,128)(2,1)} %reduce-scatter.7.cloned.1.call-done), channel_id=1, source_target_pairs={{0,16},{16,0},{1,17},{17,1},{2,18},{18,2},{3,19},{19,3},{4,20},{20... | collective-permute-start | bytes 786440 | tf_op jit(solution)/shard_map/ppermute | solution.py:127
  98.0 1.5 copy-start.8
  100.6 63.3 %all-gather.5.cloned.1.call-start = ((), (), s32[]{:S(2)}) async-start(), calls=%async_computation.12 | async-start | bytes 1392640 | tf_op jit(solution)/shard_map/all_gather | solution.py:167
  104.4 69.8 %collective-permute-start.5 = (bf16[1,2048,768]{2,1,0:T(8,128)(2,1)}, bf16[1,2048,768]{2,1,0:T(8,128)(2,1)}, u32[]{:S(2)}, u32[]{:S(2)}) collective-permute-start(bf16[1,2048,768]{2,1,0:T(8,128)(2,1)} %pad_maximum_fusion), channel_id=1, source_target_pairs={{0,16},{16,0},{1,17},{17,1},{2,18},{18,2},{3,19},{19,3},{4,20},{20... | collective-permute-start | bytes 9437192 | tf_op jit(solution)/shard_map/ppermute | solution.py:43
  135.2 4.7 %copy-start.5 = (bf16[256,2176]{1,0:T(8,128)(2,1)S(1)}, bf16[256,2176]{1,0:T(8,128)(2,1)}, u32[]{:S(2)}) copy-start(bf16[256,2176]{1,0:T(8,128)(2,1)} %all-gather.3.cloned.1.call-done) | copy-start | bytes 3342340
  135.2 4.7 %copy-start.13 = (bf16[2048,16]{0,1:T(8,128)(2,1)S(1)}, bf16[2048,16]{0,1:T(8,128)(2,1)}, u32[]{:S(2)}) copy-start(bf16[2048,16]{0,1:T(8,128)(2,1)} %param.23) | copy-start | bytes 196612
  135.2 34.1 %all-to-all-start = ((bf16[4,144,2048]{2,1,0:T(8,128)(2,1)}), bf16[4,144,2048]{2,1,0:T(8,128)(2,1)}, u32[]{:S(2)}, u32[]{:S(2)}) async-start(bf16[4,144,2048]{2,1,0:T(8,128)(2,1)} %bitcast.117), calls=%async_computation.2 | async-start | bytes 4718592 | tf_op jit(solution)/shard_map/all_to_all | solution.py:197
  169.4 4.8 %copy-start.12 = (bf16[1,2048,384]{2,1,0:T(8,128)(2,1)S(1)}, bf16[1,2048,384]{2,1,0:T(8,128)(2,1)}, u32[]{:S(2)}) copy-start(bf16[1,2048,384]{2,1,0:T(8,128)(2,1)} %param.25) | copy-start | bytes 4718596
  169.4 33.4 %all-to-all-start.2 = ((bf16[4,144,2048]{2,1,0:T(8,128)(2,1)}), bf16[4,144,2048]{2,1,0:T(8,128)(2,1)}, u32[]{:S(2)}, u32[]{:S(2)}) async-start(bf16[4,144,2048]{2,1,0:T(8,128)(2,1)} %bitcast.118), calls=%async_computation.5 | async-start | bytes 4718592 | tf_op jit(solution)/shard_map/all_to_all | solution.py:197
  202.7 33.1 %all-to-all-start.1 = ((bf16[4,144,2048]{2,1,0:T(8,128)(2,1)}), bf16[4,144,2048]{2,1,0:T(8,128)(2,1)}, u32[]{:S(2)}, u32[]{:S(2)}) async-start(bf16[4,144,2048]{2,1,0:T(8,128)(2,1)} %bitcast.124), calls=%async_computation.3 | async-start | bytes 4718592 | tf_op jit(solution)/shard_map/all_to_all | solution.py:206
  235.8 33.1 %all-to-all-start.3 = ((bf16[4,144,2048]{2,1,0:T(8,128)(2,1)}), bf16[4,144,2048]{2,1,0:T(8,128)(2,1)}, u32[]{:S(2)}, u32[]{:S(2)}) async-start(bf16[4,144,2048]{2,1,0:T(8,128)(2,1)} %bitcast.123), calls=%async_computation.6 | async-start | bytes 4718592 | tf_op jit(solution)/shard_map/all_to_all | solution.py:206
  240.3 35.5 %reduce-scatter.9.cloned.1.call-start = ((), (), s32[]{:S(2)}) async-start(), calls=%async_computation.11 | async-start | bytes 1310720 | tf_op jit(solution)/shard_map/reduce_scatter | solution.py:216
  240.6 2.9 copy-start.3
  247.3 55.1 %reduce-scatter.11.cloned.1.call-start = ((), (), s32[]{:S(2)}) async-start(), calls=%async_computation.13 | async-start | bytes 1310720 | tf_op jit(solution)/shard_map/reduce_scatter | solution.py:216
  249.6 19.3 %copy-start.4 = (f32[576,256]{1,0:T(8,128)}, f32[576,256]{1,0:T(8,128)S(1)}, u32[]{:S(2)}) copy-start(f32[576,256]{1,0:T(8,128)S(1)} %select_reduce_fusion) | copy-start | bytes 1769476
  271.6 32.7 %copy-start.1 = (bf16[1024,1024]{1,0:T(8,128)(2,1)S(1)}, bf16[1024,1024]{1,0:T(8,128)(2,1)}, u32[]{:S(2)}) copy-start(bf16[1024,1024]{1,0:T(8,128)(2,1)} %param.20) | copy-start | bytes 6291460
Sparse Core Ops, SparseCore 0:
  26.7 25.2 reduce-scatter.4
  55.6 24.8 reduce-scatter.6
  100.7 29.0 all-gather.2
  135.3 28.5 all-gather.4
  247.4 26.8 reduce-scatter.8
  276.5 25.7 reduce-scatter.10
